TPU v7x, 256 devices: a whole 4x4x8 slice. The times are simulated.
256 devices in a mesh: seg: 8 (over y, core), sec: 32 (over x, z).
Axes of the slice: x: 4, y: 4, z: 8, core: 2. Of those that a mesh axis runs over, the one named last changes fastest.
Arguments:
- theta_in: float32 [8, 64, 128, 128], P('seg', 'sec'), may hold values from -6 to 6
- left_env: float32 [9, 64, 128, 128], P(None, 'sec'), may hold values from -0.0017089844 to 0.0017089844
- site_maps: float32 [8, 64, 128, 128], P('seg', 'sec'), may hold values from -1 to 2, as said below
- right_env: float32 [8, 9, 64, 128, 128], P('seg', None, 'sec'), may hold values from -8 to 8
- mpo_mask: int32 [9, 64], P(None, 'sec'), may hold values 0 or 1
- ranks: int32 [8, 64], P('seg', 'sec'), may hold values from 64 to 128
Outputs:
- theta_out: float32 [8, 64, 128, 128], P('seg', 'sec')
- density: float32 [8, 64, 128, 128], P('seg', 'sec')
Inputs may be any that keep to these rules, and one draw needn't show every extreme that they name: `site_maps`: each block of a segment's map is the identity plus a full matrix of entries of size about 1 / (4 sqrt(128)).
All inputs are finite; a program needn't handle non-finite values. No bound on the sum of `mpo_mask` on one device may be relied on, other than what follows from the above.
Results may differ from a plain program's by a relative error of at most 0.0003.
Values sent between devices are 32-bit elements; how exact they have to be, the bound alone decides.
No kernel may reach another device: no remote copies, remote signals or barrier semaphores. Data moves between devices by JAX's collectives and lax.ppermute only.
A program may use at most 64 MiB of HBM per device.

v0:
```python
import jax
import jax.numpy as jnp
from jax import lax
from jax.sharding import PartitionSpec as P

ITERS = 4


HIGH = lax.Precision.HIGHEST
EPS = 1e-06


def from_behind(block, axis, distance):
    devices = range(lax.axis_size(axis))
    route = [(i - distance, i) for i in devices if i - distance in devices]
    return lax.ppermute(block, axis, route)


def extended(block, sides, width):
    for axis, dim in sides:
        count = lax.axis_size(axis)
        forward = [(i, i + 1) for i in range(count - 1)]
        backward = [(target, source) for source, target in forward]
        low = lax.ppermute(
            lax.slice_in_dim(block, block.shape[dim] - width, None, axis=dim), axis, forward
        )
        high = lax.ppermute(lax.slice_in_dim(block, 0, width, axis=dim), axis, backward)
        block = jnp.concatenate([low, block, high], axis=dim)
    return block


def advance_env(env, maps):
    partial_env = jnp.einsum("wkac,kcd->wkad", env, maps, precision=HIGH)
    return jnp.einsum("kab,wkad->wkbd", maps, partial_env, precision=HIGH)


def shifted_terms(padded, count, blocks):
    pieces = []
    for term in range(count):
        offset = 1 + term % 3 - 1
        pieces.append(padded[term, offset : offset + blocks])
    return jnp.stack(pieces, axis=0)


def per_device(theta_in, left_env, site_maps, right_env, mpo_mask, ranks):
    vector = theta_in[0]
    maps = site_maps[0]
    right = right_env[0]
    terms = right.shape[0]
    blocks = vector.shape[0]
    width = vector.shape[1]
    segment = lax.axis_index("seg")
    carried = left_env
    for step in range(lax.axis_size("seg") - 1):
        moved = from_behind(advance_env(carried, maps), "seg", 1)
        carried = jnp.where(segment == step + 1, moved, carried)
    weighted = carried * mpo_mask.astype(jnp.float32)[:, :, None, None]
    cells = lax.axis_size("sec") * blocks * width * width
    for step in range(ITERS):
        products = jnp.einsum("kab,wkbc->wkac", vector, right, precision=HIGH)
        padded = extended(products, (("sec", 1),), 1)
        gathered = shifted_terms(padded, terms, blocks)
        image = jnp.einsum("wkab,wkbc->kac", weighted, gathered, precision=HIGH)
        total = lax.psum(jnp.sum(image * image), "sec")
        vector = image * lax.rsqrt(total / cells + EPS)
    rows = lax.broadcasted_iota(jnp.int32, (blocks, width), 1) < ranks[0][:, None]
    trimmed = vector * rows.astype(jnp.float32)[:, :, None]
    density = jnp.einsum("kab,kcb->kac", trimmed, trimmed, precision=HIGH) / width
    return (vector[None], density[None])


def solution(mesh):
    return jax.shard_map(
        per_device,
        mesh=mesh,
        in_specs=(
            P("seg", "sec", None, None),
            P(None, "sec", None, None),
            P("seg", "sec", None, None),
            P("seg", None, "sec", None, None),
            P(None, "sec"),
            P("seg", "sec"),
        ),
        out_specs=(P("seg", "sec", None, None), P("seg", "sec", None, None)),
        check_vma=False,
    )
```

profile of v0, /device:TPU:8, one launch (start us, length us, event | category | flops | bytes accessed | tf_op | source)
XLA Modules:
  0.0 510.5 jit_solution(14464493180021632282)
XLA Ops:
  0.7 1.7 copy.8
  2.4 1.1 convolution_bitcast_fusion.17
  3.6 2.1 convolution_bitcast_fusion.16
  5.7 1.9 collective-permute-start
  7.7 15.9 %collective-permute-done = f32[9,2,128,128]{2,3,0,1:T(8,128)} collective-permute-done((f32[9,2,128,128]{2,3,0,1:T(8,128)}, f32[9,2,128,128]{2,3,0,1:T(8,128)}, u32[]{:S(2)}, u32[]{:S(2)}) %collective-permute-start) | collective-permute-done | bytes 1179680 | tf_op jit(solution)/shard_map/ppermute | solution.py:16
  23.6 1.4 broadcast_select_fusion
  25.0 1.2 convolution_bitcast_fusion.15
  26.2 2.1 convolution_bitcast_fusion.14
  28.3 1.9 collective-permute-start.1
  30.2 15.9 %collective-permute-done.1 = f32[9,2,128,128]{2,3,0,1:T(8,128)} collective-permute-done((f32[9,2,128,128]{2,3,0,1:T(8,128)}, f32[9,2,128,128]{2,3,0,1:T(8,128)}, u32[]{:S(2)}, u32[]{:S(2)}) %collective-permute-start.1) | collective-permute-done | bytes 1179680 | tf_op jit(solution)/shard_map/ppermute | solution.py:16
  46.1 2.5 convolution_bitcast_fusion.13
  48.6 1.1 convolution_bitcast_fusion.12
  49.7 1.9 collective-permute-start.2
  51.7 15.7 %collective-permute-done.2 = f32[9,2,128,128]{2,3,0,1:T(8,128)} collective-permute-done((f32[9,2,128,128]{2,3,0,1:T(8,128)S(1)}, f32[9,2,128,128]{2,3,0,1:T(8,128)}, u32[]{:S(2)}, u32[]{:S(2)}) %collective-permute-start.2) | collective-permute-done | bytes 1179680 | tf_op jit(solution)/shard_map/ppermute | solution.py:16
  67.4 1.5 broadcast_select_fusion.2
  68.8 1.2 convolution_bitcast_fusion.11
  70.0 2.2 convolution_bitcast_fusion.10
  72.2 2.1 collective-permute-start.3
  74.3 15.7 %collective-permute-done.3 = f32[9,2,128,128]{2,3,0,1:T(8,128)} collective-permute-done((f32[9,2,128,128]{2,3,0,1:T(8,128)}, f32[9,2,128,128]{2,3,0,1:T(8,128)}, u32[]{:S(2)}, u32[]{:S(2)}) %collective-permute-start.3) | collective-permute-done | bytes 1179680 | tf_op jit(solution)/shard_map/ppermute | solution.py:16
  90.0 1.2 convolution_bitcast_fusion.9
  91.2 2.1 convolution_bitcast_fusion.8
  93.4 1.9 collective-permute-start.4
  95.3 15.9 %collective-permute-done.4 = f32[9,2,128,128]{2,3,0,1:T(8,128)} collective-permute-done((f32[9,2,128,128]{2,3,0,1:T(8,128)}, f32[9,2,128,128]{2,3,0,1:T(8,128)}, u32[]{:S(2)}, u32[]{:S(2)}) %collective-permute-start.4) | collective-permute-done | bytes 1179680 | tf_op jit(solution)/shard_map/ppermute | solution.py:16
  111.4 1.2 convolution_bitcast_fusion.7
  112.6 2.1 convolution_bitcast_fusion.6
  114.7 1.9 collective-permute-start.5
  116.7 2.0 convolution_bitcast_fusion.3
  118.7 1.1 fusion.44
  119.8 4.6 collective-permute-start.7
  124.5 1.3 collective-permute-start.8
  125.8 9.8 %collective-permute-done.7 = f32[9,1,128,128]{2,3,0,1:T(8,128)} collective-permute-done((f32[9,1,128,128]{2,3,0,1:T(8,128)}, f32[9,1,128,128]{2,3,0,1:T(8,128)}, u32[]{:S(2)}, u32[]{:S(2)}) %collective-permute-start.7) | collective-permute-done | bytes 589856 | tf_op jit(solution)/shard_map/ppermute | solution.py:24
  135.6 0.8 maximum_dynamic-update-slice_fusion.15
  136.5 1.2 convolution_bitcast_fusion.5
  137.7 1.1 convolution_bitcast_fusion.4
  138.8 4.3 collective-permute-start.6
  143.2 0.9 maximum_dynamic-update-slice_fusion.13
  144.1 0.9 fusion.12
  145.0 12.1 %collective-permute-done.6 = f32[9,2,128,128]{2,3,0,1:T(8,128)S(1)} collective-permute-done((f32[9,2,128,128]{2,3,0,1:T(8,128)S(1)}, f32[9,2,128,128]{2,3,0,1:T(8,128)S(1)}, u32[]{:S(2)}, u32[]{:S(2)}) %collective-permute-start.6) | collective-permute-done | bytes 1179680 | tf_op jit(solution)/shard_map/ppermute | solution.py:16
  157.1 0.2 select_multiply_fusion
  157.3 2.7 multiply_reduce_fusion.3
  159.9 78.6 %psum.28 = f32[]{:T(128)} all-reduce(f32[]{:T(128)} %get-tuple-element.10), channel_id=1, replica_groups=mesh['seg'=8,'sec'=32] {'sec'}, use_global_device_ids=true, to_apply=%region_1.2 | all-reduce | flops 1 | bytes 8 | tf_op jit(solution)/shard_map/psum | solution.py:64
  239.2 1.1 convolution_bitcast_fusion.2
  240.4 1.3 collective-permute-start.9
  241.7 1.3 collective-permute-start.10
  243.0 6.1 %collective-permute-done.9 = f32[9,1,128,128]{3,2,0,1:T(8,128)S(1)} collective-permute-done((f32[9,1,128,128]{3,2,0,1:T(8,128)S(1)}, f32[9,1,128,128]{3,2,0,1:T(8,128)S(1)}, u32[]{:S(2)}, u32[]{:S(2)}) %collective-permute-start.9) | collective-permute-done | bytes 589856 | tf_op jit(solution)/shard_map/ppermute | solution.py:24
  249.2 4.4 collective-permute-done.10
  253.7 2.6 multiply_reduce_fusion.2
  256.4 70.2 %psum.29 = f32[]{:T(128)} all-reduce(f32[]{:T(128)} %get-tuple-element.12), channel_id=1, replica_groups=mesh['seg'=8,'sec'=32] {'sec'}, use_global_device_ids=true, to_apply=%region_3.4 | all-reduce | flops 1 | bytes 8 | tf_op jit(solution)/shard_map/psum | solution.py:64
  327.3 1.1 convolution_bitcast_fusion.1
  328.5 4.0 collective-permute-start.11
  332.5 1.3 collective-permute-start.12
  333.8 6.1 %collective-permute-done.11 = f32[9,1,128,128]{3,2,0,1:T(8,128)S(1)} collective-permute-done((f32[9,1,128,128]{3,2,0,1:T(8,128)S(1)}, f32[9,1,128,128]{3,2,0,1:T(8,128)S(1)}, u32[]{:S(2)}, u32[]{:S(2)}) %collective-permute-start.11) | collective-permute-done | bytes 589856 | tf_op jit(solution)/shard_map/ppermute | solution.py:24
  339.9 4.4 collective-permute-done.12
  344.5 2.6 multiply_reduce_fusion.1
  347.1 70.2 %psum.30 = f32[]{:T(128)} all-reduce(f32[]{:T(128)} %get-tuple-element.14), channel_id=1, replica_groups=mesh['seg'=8,'sec'=32] {'sec'}, use_global_device_ids=true, to_apply=%region_5.6 | all-reduce | flops 1 | bytes 8 | tf_op jit(solution)/shard_map/psum | solution.py:64
  418.0 1.1 convolution_bitcast_fusion
  419.2 4.0 collective-permute-start.13
  423.2 1.6 collective-permute-start.14
  424.8 5.8 %collective-permute-done.13 = f32[9,1,128,128]{3,2,0,1:T(8,128)S(1)} collective-permute-done((f32[9,1,128,128]{3,2,0,1:T(8,128)S(1)}, f32[9,1,128,128]{3,2,0,1:T(8,128)S(1)}, u32[]{:S(2)}, u32[]{:S(2)}) %collective-permute-start.13) | collective-permute-done | bytes 589856 | tf_op jit(solution)/shard_map/ppermute | solution.py:24
  430.7 4.4 collective-permute-done.14
  435.2 2.6 multiply_reduce_fusion
  437.8 70.2 %psum.31 = f32[]{:T(128)} all-reduce(f32[]{:T(128)} %get-tuple-element.16), channel_id=1, replica_groups=mesh['seg'=8,'sec'=32] {'sec'}, use_global_device_ids=true, to_apply=%region_7.8 | all-reduce | flops 1 | bytes 8 | tf_op jit(solution)/shard_map/psum | solution.py:64
  508.7 0.7 multiply_bitcast_fusion
  509.4 1.1 fusion
  (59 shorter events, 1.0 us)
Async XLA Ops:
  0.6 116.0 %copy-start = (f32[1,9,2,128,128]{4,3,2,1,0:T(8,128)S(1)}, f32[1,9,2,128,128]{4,3,2,1,0:T(8,128)}, u32[]{:S(2)}) copy-start(f32[1,9,2,128,128]{4,3,2,1,0:T(8,128)} %param.9) | copy-start | bytes 3538948
  0.6 1.8 copy-start.1
  2.4 1.2 copy-start.5
  5.7 17.8 %collective-permute-start = (f32[9,2,128,128]{2,3,0,1:T(8,128)}, f32[9,2,128,128]{2,3,0,1:T(8,128)}, u32[]{:S(2)}, u32[]{:S(2)}) collective-permute-start(f32[9,2,128,128]{2,3,0,1:T(8,128)} %convolution_bitcast_fusion.16), channel_id=1, source_target_pairs={{0,32},{32,64},{64,96},{96,128},{128,160},{160,192},{192,224},{1,3... | collective-permute-start | bytes 3538952 | tf_op jit(solution)/shard_map/ppermute | solution.py:16
  25.0 21.2 %copy-start.4 = (f32[9,2,128,128]{2,3,0,1:T(8,128)}, f32[9,2,128,128]{2,3,0,1:T(8,128)S(1)}, u32[]{:S(2)}) copy-start(f32[9,2,128,128]{2,3,0,1:T(8,128)S(1)} %broadcast_select_fusion) | copy-start | bytes 3538948
  28.3 17.8 %collective-permute-start.1 = (f32[9,2,128,128]{2,3,0,1:T(8,128)}, f32[9,2,128,128]{2,3,0,1:T(8,128)}, u32[]{:S(2)}, u32[]{:S(2)}) collective-permute-start(f32[9,2,128,128]{2,3,0,1:T(8,128)} %convolution_bitcast_fusion.14), channel_id=1, source_target_pairs={{0,32},{32,64},{64,96},{96,128},{128,160},{160,192},{192,224},{1,3... | collective-permute-start | bytes 3538952 | tf_op jit(solution)/shard_map/ppermute | solution.py:16
  49.7 17.6 %collective-permute-start.2 = (f32[9,2,128,128]{2,3,0,1:T(8,128)S(1)}, f32[9,2,128,128]{2,3,0,1:T(8,128)}, u32[]{:S(2)}, u32[]{:S(2)}) collective-permute-start(f32[9,2,128,128]{2,3,0,1:T(8,128)S(1)} %convolution_bitcast_fusion.12), channel_id=1, source_target_pairs={{0,32},{32,64},{64,96},{96,128},{128,160},{160,192},{192,224},{1,3... | collective-permute-start | bytes 3538952 | tf_op jit(solution)/shard_map/ppermute | solution.py:16
  72.2 17.8 %collective-permute-start.3 = (f32[9,2,128,128]{2,3,0,1:T(8,128)}, f32[9,2,128,128]{2,3,0,1:T(8,128)}, u32[]{:S(2)}, u32[]{:S(2)}) collective-permute-start(f32[9,2,128,128]{2,3,0,1:T(8,128)} %convolution_bitcast_fusion.10), channel_id=1, source_target_pairs={{0,32},{32,64},{64,96},{96,128},{128,160},{160,192},{192,224},{1,3... | collective-permute-start | bytes 3538952 | tf_op jit(solution)/shard_map/ppermute | solution.py:16
  93.4 17.8 %collective-permute-start.4 = (f32[9,2,128,128]{2,3,0,1:T(8,128)}, f32[9,2,128,128]{2,3,0,1:T(8,128)}, u32[]{:S(2)}, u32[]{:S(2)}) collective-permute-start(f32[9,2,128,128]{2,3,0,1:T(8,128)} %convolution_bitcast_fusion.8), channel_id=1, source_target_pairs={{0,32},{32,64},{64,96},{96,128},{128,160},{160,192},{192,224},{1,3... | collective-permute-start | bytes 3538952 | tf_op jit(solution)/shard_map/ppermute | solution.py:16
  111.4 1.2 copy-start.2
  112.6 4.1 copy-start.6
  114.7 21.7 %collective-permute-start.5 = (f32[9,2,128,128]{2,3,0,1:T(8,128)}, f32[9,2,128,128]{2,3,0,1:T(8,128)}, u32[]{:S(2)}, u32[]{:S(2)}) collective-permute-start(f32[9,2,128,128]{2,3,0,1:T(8,128)} %convolution_bitcast_fusion.6), channel_id=1, source_target_pairs={{0,32},{32,64},{64,96},{96,128},{128,160},{160,192},{192,224},{1,3... | collective-permute-start | bytes 3538952 | tf_op jit(solution)/shard_map/ppermute | solution.py:16
  118.7 7.1 %copy-start.7 = (s32[9,2]{0,1:T(2,128)S(1)}, s32[9,2]{0,1:T(2,128)}, u32[]{:S(2)}) copy-start(s32[9,2]{0,1:T(2,128)} %param.10) | copy-start | bytes 220
  119.8 15.8 %collective-permute-start.7 = (f32[9,1,128,128]{2,3,0,1:T(8,128)}, f32[9,1,128,128]{2,3,0,1:T(8,128)}, u32[]{:S(2)}, u32[]{:S(2)}) collective-permute-start(f32[9,1,128,128]{2,3,0,1:T(8,128)} %get-tuple-element.9), channel_id=1, source_target_pairs={{0,1},{1,2},{2,3},{3,4},{4,5},{5,6},{6,7},{7,8},{8,9},{9,10},{10,1... | collective-permute-start | bytes 1769480 | tf_op jit(solution)/shard_map/ppermute | solution.py:24
  124.5 18.7 %collective-permute-start.8 = (f32[9,1,128,128]{2,3,0,1:T(8,128)}, f32[9,1,128,128]{2,3,0,1:T(8,128)S(1)}, u32[]{:S(2)}, u32[]{:S(2)}) collective-permute-start(f32[9,1,128,128]{2,3,0,1:T(8,128)} %get-tuple-element.8), channel_id=1, source_target_pairs={{1,0},{2,1},{3,2},{4,3},{5,4},{6,5},{7,6},{8,7},{9,8},{10,9},{11,1... | collective-permute-start | bytes 1769480 | tf_op jit(solution)/shard_map/ppermute | solution.py:27
  125.8 10.7 %copy-start.3 = (f32[9,2,128,128]{2,3,0,1:T(8,128)S(1)}, f32[9,2,128,128]{2,3,0,1:T(8,128)}, u32[]{:S(2)}) copy-start(f32[9,2,128,128]{2,3,0,1:T(8,128)} %copy-done.2) | copy-start | bytes 3538948
  138.8 18.2 %collective-permute-start.6 = (f32[9,2,128,128]{2,3,0,1:T(8,128)S(1)}, f32[9,2,128,128]{2,3,0,1:T(8,128)S(1)}, u32[]{:S(2)}, u32[]{:S(2)}) collective-permute-start(f32[9,2,128,128]{2,3,0,1:T(8,128)S(1)} %convolution_bitcast_fusion.4), channel_id=1, source_target_pairs={{0,32},{32,64},{64,96},{96,128},{128,160},{160,192},{192,224},{1,3... | collective-permute-start | bytes 3538952 | tf_op jit(solution)/shard_map/ppermute | solution.py:16
  240.4 8.8 %collective-permute-start.9 = (f32[9,1,128,128]{3,2,0,1:T(8,128)S(1)}, f32[9,1,128,128]{3,2,0,1:T(8,128)S(1)}, u32[]{:S(2)}, u32[]{:S(2)}) collective-permute-start(f32[9,1,128,128]{3,2,0,1:T(8,128)S(1)} %get-tuple-element.7), channel_id=1, source_target_pairs={{0,1},{1,2},{2,3},{3,4},{4,5},{5,6},{6,7},{7,8},{8,9},{9,10},{10,1... | collective-permute-start | bytes 1769480 | tf_op jit(solution)/shard_map/ppermute | solution.py:24
  241.7 11.9 %collective-permute-start.10 = (f32[9,1,128,128]{3,2,0,1:T(8,128)S(1)}, f32[9,1,128,128]{3,2,0,1:T(8,128)S(1)}, u32[]{:S(2)}, u32[]{:S(2)}) collective-permute-start(f32[9,1,128,128]{3,2,0,1:T(8,128)S(1)} %get-tuple-element.6), channel_id=1, source_target_pairs={{1,0},{2,1},{3,2},{4,3},{5,4},{6,5},{7,6},{8,7},{9,8},{10,9},{11,1... | collective-permute-start | bytes 1769480 | tf_op jit(solution)/shard_map/ppermute | solution.py:27
  328.5 11.4 %collective-permute-start.11 = (f32[9,1,128,128]{3,2,0,1:T(8,128)S(1)}, f32[9,1,128,128]{3,2,0,1:T(8,128)S(1)}, u32[]{:S(2)}, u32[]{:S(2)}) collective-permute-start(f32[9,1,128,128]{3,2,0,1:T(8,128)S(1)} %get-tuple-element.5), channel_id=1, source_target_pairs={{0,1},{1,2},{2,3},{3,4},{4,5},{5,6},{6,7},{7,8},{8,9},{9,10},{10,1... | collective-permute-start | bytes 1769480 | tf_op jit(solution)/shard_map/ppermute | solution.py:24
  332.5 11.9 %collective-permute-start.12 = (f32[9,1,128,128]{3,2,0,1:T(8,128)S(1)}, f32[9,1,128,128]{3,2,0,1:T(8,128)S(1)}, u32[]{:S(2)}, u32[]{:S(2)}) collective-permute-start(f32[9,1,128,128]{3,2,0,1:T(8,128)S(1)} %get-tuple-element.4), channel_id=1, source_target_pairs={{1,0},{2,1},{3,2},{4,3},{5,4},{6,5},{7,6},{8,7},{9,8},{10,9},{11,1... | collective-permute-start | bytes 1769480 | tf_op jit(solution)/shard_map/ppermute | solution.py:27
  419.1 5.6 %copy-start.8 = (s32[1,2]{1,0:T(1,128)S(1)}, s32[1,2]{1,0:T(1,128)}, u32[]{:S(2)}) copy-start(s32[1,2]{1,0:T(1,128)} %param.11) | copy-start | bytes 28
  419.2 11.4 %collective-permute-start.13 = (f32[9,1,128,128]{3,2,0,1:T(8,128)S(1)}, f32[9,1,128,128]{3,2,0,1:T(8,128)S(1)}, u32[]{:S(2)}, u32[]{:S(2)}) collective-permute-start(f32[9,1,128,128]{3,2,0,1:T(8,128)S(1)} %get-tuple-element.3), channel_id=1, source_target_pairs={{0,1},{1,2},{2,3},{3,4},{4,5},{5,6},{6,7},{7,8},{8,9},{9,10},{10,1... | collective-permute-start | bytes 1769480 | tf_op jit(solution)/shard_map/ppermute | solution.py:24
  423.2 11.9 %collective-permute-start.14 = (f32[9,1,128,128]{3,2,0,1:T(8,128)S(1)}, f32[9,1,128,128]{3,2,0,1:T(8,128)S(1)}, u32[]{:S(2)}, u32[]{:S(2)}) collective-permute-start(f32[9,1,128,128]{3,2,0,1:T(8,128)S(1)} %get-tuple-element.2), channel_id=1, source_target_pairs={{1,0},{2,1},{3,2},{4,3},{5,4},{6,5},{7,6},{8,7},{9,8},{10,9},{11,1... | collective-permute-start | bytes 1769480 | tf_op jit(solution)/shard_map/ppermute | solution.py:27
where the time goes:
time: 512 us; the launch traced here: 511 us
  blocking collectives  289 us (56%)
  waiting for transfers between devices  132 us (26%)
  matrix products  39.5 us (8%)
  starting transfers between devices  35.2 us (7%)
  other arithmetic  6.77 us (1%)
    psum x4, blocking collectives, per_device(): total = lax.psum(jnp.sum(image * image), 'sec')  289 us
    ppermute x7, waiting for transfers between devices, from_behind(): return lax.ppermute(block, axis, route)  91.2 us
    ppermute x4, waiting for transfers between devices, extended(): lax.ppermute(lax.slice_in_dim(block, block.shape[dim] - width, None, axis...  27.9 us
    ppermute x7, starting transfers between devices, from_behind(): return lax.ppermute(block, axis, route)  15.9 us
    ppermute x4, starting transfers between devices, extended(): lax.ppermute(lax.slice_in_dim(block, block.shape[dim] - width, None, axis...  13.9 us
    ppermute x4, waiting for transfers between devices, extended(): lax.ppermute(lax.slice_in_dim(block, 0, width, axis=dim), axis, backward)  13.2 us
    dot_general x7, matrix products, advance_env(): return jnp.einsum('kab,wkad->wkbd', maps, partial_env, precision=HIGH)  13 us
    dot_general x4, matrix products, per_device(): image = jnp.einsum('wkab,wkbc->kac', weighted, gathered, precision=HIGH)  10.5 us
  transfers between devices with their start and end apart: 15, of which 13 were waited for; matrix products, arithmetic and copies ran while one was open for 2% of the time, Pallas kernels for 0%

commit v1 on v0

v1 whole, which is shorter than its diff:
```python
import jax
import jax.numpy as jnp
from jax import lax
from jax.sharding import PartitionSpec as P

ITERS = 4


HIGH = lax.Precision.HIGHEST
EPS = 1e-06
LIFT = 1024.0


def shifted(block, axis, step):
    count = lax.axis_size(axis)
    route = [(i, i + step) for i in range(count) if 0 <= i + step < count]
    return lax.ppermute(block, axis, route)


def gathered_sum(value, axis):
    count = lax.axis_size(axis)
    spread = jnp.broadcast_to(value.reshape(1, 1), (count, 1))
    return jnp.sum(lax.all_to_all(spread, axis, 0, 0, tiled=True))


def mm(spec, a, b):
    return jnp.einsum(spec, a, b, precision=HIGH)


def left_environment(left_env, maps):
    segments = lax.axis_size("seg")
    segment = lax.axis_index("seg")
    spread = jnp.broadcast_to(maps[None], (segments,) + maps.shape)
    every = lax.all_to_all(spread, "seg", 0, 0, tiled=True)
    width = maps.shape[-1]
    prefix = jnp.broadcast_to(jnp.eye(width, dtype=jnp.float32), maps.shape)
    for step in range(segments - 1):
        grown = mm("kab,kbc->kac", prefix, every[step])
        prefix = jnp.where(step < segment, grown, prefix)
    right_side = mm("wkbc,kcd->wkbd", left_env, prefix)
    return mm("kba,wkbd->wkad", prefix, right_side)


def apply_terms(vector, right, ordered):
    products = mm("kab,wkbc->wkac", vector, right)
    from_left = shifted(products[0::3, 1], "sec", 1)
    from_right = shifted(products[2::3, 0], "sec", -1)
    lower = jnp.stack([from_left, products[0::3, 0]], axis=1)
    upper = jnp.stack([products[2::3, 1], from_right], axis=1)
    terms = jnp.concatenate([lower, products[1::3], upper], axis=0)
    return mm("wkab,wkbc->kac", ordered, terms)


def per_device(theta_in, left_env, site_maps, right_env, mpo_mask, ranks):
    vector = theta_in[0]
    maps = site_maps[0]
    right = right_env[0]
    blocks = vector.shape[0]
    width = vector.shape[1]
    cells = lax.axis_size("sec") * blocks * width * width
    env = left_environment(left_env, maps)
    weighted = env * mpo_mask.astype(jnp.float32)[:, :, None, None]
    ordered = jnp.concatenate([weighted[0::3], weighted[1::3], weighted[2::3]], axis=0)
    current = apply_terms(vector, right, ordered)
    for step in range(ITERS):
        total = gathered_sum(jnp.sum(current * current), "sec")
        scale = lax.rsqrt(total / cells + EPS)
        if step + 1 < ITERS:
            image = apply_terms(current * LIFT, right, ordered)
            current = image * (scale / LIFT)
        else:
            current = current * scale
    rows = lax.broadcasted_iota(jnp.int32, (blocks, width), 1) < ranks[0][:, None]
    trimmed = current * rows.astype(jnp.float32)[:, :, None]
    density = mm("kab,kcb->kac", trimmed, trimmed) / width
    return (current[None], density[None])


def solution(mesh):
    return jax.shard_map(
        per_device,
        mesh=mesh,
        in_specs=(
            P("seg", "sec", None, None),
            P(None, "sec", None, None),
            P("seg", "sec", None, None),
            P("seg", None, "sec", None, None),
            P(None, "sec"),
            P("seg", "sec"),
        ),
        out_specs=(P("seg", "sec", None, None), P("seg", "sec", None, None)),
        check_vma=False,
    )
```

time: 512 us -> 144 us (0.28)
  blocking collectives: 289 us -> 0 us
  waiting for transfers between devices: 132 us -> 43.5 us
  starting transfers between devices: 35.2 us -> 53.5 us
  matrix products: 39.5 us -> 25.2 us
  local copies, waits for them, and re-layouts: 3.33 us -> 14 us
    psum x4 -> x0, blocking collectives: 289 us -> none  [per_device(): total = lax.psum(jnp.sum(image * image), 'sec')]
    ppermute x15 -> x8, waiting for transfers between devices: 132 us -> 0.02 us  [shifted(): return lax.ppermute(block, axis, route)]
    all_to_all x0 -> x5, waiting for transfers between devices: none -> 43.5 us  [the longest x4 36.3 us: gathered_sum(): return jnp.sum(lax.all_to_all(spread, axis, 0, 0, tiled=True))]
    all_to_all x0 -> x5, starting transfers between devices: none -> 35.1 us  [the longest x4 29.3 us: gathered_sum(): return jnp.sum(lax.all_to_all(spread, axis, 0, 0, tiled=True))]
    ppermute x15 -> x8, starting transfers between devices: 35.2 us -> 18.3 us  [shifted(): return lax.ppermute(block, axis, route)]
    dot_general x23 -> x18, matrix products: 39.5 us -> 25.2 us  [mm(): return jnp.einsum(spec, a, b, precision=HIGH)]
    broadcast_in_dim x0 -> x5, local copies, waits for them, and re-layouts: none -> 7.11 us  [the longest x4 5.04 us: gathered_sum(): spread = jnp.broadcast_to(value.reshape(1, 1), (count, 1))]
  transfers between devices with their start and end apart: 15 -> 13, of which waited for: 13 -> 5; matrix products, arithmetic and copies ran while one was open for 2% -> 11% of each run, Pallas kernels for 0% -> 0%
where the time goes in v1:
time: 144 us; the launch traced here: 143 us
  starting transfers between devices  53.5 us (37%)
  waiting for transfers between devices  43.5 us (30%)
  matrix products  25.2 us (18%)
  local copies, waits for them, and re-layouts  14 us (10%)
  between operations  3.73 us (3%)
  other arithmetic  3.29 us (2%)
    all_to_all x4, waiting for transfers between devices, gathered_sum(): return jnp.sum(lax.all_to_all(spread, axis, 0, 0, tiled=True))  36.3 us
    all_to_all x4, starting transfers between devices, gathered_sum(): return jnp.sum(lax.all_to_all(spread, axis, 0, 0, tiled=True))  29.3 us
    dot_general x18, matrix products, mm(): return jnp.einsum(spec, a, b, precision=HIGH)  25.2 us
    ppermute x8, starting transfers between devices, shifted(): return lax.ppermute(block, axis, route)  18.3 us
    all_to_all x1, waiting for transfers between devices, left_environment(): every = lax.all_to_all(spread, 'seg', 0, 0, tiled=True)  7.22 us
    all_to_all x1, starting transfers between devices, left_environment(): every = lax.all_to_all(spread, 'seg', 0, 0, tiled=True)  5.78 us
    broadcast_in_dim x4, local copies, waits for them, and re-layouts, gathered_sum(): spread = jnp.broadcast_to(value.reshape(1, 1), (count, 1))  5.04 us
    slice x4, local copies, waits for them, and re-layouts, apply_terms(): terms = jnp.concatenate([lower, products[1::3], upper], axis=0)  3.08 us
  transfers between devices with their start and end apart: 13, of which 5 were waited for; matrix products, arithmetic and copies ran while one was open for 11% of the time, Pallas kernels for 0%

profile of v1, /device:TPU:8, one launch (start us, length us, event | category | flops | bytes accessed | tf_op | source)
XLA Modules:
  0.0 143.2 jit_solution(10179257962518796858)
XLA Ops:
  0.6 0.0 copy-start
  0.6 2.1 %broadcast_in_dim.42 = f32[8,2,128,128]{3,2,1,0:T(8,128)} broadcast(f32[2,128,128]{2,1,0:T(8,128)} %bitcast.133), dimensions={1,2,3} | broadcast | bytes 1179648 | tf_op jit(solution)/shard_map/broadcast_in_dim | solution.py:33
  2.7 5.8 %all-to-all-start = ((f32[8,2,128,128]{3,2,1,0:T(8,128)}), f32[8,2,128,128]{3,2,1,0:T(8,128)S(1)}, u32[]{:S(2)}, u32[]{:S(2)}) async-start(f32[8,2,128,128]{3,2,1,0:T(8,128)} %broadcast_in_dim.42), calls=%async_computation | async-start | bytes 2097152 | tf_op jit(solution)/shard_map/all_to_all | solution.py:34
  8.5 2.0 %convolution_bitcast_fusion.3 = f32[9,2,128,128]{2,3,0,1:T(8,128)S(1)} fusion(f32[1,2,128,128]{3,2,1,0:T(8,128)S(1)} %copy-done.3, f32[1,9,2,128,128]{4,3,2,1,0:T(8,128)S(1)} %copy-done), kind=kOutput, calls=%fused_computation.3 | convolution fusion | flops 452984832 | bytes 2490368 | tf_op jit(solution)/shard_map/kab,wkbc->wkac/dot_general | solution.py:27
  10.5 0.0 copy-start.4
  10.5 0.1 slice_bitcast_fusion.7
  10.6 3.1 %collective-permute-start = (f32[3,128,128]{1,2,0:T(8,128)S(1)}, f32[3,128,128]{1,2,0:T(8,128)S(1)}, u32[]{:S(2)}, u32[]{:S(2)}) collective-permute-start(f32[3,128,128]{1,2,0:T(8,128)S(1)} %get-tuple-element.17), channel_id=1, source_target_pairs={{0,1},{1,2},{2,3},{3,4},{4,5},{5,6},{6,7},{7,8},{8,9},{9,10},{10,1... | collective-permute-start | bytes 589832 | tf_op jit(solution)/shard_map/ppermute | solution.py:17
  13.7 1.3 collective-permute-start.1
  15.0 0.8 slice.102
  15.8 7.2 %all-to-all-done = f32[8,2,128,128]{3,2,1,0:T(8,128)S(1)} async-done(((f32[8,2,128,128]{3,2,1,0:T(8,128)}), f32[8,2,128,128]{3,2,1,0:T(8,128)S(1)}, u32[]{:S(2)}, u32[]{:S(2)}) %all-to-all-start) | async-done | bytes 1048608 | tf_op jit(solution)/shard_map/all_to_all | solution.py:34
  23.0 0.3 convolution_select_fusion.6
  23.3 0.0 copy-start.1
  23.3 0.3 convolution_select_fusion.5
  23.6 0.3 convolution_select_fusion.4
  23.9 0.3 convolution_select_fusion.3
  24.1 0.3 convolution_select_fusion.2
  24.4 0.3 convolution_select_fusion.1
  24.7 0.3 fusion.42
  25.0 1.3 convolution_bitcast_fusion.5
  26.2 1.1 fusion
  27.4 0.1 fusion.92
  27.5 0.0 collective-permute-done.1
  27.5 0.9 copy-done.2
  28.4 2.7 %multiply_reduce_fusion.3 = (f32[]{:T(128)}, f32[2,128,128]{2,1,0:T(8,128)S(1)}) fusion(f32[3,1,128,128]{2,3,0,1:T(8,128)S(1)} %bitcast.135, f32[3,1,128,128]{2,3,0,1:T(8,128)S(1)} %get-tuple-element.19, f32[3,2,128,128]{2,3,0,1:T(8,128)S(1)} %copy-done.2, f32[3,1,128,128]{2,3,0,1:T(8,128)S(1)} %get-tuple-element.20, f32[3,1,128,128]{2,3,0,1:T(8,128)S(1)} %bitcast.134, ...), kind=kOutput, calls=%fused_computation.95 | convolution fusion | flops 454819840 | bytes 2490372 | tf_op jit(solution)/shard_map/wkab,wkbc->kac/dot_general | solution.py:27
  31.0 1.1 convolution_bitcast_fusion.2
  32.1 0.9 slice_bitcast_fusion.5
  33.1 3.7 %collective-permute-start.2 = (f32[3,128,128]{2,1,0:T(8,128)}, f32[3,128,128]{2,1,0:T(8,128)}, u32[]{:S(2)}, u32[]{:S(2)}) collective-permute-start(f32[3,128,128]{2,1,0:T(8,128)} %get-tuple-element.10), channel_id=1, source_target_pairs={{0,1},{1,2},{2,3},{3,4},{4,5},{5,6},{6,7},{7,8},{8,9},{9,10},{10,1... | collective-permute-start | bytes 589832 | tf_op jit(solution)/shard_map/ppermute | solution.py:17
  36.8 1.3 collective-permute-start.3
  38.1 1.3 broadcast_in_dim.43
  39.3 12.8 %all-to-all-start.1 = ((f32[32,1,1]{2,1,0:T(1,128)}), f32[32,1,1]{2,1,0:T(1,128)S(1)}, u32[]{:S(2)}, u32[]{:S(2)}) async-start(f32[32,1,1]{2,1,0:T(1,128)} %broadcast_in_dim.43), calls=%async_computation.1 | async-start | bytes 32768 | tf_op jit(solution)/shard_map/all_to_all | solution.py:23
  52.1 0.8 slice.107
  52.9 8.8 %all-to-all-done.1 = f32[32,1,1]{2,1,0:T(1,128)S(1)} async-done(((f32[32,1,1]{2,1,0:T(1,128)}), f32[32,1,1]{2,1,0:T(1,128)S(1)}, u32[]{:S(2)}, u32[]{:S(2)}) %all-to-all-start.1) | async-done | bytes 160 | tf_op jit(solution)/shard_map/all_to_all | solution.py:23
  61.7 0.6 reduce_sum.73
  63.0 4.0 %multiply_reduce_fusion.2 = (f32[]{:T(128)}, f32[2,128,128]{2,1,0:T(8,128)S(1)}) fusion(f32[]{:T(128)S(6)} %div.28, f32[3,1,128,128]{3,2,0,1:T(8,128)} %bitcast.30, f32[3,1,128,128]{3,2,0,1:T(8,128)} %get-tuple-element.12, f32[3,2,128,128]{3,2,0,1:T(8,128)} %slice.107, f32[3,1,128,128]{3,2,0,1:T(8,128)} %get-tuple-element.13, ...), kind=kOutput, calls=%fused_computation.93 | convolution fusion | flops 454852608 | bytes 2490376 | tf_op jit(solution)/shard_map/wkab,wkbc->kac/dot_general | solution.py:27
  67.0 1.1 convolution_bitcast_fusion.1
  68.1 0.9 slice_bitcast_fusion.3
  69.0 3.2 %collective-permute-start.4 = (f32[3,128,128]{2,1,0:T(8,128)}, f32[3,128,128]{2,1,0:T(8,128)}, u32[]{:S(2)}, u32[]{:S(2)}) collective-permute-start(f32[3,128,128]{2,1,0:T(8,128)} %get-tuple-element.6), channel_id=1, source_target_pairs={{0,1},{1,2},{2,3},{3,4},{4,5},{5,6},{6,7},{7,8},{8,9},{9,10},{10,1... | collective-permute-start | bytes 589832 | tf_op jit(solution)/shard_map/ppermute | solution.py:17
  72.2 1.3 collective-permute-start.5
  73.5 1.3 broadcast_in_dim.44
  74.7 6.4 %all-to-all-start.2 = ((f32[32,1,1]{2,1,0:T(1,128)}), f32[32,1,1]{2,1,0:T(1,128)S(1)}, u32[]{:S(2)}, u32[]{:S(2)}) async-start(f32[32,1,1]{2,1,0:T(1,128)} %broadcast_in_dim.44), calls=%async_computation.2 | async-start | bytes 32768 | tf_op jit(solution)/shard_map/all_to_all | solution.py:23
  81.1 0.8 slice.112
  81.9 8.9 %all-to-all-done.2 = f32[32,1,1]{2,1,0:T(1,128)S(1)} async-done(((f32[32,1,1]{2,1,0:T(1,128)}), f32[32,1,1]{2,1,0:T(1,128)S(1)}, u32[]{:S(2)}, u32[]{:S(2)}) %all-to-all-start.2) | async-done | bytes 160 | tf_op jit(solution)/shard_map/all_to_all | solution.py:23
  90.8 0.6 reduce_sum.75
  92.2 0.0 collective-permute-done.4
  92.2 0.0 collective-permute-done.5
  92.2 4.0 %multiply_reduce_fusion.1 = (f32[]{:T(128)}, f32[2,128,128]{2,1,0:T(8,128)S(1)}) fusion(f32[]{:T(128)S(6)} %div.30, f32[3,1,128,128]{3,2,0,1:T(8,128)} %bitcast.39, f32[3,1,128,128]{3,2,0,1:T(8,128)} %get-tuple-element.8, f32[3,2,128,128]{3,2,0,1:T(8,128)} %slice.112, f32[3,1,128,128]{3,2,0,1:T(8,128)} %get-tuple-element.9, ...), kind=kOutput, calls=%fused_computation.91 | convolution fusion | flops 454852608 | bytes 2490376 | tf_op jit(solution)/shard_map/wkab,wkbc->kac/dot_general | solution.py:27
  96.1 1.1 convolution_bitcast_fusion
  97.2 0.9 slice_bitcast_fusion.1
  98.2 3.2 %collective-permute-start.6 = (f32[3,128,128]{2,1,0:T(8,128)}, f32[3,128,128]{2,1,0:T(8,128)}, u32[]{:S(2)}, u32[]{:S(2)}) collective-permute-start(f32[3,128,128]{2,1,0:T(8,128)} %get-tuple-element.2), channel_id=1, source_target_pairs={{0,1},{1,2},{2,3},{3,4},{4,5},{5,6},{6,7},{7,8},{8,9},{9,10},{10,1... | collective-permute-start | bytes 589832 | tf_op jit(solution)/shard_map/ppermute | solution.py:17
  101.4 1.3 collective-permute-start.7
  102.7 1.3 broadcast_in_dim.45
  103.9 6.4 %all-to-all-start.3 = ((f32[32,1,1]{2,1,0:T(1,128)}), f32[32,1,1]{2,1,0:T(1,128)S(1)}, u32[]{:S(2)}, u32[]{:S(2)}) async-start(f32[32,1,1]{2,1,0:T(1,128)} %broadcast_in_dim.45), calls=%async_computation.3 | async-start | bytes 32768 | tf_op jit(solution)/shard_map/all_to_all | solution.py:23
  110.3 0.8 slice.117
  111.1 8.9 %all-to-all-done.3 = f32[32,1,1]{2,1,0:T(1,128)S(1)} async-done(((f32[32,1,1]{2,1,0:T(1,128)}), f32[32,1,1]{2,1,0:T(1,128)S(1)}, u32[]{:S(2)}, u32[]{:S(2)}) %all-to-all-start.3) | async-done | bytes 160 | tf_op jit(solution)/shard_map/all_to_all | solution.py:23
  120.0 0.6 reduce_sum.77
  121.4 0.0 copy-start.5
  121.4 3.9 %multiply_reduce_fusion = (f32[]{:T(128)}, f32[2,128,128]{2,1,0:T(8,128)S(1)}) fusion(f32[]{:T(128)S(6)} %div.32, f32[3,1,128,128]{3,2,0,1:T(8,128)} %bitcast.48, f32[3,1,128,128]{3,2,0,1:T(8,128)} %get-tuple-element.4, f32[3,2,128,128]{3,2,0,1:T(8,128)} %slice.117, f32[3,1,128,128]{3,2,0,1:T(8,128)} %get-tuple-element.5, f32[3,1,128,128]{3,2,0,1:T(8,128)} %bitcast.46, ...), kind=kOutput, calls=%fused_computation.90 | convolution fusion | flops 454852608 | bytes 2490376 | tf_op jit(solution)/shard_map/wkab,wkbc->kac/dot_general | solution.py:27
  125.3 1.3 broadcast_in_dim.46
  126.6 3.8 %all-to-all-start.4 = ((f32[32,1,1]{2,1,0:T(1,128)}), f32[32,1,1]{2,1,0:T(1,128)S(1)}, u32[]{:S(2)}, u32[]{:S(2)}) async-start(f32[32,1,1]{2,1,0:T(1,128)} %broadcast_in_dim.46), calls=%async_computation.4 | async-start | bytes 32768 | tf_op jit(solution)/shard_map/all_to_all | solution.py:23
  130.4 0.1 compare_convert_fusion
  130.5 9.6 %all-to-all-done.4 = f32[32,1,1]{2,1,0:T(1,128)S(1)} async-done(((f32[32,1,1]{2,1,0:T(1,128)}), f32[32,1,1]{2,1,0:T(1,128)S(1)}, u32[]{:S(2)}, u32[]{:S(2)}) %all-to-all-start.4) | async-done | bytes 160 | tf_op jit(solution)/shard_map/all_to_all | solution.py:23
  140.1 0.6 reduce_sum.79
  141.5 0.7 multiply_bitcast_fusion
  142.1 1.1 fusion.55
  (14 shorter events, 0.0 us)
Async XLA Ops:
  0.6 7.9 %copy-start = (f32[1,9,2,128,128]{4,3,2,1,0:T(8,128)S(1)}, f32[1,9,2,128,128]{4,3,2,1,0:T(8,128)}, u32[]{:S(2)}) copy-start(f32[1,9,2,128,128]{4,3,2,1,0:T(8,128)} %param.9) | copy-start | bytes 3538948
  2.7 5.8 %copy-start.3 = (f32[1,2,128,128]{3,2,1,0:T(8,128)S(1)}, f32[1,2,128,128]{3,2,1,0:T(8,128)}, u32[]{:S(2)}) copy-start(f32[1,2,128,128]{3,2,1,0:T(8,128)} %param.6) | copy-start | bytes 393220
  2.7 20.3 %all-to-all-start = ((f32[8,2,128,128]{3,2,1,0:T(8,128)}), f32[8,2,128,128]{3,2,1,0:T(8,128)S(1)}, u32[]{:S(2)}, u32[]{:S(2)}) async-start(f32[8,2,128,128]{3,2,1,0:T(8,128)} %broadcast_in_dim.42), calls=%async_computation | async-start | bytes 2097152 | tf_op jit(solution)/shard_map/all_to_all | solution.py:34
  10.5 5.3 %copy-start.4 = (s32[9,2]{0,1:T(2,128)S(1)}, s32[9,2]{0,1:T(2,128)}, u32[]{:S(2)}) copy-start(s32[9,2]{0,1:T(2,128)} %param.10) | copy-start | bytes 220
  10.6 16.9 %collective-permute-start = (f32[3,128,128]{1,2,0:T(8,128)S(1)}, f32[3,128,128]{1,2,0:T(8,128)S(1)}, u32[]{:S(2)}, u32[]{:S(2)}) collective-permute-start(f32[3,128,128]{1,2,0:T(8,128)S(1)} %get-tuple-element.17), channel_id=1, source_target_pairs={{0,1},{1,2},{2,3},{3,4},{4,5},{5,6},{6,7},{7,8},{8,9},{9,10},{10,1... | collective-permute-start | bytes 589832 | tf_op jit(solution)/shard_map/ppermute | solution.py:17
  13.7 13.8 %collective-permute-start.1 = (f32[3,128,128]{1,2,0:T(8,128)S(1)}, f32[3,128,128]{1,2,0:T(8,128)S(1)}, u32[]{:S(2)}, u32[]{:S(2)}) collective-permute-start(f32[3,128,128]{1,2,0:T(8,128)S(1)} %get-tuple-element.18), channel_id=1, source_target_pairs={{1,0},{2,1},{3,2},{4,3},{5,4},{6,5},{7,6},{8,7},{9,8},{10,9},{11,1... | collective-permute-start | bytes 589832 | tf_op jit(solution)/shard_map/ppermute | solution.py:17
  23.3 1.7 %copy-start.1 = (f32[9,2,128,128]{3,2,1,0:T(8,128)S(1)}, f32[9,2,128,128]{3,2,1,0:T(8,128)}, u32[]{:S(2)}) copy-start(f32[9,2,128,128]{3,2,1,0:T(8,128)} %param.7) | copy-start | bytes 3538948
  27.4 1.0 copy-start.2
  33.1 29.9 %collective-permute-start.2 = (f32[3,128,128]{2,1,0:T(8,128)}, f32[3,128,128]{2,1,0:T(8,128)}, u32[]{:S(2)}, u32[]{:S(2)}) collective-permute-start(f32[3,128,128]{2,1,0:T(8,128)} %get-tuple-element.10), channel_id=1, source_target_pairs={{0,1},{1,2},{2,3},{3,4},{4,5},{5,6},{6,7},{7,8},{8,9},{9,10},{10,1... | collective-permute-start | bytes 589832 | tf_op jit(solution)/shard_map/ppermute | solution.py:17
  36.8 26.2 %collective-permute-start.3 = (f32[3,128,128]{2,1,0:T(8,128)}, f32[3,128,128]{2,1,0:T(8,128)}, u32[]{:S(2)}, u32[]{:S(2)}) collective-permute-start(f32[3,128,128]{2,1,0:T(8,128)} %get-tuple-element.11), channel_id=1, source_target_pairs={{1,0},{2,1},{3,2},{4,3},{5,4},{6,5},{7,6},{8,7},{9,8},{10,9},{11,1... | collective-permute-start | bytes 589832 | tf_op jit(solution)/shard_map/ppermute | solution.py:17
  39.3 22.3 %all-to-all-start.1 = ((f32[32,1,1]{2,1,0:T(1,128)}), f32[32,1,1]{2,1,0:T(1,128)S(1)}, u32[]{:S(2)}, u32[]{:S(2)}) async-start(f32[32,1,1]{2,1,0:T(1,128)} %broadcast_in_dim.43), calls=%async_computation.1 | async-start | bytes 32768 | tf_op jit(solution)/shard_map/all_to_all | solution.py:23
  69.0 23.2 %collective-permute-start.4 = (f32[3,128,128]{2,1,0:T(8,128)}, f32[3,128,128]{2,1,0:T(8,128)}, u32[]{:S(2)}, u32[]{:S(2)}) collective-permute-start(f32[3,128,128]{2,1,0:T(8,128)} %get-tuple-element.6), channel_id=1, source_target_pairs={{0,1},{1,2},{2,3},{3,4},{4,5},{5,6},{6,7},{7,8},{8,9},{9,10},{10,1... | collective-permute-start | bytes 589832 | tf_op jit(solution)/shard_map/ppermute | solution.py:17
  72.2 20.0 %collective-permute-start.5 = (f32[3,128,128]{2,1,0:T(8,128)}, f32[3,128,128]{2,1,0:T(8,128)}, u32[]{:S(2)}, u32[]{:S(2)}) collective-permute-start(f32[3,128,128]{2,1,0:T(8,128)} %get-tuple-element.7), channel_id=1, source_target_pairs={{1,0},{2,1},{3,2},{4,3},{5,4},{6,5},{7,6},{8,7},{9,8},{10,9},{11,1... | collective-permute-start | bytes 589832 | tf_op jit(solution)/shard_map/ppermute | solution.py:17
  74.7 16.1 %all-to-all-start.2 = ((f32[32,1,1]{2,1,0:T(1,128)}), f32[32,1,1]{2,1,0:T(1,128)S(1)}, u32[]{:S(2)}, u32[]{:S(2)}) async-start(f32[32,1,1]{2,1,0:T(1,128)} %broadcast_in_dim.44), calls=%async_computation.2 | async-start | bytes 32768 | tf_op jit(solution)/shard_map/all_to_all | solution.py:23
  98.2 23.2 %collective-permute-start.6 = (f32[3,128,128]{2,1,0:T(8,128)}, f32[3,128,128]{2,1,0:T(8,128)}, u32[]{:S(2)}, u32[]{:S(2)}) collective-permute-start(f32[3,128,128]{2,1,0:T(8,128)} %get-tuple-element.2), channel_id=1, source_target_pairs={{0,1},{1,2},{2,3},{3,4},{4,5},{5,6},{6,7},{7,8},{8,9},{9,10},{10,1... | collective-permute-start | bytes 589832 | tf_op jit(solution)/shard_map/ppermute | solution.py:17
  101.4 20.0 %collective-permute-start.7 = (f32[3,128,128]{2,1,0:T(8,128)}, f32[3,128,128]{2,1,0:T(8,128)}, u32[]{:S(2)}, u32[]{:S(2)}) collective-permute-start(f32[3,128,128]{2,1,0:T(8,128)} %get-tuple-element.3), channel_id=1, source_target_pairs={{1,0},{2,1},{3,2},{4,3},{5,4},{6,5},{7,6},{8,7},{9,8},{10,9},{11,1... | collective-permute-start | bytes 589832 | tf_op jit(solution)/shard_map/ppermute | solution.py:17
  103.9 16.1 %all-to-all-start.3 = ((f32[32,1,1]{2,1,0:T(1,128)}), f32[32,1,1]{2,1,0:T(1,128)S(1)}, u32[]{:S(2)}, u32[]{:S(2)}) async-start(f32[32,1,1]{2,1,0:T(1,128)} %broadcast_in_dim.45), calls=%async_computation.3 | async-start | bytes 32768 | tf_op jit(solution)/shard_map/all_to_all | solution.py:23
  121.4 9.0 %copy-start.5 = (s32[1,2]{1,0:T(1,128)S(1)}, s32[1,2]{1,0:T(1,128)}, u32[]{:S(2)}) copy-start(s32[1,2]{1,0:T(1,128)} %param.11) | copy-start | bytes 28
  126.6 13.5 %all-to-all-start.4 = ((f32[32,1,1]{2,1,0:T(1,128)}), f32[32,1,1]{2,1,0:T(1,128)S(1)}, u32[]{:S(2)}, u32[]{:S(2)}) async-start(f32[32,1,1]{2,1,0:T(1,128)} %broadcast_in_dim.46), calls=%async_computation.4 | async-start | bytes 32768 | tf_op jit(solution)/shard_map/all_to_all | solution.py:23

commit v2 on v1

--- a/solution.py
+++ b/solution.py
@@ -17,9 +17,10 @@
     return lax.ppermute(block, axis, route)
 
 
-def gathered_sum(value, axis):
+def gathered_sum(vector, axis):
     count = lax.axis_size(axis)
-    spread = jnp.broadcast_to(value.reshape(1, 1), (count, 1))
+    row = jnp.sum(vector * vector, axis=(0, 1))
+    spread = jnp.broadcast_to(row[None], (count, row.shape[0]))
     return jnp.sum(lax.all_to_all(spread, axis, 0, 0, tiled=True))
 
 
@@ -37,33 +38,39 @@
     for step in range(segments - 1):
         grown = mm("kab,kbc->kac", prefix, every[step])
         prefix = jnp.where(step < segment, grown, prefix)
-    right_side = mm("wkbc,kcd->wkbd", left_env, prefix)
-    return mm("kba,wkbd->wkad", prefix, right_side)
+    right_side = mm("kwbc,kcd->kwbd", left_env, prefix)
+    return mm("kba,kwbd->kwad", prefix, right_side)
+
+
+def grouped(terms, axis):
+    pick = lambda start: lax.slice_in_dim(terms, start, None, 3, axis=axis)
+    return jnp.concatenate([pick(0), pick(1), pick(2)], axis=axis)
 
 
 def apply_terms(vector, right, ordered):
-    products = mm("kab,wkbc->wkac", vector, right)
-    from_left = shifted(products[0::3, 1], "sec", 1)
-    from_right = shifted(products[2::3, 0], "sec", -1)
-    lower = jnp.stack([from_left, products[0::3, 0]], axis=1)
-    upper = jnp.stack([products[2::3, 1], from_right], axis=1)
-    terms = jnp.concatenate([lower, products[1::3], upper], axis=0)
-    return mm("wkab,wkbc->kac", ordered, terms)
+    products = mm("kab,kwbc->kwac", vector, right)
+    group = right.shape[1] // 3
+    from_left = shifted(products[1, :group], "sec", 1)
+    from_right = shifted(products[0, 2 * group :], "sec", -1)
+    first = jnp.concatenate([from_left, products[0, group : 2 * group], products[1, 2 * group :]], axis=0)
+    second = jnp.concatenate([products[0, :group], products[1, group : 2 * group], from_right], axis=0)
+    terms = jnp.stack([first, second], axis=0)
+    return lax.optimization_barrier(mm("kwab,kwbc->kac", ordered, terms))
 
 
 def per_device(theta_in, left_env, site_maps, right_env, mpo_mask, ranks):
     vector = theta_in[0]
     maps = site_maps[0]
-    right = right_env[0]
+    right = grouped(jnp.swapaxes(right_env[0], 0, 1), 1)
     blocks = vector.shape[0]
     width = vector.shape[1]
     cells = lax.axis_size("sec") * blocks * width * width
-    env = left_environment(left_env, maps)
-    weighted = env * mpo_mask.astype(jnp.float32)[:, :, None, None]
-    ordered = jnp.concatenate([weighted[0::3], weighted[1::3], weighted[2::3]], axis=0)
+    env = left_environment(jnp.swapaxes(left_env, 0, 1), maps)
+    weighted = env * jnp.swapaxes(mpo_mask, 0, 1).astype(jnp.float32)[:, :, None, None]
+    ordered = grouped(weighted, 1)
     current = apply_terms(vector, right, ordered)
     for step in range(ITERS):
-        total = gathered_sum(jnp.sum(current * current), "sec")
+        total = gathered_sum(current, "sec")
         scale = lax.rsqrt(total / cells + EPS)
         if step + 1 < ITERS:
             image = apply_terms(current * LIFT, right, ordered)

time: 144 us -> 150 us (1.042)
  blocking collectives: 0 us -> 54.3 us
  waiting for transfers between devices: 43.5 us -> 15.2 us
  starting transfers between devices: 53.5 us -> 28.4 us
  other arithmetic: 3.29 us -> 13.3 us
  local copies, waits for them, and re-layouts: 14 us -> 9.9 us
    all_to_all x0 -> x3, blocking collectives: none -> 54.3 us  [gathered_sum(): return jnp.sum(lax.all_to_all(spread, axis, 0, 0, tiled=True))]
    all_to_all x4 -> x1, waiting for transfers between devices: 36.3 us -> 9.63 us  [gathered_sum(): return jnp.sum(lax.all_to_all(spread, axis, 0, 0, tiled=True))]
    all_to_all x4 -> x1, starting transfers between devices: 29.3 us -> 3.83 us  [gathered_sum(): return jnp.sum(lax.all_to_all(spread, axis, 0, 0, tiled=True))]
    another operation x0 -> x8, other arithmetic: none -> 9.95 us  [apply_terms(): terms = jnp.stack([first, second], axis=0)]
    all_to_all x1, waiting for transfers between devices: 7.22 us -> 0.01 us  [left_environment(): every = lax.all_to_all(spread, 'seg', 0, 0, tiled=True)]
    ppermute x8, waiting for transfers between devices: 0.02 us -> 5.54 us  [shifted(): return lax.ppermute(block, axis, route)]
    broadcast_in_dim x4, local copies, waits for them, and re-layouts: 5.04 us -> 0.66 us  [gathered_sum(): spread = jnp.broadcast_to(row[None], (count, row.shape[0]))]
    slice x5 -> x2, local copies, waits for them, and re-layouts: 3.16 us -> 0.18 us  [grouped(): pick = lambda start: lax.slice_in_dim(terms, start, None, 3, axis=axis)]
  transfers between devices with their start and end apart: 13 -> 10, of which waited for: 5 -> 3; matrix products, arithmetic and copies ran while one was open for 11% -> 8% of each run, Pallas kernels for 0% -> 0%
where the time goes in v2:
time: 150 us; the launch traced here: 149 us
  blocking collectives  54.3 us (36%)
  starting transfers between devices  28.4 us (19%)
  matrix products  24.5 us (16%)
  waiting for transfers between devices  15.2 us (10%)
  other arithmetic  13.3 us (9%)
  local copies, waits for them, and re-layouts  9.9 us (7%)
  between operations  3.86 us (3%)
    all_to_all x3, blocking collectives, gathered_sum(): return jnp.sum(lax.all_to_all(spread, axis, 0, 0, tiled=True))  54.3 us
    dot_general x18, matrix products, mm(): return jnp.einsum(spec, a, b, precision=HIGH)  24.5 us
    ppermute x8, starting transfers between devices, shifted(): return lax.ppermute(block, axis, route)  18.1 us
    another operation x8, other arithmetic, apply_terms(): terms = jnp.stack([first, second], axis=0)  9.95 us
    all_to_all x1, waiting for transfers between devices, gathered_sum(): return jnp.sum(lax.all_to_all(spread, axis, 0, 0, tiled=True))  9.63 us
    all_to_all x1, starting transfers between devices, left_environment(): every = lax.all_to_all(spread, 'seg', 0, 0, tiled=True)  6.44 us
    ppermute x8, waiting for transfers between devices, shifted(): return lax.ppermute(block, axis, route)  5.54 us
    all_to_all x1, starting transfers between devices, gathered_sum(): return jnp.sum(lax.all_to_all(spread, axis, 0, 0, tiled=True))  3.83 us
  transfers between devices with their start and end apart: 10, of which 3 were waited for; matrix products, arithmetic and copies ran while one was open for 8% of the time, Pallas kernels for 0%

profile of v2, /device:TPU:8, one launch (start us, length us, event | category | flops | bytes accessed | tf_op | source)
XLA Modules:
  0.0 149.3 jit_solution(865539913453238879)
XLA Ops:
  0.6 2.1 %broadcast_in_dim.22 = f32[8,2,128,128]{3,2,1,0:T(8,128)} broadcast(f32[2,128,128]{2,1,0:T(8,128)} %bitcast.166), dimensions={1,2,3} | broadcast | bytes 1179648 | tf_op jit(solution)/shard_map/broadcast_in_dim | solution.py:34
  2.8 6.4 %all-to-all-start = ((f32[8,2,128,128]{3,2,1,0:T(8,128)}), f32[8,2,128,128]{3,2,1,0:T(8,128)}, u32[]{:S(2)}, u32[]{:S(2)}) async-start(f32[8,2,128,128]{3,2,1,0:T(8,128)} %broadcast_in_dim.22), calls=%async_computation | async-start | bytes 2097152 | tf_op jit(solution)/shard_map/all_to_all | solution.py:35
  9.2 0.4 copy.28
  9.6 0.1 fusion.66
  9.7 0.8 copy-done.11
  10.5 1.1 convolution_bitcast_fusion.3
  11.7 0.9 slice_bitcast_fusion.23
  12.5 3.2 %collective-permute-start = (f32[3,128,128]{1,2,0:T(8,128)}, f32[3,128,128]{1,2,0:T(8,128)}, u32[]{:S(2)}, u32[]{:S(2)}) collective-permute-start(f32[3,128,128]{1,2,0:T(8,128)} %get-tuple-element.23), channel_id=1, source_target_pairs={{0,1},{1,2},{2,3},{3,4},{4,5},{5,6},{6,7},{7,8},{8,9},{9,10},{10,1... | collective-permute-start | bytes 589832 | tf_op jit(solution)/shard_map/ppermute | solution.py:17
  15.7 1.3 collective-permute-start.1
  17.1 2.8 %collective-permute-done = f32[3,128,128]{1,2,0:T(8,128)} collective-permute-done((f32[3,128,128]{1,2,0:T(8,128)}, f32[3,128,128]{1,2,0:T(8,128)}, u32[]{:S(2)}, u32[]{:S(2)}) %collective-permute-start) | collective-permute-done | bytes 196640 | tf_op jit(solution)/shard_map/ppermute | solution.py:17
  19.8 1.8 %maximum_bitcast_fusion = f32[1,9,128,128]{2,3,1,0:T(8,128)} fusion(f32[3,128,128]{1,2,0:T(8,128)S(1)} %get-tuple-element.27, f32[3,128,128]{1,2,0:T(8,128)S(1)} %get-tuple-element.28, f32[3,128,128]{1,2,0:T(8,128)} %collective-permute-done), kind=kLoop, calls=%fused_computation.40 | loop fusion | flops 294912 | bytes 1179648 | tf_op jit(solution)/shard_map/stack | solution.py:57
  21.6 2.8 %collective-permute-done.1 = f32[3,128,128]{1,2,0:T(8,128)} collective-permute-done((f32[3,128,128]{1,2,0:T(8,128)S(1)}, f32[3,128,128]{1,2,0:T(8,128)}, u32[]{:S(2)}, u32[]{:S(2)}) %collective-permute-start.1) | collective-permute-done | bytes 196640 | tf_op jit(solution)/shard_map/ppermute | solution.py:17
  24.4 1.8 %maximum_bitcast_fusion.1 = f32[1,9,128,128]{2,3,1,0:T(8,128)} fusion(f32[3,128,128]{1,2,0:T(8,128)} %collective-permute-done.1, f32[3,128,128]{1,2,0:T(8,128)S(1)} %copy-done.4, f32[3,128,128]{1,2,0:T(8,128)S(1)} %copy-done.5), kind=kLoop, calls=%fused_computation.41 | loop fusion | flops 294912 | bytes 1179648 | tf_op jit(solution)/shard_map/stack | solution.py:57
  26.2 1.2 convolution_select_fusion.6
  27.4 1.2 convolution_select_fusion.5
  28.6 1.2 convolution_select_fusion.4
  29.8 1.2 convolution_select_fusion.3
  30.9 1.2 convolution_select_fusion.2
  32.1 1.2 convolution_select_fusion.1
  33.3 1.2 fusion.18
  34.5 1.3 convolution_bitcast_fusion.4
  35.8 1.1 fusion
  36.9 0.1 fusion.65
  37.0 0.9 copy-done.1
  37.9 0.2 copy-done.2
  38.1 2.1 %fusion.28 = f32[2,128,128]{2,1,0:T(8,128)S(1)} fusion(f32[1,9,128,128]{2,3,1,0:T(8,128)S(1)} %copy-done.2, f32[1,9,128,128]{2,3,1,0:T(8,128)S(1)} %copy-done.1, f32[2,3,128,128]{2,3,1,0:T(8,128)S(1)} %get-tuple-element.21, f32[2,3,128,128]{2,3,1,0:T(8,128)S(1)} %get-tuple-element.22, f32[2,3,128,128]{2,3,1,0:T(8,128)S(1)} %get-tuple-element.20), kind=kOutput, calls=%fused_computation.37 | convolution fusion | flops 453869568 | bytes 2490368 | tf_op jit(solution)/shard_map/kwab,kwbc->kac/dot_general | solution.py:28
  40.2 1.1 convolution_bitcast_fusion.2
  41.3 1.1 slice_bitcast_fusion.17
  42.4 4.0 %collective-permute-start.2 = (f32[3,128,128]{1,2,0:T(8,128)}, f32[3,128,128]{1,2,0:T(8,128)}, u32[]{:S(2)}, u32[]{:S(2)}) collective-permute-start(f32[3,128,128]{1,2,0:T(8,128)} %get-tuple-element.14), channel_id=1, source_target_pairs={{0,1},{1,2},{2,3},{3,4},{4,5},{5,6},{6,7},{7,8},{8,9},{9,10},{10,1... | collective-permute-start | bytes 589832 | tf_op jit(solution)/shard_map/ppermute | solution.py:17
  46.4 1.3 collective-permute-start.3
  47.8 21.7 %all_to_all.29 = f32[32,1,128]{2,1,0:T(1,128)S(1)} all-to-all(f32[32,1,128]{2,1,0:T(1,128)S(1)} %broadcast_in_dim.23), channel_id=1, replica_groups=mesh['seg'=8,'sec'=32] {'sec'}, dimensions={0} | all-to-all | bytes 32768 | tf_op jit(solution)/shard_map/all_to_all | solution.py:24
  69.4 0.6 reduce_sum.73
  70.8 1.2 maximum_bitcast_fusion.2
  72.0 1.0 maximum_bitcast_fusion.3
  73.0 2.1 %fusion.25 = f32[2,128,128]{2,1,0:T(8,128)S(1)} fusion(f32[1,9,128,128]{2,3,1,0:T(8,128)S(1)} %maximum_bitcast_fusion.3, f32[1,9,128,128]{2,3,1,0:T(8,128)S(1)} %maximum_bitcast_fusion.2, f32[2,3,128,128]{2,3,1,0:T(8,128)S(1)} %get-tuple-element.21, f32[2,3,128,128]{2,3,1,0:T(8,128)S(1)} %get-tuple-element.22, f32[2,3,128,128]{2,3,1,0:T(8,128)S(1)} %get-tuple-element.20), kind=kOutput, calls=%fused_computation.36 | convolution fusion | flops 453869568 | bytes 2490368 | tf_op jit(solution)/shard_map/kwab,kwbc->kac/dot_general | solution.py:28
  75.1 1.1 convolution_bitcast_fusion.1
  76.2 1.1 slice_bitcast_fusion.11
  77.3 3.2 %collective-permute-start.4 = (f32[3,128,128]{1,2,0:T(8,128)}, f32[3,128,128]{1,2,0:T(8,128)}, u32[]{:S(2)}, u32[]{:S(2)}) collective-permute-start(f32[3,128,128]{1,2,0:T(8,128)} %get-tuple-element.8), channel_id=1, source_target_pairs={{0,1},{1,2},{2,3},{3,4},{4,5},{5,6},{6,7},{7,8},{8,9},{9,10},{10,1... | collective-permute-start | bytes 589832 | tf_op jit(solution)/shard_map/ppermute | solution.py:17
  80.5 1.3 collective-permute-start.5
  81.8 0.1 multiply_reduce_fusion.2
  81.8 16.0 %all_to_all.30 = f32[32,1,128]{2,1,0:T(1,128)S(1)} all-to-all(f32[32,1,128]{2,1,0:T(1,128)S(1)} %broadcast_in_dim.48), channel_id=1, replica_groups=mesh['seg'=8,'sec'=32] {'sec'}, dimensions={0} | all-to-all | bytes 32768 | tf_op jit(solution)/shard_map/all_to_all | solution.py:24
  97.8 0.6 reduce_sum.75
  99.1 1.2 maximum_bitcast_fusion.4
  100.4 1.0 maximum_bitcast_fusion.5
  101.4 2.1 %fusion.22 = f32[2,128,128]{2,1,0:T(8,128)S(1)} fusion(f32[1,9,128,128]{2,3,1,0:T(8,128)S(1)} %maximum_bitcast_fusion.5, f32[1,9,128,128]{2,3,1,0:T(8,128)S(1)} %maximum_bitcast_fusion.4, f32[2,3,128,128]{2,3,1,0:T(8,128)S(1)} %get-tuple-element.21, f32[2,3,128,128]{2,3,1,0:T(8,128)S(1)} %get-tuple-element.22, f32[2,3,128,128]{2,3,1,0:T(8,128)S(1)} %get-tuple-element.20), kind=kOutput, calls=%fused_computation.35 | convolution fusion | flops 453869568 | bytes 2490368 | tf_op jit(solution)/shard_map/kwab,kwbc->kac/dot_general | solution.py:28
  103.4 1.1 convolution_bitcast_fusion
  104.6 0.9 slice_bitcast_fusion.5
  105.4 2.5 %collective-permute-start.6 = (f32[3,128,128]{1,2,0:T(8,128)S(1)}, f32[3,128,128]{1,2,0:T(8,128)S(1)}, u32[]{:S(2)}, u32[]{:S(2)}) collective-permute-start(f32[3,128,128]{1,2,0:T(8,128)S(1)} %get-tuple-element.2), channel_id=1, source_target_pairs={{0,1},{1,2},{2,3},{3,4},{4,5},{5,6},{6,7},{7,8},{8,9},{9,10},{10,1... | collective-permute-start | bytes 589832 | tf_op jit(solution)/shard_map/ppermute | solution.py:17
  108.0 1.3 collective-permute-start.7
  109.3 0.1 multiply_reduce_fusion.1
  109.3 16.6 %all_to_all.31 = f32[32,1,128]{2,1,0:T(1,128)S(1)} all-to-all(f32[32,1,128]{2,1,0:T(1,128)S(1)} %broadcast_in_dim.49), channel_id=1, replica_groups=mesh['seg'=8,'sec'=32] {'sec'}, dimensions={0} | all-to-all | bytes 32768 | tf_op jit(solution)/shard_map/all_to_all | solution.py:24
  126.0 0.6 reduce_sum.77
  127.3 0.7 copy-done.10
  127.9 1.1 maximum_bitcast_fusion.6
  129.0 1.0 maximum_bitcast_fusion.7
  130.0 2.0 %fusion.19 = f32[2,128,128]{2,1,0:T(8,128)S(1)} fusion(f32[1,9,128,128]{2,3,1,0:T(8,128)S(1)} %maximum_bitcast_fusion.7, f32[1,9,128,128]{2,3,1,0:T(8,128)S(1)} %maximum_bitcast_fusion.6, f32[2,3,128,128]{2,3,1,0:T(8,128)S(1)} %get-tuple-element.21, f32[2,3,128,128]{2,3,1,0:T(8,128)S(1)} %get-tuple-element.22, f32[2,3,128,128]{2,3,1,0:T(8,128)S(1)} %get-tuple-element.20), kind=kOutput, calls=%fused_computation.34 | convolution fusion | flops 453869568 | bytes 2490368 | tf_op jit(solution)/shard_map/kwab,kwbc->kac/dot_general | solution.py:28
  132.0 0.1 multiply_reduce_fusion
  132.1 0.6 broadcast_in_dim.50
  132.7 3.8 %all-to-all-start.4 = ((f32[32,1,128]{2,1,0:T(1,128)}), f32[32,1,128]{2,1,0:T(1,128)S(1)}, u32[]{:S(2)}, u32[]{:S(2)}) async-start(f32[32,1,128]{2,1,0:T(1,128)} %broadcast_in_dim.50), calls=%async_computation.4 | async-start | bytes 32768 | tf_op jit(solution)/shard_map/all_to_all | solution.py:24
  136.6 0.1 compare_convert_fusion
  136.6 9.6 %all-to-all-done.4 = f32[32,1,128]{2,1,0:T(1,128)S(1)} async-done(((f32[32,1,128]{2,1,0:T(1,128)}), f32[32,1,128]{2,1,0:T(1,128)S(1)}, u32[]{:S(2)}, u32[]{:S(2)}) %all-to-all-start.4) | async-done | bytes 16416 | tf_op jit(solution)/shard_map/all_to_all | solution.py:24
  146.3 0.6 reduce_sum.79
  147.6 0.7 multiply_bitcast_fusion
  148.2 1.1 fusion.31
  (37 shorter events, 0.3 us)
Async XLA Ops:
  0.6 33.9 %copy-start = (f32[9,2,128,128]{3,2,1,0:T(8,128)S(1)}, f32[9,2,128,128]{3,2,1,0:T(8,128)}, u32[]{:S(2)}) copy-start(f32[9,2,128,128]{3,2,1,0:T(8,128)} %param.7) | copy-start | bytes 3538948
  2.8 6.4 %copy-start.3 = (f32[1,9,2,128,128]{4,3,2,1,0:T(8,128)S(1)}, f32[1,9,2,128,128]{4,3,2,1,0:T(8,128)}, u32[]{:S(2)}) copy-start(f32[1,9,2,128,128]{4,3,2,1,0:T(8,128)} %param.9) | copy-start | bytes 3538948
  2.8 23.4 %all-to-all-start = ((f32[8,2,128,128]{3,2,1,0:T(8,128)}), f32[8,2,128,128]{3,2,1,0:T(8,128)}, u32[]{:S(2)}, u32[]{:S(2)}) async-start(f32[8,2,128,128]{3,2,1,0:T(8,128)} %broadcast_in_dim.22), calls=%async_computation | async-start | bytes 2097152 | tf_op jit(solution)/shard_map/all_to_all | solution.py:35
  9.6 0.9 copy-start.11
  11.6 5.4 %copy-start.12 = (s32[9,2]{0,1:T(2,128)S(1)}, s32[9,2]{0,1:T(2,128)}, u32[]{:S(2)}) copy-start(s32[9,2]{0,1:T(2,128)} %param.10) | copy-start | bytes 220
  12.5 11.9 %copy-start.4 = (f32[3,128,128]{1,2,0:T(8,128)S(1)}, f32[3,128,128]{1,2,0:T(8,128)}, u32[]{:S(2)}) copy-start(f32[3,128,128]{1,2,0:T(8,128)} %get-tuple-element.25) | copy-start | bytes 589828
  12.5 11.9 %copy-start.5 = (f32[3,128,128]{1,2,0:T(8,128)S(1)}, f32[3,128,128]{1,2,0:T(8,128)}, u32[]{:S(2)}) copy-start(f32[3,128,128]{1,2,0:T(8,128)} %get-tuple-element.26) | copy-start | bytes 589828
  12.5 7.3 %collective-permute-start = (f32[3,128,128]{1,2,0:T(8,128)}, f32[3,128,128]{1,2,0:T(8,128)}, u32[]{:S(2)}, u32[]{:S(2)}) collective-permute-start(f32[3,128,128]{1,2,0:T(8,128)} %get-tuple-element.23), channel_id=1, source_target_pairs={{0,1},{1,2},{2,3},{3,4},{4,5},{5,6},{6,7},{7,8},{8,9},{9,10},{10,1... | collective-permute-start | bytes 589832 | tf_op jit(solution)/shard_map/ppermute | solution.py:17
  15.7 8.7 %collective-permute-start.1 = (f32[3,128,128]{1,2,0:T(8,128)S(1)}, f32[3,128,128]{1,2,0:T(8,128)}, u32[]{:S(2)}, u32[]{:S(2)}) collective-permute-start(f32[3,128,128]{1,2,0:T(8,128)S(1)} %get-tuple-element.24), channel_id=1, source_target_pairs={{1,0},{2,1},{3,2},{4,3},{5,4},{6,5},{7,6},{8,7},{9,8},{10,9},{11,1... | collective-permute-start | bytes 589832 | tf_op jit(solution)/shard_map/ppermute | solution.py:17
  36.9 1.1 copy-start.1
  36.9 1.2 copy-start.2
  42.4 28.4 %collective-permute-start.2 = (f32[3,128,128]{1,2,0:T(8,128)}, f32[3,128,128]{1,2,0:T(8,128)}, u32[]{:S(2)}, u32[]{:S(2)}) collective-permute-start(f32[3,128,128]{1,2,0:T(8,128)} %get-tuple-element.14), channel_id=1, source_target_pairs={{0,1},{1,2},{2,3},{3,4},{4,5},{5,6},{6,7},{7,8},{8,9},{9,10},{10,1... | collective-permute-start | bytes 589832 | tf_op jit(solution)/shard_map/ppermute | solution.py:17
  46.4 25.6 %collective-permute-start.3 = (f32[3,128,128]{1,2,0:T(8,128)}, f32[3,128,128]{1,2,0:T(8,128)}, u32[]{:S(2)}, u32[]{:S(2)}) collective-permute-start(f32[3,128,128]{1,2,0:T(8,128)} %get-tuple-element.15), channel_id=1, source_target_pairs={{1,0},{2,1},{3,2},{4,3},{5,4},{6,5},{7,6},{8,7},{9,8},{10,9},{11,1... | collective-permute-start | bytes 589832 | tf_op jit(solution)/shard_map/ppermute | solution.py:17
  70.7 1.3 copy-start.8
  70.7 1.3 copy-start.9
  77.3 21.8 %collective-permute-start.4 = (f32[3,128,128]{1,2,0:T(8,128)}, f32[3,128,128]{1,2,0:T(8,128)}, u32[]{:S(2)}, u32[]{:S(2)}) collective-permute-start(f32[3,128,128]{1,2,0:T(8,128)} %get-tuple-element.8), channel_id=1, source_target_pairs={{0,1},{1,2},{2,3},{3,4},{4,5},{5,6},{6,7},{7,8},{8,9},{9,10},{10,1... | collective-permute-start | bytes 589832 | tf_op jit(solution)/shard_map/ppermute | solution.py:17
  80.5 19.9 %collective-permute-start.5 = (f32[3,128,128]{1,2,0:T(8,128)}, f32[3,128,128]{1,2,0:T(8,128)}, u32[]{:S(2)}, u32[]{:S(2)}) collective-permute-start(f32[3,128,128]{1,2,0:T(8,128)} %get-tuple-element.9), channel_id=1, source_target_pairs={{1,0},{2,1},{3,2},{4,3},{5,4},{6,5},{7,6},{8,7},{9,8},{10,9},{11,1... | collective-permute-start | bytes 589832 | tf_op jit(solution)/shard_map/ppermute | solution.py:17
  99.1 1.3 copy-start.6
  99.1 1.3 copy-start.7
  105.4 21.8 %collective-permute-start.6 = (f32[3,128,128]{1,2,0:T(8,128)S(1)}, f32[3,128,128]{1,2,0:T(8,128)S(1)}, u32[]{:S(2)}, u32[]{:S(2)}) collective-permute-start(f32[3,128,128]{1,2,0:T(8,128)S(1)} %get-tuple-element.2), channel_id=1, source_target_pairs={{0,1},{1,2},{2,3},{3,4},{4,5},{5,6},{6,7},{7,8},{8,9},{9,10},{10,1... | collective-permute-start | bytes 589832 | tf_op jit(solution)/shard_map/ppermute | solution.py:17
  108.0 21.0 %collective-permute-start.7 = (f32[3,128,128]{1,2,0:T(8,128)}, f32[3,128,128]{1,2,0:T(8,128)}, u32[]{:S(2)}, u32[]{:S(2)}) collective-permute-start(f32[3,128,128]{1,2,0:T(8,128)} %get-tuple-element.3), channel_id=1, source_target_pairs={{1,0},{2,1},{3,2},{4,3},{5,4},{6,5},{7,6},{8,7},{9,8},{10,9},{11,1... | collective-permute-start | bytes 589832 | tf_op jit(solution)/shard_map/ppermute | solution.py:17
  127.3 0.7 copy-start.10
  130.0 6.6 %copy-start.13 = (s32[1,2]{1,0:T(1,128)S(1)}, s32[1,2]{1,0:T(1,128)}, u32[]{:S(2)}) copy-start(s32[1,2]{1,0:T(1,128)} %param.11) | copy-start | bytes 28
  132.7 13.6 %all-to-all-start.4 = ((f32[32,1,128]{2,1,0:T(1,128)}), f32[32,1,128]{2,1,0:T(1,128)S(1)}, u32[]{:S(2)}, u32[]{:S(2)}) async-start(f32[32,1,128]{2,1,0:T(1,128)} %broadcast_in_dim.50), calls=%async_computation.4 | async-start | bytes 32768 | tf_op jit(solution)/shard_map/all_to_all | solution.py:24

commit v3 on v1

--- a/solution.py
+++ b/solution.py
@@ -9,6 +9,7 @@
 HIGH = lax.Precision.HIGHEST
 EPS = 1e-06
 LIFT = 1024.0
+SHRINK = 2.0**-50
 
 
 def shifted(block, axis, step):
@@ -17,10 +18,11 @@
     return lax.ppermute(block, axis, route)
 
 
-def gathered_sum(value, axis):
+def gathered_sums(values, axis):
     count = lax.axis_size(axis)
-    spread = jnp.broadcast_to(value.reshape(1, 1), (count, 1))
-    return jnp.sum(lax.all_to_all(spread, axis, 0, 0, tiled=True))
+    row = jnp.stack(values)
+    spread = jnp.broadcast_to(row[None], (count, row.shape[0]))
+    return jnp.sum(lax.all_to_all(spread, axis, 0, 0, tiled=True), axis=0)
 
 
 def mm(spec, a, b):
@@ -51,6 +53,19 @@
     return mm("wkab,wkbc->kac", ordered, terms)
 
 
+def square_sums(normal, lifted):
+    return [jnp.sum(normal * normal), jnp.sum(lifted * lifted), jnp.sum(jnp.square(lifted * SHRINK))]
+
+
+def scales(sums, cells):
+    first = lax.rsqrt(sums[0] / cells + EPS)
+    step = first / LIFT
+    plain = step * step * sums[1]
+    shrunk = jnp.square(step / SHRINK) * sums[2]
+    second = lax.rsqrt(jnp.where(jnp.isfinite(sums[1]), plain, shrunk) / cells + EPS)
+    return first, second
+
+
 def per_device(theta_in, left_env, site_maps, right_env, mpo_mask, ranks):
     vector = theta_in[0]
     maps = site_maps[0]
@@ -62,14 +77,14 @@
     weighted = env * mpo_mask.astype(jnp.float32)[:, :, None, None]
     ordered = jnp.concatenate([weighted[0::3], weighted[1::3], weighted[2::3]], axis=0)
     current = apply_terms(vector, right, ordered)
-    for step in range(ITERS):
-        total = gathered_sum(jnp.sum(current * current), "sec")
-        scale = lax.rsqrt(total / cells + EPS)
-        if step + 1 < ITERS:
-            image = apply_terms(current * LIFT, right, ordered)
-            current = image * (scale / LIFT)
+    for pair in range(ITERS // 2):
+        lifted = apply_terms(current * LIFT, right, ordered)
+        first, second = scales(gathered_sums(square_sums(current, lifted), "sec"), cells)
+        current = lifted * (first / LIFT)
+        if 2 * pair + 2 < ITERS:
+            current = apply_terms(current * LIFT, right, ordered) * (second / LIFT)
         else:
-            current = current * scale
+            current = current * second
     rows = lax.broadcasted_iota(jnp.int32, (blocks, width), 1) < ranks[0][:, None]
     trimmed = current * rows.astype(jnp.float32)[:, :, None]
     density = mm("kab,kcb->kac", trimmed, trimmed) / width

time: 144 us -> 126 us (0.88)
  starting transfers between devices: 53.5 us -> 32.4 us
  blocking collectives: 0 us -> 20.6 us
  waiting for transfers between devices: 43.5 us -> 33.4 us
  local copies, waits for them, and re-layouts: 14 us -> 5.03 us
  matrix products: 25.2 us -> 22.3 us
  between operations: 3.73 us -> 6.29 us
  other arithmetic: 3.29 us -> 4.83 us
    all_to_all x4 -> x1, waiting for transfers between devices: 36.3 us -> 9.63 us  [gathered_sums(): return jnp.sum(lax.all_to_all(spread, axis, 0, 0, tiled=True), axis=0)]
    all_to_all x0 -> x1, blocking collectives: none -> 20.6 us  [gathered_sums(): return jnp.sum(lax.all_to_all(spread, axis, 0, 0, tiled=True), axis=0)]
    all_to_all x4 -> x1, starting transfers between devices: 29.3 us -> 9.43 us  [gathered_sums(): return jnp.sum(lax.all_to_all(spread, axis, 0, 0, tiled=True), axis=0)]
    ppermute x8, waiting for transfers between devices: 0.02 us -> 17.2 us  [shifted(): return lax.ppermute(block, axis, route)]
    broadcast_in_dim x4 -> x2, local copies, waits for them, and re-layouts: 5.04 us -> 0.63 us  [gathered_sums(): spread = jnp.broadcast_to(row[None], (count, row.shape[0]))]
    another operation x0 -> x2, other arithmetic: none -> 3.97 us  [gathered_sums(): row = jnp.stack(values)]
    slice x4, local copies, waits for them, and re-layouts: 3.08 us -> 0.11 us  [apply_terms(): terms = jnp.concatenate([lower, products[1::3], upper], axis=0)]
    dot_general x18, matrix products: 25.2 us -> 22.3 us  [mm(): return jnp.einsum(spec, a, b, precision=HIGH)]
  transfers between devices with their start and end apart: 13 -> 10, of which waited for: 5 -> 7; matrix products, arithmetic and copies ran while one was open for 11% -> 6% of each run, Pallas kernels for 0% -> 0%
where the time goes in v3:
time: 126 us; the launch traced here: 125 us
  waiting for transfers between devices  33.4 us (27%)
  starting transfers between devices  32.4 us (26%)
  matrix products  22.3 us (18%)
  blocking collectives  20.6 us (16%)
  between operations  6.29 us (5%)
  local copies, waits for them, and re-layouts  5.03 us (4%)
  other arithmetic  4.83 us (4%)
    dot_general x18, matrix products, mm(): return jnp.einsum(spec, a, b, precision=HIGH)  22.3 us
    all_to_all x1, blocking collectives, gathered_sums(): return jnp.sum(lax.all_to_all(spread, axis, 0, 0, tiled=True), axis=0)  20.6 us
    ppermute x8, waiting for transfers between devices, shifted(): return lax.ppermute(block, axis, route)  17.2 us
    ppermute x8, starting transfers between devices, shifted(): return lax.ppermute(block, axis, route)  17.2 us
    all_to_all x1, waiting for transfers between devices, gathered_sums(): return jnp.sum(lax.all_to_all(spread, axis, 0, 0, tiled=True), axis=0)  9.63 us
    all_to_all x1, starting transfers between devices, gathered_sums(): return jnp.sum(lax.all_to_all(spread, axis, 0, 0, tiled=True), axis=0)  9.43 us
    all_to_all x1, waiting for transfers between devices, left_environment(): every = lax.all_to_all(spread, 'seg', 0, 0, tiled=True)  6.63 us
    all_to_all x1, starting transfers between devices, left_environment(): every = lax.all_to_all(spread, 'seg', 0, 0, tiled=True)  5.78 us
  transfers between devices with their start and end apart: 10, of which 7 were waited for; matrix products, arithmetic and copies ran while one was open for 6% of the time, Pallas kernels for 0%

profile of v3, /device:TPU:8, one launch (start us, length us, event | category | flops | bytes accessed | tf_op | source)
XLA Modules:
  0.0 124.8 jit_solution(2721218929016970211)
XLA Ops:
  0.6 0.0 copy-start
  0.6 2.1 %broadcast_in_dim.34 = f32[8,2,128,128]{3,2,1,0:T(8,128)} broadcast(f32[2,128,128]{2,1,0:T(8,128)} %bitcast.139), dimensions={1,2,3} | broadcast | bytes 1179648 | tf_op jit(solution)/shard_map/broadcast_in_dim | solution.py:35
  2.7 0.0 copy-start.2
  2.7 5.8 %all-to-all-start = ((f32[8,2,128,128]{3,2,1,0:T(8,128)}), f32[8,2,128,128]{3,2,1,0:T(8,128)S(1)}, u32[]{:S(2)}, u32[]{:S(2)}) async-start(f32[8,2,128,128]{3,2,1,0:T(8,128)} %broadcast_in_dim.34), calls=%async_computation | async-start | bytes 2097152 | tf_op jit(solution)/shard_map/all_to_all | solution.py:36
  8.5 0.0 copy-done
  8.5 0.0 copy-done.2
  8.5 2.0 %convolution_bitcast_fusion.3 = f32[9,2,128,128]{2,3,0,1:T(8,128)S(1)} fusion(f32[1,2,128,128]{3,2,1,0:T(8,128)S(1)} %copy-done.2, f32[1,9,2,128,128]{4,3,2,1,0:T(8,128)S(1)} %copy-done), kind=kOutput, calls=%fused_computation.3 | convolution fusion | flops 452984832 | bytes 2490368 | tf_op jit(solution)/shard_map/kab,wkbc->wkac/dot_general | solution.py:29
  10.5 0.0 copy-start.3
  10.5 0.7 slice_bitcast_fusion.7
  11.3 3.8 %collective-permute-start = (f32[3,128,128]{1,2,0:T(8,128)}, f32[3,128,128]{1,2,0:T(8,128)}, u32[]{:S(2)}, u32[]{:S(2)}) collective-permute-start(f32[3,128,128]{1,2,0:T(8,128)} %get-tuple-element.21), channel_id=1, source_target_pairs={{0,1},{1,2},{2,3},{3,4},{4,5},{5,6},{6,7},{7,8},{8,9},{9,10},{10,1... | collective-permute-start | bytes 589832 | tf_op jit(solution)/shard_map/ppermute | solution.py:18
  15.0 1.3 %collective-permute-start.1 = (f32[3,128,128]{1,2,0:T(8,128)S(1)}, f32[3,128,128]{1,2,0:T(8,128)}, u32[]{:S(2)}, u32[]{:S(2)}) collective-permute-start(f32[3,128,128]{1,2,0:T(8,128)S(1)} %get-tuple-element.22), channel_id=1, source_target_pairs={{1,0},{2,1},{3,2},{4,3},{5,4},{6,5},{7,6},{8,7},{9,8},{10,9},{11,1... | collective-permute-start | bytes 589832 | tf_op jit(solution)/shard_map/ppermute | solution.py:18
  16.4 0.0 copy-done.3
  16.4 6.6 %all-to-all-done = f32[8,2,128,128]{3,2,1,0:T(8,128)S(1)} async-done(((f32[8,2,128,128]{3,2,1,0:T(8,128)}), f32[8,2,128,128]{3,2,1,0:T(8,128)S(1)}, u32[]{:S(2)}, u32[]{:S(2)}) %all-to-all-start) | async-done | bytes 1048608 | tf_op jit(solution)/shard_map/all_to_all | solution.py:36
  23.0 0.3 convolution_select_fusion.6
  23.3 0.0 copy-start.1
  23.3 0.3 convolution_select_fusion.5
  23.6 0.3 convolution_select_fusion.4
  23.9 0.3 convolution_select_fusion.3
  24.1 0.3 convolution_select_fusion.2
  24.4 0.3 convolution_select_fusion.1
  24.7 0.3 fusion.42
  25.0 0.0 copy-done.1
  25.0 1.3 %convolution_bitcast_fusion.5 = f32[9,2,128,128]{2,3,0,1:T(8,128)S(1)} fusion(f32[2,128,128,1]{2,1,3,0:T(8,128)S(1)} %fusion.42, f32[9,2,128,128]{3,2,1,0:T(8,128)S(1)} %copy-done.1), kind=kOutput, calls=%fused_computation.5 | convolution fusion | flops 452984832 | bytes 2490368 | tf_op jit(solution)/shard_map/wkbc,kcd->wkbd/dot_general | solution.py:29
  26.2 1.1 fusion
  27.4 0.1 fusion.89
  27.5 0.0 collective-permute-done
  27.5 0.0 collective-permute-done.1
  27.5 3.7 %multiply_reduce_fusion.5 = (f32[]{:T(128)}, f32[2,128,128]{2,1,0:T(8,128)S(1)}) fusion(f32[3,1,128,128]{2,3,0,1:T(8,128)} %bitcast.21, f32[3,1,128,128]{2,3,0,1:T(8,128)S(1)} %get-tuple-element.23, f32[3,2,128,128]{2,3,0,1:T(8,128)S(1)} %slice.122, f32[3,1,128,128]{2,3,0,1:T(8,128)S(1)} %get-tuple-element.24, f32[3,1,128,128]{2,3,0,1:T(8,128)} %bitcast.19, ...), kind=kOutput, calls=%fused_computation.97 | convolution fusion | flops 454819840 | bytes 2490372 | tf_op jit(solution)/shard_map/wkab,wkbc->kac/dot_general | solution.py:29
  31.2 1.1 convolution_bitcast_fusion.2
  32.3 0.1 slice_bitcast_fusion.5
  32.3 3.1 %collective-permute-start.2 = (f32[3,128,128]{2,1,0:T(8,128)S(1)}, f32[3,128,128]{2,1,0:T(8,128)S(1)}, u32[]{:S(2)}, u32[]{:S(2)}) collective-permute-start(f32[3,128,128]{2,1,0:T(8,128)S(1)} %get-tuple-element.14), channel_id=1, source_target_pairs={{0,1},{1,2},{2,3},{3,4},{4,5},{5,6},{6,7},{7,8},{8,9},{9,10},{10,1... | collective-permute-start | bytes 589832 | tf_op jit(solution)/shard_map/ppermute | solution.py:18
  35.4 1.5 %collective-permute-start.3 = (f32[3,128,128]{2,1,0:T(8,128)S(1)}, f32[3,128,128]{2,1,0:T(8,128)S(1)}, u32[]{:S(2)}, u32[]{:S(2)}) collective-permute-start(f32[3,128,128]{2,1,0:T(8,128)S(1)} %get-tuple-element.15), channel_id=1, source_target_pairs={{1,0},{2,1},{3,2},{4,3},{5,4},{6,5},{7,6},{8,7},{9,8},{10,9},{11,1... | collective-permute-start | bytes 589832 | tf_op jit(solution)/shard_map/ppermute | solution.py:18
  36.9 2.4 %collective-permute-done.2 = f32[3,128,128]{2,1,0:T(8,128)S(1)} collective-permute-done((f32[3,128,128]{2,1,0:T(8,128)S(1)}, f32[3,128,128]{2,1,0:T(8,128)S(1)}, u32[]{:S(2)}, u32[]{:S(2)}) %collective-permute-start.2) | collective-permute-done | bytes 196640 | tf_op jit(solution)/shard_map/ppermute | solution.py:18
  39.3 4.3 %collective-permute-done.3 = f32[3,128,128]{2,1,0:T(8,128)S(1)} collective-permute-done((f32[3,128,128]{2,1,0:T(8,128)S(1)}, f32[3,128,128]{2,1,0:T(8,128)S(1)}, u32[]{:S(2)}, u32[]{:S(2)}) %collective-permute-start.3) | collective-permute-done | bytes 196640 | tf_op jit(solution)/shard_map/ppermute | solution.py:18
  43.6 2.7 %multiply_reduce_fusion.4 = (f32[]{:T(128)}, f32[]{:T(128)}, f32[2,128,128]{2,1,0:T(8,128)S(1)}) fusion(f32[3,1,128,128]{3,2,0,1:T(8,128)S(1)} %bitcast.145, f32[3,1,128,128]{3,2,0,1:T(8,128)S(1)} %get-tuple-element.16, f32[3,2,128,128]{3,2,0,1:T(8,128)S(1)} %slice.127, f32[3,1,128,128]{3,2,0,1:T(8,128)S(1)} %get-tuple-element.17, ...), kind=kOutput, calls=%fused_computation.96 | convolution fusion | flops 454918144 | bytes 2490376 | tf_op jit(solution)/shard_map/wkab,wkbc->kac/dot_general | solution.py:29
  46.3 2.0 %pad_maximum_fusion.5 = f32[3]{0:T(128)S(1)} fusion(f32[1]{0:T(128)} %bitcast.35, f32[1]{0:T(128)} %bitcast.34, f32[1]{0:T(128)} %bitcast.33), kind=kLoop, calls=%fused_computation.111 | loop fusion | flops 6 | bytes 24 | tf_op jit(solution)/shard_map/stack | solution.py:23
  48.3 20.6 %all_to_all.17 = f32[32,1,3]{2,1,0:T(1,128)S(1)} all-to-all(f32[32,1,3]{2,1,0:T(1,128)S(1)} %broadcast_in_dim.35), channel_id=1, replica_groups=mesh['seg'=8,'sec'=32] {'sec'}, dimensions={0} | all-to-all | bytes 768 | tf_op jit(solution)/shard_map/all_to_all | solution.py:25
  68.9 0.1 reduce_sum.75
  68.9 0.6 fusion.91
  70.2 1.1 convolution_bitcast_fusion.1
  71.3 0.1 slice_bitcast_fusion.3
  71.4 2.5 %collective-permute-start.4 = (f32[3,128,128]{2,1,0:T(8,128)S(1)}, f32[3,128,128]{2,1,0:T(8,128)S(1)}, u32[]{:S(2)}, u32[]{:S(2)}) collective-permute-start(f32[3,128,128]{2,1,0:T(8,128)S(1)} %get-tuple-element.10), channel_id=1, source_target_pairs={{0,1},{1,2},{2,3},{3,4},{4,5},{5,6},{6,7},{7,8},{8,9},{9,10},{10,1... | collective-permute-start | bytes 589832 | tf_op jit(solution)/shard_map/ppermute | solution.py:18
  73.9 1.3 %collective-permute-start.5 = (f32[3,128,128]{2,1,0:T(8,128)S(1)}, f32[3,128,128]{2,1,0:T(8,128)S(1)}, u32[]{:S(2)}, u32[]{:S(2)}) collective-permute-start(f32[3,128,128]{2,1,0:T(8,128)S(1)} %get-tuple-element.11), channel_id=1, source_target_pairs={{1,0},{2,1},{3,2},{4,3},{5,4},{6,5},{7,6},{8,7},{9,8},{10,9},{11,1... | collective-permute-start | bytes 589832 | tf_op jit(solution)/shard_map/ppermute | solution.py:18
  77.2 0.0 collective-permute-done.4
  77.2 4.2 %collective-permute-done.5 = f32[3,128,128]{2,1,0:T(8,128)S(1)} collective-permute-done((f32[3,128,128]{2,1,0:T(8,128)S(1)}, f32[3,128,128]{2,1,0:T(8,128)S(1)}, u32[]{:S(2)}, u32[]{:S(2)}) %collective-permute-start.5) | collective-permute-done | bytes 196640 | tf_op jit(solution)/shard_map/ppermute | solution.py:18
  81.5 2.6 %multiply_reduce_fusion.2 = (f32[]{:T(128)}, f32[2,128,128]{2,1,0:T(8,128)S(1)}) fusion(f32[]{:T(128)} %bitcast.46, f32[3,1,128,128]{3,2,0,1:T(8,128)S(1)} %bitcast.141, f32[3,1,128,128]{3,2,0,1:T(8,128)S(1)} %get-tuple-element.12, f32[3,2,128,128]{3,2,0,1:T(8,128)S(1)} %slice.133, f32[3,1,128,128]{3,2,0,1:T(8,128)S(1)} %get-tuple-element.13, ...), kind=kOutput, calls=%fused_computation.91 | convolution fusion | flops 454852608 | bytes 2490376 | tf_op jit(solution)/shard_map/wkab,wkbc->kac/dot_general | solution.py:29
  84.1 1.1 convolution_bitcast_fusion
  85.2 0.1 slice_bitcast_fusion.1
  85.3 2.5 %collective-permute-start.6 = (f32[3,128,128]{2,1,0:T(8,128)S(1)}, f32[3,128,128]{2,1,0:T(8,128)S(1)}, u32[]{:S(2)}, u32[]{:S(2)}) collective-permute-start(f32[3,128,128]{2,1,0:T(8,128)S(1)} %get-tuple-element.6), channel_id=1, source_target_pairs={{0,1},{1,2},{2,3},{3,4},{4,5},{5,6},{6,7},{7,8},{8,9},{9,10},{10,1... | collective-permute-start | bytes 589832 | tf_op jit(solution)/shard_map/ppermute | solution.py:18
  87.8 1.3 %collective-permute-start.7 = (f32[3,128,128]{2,1,0:T(8,128)S(1)}, f32[3,128,128]{2,1,0:T(8,128)S(1)}, u32[]{:S(2)}, u32[]{:S(2)}) collective-permute-start(f32[3,128,128]{2,1,0:T(8,128)S(1)} %get-tuple-element.7), channel_id=1, source_target_pairs={{1,0},{2,1},{3,2},{4,3},{5,4},{6,5},{7,6},{8,7},{9,8},{10,9},{11,1... | collective-permute-start | bytes 589832 | tf_op jit(solution)/shard_map/ppermute | solution.py:18
  89.1 1.8 %collective-permute-done.6 = f32[3,128,128]{2,1,0:T(8,128)S(1)} collective-permute-done((f32[3,128,128]{2,1,0:T(8,128)S(1)}, f32[3,128,128]{2,1,0:T(8,128)S(1)}, u32[]{:S(2)}, u32[]{:S(2)}) %collective-permute-start.6) | collective-permute-done | bytes 196640 | tf_op jit(solution)/shard_map/ppermute | solution.py:18
  90.9 4.4 %collective-permute-done.7 = f32[3,128,128]{2,1,0:T(8,128)S(1)} collective-permute-done((f32[3,128,128]{2,1,0:T(8,128)S(1)}, f32[3,128,128]{2,1,0:T(8,128)S(1)}, u32[]{:S(2)}, u32[]{:S(2)}) %collective-permute-start.7) | collective-permute-done | bytes 196640 | tf_op jit(solution)/shard_map/ppermute | solution.py:18
  95.3 0.0 copy-start.4
  95.3 2.7 %multiply_reduce_fusion.1 = (f32[]{:T(128)}, f32[]{:T(128)}, f32[2,128,128]{2,1,0:T(8,128)S(1)}) fusion(f32[3,1,128,128]{3,2,0,1:T(8,128)S(1)} %bitcast.144, f32[3,1,128,128]{3,2,0,1:T(8,128)S(1)} %get-tuple-element.8, f32[3,2,128,128]{3,2,0,1:T(8,128)S(1)} %slice.140, f32[3,1,128,128]{3,2,0,1:T(8,128)S(1)} %get-tuple-element.9, ...), kind=kOutput, calls=%fused_computation.90 | convolution fusion | flops 454918144 | bytes 2490376 | tf_op jit(solution)/shard_map/wkab,wkbc->kac/dot_general | solution.py:29
  98.0 2.0 %pad_maximum_fusion.6 = f32[3]{0:T(128)S(1)} fusion(f32[1]{0:T(128)} %bitcast.58, f32[1]{0:T(128)} %bitcast.57, f32[1]{0:T(128)} %bitcast.56), kind=kLoop, calls=%fused_computation.112 | loop fusion | flops 6 | bytes 24 | tf_op jit(solution)/shard_map/stack | solution.py:23
  100.0 0.6 broadcast_in_dim.36
  100.6 9.4 %all-to-all-start.2 = ((f32[32,1,3]{2,1,0:T(1,128)}), f32[32,1,3]{2,1,0:T(1,128)S(1)}, u32[]{:S(2)}, u32[]{:S(2)}) async-start(f32[32,1,3]{2,1,0:T(1,128)} %broadcast_in_dim.36), calls=%async_computation.2 | async-start | bytes 32768 | tf_op jit(solution)/shard_map/all_to_all | solution.py:25
  110.0 0.0 copy-done.4
  110.0 0.1 compare_convert_fusion
  110.1 9.6 %all-to-all-done.2 = f32[32,1,3]{2,1,0:T(1,128)S(1)} async-done(((f32[32,1,3]{2,1,0:T(1,128)}), f32[32,1,3]{2,1,0:T(1,128)S(1)}, u32[]{:S(2)}, u32[]{:S(2)}) %all-to-all-start.2) | async-done | bytes 416 | tf_op jit(solution)/shard_map/all_to_all | solution.py:25
  119.7 0.1 reduce_sum.79
  119.8 0.6 fusion.90
  123.0 0.7 fusion.72
  123.7 1.1 fusion.55
  (7 shorter events, 0.1 us)
Async XLA Ops:
  0.6 7.9 %copy-start = (f32[1,9,2,128,128]{4,3,2,1,0:T(8,128)S(1)}, f32[1,9,2,128,128]{4,3,2,1,0:T(8,128)}, u32[]{:S(2)}) copy-start(f32[1,9,2,128,128]{4,3,2,1,0:T(8,128)} %param.9) | copy-start | bytes 3538948
  2.7 5.8 %copy-start.2 = (f32[1,2,128,128]{3,2,1,0:T(8,128)S(1)}, f32[1,2,128,128]{3,2,1,0:T(8,128)}, u32[]{:S(2)}) copy-start(f32[1,2,128,128]{3,2,1,0:T(8,128)} %param.6) | copy-start | bytes 393220
  2.7 20.3 %all-to-all-start = ((f32[8,2,128,128]{3,2,1,0:T(8,128)}), f32[8,2,128,128]{3,2,1,0:T(8,128)S(1)}, u32[]{:S(2)}, u32[]{:S(2)}) async-start(f32[8,2,128,128]{3,2,1,0:T(8,128)} %broadcast_in_dim.34), calls=%async_computation | async-start | bytes 2097152 | tf_op jit(solution)/shard_map/all_to_all | solution.py:36
  10.5 5.8 %copy-start.3 = (s32[9,2]{0,1:T(2,128)S(1)}, s32[9,2]{0,1:T(2,128)}, u32[]{:S(2)}) copy-start(s32[9,2]{0,1:T(2,128)} %param.10) | copy-start | bytes 220
  11.3 16.2 %collective-permute-start = (f32[3,128,128]{1,2,0:T(8,128)}, f32[3,128,128]{1,2,0:T(8,128)}, u32[]{:S(2)}, u32[]{:S(2)}) collective-permute-start(f32[3,128,128]{1,2,0:T(8,128)} %get-tuple-element.21), channel_id=1, source_target_pairs={{0,1},{1,2},{2,3},{3,4},{4,5},{5,6},{6,7},{7,8},{8,9},{9,10},{10,1... | collective-permute-start | bytes 589832 | tf_op jit(solution)/shard_map/ppermute | solution.py:18
  15.0 12.5 %collective-permute-start.1 = (f32[3,128,128]{1,2,0:T(8,128)S(1)}, f32[3,128,128]{1,2,0:T(8,128)}, u32[]{:S(2)}, u32[]{:S(2)}) collective-permute-start(f32[3,128,128]{1,2,0:T(8,128)S(1)} %get-tuple-element.22), channel_id=1, source_target_pairs={{1,0},{2,1},{3,2},{4,3},{5,4},{6,5},{7,6},{8,7},{9,8},{10,9},{11,1... | collective-permute-start | bytes 589832 | tf_op jit(solution)/shard_map/ppermute | solution.py:18
  23.3 1.7 %copy-start.1 = (f32[9,2,128,128]{3,2,1,0:T(8,128)S(1)}, f32[9,2,128,128]{3,2,1,0:T(8,128)}, u32[]{:S(2)}) copy-start(f32[9,2,128,128]{3,2,1,0:T(8,128)} %param.7) | copy-start | bytes 3538948
  32.3 7.0 %collective-permute-start.2 = (f32[3,128,128]{2,1,0:T(8,128)S(1)}, f32[3,128,128]{2,1,0:T(8,128)S(1)}, u32[]{:S(2)}, u32[]{:S(2)}) collective-permute-start(f32[3,128,128]{2,1,0:T(8,128)S(1)} %get-tuple-element.14), channel_id=1, source_target_pairs={{0,1},{1,2},{2,3},{3,4},{4,5},{5,6},{6,7},{7,8},{8,9},{9,10},{10,1... | collective-permute-start | bytes 589832 | tf_op jit(solution)/shard_map/ppermute | solution.py:18
  35.4 8.2 %collective-permute-start.3 = (f32[3,128,128]{2,1,0:T(8,128)S(1)}, f32[3,128,128]{2,1,0:T(8,128)S(1)}, u32[]{:S(2)}, u32[]{:S(2)}) collective-permute-start(f32[3,128,128]{2,1,0:T(8,128)S(1)} %get-tuple-element.15), channel_id=1, source_target_pairs={{1,0},{2,1},{3,2},{4,3},{5,4},{6,5},{7,6},{8,7},{9,8},{10,9},{11,1... | collective-permute-start | bytes 589832 | tf_op jit(solution)/shard_map/ppermute | solution.py:18
  71.4 5.9 %collective-permute-start.4 = (f32[3,128,128]{2,1,0:T(8,128)S(1)}, f32[3,128,128]{2,1,0:T(8,128)S(1)}, u32[]{:S(2)}, u32[]{:S(2)}) collective-permute-start(f32[3,128,128]{2,1,0:T(8,128)S(1)} %get-tuple-element.10), channel_id=1, source_target_pairs={{0,1},{1,2},{2,3},{3,4},{4,5},{5,6},{6,7},{7,8},{8,9},{9,10},{10,1... | collective-permute-start | bytes 589832 | tf_op jit(solution)/shard_map/ppermute | solution.py:18
  73.9 7.6 %collective-permute-start.5 = (f32[3,128,128]{2,1,0:T(8,128)S(1)}, f32[3,128,128]{2,1,0:T(8,128)S(1)}, u32[]{:S(2)}, u32[]{:S(2)}) collective-permute-start(f32[3,128,128]{2,1,0:T(8,128)S(1)} %get-tuple-element.11), channel_id=1, source_target_pairs={{1,0},{2,1},{3,2},{4,3},{5,4},{6,5},{7,6},{8,7},{9,8},{10,9},{11,1... | collective-permute-start | bytes 589832 | tf_op jit(solution)/shard_map/ppermute | solution.py:18
  85.3 5.6 %collective-permute-start.6 = (f32[3,128,128]{2,1,0:T(8,128)S(1)}, f32[3,128,128]{2,1,0:T(8,128)S(1)}, u32[]{:S(2)}, u32[]{:S(2)}) collective-permute-start(f32[3,128,128]{2,1,0:T(8,128)S(1)} %get-tuple-element.6), channel_id=1, source_target_pairs={{0,1},{1,2},{2,3},{3,4},{4,5},{5,6},{6,7},{7,8},{8,9},{9,10},{10,1... | collective-permute-start | bytes 589832 | tf_op jit(solution)/shard_map/ppermute | solution.py:18
  87.8 7.6 %collective-permute-start.7 = (f32[3,128,128]{2,1,0:T(8,128)S(1)}, f32[3,128,128]{2,1,0:T(8,128)S(1)}, u32[]{:S(2)}, u32[]{:S(2)}) collective-permute-start(f32[3,128,128]{2,1,0:T(8,128)S(1)} %get-tuple-element.7), channel_id=1, source_target_pairs={{1,0},{2,1},{3,2},{4,3},{5,4},{6,5},{7,6},{8,7},{9,8},{10,9},{11,1... | collective-permute-start | bytes 589832 | tf_op jit(solution)/shard_map/ppermute | solution.py:18
  95.3 14.7 %copy-start.4 = (s32[1,2]{1,0:T(1,128)S(1)}, s32[1,2]{1,0:T(1,128)}, u32[]{:S(2)}) copy-start(s32[1,2]{1,0:T(1,128)} %param.11) | copy-start | bytes 28
  100.6 19.2 %all-to-all-start.2 = ((f32[32,1,3]{2,1,0:T(1,128)}), f32[32,1,3]{2,1,0:T(1,128)S(1)}, u32[]{:S(2)}, u32[]{:S(2)}) async-start(f32[32,1,3]{2,1,0:T(1,128)} %broadcast_in_dim.36), calls=%async_computation.2 | async-start | bytes 32768 | tf_op jit(solution)/shard_map/all_to_all | solution.py:25

commit v4 on v3

--- a/solution.py
+++ b/solution.py
@@ -20,7 +20,7 @@
 
 def gathered_sums(values, axis):
     count = lax.axis_size(axis)
-    row = jnp.stack(values)
+    row = values
     spread = jnp.broadcast_to(row[None], (count, row.shape[0]))
     return jnp.sum(lax.all_to_all(spread, axis, 0, 0, tiled=True), axis=0)
 
@@ -43,18 +43,22 @@
     return mm("kba,wkbd->wkad", prefix, right_side)
 
 
-def apply_terms(vector, right, ordered):
+def apply_terms(vector, right, banded, edges):
+    group = right.shape[0] // 3
+    to_right = mm("ab,wbc->wac", vector[1], right[:group, 1])
+    to_left = mm("ab,wbc->wac", vector[0], right[2 * group :, 0])
+    from_left = shifted(to_right, "sec", 1)
+    from_right = shifted(to_left, "sec", -1)
     products = mm("kab,wkbc->wkac", vector, right)
-    from_left = shifted(products[0::3, 1], "sec", 1)
-    from_right = shifted(products[2::3, 0], "sec", -1)
-    lower = jnp.stack([from_left, products[0::3, 0]], axis=1)
-    upper = jnp.stack([products[2::3, 1], from_right], axis=1)
-    terms = jnp.concatenate([lower, products[1::3], upper], axis=0)
-    return mm("wkab,wkbc->kac", ordered, terms)
+    inner = mm("kawjb,wjbc->kac", banded, products)
+    lower = inner[0] + mm("wab,wbc->ac", edges[0], from_left)
+    upper = inner[1] + mm("wab,wbc->ac", edges[1], from_right)
+    return jnp.stack([lower, upper], axis=0)
 
 
 def square_sums(normal, lifted):
-    return [jnp.sum(normal * normal), jnp.sum(lifted * lifted), jnp.sum(jnp.square(lifted * SHRINK))]
+    stacked = jnp.stack([normal, lifted, lifted * SHRINK], axis=0)
+    return jnp.sum(stacked * stacked, axis=(1, 2, 3))
 
 
 def scales(sums, cells):
@@ -75,14 +79,21 @@
     cells = lax.axis_size("sec") * blocks * width * width
     env = left_environment(left_env, maps)
     weighted = env * mpo_mask.astype(jnp.float32)[:, :, None, None]
+    right = jnp.concatenate([right[0::3], right[1::3], right[2::3]], axis=0)
     ordered = jnp.concatenate([weighted[0::3], weighted[1::3], weighted[2::3]], axis=0)
-    current = apply_terms(vector, right, ordered)
+    group = ordered.shape[0] // 3
+    shift = jnp.repeat(jnp.arange(-1, 2), group)
+    source = jnp.arange(blocks)[:, None, None] + shift[None, :, None]
+    keep = (source == jnp.arange(blocks)[None, None, :]).astype(jnp.float32)
+    banded = jnp.transpose(ordered, (1, 2, 0, 3))[:, :, :, None, :] * keep[:, None, :, :, None]
+    edges = (ordered[:group, 0], ordered[2 * group :, blocks - 1])
+    current = apply_terms(vector, right, banded, edges)
     for pair in range(ITERS // 2):
-        lifted = apply_terms(current * LIFT, right, ordered)
+        lifted = apply_terms(current * LIFT, right, banded, edges)
         first, second = scales(gathered_sums(square_sums(current, lifted), "sec"), cells)
         current = lifted * (first / LIFT)
         if 2 * pair + 2 < ITERS:
-            current = apply_terms(current * LIFT, right, ordered) * (second / LIFT)
+            current = apply_terms(current * LIFT, right, banded, edges) * (second / LIFT)
         else:
             current = current * second
     rows = lax.broadcasted_iota(jnp.int32, (blocks, width), 1) < ranks[0][:, None]

time: 126 us -> 136 us (1.079)
  matrix products: 22.3 us -> 37.8 us
  waiting for transfers between devices: 33.4 us -> 24.7 us
  local copies, waits for them, and re-layouts: 5.03 us -> 9.33 us
    dot_general x18 -> x34, matrix products: 22.3 us -> 37.8 us  [mm(): return jnp.einsum(spec, a, b, precision=HIGH)]
    ppermute x8, waiting for transfers between devices: 17.2 us -> 11.4 us  [shifted(): return lax.ppermute(block, axis, route)]
    another operation x2 -> x3, other arithmetic: 3.97 us -> 0.04 us  [square_sums(): stacked = jnp.stack([normal, lifted, lifted * SHRINK], axis=0)]
    all_to_all x1, waiting for transfers between devices: 6.63 us -> 3.64 us  [left_environment(): every = lax.all_to_all(spread, 'seg', 0, 0, tiled=True)]
    unnamed x10 -> x31, local copies, waits for them, and re-layouts: 0.03 us -> 2.67 us
    transpose x0 -> x1, local copies, waits for them, and re-layouts: none -> 1.63 us  [per_device(): jnp.transpose(ordered, (1, 2, 0, 3))[:, :, :, None, :]]
    mul x0 -> x6, other arithmetic: none -> 1.61 us  [the longest x1 0.89 us: per_device(): current * LIFT]
  transfers between devices with their start and end apart: 10 -> 10, of which waited for: 7 -> 6; matrix products, arithmetic and copies ran while one was open for 6% -> 24% of each run, Pallas kernels for 0% -> 0%
where the time goes in v4:
time: 136 us; the launch traced here: 135 us
  matrix products  37.8 us (28%)
  starting transfers between devices  32.1 us (24%)
  waiting for transfers between devices  24.7 us (18%)
  blocking collectives  20.6 us (15%)
  local copies, waits for them, and re-layouts  9.33 us (7%)
  between operations  6.49 us (5%)
  other arithmetic  3.77 us (3%)
    dot_general x34, matrix products, mm(): return jnp.einsum(spec, a, b, precision=HIGH)  37.8 us
    all_to_all x1, blocking collectives, gathered_sums(): return jnp.sum(lax.all_to_all(spread, axis, 0, 0, tiled=True), axis=0)  20.6 us
    ppermute x8, starting transfers between devices, shifted(): return lax.ppermute(block, axis, route)  16.2 us
    ppermute x8, waiting for transfers between devices, shifted(): return lax.ppermute(block, axis, route)  11.4 us
    all_to_all x1, waiting for transfers between devices, gathered_sums(): return jnp.sum(lax.all_to_all(spread, axis, 0, 0, tiled=True), axis=0)  9.63 us
    all_to_all x1, starting transfers between devices, gathered_sums(): return jnp.sum(lax.all_to_all(spread, axis, 0, 0, tiled=True), axis=0)  9.44 us
    all_to_all x1, starting transfers between devices, left_environment(): every = lax.all_to_all(spread, 'seg', 0, 0, tiled=True)  6.43 us
    all_to_all x1, waiting for transfers between devices, left_environment(): every = lax.all_to_all(spread, 'seg', 0, 0, tiled=True)  3.64 us
  transfers between devices with their start and end apart: 10, of which 6 were waited for; matrix products, arithmetic and copies ran while one was open for 24% of the time, Pallas kernels for 0%

profile of v4, /device:TPU:8, one launch (start us, length us, event | category | flops | bytes accessed | tf_op | source)
XLA Modules:
  0.0 134.8 jit_solution(16512072374073382214)
XLA Ops:
  0.6 2.1 %broadcast_in_dim.18 = f32[8,2,128,128]{3,2,1,0:T(8,128)} broadcast(f32[2,128,128]{2,1,0:T(8,128)} %bitcast.310), dimensions={1,2,3} | broadcast | bytes 1179648 | tf_op jit(solution)/shard_map/broadcast_in_dim | solution.py:35
  2.7 6.4 %all-to-all-start = ((f32[8,2,128,128]{3,2,1,0:T(8,128)}), f32[8,2,128,128]{3,2,1,0:T(8,128)}, u32[]{:S(2)}, u32[]{:S(2)}) async-start(f32[8,2,128,128]{3,2,1,0:T(8,128)} %broadcast_in_dim.18), calls=%async_computation | async-start | bytes 2097152 | tf_op jit(solution)/shard_map/all_to_all | solution.py:36
  9.2 0.4 copy.55
  9.7 0.8 copy-done.10
  10.5 1.0 convolution_bitcast_fusion.13
  11.5 3.1 %collective-permute-start = (f32[3,128,128]{1,2,0:T(8,128)}, f32[3,128,128]{1,2,0:T(8,128)}, u32[]{:S(2)}, u32[]{:S(2)}) collective-permute-start(f32[3,128,128]{1,2,0:T(8,128)} %convolution_bitcast_fusion.13), channel_id=1, source_target_pairs={{0,1},{1,2},{2,3},{3,4},{4,5},{5,6},{6,7},{7,8},{8,9},{9,10},{10,1... | collective-permute-start | bytes 589832 | tf_op jit(solution)/shard_map/ppermute | solution.py:18
  14.6 1.0 convolution_bitcast_fusion.12
  15.6 1.3 collective-permute-start.1
  17.1 3.1 %convolution_bitcast_fusion.3 = f32[9,2,128,128,1]{2,3,0,4,1:T(8,128)} fusion(f32[3,2,128,128]{2,3,0,1:T(8,128)S(1)} %get-tuple-element.6, f32[3,2,128,128]{2,3,0,1:T(8,128)S(1)} %get-tuple-element.7, f32[3,2,128,128]{2,3,0,1:T(8,128)S(1)} %get-tuple-element.5, f32[1,2,128,128]{3,2,1,0:T(8,128)} %param.6), kind=kOutput, calls=%fused_computation.11 | convolution fusion | flops 453574656 | bytes 2490368 | tf_op jit(solution)/shard_map/kab,wkbc->wkac/dot_general | solution.py:29
  20.2 3.6 %all-to-all-done = f32[8,2,128,128]{3,2,1,0:T(8,128)} async-done(((f32[8,2,128,128]{3,2,1,0:T(8,128)}), f32[8,2,128,128]{3,2,1,0:T(8,128)}, u32[]{:S(2)}, u32[]{:S(2)}) %all-to-all-start) | async-done | bytes 1048608 | tf_op jit(solution)/shard_map/all_to_all | solution.py:36
  23.8 1.2 convolution_select_fusion.6
  25.0 1.2 convolution_select_fusion.5
  26.2 1.2 convolution_select_fusion.4
  27.4 1.2 convolution_select_fusion.3
  28.5 1.2 convolution_select_fusion.2
  29.7 1.2 convolution_select_fusion.1
  30.9 1.2 fusion.18
  32.1 1.3 convolution_bitcast_fusion.5
  33.4 1.1 fusion.8
  34.6 0.7 copy-done.1
  35.5 1.1 maximum_bitcast_fusion
  36.6 1.6 %copy.54 = f32[2,128,9,128]{3,1,2,0:T(8,128)S(1)} copy(f32[2,128,9,128]{1,3,2,0:T(8,128)} %maximum_bitcast_fusion) | data formatting | bytes 2359296 | tf_op jit(solution)/shard_map/transpose | solution.py:88
  38.2 3.4 %fusion.19 = f32[2,128,128]{2,1,0:T(8,128)S(1)} fusion(f32[9,2,128,128,1]{2,3,0,4,1:T(8,128)} %convolution_bitcast_fusion.3, f32[2,9,2]{1,0,2:T(2,128)S(1)} %compare_convert_fusion, f32[2,128,9,128]{3,1,2,0:T(8,128)S(1)} %copy.54), kind=kOutput, calls=%fused_computation.42 | convolution fusion | flops 906559488 | bytes 2490512 | tf_op jit(solution)/shard_map/kawjb,wjbc->kac/dot_general | solution.py:29
  41.6 1.4 %fusion.33 = f32[1,128,128]{2,1,0:T(8,128)S(1)} fusion(f32[3,128,128]{1,2,0:T(8,128)} %collective-permute-done, f32[3,2,128,128]{2,3,0,1:T(8,128)S(1)} %copy-done.5, f32[2,128,128]{2,1,0:T(8,128)S(1)} %fusion.19), kind=kOutput, calls=%fused_computation.57 | convolution fusion | flops 75513856 | bytes 524288 | tf_op jit(solution)/shard_map/wab,wbc->ac/dot_general | solution.py:29
  43.1 1.4 %fusion.35 = f32[1,128,128]{2,1,0:T(8,128)S(1)} fusion(f32[3,128,128]{1,2,0:T(8,128)} %collective-permute-done.1, f32[3,2,128,128]{2,3,0,1:T(8,128)S(1)} %copy-done.2, f32[2,128,128]{2,1,0:T(8,128)S(1)} %fusion.19), kind=kOutput, calls=%fused_computation.59 | convolution fusion | flops 75513856 | bytes 524288 | tf_op jit(solution)/shard_map/wab,wbc->ac/dot_general | solution.py:29
  44.6 1.1 convolution_bitcast_fusion.2
  45.7 0.4 convolution_bitcast_fusion.11
  46.1 0.4 convolution_bitcast_fusion.10
  46.5 2.6 %collective-permute-start.2 = (f32[3,128,128]{2,1,0:T(8,128)S(1)}, f32[3,128,128]{2,1,0:T(8,128)S(1)}, u32[]{:S(2)}, u32[]{:S(2)}) collective-permute-start(f32[3,128,128]{2,1,0:T(8,128)S(1)} %convolution_bitcast_fusion.11), channel_id=1, source_target_pairs={{0,1},{1,2},{2,3},{3,4},{4,5},{5,6},{6,7},{7,8},{8,9},{9,10},{10,1... | collective-permute-start | bytes 589832 | tf_op jit(solution)/shard_map/ppermute | solution.py:18
  49.1 1.3 collective-permute-start.3
  50.4 2.1 %fusion.22 = f32[2,128,128]{2,1,0:T(8,128)S(1)} fusion(f32[9,2,128,128,1]{2,3,0,4,1:T(8,128)S(1)} %convolution_bitcast_fusion.2, f32[2,9,2]{1,0,2:T(2,128)S(1)} %compare_convert_fusion, f32[2,128,9,128]{3,1,2,0:T(8,128)S(1)} %copy.54), kind=kOutput, calls=%fused_computation.43 | convolution fusion | flops 906559488 | bytes 2490512 | tf_op jit(solution)/shard_map/kawjb,wjbc->kac/dot_general | solution.py:29
  52.5 0.4 collective-permute-done.2
  52.8 0.5 fusion.36
  53.3 4.0 %collective-permute-done.3 = f32[3,128,128]{2,1,0:T(8,128)S(1)} collective-permute-done((f32[3,128,128]{2,1,0:T(8,128)S(1)}, f32[3,128,128]{2,1,0:T(8,128)S(1)}, u32[]{:S(2)}, u32[]{:S(2)}) %collective-permute-start.3) | collective-permute-done | bytes 196640 | tf_op jit(solution)/shard_map/ppermute | solution.py:18
  57.3 0.5 fusion.37
  57.9 0.6 copy-done.9
  58.6 20.6 %all_to_all.17 = f32[32,1,3]{2,1,0:T(1,128)S(1)} all-to-all(f32[32,1,3]{2,1,0:T(1,128)S(1)} %broadcast_in_dim.20), channel_id=1, replica_groups=mesh['seg'=8,'sec'=32] {'sec'}, dimensions={0} | all-to-all | bytes 768 | tf_op jit(solution)/shard_map/all_to_all | solution.py:25
  79.2 0.6 reduce_sum.37
  79.7 1.4 %fusion.75 = (f32[1]{0:T(128)}, f32[1]{0:T(128)}, f32[1]{0:T(128)}) fusion(f32[3]{0:T(128)} %reduce_sum.37), kind=kLoop, calls=%fused_computation.139 | loop fusion | bytes 24 | tf_op jit(solution)/shard_map/slice | solution.py:68
  81.8 0.9 multiply_multiply_fusion.1
  82.6 0.4 convolution_bitcast_fusion.9
  83.0 1.1 convolution_bitcast_fusion.1
  84.2 0.4 convolution_bitcast_fusion.8
  86.6 2.7 %collective-permute-start.4 = (f32[3,128,128]{2,1,0:T(8,128)S(1)}, f32[3,128,128]{2,1,0:T(8,128)S(1)}, u32[]{:S(2)}, u32[]{:S(2)}) collective-permute-start(f32[3,128,128]{2,1,0:T(8,128)S(1)} %convolution_bitcast_fusion.9), channel_id=1, source_target_pairs={{0,1},{1,2},{2,3},{3,4},{4,5},{5,6},{6,7},{7,8},{8,9},{9,10},{10,1... | collective-permute-start | bytes 589832 | tf_op jit(solution)/shard_map/ppermute | solution.py:18
  89.3 1.3 collective-permute-start.5
  90.6 2.1 %fusion.25 = f32[2,128,128]{2,1,0:T(8,128)S(1)} fusion(f32[9,2,128,128,1]{2,3,0,4,1:T(8,128)S(1)} %convolution_bitcast_fusion.1, f32[2,9,2]{1,0,2:T(2,128)S(1)} %copy-done.12, f32[2,128,9,128]{3,1,2,0:T(8,128)S(1)} %copy.54), kind=kOutput, calls=%fused_computation.44 | convolution fusion | flops 906559488 | bytes 2490512 | tf_op jit(solution)/shard_map/kawjb,wjbc->kac/dot_general | solution.py:29
  92.7 0.5 fusion.38
  93.2 3.7 %collective-permute-done.5 = f32[3,128,128]{2,1,0:T(8,128)S(1)} collective-permute-done((f32[3,128,128]{2,1,0:T(8,128)S(1)}, f32[3,128,128]{2,1,0:T(8,128)S(1)}, u32[]{:S(2)}, u32[]{:S(2)}) %collective-permute-start.5) | collective-permute-done | bytes 196640 | tf_op jit(solution)/shard_map/ppermute | solution.py:18
  96.8 0.5 fusion.39
  97.3 0.4 convolution_bitcast_fusion.7
  97.7 1.1 convolution_bitcast_fusion
  98.9 0.4 convolution_bitcast_fusion.6
  99.2 2.5 %collective-permute-start.6 = (f32[3,128,128]{2,1,0:T(8,128)S(1)}, f32[3,128,128]{2,1,0:T(8,128)S(1)}, u32[]{:S(2)}, u32[]{:S(2)}) collective-permute-start(f32[3,128,128]{2,1,0:T(8,128)S(1)} %convolution_bitcast_fusion.7), channel_id=1, source_target_pairs={{0,1},{1,2},{2,3},{3,4},{4,5},{5,6},{6,7},{7,8},{8,9},{9,10},{10,1... | collective-permute-start | bytes 589832 | tf_op jit(solution)/shard_map/ppermute | solution.py:18
  101.7 1.5 %collective-permute-start.7 = (f32[3,128,128]{2,1,0:T(8,128)S(1)}, f32[3,128,128]{2,1,0:T(8,128)S(1)}, u32[]{:S(2)}, u32[]{:S(2)}) collective-permute-start(f32[3,128,128]{2,1,0:T(8,128)S(1)} %convolution_bitcast_fusion.6), channel_id=1, source_target_pairs={{1,0},{2,1},{3,2},{4,3},{5,4},{6,5},{7,6},{8,7},{9,8},{10,9},{11,1... | collective-permute-start | bytes 589832 | tf_op jit(solution)/shard_map/ppermute | solution.py:18
  103.3 2.1 %fusion.28 = f32[2,128,128]{2,1,0:T(8,128)S(1)} fusion(f32[9,2,128,128,1]{2,3,0,4,1:T(8,128)S(1)} %convolution_bitcast_fusion, f32[2,9,2]{1,0,2:T(2,128)S(1)} %copy-done.12, f32[2,128,9,128]{3,1,2,0:T(8,128)S(1)} %copy.54), kind=kOutput, calls=%fused_computation.45 | convolution fusion | flops 906559488 | bytes 2490512 | tf_op jit(solution)/shard_map/kawjb,wjbc->kac/dot_general | solution.py:29
  105.4 0.5 fusion.40
  105.9 3.4 %collective-permute-done.7 = f32[3,128,128]{2,1,0:T(8,128)S(1)} collective-permute-done((f32[3,128,128]{2,1,0:T(8,128)S(1)}, f32[3,128,128]{2,1,0:T(8,128)S(1)}, u32[]{:S(2)}, u32[]{:S(2)}) %collective-permute-start.7) | collective-permute-done | bytes 196640 | tf_op jit(solution)/shard_map/ppermute | solution.py:18
  109.3 0.5 fusion.41
  110.0 0.6 broadcast_in_dim.42
  110.6 9.4 %all-to-all-start.2 = ((f32[32,1,3]{2,1,0:T(1,128)}), f32[32,1,3]{2,1,0:T(1,128)S(1)}, u32[]{:S(2)}, u32[]{:S(2)}) async-start(f32[32,1,3]{2,1,0:T(1,128)} %broadcast_in_dim.42), calls=%async_computation.2 | async-start | bytes 32768 | tf_op jit(solution)/shard_map/all_to_all | solution.py:25
  120.1 9.6 %all-to-all-done.2 = f32[32,1,3]{2,1,0:T(1,128)S(1)} async-done(((f32[32,1,3]{2,1,0:T(1,128)}), f32[32,1,3]{2,1,0:T(1,128)S(1)}, u32[]{:S(2)}, u32[]{:S(2)}) %all-to-all-start.2) | async-done | bytes 416 | tf_op jit(solution)/shard_map/all_to_all | solution.py:25
  129.8 0.6 fusion.74
  133.0 0.7 multiply_multiply_fusion
  133.7 1.1 fusion.31
  (52 shorter events, 1.1 us)
Async XLA Ops:
  0.6 31.5 %copy-start = (f32[9,2,128,128]{3,2,1,0:T(8,128)S(1)}, f32[9,2,128,128]{3,2,1,0:T(8,128)}, u32[]{:S(2)}) copy-start(f32[9,2,128,128]{3,2,1,0:T(8,128)} %param.7) | copy-start | bytes 3538948
  2.7 6.4 %copy-start.7 = (f32[1,9,2,128,128]{4,3,2,1,0:T(8,128)S(1)}, f32[1,9,2,128,128]{4,3,2,1,0:T(8,128)}, u32[]{:S(2)}) copy-start(f32[1,9,2,128,128]{4,3,2,1,0:T(8,128)} %param.9) | copy-start | bytes 3538948
  2.7 21.1 %all-to-all-start = ((f32[8,2,128,128]{3,2,1,0:T(8,128)}), f32[8,2,128,128]{3,2,1,0:T(8,128)}, u32[]{:S(2)}, u32[]{:S(2)}) async-start(f32[8,2,128,128]{3,2,1,0:T(8,128)} %broadcast_in_dim.18), calls=%async_computation | async-start | bytes 2097152 | tf_op jit(solution)/shard_map/all_to_all | solution.py:36
  9.5 0.9 copy-start.10
  9.6 7.3 %copy-start.13 = (s32[9,2]{0,1:T(2,128)S(1)}, s32[9,2]{0,1:T(2,128)}, u32[]{:S(2)}) copy-start(s32[9,2]{0,1:T(2,128)} %param.10) | copy-start | bytes 220
  11.5 30.2 %collective-permute-start = (f32[3,128,128]{1,2,0:T(8,128)}, f32[3,128,128]{1,2,0:T(8,128)}, u32[]{:S(2)}, u32[]{:S(2)}) collective-permute-start(f32[3,128,128]{1,2,0:T(8,128)} %convolution_bitcast_fusion.13), channel_id=1, source_target_pairs={{0,1},{1,2},{2,3},{3,4},{4,5},{5,6},{6,7},{7,8},{8,9},{9,10},{10,1... | collective-permute-start | bytes 589832 | tf_op jit(solution)/shard_map/ppermute | solution.py:18
  15.6 27.5 %collective-permute-start.1 = (f32[3,128,128]{1,2,0:T(8,128)}, f32[3,128,128]{1,2,0:T(8,128)}, u32[]{:S(2)}, u32[]{:S(2)}) collective-permute-start(f32[3,128,128]{1,2,0:T(8,128)} %convolution_bitcast_fusion.12), channel_id=1, source_target_pairs={{1,0},{2,1},{3,2},{4,3},{5,4},{6,5},{7,6},{8,7},{9,8},{10,9},{11,1... | collective-permute-start | bytes 589832 | tf_op jit(solution)/shard_map/ppermute | solution.py:18
  20.2 30.2 %copy-start.11 = (f32[2,9,2]{1,0,2:T(2,128)}, f32[2,9,2]{1,0,2:T(2,128)S(1)}, u32[]{:S(2)}) copy-start(f32[2,9,2]{1,0,2:T(2,128)S(1)} %compare_convert_fusion) | copy-start | bytes 436
  34.6 0.8 copy-start.1
  34.6 0.9 copy-start.4
  38.2 3.4 %copy-start.5 = (f32[3,2,128,128]{2,3,0,1:T(8,128)S(1)}, f32[3,2,128,128]{2,3,0,1:T(8,128)}, u32[]{:S(2)}) copy-start(f32[3,2,128,128]{2,3,0,1:T(8,128)} %copy-done.4) | copy-start | bytes 1179652
  38.2 4.9 %copy-start.2 = (f32[3,2,128,128]{2,3,0,1:T(8,128)S(1)}, f32[3,2,128,128]{2,3,0,1:T(8,128)}, u32[]{:S(2)}) copy-start(f32[3,2,128,128]{2,3,0,1:T(8,128)} %copy-done.1) | copy-start | bytes 1179652
  46.5 6.4 %collective-permute-start.2 = (f32[3,128,128]{2,1,0:T(8,128)S(1)}, f32[3,128,128]{2,1,0:T(8,128)S(1)}, u32[]{:S(2)}, u32[]{:S(2)}) collective-permute-start(f32[3,128,128]{2,1,0:T(8,128)S(1)} %convolution_bitcast_fusion.11), channel_id=1, source_target_pairs={{0,1},{1,2},{2,3},{3,4},{4,5},{5,6},{6,7},{7,8},{8,9},{9,10},{10,1... | collective-permute-start | bytes 589832 | tf_op jit(solution)/shard_map/ppermute | solution.py:18
  49.1 8.2 %collective-permute-start.3 = (f32[3,128,128]{2,1,0:T(8,128)S(1)}, f32[3,128,128]{2,1,0:T(8,128)S(1)}, u32[]{:S(2)}, u32[]{:S(2)}) collective-permute-start(f32[3,128,128]{2,1,0:T(8,128)S(1)} %convolution_bitcast_fusion.10), channel_id=1, source_target_pairs={{1,0},{2,1},{3,2},{4,3},{5,4},{6,5},{7,6},{8,7},{9,8},{10,9},{11,1... | collective-permute-start | bytes 589832 | tf_op jit(solution)/shard_map/ppermute | solution.py:18
  53.3 4.5 %copy-start.8 = (f32[128,128]{1,0:T(8,128)}, f32[128,128]{1,0:T(8,128)S(1)}, u32[]{:S(2)}) copy-start(f32[128,128]{1,0:T(8,128)S(1)} %fusion.36) | copy-start | bytes 196612
  57.8 0.6 copy-start.9
  83.0 7.5 %copy-start.12 = (f32[2,9,2]{1,0,2:T(2,128)S(1)}, f32[2,9,2]{1,0,2:T(2,128)}, u32[]{:S(2)}) copy-start(f32[2,9,2]{1,0,2:T(2,128)} %copy-done.11) | copy-start | bytes 436
  86.5 6.1 %copy-start.6 = (f32[3,2,128,128]{2,3,0,1:T(8,128)S(1)}, f32[3,2,128,128]{2,3,0,1:T(8,128)}, u32[]{:S(2)}) copy-start(f32[3,2,128,128]{2,3,0,1:T(8,128)} %copy-done.4) | copy-start | bytes 1179652
  86.6 10.3 %copy-start.3 = (f32[3,2,128,128]{2,3,0,1:T(8,128)S(1)}, f32[3,2,128,128]{2,3,0,1:T(8,128)}, u32[]{:S(2)}) copy-start(f32[3,2,128,128]{2,3,0,1:T(8,128)} %copy-done.1) | copy-start | bytes 1179652
  86.6 6.1 %collective-permute-start.4 = (f32[3,128,128]{2,1,0:T(8,128)S(1)}, f32[3,128,128]{2,1,0:T(8,128)S(1)}, u32[]{:S(2)}, u32[]{:S(2)}) collective-permute-start(f32[3,128,128]{2,1,0:T(8,128)S(1)} %convolution_bitcast_fusion.9), channel_id=1, source_target_pairs={{0,1},{1,2},{2,3},{3,4},{4,5},{5,6},{6,7},{7,8},{8,9},{9,10},{10,1... | collective-permute-start | bytes 589832 | tf_op jit(solution)/shard_map/ppermute | solution.py:18
  89.3 7.6 %collective-permute-start.5 = (f32[3,128,128]{2,1,0:T(8,128)S(1)}, f32[3,128,128]{2,1,0:T(8,128)S(1)}, u32[]{:S(2)}, u32[]{:S(2)}) collective-permute-start(f32[3,128,128]{2,1,0:T(8,128)S(1)} %convolution_bitcast_fusion.8), channel_id=1, source_target_pairs={{1,0},{2,1},{3,2},{4,3},{5,4},{6,5},{7,6},{8,7},{9,8},{10,9},{11,1... | collective-permute-start | bytes 589832 | tf_op jit(solution)/shard_map/ppermute | solution.py:18
  99.2 6.1 %collective-permute-start.6 = (f32[3,128,128]{2,1,0:T(8,128)S(1)}, f32[3,128,128]{2,1,0:T(8,128)S(1)}, u32[]{:S(2)}, u32[]{:S(2)}) collective-permute-start(f32[3,128,128]{2,1,0:T(8,128)S(1)} %convolution_bitcast_fusion.7), channel_id=1, source_target_pairs={{0,1},{1,2},{2,3},{3,4},{4,5},{5,6},{6,7},{7,8},{8,9},{9,10},{10,1... | collective-permute-start | bytes 589832 | tf_op jit(solution)/shard_map/ppermute | solution.py:18
  101.7 7.6 %collective-permute-start.7 = (f32[3,128,128]{2,1,0:T(8,128)S(1)}, f32[3,128,128]{2,1,0:T(8,128)S(1)}, u32[]{:S(2)}, u32[]{:S(2)}) collective-permute-start(f32[3,128,128]{2,1,0:T(8,128)S(1)} %convolution_bitcast_fusion.6), channel_id=1, source_target_pairs={{1,0},{2,1},{3,2},{4,3},{5,4},{6,5},{7,6},{8,7},{9,8},{10,9},{11,1... | collective-permute-start | bytes 589832 | tf_op jit(solution)/shard_map/ppermute | solution.py:18
  105.3 14.7 %copy-start.14 = (s32[1,2]{1,0:T(1,128)S(1)}, s32[1,2]{1,0:T(1,128)}, u32[]{:S(2)}) copy-start(s32[1,2]{1,0:T(1,128)} %param.11) | copy-start | bytes 28
  110.6 19.2 %all-to-all-start.2 = ((f32[32,1,3]{2,1,0:T(1,128)}), f32[32,1,3]{2,1,0:T(1,128)S(1)}, u32[]{:S(2)}, u32[]{:S(2)}) async-start(f32[32,1,3]{2,1,0:T(1,128)} %broadcast_in_dim.42), calls=%async_computation.2 | async-start | bytes 32768 | tf_op jit(solution)/shard_map/all_to_all | solution.py:25

commit v5 on v3

--- a/solution.py
+++ b/solution.py
@@ -20,7 +20,7 @@
 
 def gathered_sums(values, axis):
     count = lax.axis_size(axis)
-    row = jnp.stack(values)
+    row = values
     spread = jnp.broadcast_to(row[None], (count, row.shape[0]))
     return jnp.sum(lax.all_to_all(spread, axis, 0, 0, tiled=True), axis=0)
 
@@ -43,10 +43,10 @@
     return mm("kba,wkbd->wkad", prefix, right_side)
 
 
-def apply_terms(vector, right, ordered):
+def apply_terms(vector, right, halo, ordered):
+    from_left = mm("ab,wbc->wac", shifted(vector[1], "sec", 1), halo[0])
+    from_right = mm("ab,wbc->wac", shifted(vector[0], "sec", -1), halo[1])
     products = mm("kab,wkbc->wkac", vector, right)
-    from_left = shifted(products[0::3, 1], "sec", 1)
-    from_right = shifted(products[2::3, 0], "sec", -1)
     lower = jnp.stack([from_left, products[0::3, 0]], axis=1)
     upper = jnp.stack([products[2::3, 1], from_right], axis=1)
     terms = jnp.concatenate([lower, products[1::3], upper], axis=0)
@@ -54,7 +54,8 @@
 
 
 def square_sums(normal, lifted):
-    return [jnp.sum(normal * normal), jnp.sum(lifted * lifted), jnp.sum(jnp.square(lifted * SHRINK))]
+    stacked = jnp.stack([normal, lifted, lifted * SHRINK], axis=0)
+    return jnp.sum(stacked * stacked, axis=(1, 2, 3))
 
 
 def scales(sums, cells):
@@ -76,13 +77,14 @@
     env = left_environment(left_env, maps)
     weighted = env * mpo_mask.astype(jnp.float32)[:, :, None, None]
     ordered = jnp.concatenate([weighted[0::3], weighted[1::3], weighted[2::3]], axis=0)
-    current = apply_terms(vector, right, ordered)
+    halo = (shifted(right[0::3, 1], "sec", 1), shifted(right[2::3, 0], "sec", -1))
+    current = apply_terms(vector, right, halo, ordered)
     for pair in range(ITERS // 2):
-        lifted = apply_terms(current * LIFT, right, ordered)
+        lifted = apply_terms(current * LIFT, right, halo, ordered)
         first, second = scales(gathered_sums(square_sums(current, lifted), "sec"), cells)
         current = lifted * (first / LIFT)
         if 2 * pair + 2 < ITERS:
-            current = apply_terms(current * LIFT, right, ordered) * (second / LIFT)
+            current = apply_terms(current * LIFT, right, halo, ordered) * (second / LIFT)
         else:
             current = current * second
     rows = lax.broadcasted_iota(jnp.int32, (blocks, width), 1) < ranks[0][:, None]

time: 126 us -> 138 us (1.095)
  matrix products: 22.3 us -> 36.7 us
  waiting for transfers between devices: 33.4 us -> 19.3 us
  starting transfers between devices: 32.4 us -> 40.3 us
  local copies, waits for them, and re-layouts: 5.03 us -> 10.1 us
  other arithmetic: 4.83 us -> 1.19 us
  blocking collectives: 20.6 us -> 22.7 us
    dot_general x18 -> x26, matrix products: 22.3 us -> 36.7 us  [mm(): return jnp.einsum(spec, a, b, precision=HIGH)]
    ppermute x8 -> x10, waiting for transfers between devices: 17.2 us -> 9.62 us  [shifted(): return lax.ppermute(block, axis, route)]
    ppermute x8 -> x10, starting transfers between devices: 17.2 us -> 23.8 us  [shifted(): return lax.ppermute(block, axis, route)]
    all_to_all x1, waiting for transfers between devices: 6.63 us -> 0.01 us  [left_environment(): every = lax.all_to_all(spread, 'seg', 0, 0, tiled=True)]
    another operation x2, other arithmetic: 3.97 us -> 0.02 us  [square_sums(): stacked = jnp.stack([normal, lifted, lifted * SHRINK], axis=0)]
    all_to_all x1, blocking collectives: 20.6 us -> 22.7 us  [gathered_sums(): return jnp.sum(lax.all_to_all(spread, axis, 0, 0, tiled=True), axis=0)]
    squeeze x4 -> x6, local copies, waits for them, and re-layouts: 0.9 us -> 2.72 us  [the longest x4 1.56 us: apply_terms(): from_left = mm('ab,wbc->wac', shifted(vector[1], 'sec', 1), halo[0])]
    unnamed x10 -> x21, local copies, waits for them, and re-layouts: 0.03 us -> 1.6 us
  transfers between devices with their start and end apart: 10 -> 12, of which waited for: 7 -> 4; matrix products, arithmetic and copies ran while one was open for 6% -> 12% of each run, Pallas kernels for 0% -> 0%
where the time goes in v5:
time: 138 us; the launch traced here: 137 us
  starting transfers between devices  40.3 us (29%)
  matrix products  36.7 us (27%)
  blocking collectives  22.7 us (16%)
  waiting for transfers between devices  19.3 us (14%)
  local copies, waits for them, and re-layouts  10.1 us (7%)
  between operations  6.45 us (5%)
    dot_general x26, matrix products, mm(): return jnp.einsum(spec, a, b, precision=HIGH)  36.7 us
    ppermute x10, starting transfers between devices, shifted(): return lax.ppermute(block, axis, route)  23.8 us
    all_to_all x1, blocking collectives, gathered_sums(): return jnp.sum(lax.all_to_all(spread, axis, 0, 0, tiled=True), axis=0)  22.7 us
    all_to_all x1, starting transfers between devices, gathered_sums(): return jnp.sum(lax.all_to_all(spread, axis, 0, 0, tiled=True), axis=0)  10 us
    all_to_all x1, waiting for transfers between devices, gathered_sums(): return jnp.sum(lax.all_to_all(spread, axis, 0, 0, tiled=True), axis=0)  9.63 us
    ppermute x10, waiting for transfers between devices, shifted(): return lax.ppermute(block, axis, route)  9.62 us
    all_to_all x1, starting transfers between devices, left_environment(): every = lax.all_to_all(spread, 'seg', 0, 0, tiled=True)  6.44 us
  transfers between devices with their start and end apart: 12, of which 4 were waited for; matrix products, arithmetic and copies ran while one was open for 12% of the time, Pallas kernels for 0%

profile of v5, /device:TPU:8, one launch (start us, length us, event | category | flops | bytes accessed | tf_op | source)
XLA Modules:
  0.0 136.6 jit_solution(8170160102360575719)
XLA Ops:
  0.6 2.1 %broadcast_in_dim.34 = f32[8,2,128,128]{3,2,1,0:T(8,128)} broadcast(f32[2,128,128]{2,1,0:T(8,128)} %bitcast.221), dimensions={1,2,3} | broadcast | bytes 1179648 | tf_op jit(solution)/shard_map/broadcast_in_dim | solution.py:35
  2.7 6.4 %all-to-all-start = ((f32[8,2,128,128]{3,2,1,0:T(8,128)}), f32[8,2,128,128]{3,2,1,0:T(8,128)}, u32[]{:S(2)}, u32[]{:S(2)}) async-start(f32[8,2,128,128]{3,2,1,0:T(8,128)} %broadcast_in_dim.34), calls=%async_computation | async-start | bytes 2097152 | tf_op jit(solution)/shard_map/all_to_all | solution.py:36
  9.2 0.4 copy.59
  9.5 0.8 slice_bitcast_fusion.1
  10.3 1.3 collective-permute-start.2
  11.6 1.5 %slice_bitcast_fusion.23 = (f32[128,128]{1,0:T(8,128)}, f32[128,128]{1,0:T(8,128)}) fusion(f32[1,2,128,128]{3,2,1,0:T(8,128)} %param.6), kind=kLoop, calls=%fused_computation.116 | loop fusion | bytes 262144 | tf_op jit(solution)/shard_map/squeeze | solution.py:47
  13.1 1.3 collective-permute-start.3
  14.4 5.9 %collective-permute-start = (f32[3,128,128]{1,2,0:T(8,128)}, f32[3,128,128]{1,2,0:T(8,128)}, u32[]{:S(2)}, u32[]{:S(2)}) collective-permute-start(f32[3,128,128]{1,2,0:T(8,128)} %get-tuple-element.11), channel_id=1, source_target_pairs={{0,1},{1,2},{2,3},{3,4},{4,5},{5,6},{6,7},{7,8},{8,9},{9,10},{10,1... | collective-permute-start | bytes 589832 | tf_op jit(solution)/shard_map/ppermute | solution.py:18
  20.3 3.9 %collective-permute-start.1 = (f32[128,128]{1,0:T(8,128)}, f32[128,128]{1,0:T(8,128)}, u32[]{:S(2)}, u32[]{:S(2)}) collective-permute-start(f32[128,128]{1,0:T(8,128)} %get-tuple-element.21), channel_id=1, source_target_pairs={{0,1},{1,2},{2,3},{3,4},{4,5},{5,6},{6,7},{7,8},{8,9},{9,10},{10,1... | collective-permute-start | bytes 196616 | tf_op jit(solution)/shard_map/ppermute | solution.py:18
  24.2 2.0 %convolution_bitcast_fusion.3 = f32[9,2,128,128]{2,3,0,1:T(8,128)S(1)} fusion(f32[1,2,128,128]{3,2,1,0:T(8,128)} %param.6, f32[1,9,2,128,128]{3,4,1,2,0:T(8,128)S(1)} %copy.59), kind=kOutput, calls=%fused_computation.3 | convolution fusion | flops 452984832 | bytes 2490368 | tf_op jit(solution)/shard_map/kab,wkbc->wkac/dot_general | solution.py:29
  26.2 0.8 fusion.85
  27.0 0.8 slice.131
  27.8 0.4 copy.84
  28.2 1.3 convolution_bitcast_fusion.12
  29.5 1.9 %convolution_bitcast_fusion.13 = f32[3,1,128,128]{2,3,0,1:T(8,128)} fusion(f32[3,128,128]{1,2,0:T(8,128)} %collective-permute-done, f32[128,128]{1,0:T(8,128)} %collective-permute-done.1), kind=kOutput, calls=%fused_computation.56 | convolution fusion | flops 75497472 | bytes 458752 | tf_op jit(solution)/shard_map/ab,wbc->wac/dot_general | solution.py:29
  31.4 1.2 convolution_select_fusion.6
  32.6 1.2 convolution_select_fusion.5
  33.8 1.2 convolution_select_fusion.4
  35.0 1.2 convolution_select_fusion.3
  36.1 1.2 convolution_select_fusion.2
  37.3 1.2 convolution_select_fusion.1
  38.5 1.2 fusion.42
  39.7 1.3 convolution_bitcast_fusion.5
  41.0 1.1 fusion
  42.1 0.1 fusion.84
  42.2 0.8 copy-done.4
  43.1 0.2 copy-done.5
  43.3 0.1 copy-done.6
  43.4 0.1 copy-done.7
  43.4 2.1 %bitcast_multiply_fusion.4 = (f32[2,128,128]{2,1,0:T(8,128)S(1)}, f32[2,128,128,1]{2,1,3,0:T(8,128)S(1)}) fusion(f32[3,1,128,128]{2,3,0,1:T(8,128)S(1)} %convolution_bitcast_fusion.12, f32[3,1,128,128]{2,3,0,1:T(8,128)S(1)} %copy-done.7, f32[3,2,128,128]{2,3,0,1:T(8,128)S(1)} %copy-done.4, f32[3,1,128,128]{2,3,0,1:T(8,128)S(1)} %copy-done.6, ...), kind=kOutput, calls=%fused_computation.94 | convolution fusion | flops 454787072 | bytes 2621440 | tf_op jit(solution)/shard_map/wkab,wkbc->kac/dot_general | solution.py:29
  45.5 1.8 %collective-permute-start.4 = (f32[128,128]{1,0:T(8,128)S(1)}, f32[128,128]{1,0:T(8,128)S(1)}, u32[]{:S(2)}, u32[]{:S(2)}) collective-permute-start(f32[128,128]{1,0:T(8,128)S(1)} %get-tuple-element.19), channel_id=1, source_target_pairs={{0,1},{1,2},{2,3},{3,4},{4,5},{5,6},{6,7},{7,8},{8,9},{9,10},{10,1... | collective-permute-start | bytes 196616 | tf_op jit(solution)/shard_map/ppermute | solution.py:18
  47.3 1.3 convolution_bitcast_fusion.2
  48.7 1.5 %collective-permute-start.5 = (f32[128,128]{1,0:T(8,128)S(1)}, f32[128,128]{1,0:T(8,128)S(1)}, u32[]{:S(2)}, u32[]{:S(2)}) collective-permute-start(f32[128,128]{1,0:T(8,128)S(1)} %get-tuple-element.20), channel_id=1, source_target_pairs={{1,0},{2,1},{3,2},{4,3},{5,4},{6,5},{7,6},{8,7},{9,8},{10,9},{11,1... | collective-permute-start | bytes 196616 | tf_op jit(solution)/shard_map/ppermute | solution.py:18
  50.2 1.3 convolution_bitcast_fusion.11
  51.5 4.5 %collective-permute-done.5 = f32[128,128]{1,0:T(8,128)S(1)} collective-permute-done((f32[128,128]{1,0:T(8,128)S(1)}, f32[128,128]{1,0:T(8,128)S(1)}, u32[]{:S(2)}, u32[]{:S(2)}) %collective-permute-start.5) | collective-permute-done | bytes 65568 | tf_op jit(solution)/shard_map/ppermute | solution.py:18
  55.9 1.3 convolution_bitcast_fusion.10
  57.3 2.1 %fusion.11 = f32[2,128,128,1]{2,1,3,0:T(8,128)S(1)} fusion(f32[3,1,128,128]{3,2,0,1:T(8,128)S(1)} %convolution_bitcast_fusion.10, f32[3,1,128,128]{3,2,0,1:T(8,128)S(1)} %get-tuple-element.7, f32[3,2,128,128]{3,2,0,1:T(8,128)S(1)} %slice.137, f32[3,1,128,128]{3,2,0,1:T(8,128)S(1)} %get-tuple-element.6, ...), kind=kOutput, calls=%fused_computation.18 | convolution fusion | flops 454754304 | bytes 2490368 | tf_op jit(solution)/shard_map/wkab,wkbc->kac/dot_general | solution.py:29
  59.3 0.1 fusion.50
  59.5 22.7 %all_to_all.17 = f32[32,1,3]{2,1,0:T(1,128)S(1)} all-to-all(f32[32,1,3]{2,1,0:T(1,128)S(1)} %broadcast_in_dim.35), channel_id=1, replica_groups=mesh['seg'=8,'sec'=32] {'sec'}, dimensions={0} | all-to-all | bytes 768 | tf_op jit(solution)/shard_map/all_to_all | solution.py:25
  82.2 0.1 reduce_sum.37
  82.3 0.7 fusion.87
  83.6 1.3 convolution_bitcast_fusion.1
  84.9 2.7 %collective-permute-start.6 = (f32[128,128]{1,0:T(8,128)S(1)}, f32[128,128]{1,0:T(8,128)S(1)}, u32[]{:S(2)}, u32[]{:S(2)}) collective-permute-start(f32[128,128]{1,0:T(8,128)S(1)} %get-tuple-element.17), channel_id=1, source_target_pairs={{0,1},{1,2},{2,3},{3,4},{4,5},{5,6},{6,7},{7,8},{8,9},{9,10},{10,1... | collective-permute-start | bytes 196616 | tf_op jit(solution)/shard_map/ppermute | solution.py:18
  87.6 1.3 collective-permute-start.7
  90.9 1.3 convolution_bitcast_fusion.9
  92.2 1.6 %collective-permute-done.7 = f32[128,128]{1,0:T(8,128)S(1)} collective-permute-done((f32[128,128]{1,0:T(8,128)S(1)}, f32[128,128]{1,0:T(8,128)S(1)}, u32[]{:S(2)}, u32[]{:S(2)}) %collective-permute-start.7) | collective-permute-done | bytes 65568 | tf_op jit(solution)/shard_map/ppermute | solution.py:18
  93.8 1.3 convolution_bitcast_fusion.8
  95.1 2.1 %broadcast_multiply_fusion = (f32[2,128,128]{2,1,0:T(8,128)S(1)}, f32[2,128,128]{2,1,0:T(8,128)S(1)}) fusion(f32[]{:T(128)} %bitcast.62, f32[3,1,128,128]{3,2,0,1:T(8,128)S(1)} %convolution_bitcast_fusion.8, f32[3,1,128,128]{3,2,0,1:T(8,128)S(1)} %get-tuple-element.5, f32[3,2,128,128]{3,2,0,1:T(8,128)S(1)} %slice.143, ...), kind=kOutput, calls=%fused_computation.114 | convolution fusion | flops 454819840 | bytes 2621444 | tf_op jit(solution)/shard_map/wkab,wkbc->kac/dot_general | solution.py:29
  97.2 3.0 %collective-permute-start.8 = (f32[128,128]{1,0:T(8,128)S(1)}, f32[128,128]{1,0:T(8,128)S(1)}, u32[]{:S(2)}, u32[]{:S(2)}) collective-permute-start(f32[128,128]{1,0:T(8,128)S(1)} %get-tuple-element.15), channel_id=1, source_target_pairs={{0,1},{1,2},{2,3},{3,4},{4,5},{5,6},{6,7},{7,8},{8,9},{9,10},{10,1... | collective-permute-start | bytes 196616 | tf_op jit(solution)/shard_map/ppermute | solution.py:18
  100.2 1.3 convolution_bitcast_fusion
  101.5 1.3 collective-permute-start.9
  102.8 1.3 convolution_bitcast_fusion.7
  104.1 3.6 %collective-permute-done.9 = f32[128,128]{1,0:T(8,128)S(1)} collective-permute-done((f32[128,128]{1,0:T(8,128)S(1)}, f32[128,128]{1,0:T(8,128)S(1)}, u32[]{:S(2)}, u32[]{:S(2)}) %collective-permute-start.9) | collective-permute-done | bytes 65568 | tf_op jit(solution)/shard_map/ppermute | solution.py:18
  107.7 1.3 convolution_bitcast_fusion.6
  109.0 2.1 %fusion.31 = f32[2,128,128,1]{2,1,3,0:T(8,128)S(1)} fusion(f32[3,1,128,128]{3,2,0,1:T(8,128)S(1)} %convolution_bitcast_fusion.6, f32[3,1,128,128]{3,2,0,1:T(8,128)S(1)} %get-tuple-element.3, f32[3,2,128,128]{3,2,0,1:T(8,128)S(1)} %slice.150, f32[3,1,128,128]{3,2,0,1:T(8,128)S(1)} %get-tuple-element.2, f32[3,1,128,128]{3,2,0,1:T(8,128)S(1)} %convolution_bitcast_fusion.7, ...), kind=kOutput, calls=%fused_computation.38 | convolution fusion | flops 454754304 | bytes 2490368 | tf_op jit(solution)/shard_map/wkab,wkbc->kac/dot_general | solution.py:29
  111.1 0.1 fusion.51
  111.2 0.6 broadcast_in_dim.36
  111.9 10.0 %all-to-all-start.2 = ((f32[32,1,3]{2,1,0:T(1,128)}), f32[32,1,3]{2,1,0:T(1,128)S(1)}, u32[]{:S(2)}, u32[]{:S(2)}) async-start(f32[32,1,3]{2,1,0:T(1,128)} %broadcast_in_dim.36), calls=%async_computation.2 | async-start | bytes 32768 | tf_op jit(solution)/shard_map/all_to_all | solution.py:25
  121.9 0.1 compare_convert_fusion
  121.9 9.6 %all-to-all-done.2 = f32[32,1,3]{2,1,0:T(1,128)S(1)} async-done(((f32[32,1,3]{2,1,0:T(1,128)}), f32[32,1,3]{2,1,0:T(1,128)S(1)}, u32[]{:S(2)}, u32[]{:S(2)}) %all-to-all-start.2) | async-done | bytes 416 | tf_op jit(solution)/shard_map/all_to_all | solution.py:25
  131.6 0.1 reduce_sum.39
  131.6 0.6 fusion.86
  134.8 0.7 fusion.62
  135.5 1.1 fusion.46
  (39 shorter events, 0.3 us)
Async XLA Ops:
  0.6 39.1 %copy-start = (f32[9,2,128,128]{3,2,1,0:T(8,128)S(1)}, f32[9,2,128,128]{3,2,1,0:T(8,128)}, u32[]{:S(2)}) copy-start(f32[9,2,128,128]{3,2,1,0:T(8,128)} %param.7) | copy-start | bytes 3538948
  2.7 6.4 %copy-start.1 = (f32[1,9,2,128,128]{4,3,2,1,0:T(8,128)S(1)}, f32[1,9,2,128,128]{4,3,2,1,0:T(8,128)}, u32[]{:S(2)}) copy-start(f32[1,9,2,128,128]{4,3,2,1,0:T(8,128)} %param.9) | copy-start | bytes 3538948
  2.7 28.7 %all-to-all-start = ((f32[8,2,128,128]{3,2,1,0:T(8,128)}), f32[8,2,128,128]{3,2,1,0:T(8,128)}, u32[]{:S(2)}, u32[]{:S(2)}) async-start(f32[8,2,128,128]{3,2,1,0:T(8,128)} %broadcast_in_dim.34), calls=%async_computation | async-start | bytes 2097152 | tf_op jit(solution)/shard_map/all_to_all | solution.py:36
  10.3 17.9 %collective-permute-start.2 = (f32[3,128,128]{1,2,0:T(8,128)}, f32[3,128,128]{1,2,0:T(8,128)}, u32[]{:S(2)}, u32[]{:S(2)}) collective-permute-start(f32[3,128,128]{1,2,0:T(8,128)} %get-tuple-element.12), channel_id=1, source_target_pairs={{1,0},{2,1},{3,2},{4,3},{5,4},{6,5},{7,6},{8,7},{9,8},{10,9},{11,1... | collective-permute-start | bytes 589832 | tf_op jit(solution)/shard_map/ppermute | solution.py:18
  13.1 15.0 %collective-permute-start.3 = (f32[128,128]{1,0:T(8,128)}, f32[128,128]{1,0:T(8,128)}, u32[]{:S(2)}, u32[]{:S(2)}) collective-permute-start(f32[128,128]{1,0:T(8,128)} %get-tuple-element.22), channel_id=1, source_target_pairs={{1,0},{2,1},{3,2},{4,3},{5,4},{6,5},{7,6},{8,7},{9,8},{10,9},{11,1... | collective-permute-start | bytes 196616 | tf_op jit(solution)/shard_map/ppermute | solution.py:18
  14.4 15.0 %collective-permute-start = (f32[3,128,128]{1,2,0:T(8,128)}, f32[3,128,128]{1,2,0:T(8,128)}, u32[]{:S(2)}, u32[]{:S(2)}) collective-permute-start(f32[3,128,128]{1,2,0:T(8,128)} %get-tuple-element.11), channel_id=1, source_target_pairs={{0,1},{1,2},{2,3},{3,4},{4,5},{5,6},{6,7},{7,8},{8,9},{9,10},{10,1... | collective-permute-start | bytes 589832 | tf_op jit(solution)/shard_map/ppermute | solution.py:18
  20.3 9.2 %collective-permute-start.1 = (f32[128,128]{1,0:T(8,128)}, f32[128,128]{1,0:T(8,128)}, u32[]{:S(2)}, u32[]{:S(2)}) collective-permute-start(f32[128,128]{1,0:T(8,128)} %get-tuple-element.21), channel_id=1, source_target_pairs={{0,1},{1,2},{2,3},{3,4},{4,5},{5,6},{6,7},{7,8},{8,9},{9,10},{10,1... | collective-permute-start | bytes 196616 | tf_op jit(solution)/shard_map/ppermute | solution.py:18
  26.2 1.6 %copy-start.8 = (s32[9,2]{0,1:T(2,128)S(1)}, s32[9,2]{0,1:T(2,128)}, u32[]{:S(2)}) copy-start(s32[9,2]{0,1:T(2,128)} %param.10) | copy-start | bytes 220
  42.1 1.0 copy-start.4
  42.1 1.2 copy-start.5
  42.1 1.3 copy-start.6
  42.1 1.3 copy-start.7
  42.2 15.0 %copy-start.2 = (f32[3,2,128,128]{2,3,0,1:T(8,128)}, f32[3,2,128,128]{2,3,0,1:T(8,128)S(1)}, u32[]{:S(2)}) copy-start(f32[3,2,128,128]{2,3,0,1:T(8,128)S(1)} %get-tuple-element.10) | copy-start | bytes 1179652
  45.5 4.6 %collective-permute-start.4 = (f32[128,128]{1,0:T(8,128)S(1)}, f32[128,128]{1,0:T(8,128)S(1)}, u32[]{:S(2)}, u32[]{:S(2)}) collective-permute-start(f32[128,128]{1,0:T(8,128)S(1)} %get-tuple-element.19), channel_id=1, source_target_pairs={{0,1},{1,2},{2,3},{3,4},{4,5},{5,6},{6,7},{7,8},{8,9},{9,10},{10,1... | collective-permute-start | bytes 196616 | tf_op jit(solution)/shard_map/ppermute | solution.py:18
  48.7 7.3 %collective-permute-start.5 = (f32[128,128]{1,0:T(8,128)S(1)}, f32[128,128]{1,0:T(8,128)S(1)}, u32[]{:S(2)}, u32[]{:S(2)}) collective-permute-start(f32[128,128]{1,0:T(8,128)S(1)} %get-tuple-element.20), channel_id=1, source_target_pairs={{1,0},{2,1},{3,2},{4,3},{5,4},{6,5},{7,6},{8,7},{9,8},{10,9},{11,1... | collective-permute-start | bytes 196616 | tf_op jit(solution)/shard_map/ppermute | solution.py:18
  84.9 10.2 %copy-start.3 = (f32[3,2,128,128]{2,3,0,1:T(8,128)S(1)}, f32[3,2,128,128]{2,3,0,1:T(8,128)}, u32[]{:S(2)}) copy-start(f32[3,2,128,128]{2,3,0,1:T(8,128)} %copy-done.2) | copy-start | bytes 1179652
  84.9 6.0 %collective-permute-start.6 = (f32[128,128]{1,0:T(8,128)S(1)}, f32[128,128]{1,0:T(8,128)S(1)}, u32[]{:S(2)}, u32[]{:S(2)}) collective-permute-start(f32[128,128]{1,0:T(8,128)S(1)} %get-tuple-element.17), channel_id=1, source_target_pairs={{0,1},{1,2},{2,3},{3,4},{4,5},{5,6},{6,7},{7,8},{8,9},{9,10},{10,1... | collective-permute-start | bytes 196616 | tf_op jit(solution)/shard_map/ppermute | solution.py:18
  87.6 6.2 %collective-permute-start.7 = (f32[128,128]{1,0:T(8,128)S(1)}, f32[128,128]{1,0:T(8,128)S(1)}, u32[]{:S(2)}, u32[]{:S(2)}) collective-permute-start(f32[128,128]{1,0:T(8,128)S(1)} %get-tuple-element.18), channel_id=1, source_target_pairs={{1,0},{2,1},{3,2},{4,3},{5,4},{6,5},{7,6},{8,7},{9,8},{10,9},{11,1... | collective-permute-start | bytes 196616 | tf_op jit(solution)/shard_map/ppermute | solution.py:18
  97.2 5.6 %collective-permute-start.8 = (f32[128,128]{1,0:T(8,128)S(1)}, f32[128,128]{1,0:T(8,128)S(1)}, u32[]{:S(2)}, u32[]{:S(2)}) collective-permute-start(f32[128,128]{1,0:T(8,128)S(1)} %get-tuple-element.15), channel_id=1, source_target_pairs={{0,1},{1,2},{2,3},{3,4},{4,5},{5,6},{6,7},{7,8},{8,9},{9,10},{10,1... | collective-permute-start | bytes 196616 | tf_op jit(solution)/shard_map/ppermute | solution.py:18
  101.5 6.2 %collective-permute-start.9 = (f32[128,128]{1,0:T(8,128)S(1)}, f32[128,128]{1,0:T(8,128)S(1)}, u32[]{:S(2)}, u32[]{:S(2)}) collective-permute-start(f32[128,128]{1,0:T(8,128)S(1)} %get-tuple-element.16), channel_id=1, source_target_pairs={{1,0},{2,1},{3,2},{4,3},{5,4},{6,5},{7,6},{8,7},{9,8},{10,9},{11,1... | collective-permute-start | bytes 196616 | tf_op jit(solution)/shard_map/ppermute | solution.py:18
  109.0 12.9 %copy-start.9 = (s32[1,2]{1,0:T(1,128)S(1)}, s32[1,2]{1,0:T(1,128)}, u32[]{:S(2)}) copy-start(s32[1,2]{1,0:T(1,128)} %param.11) | copy-start | bytes 28
  111.9 19.7 %all-to-all-start.2 = ((f32[32,1,3]{2,1,0:T(1,128)}), f32[32,1,3]{2,1,0:T(1,128)S(1)}, u32[]{:S(2)}, u32[]{:S(2)}) async-start(f32[32,1,3]{2,1,0:T(1,128)} %broadcast_in_dim.36), calls=%async_computation.2 | async-start | bytes 32768 | tf_op jit(solution)/shard_map/all_to_all | solution.py:25

commit v6 on v3

--- a/solution.py
+++ b/solution.py
@@ -20,7 +20,7 @@
 
 def gathered_sums(values, axis):
     count = lax.axis_size(axis)
-    row = jnp.stack(values)
+    row = values
     spread = jnp.broadcast_to(row[None], (count, row.shape[0]))
     return jnp.sum(lax.all_to_all(spread, axis, 0, 0, tiled=True), axis=0)
 
@@ -43,18 +43,30 @@
     return mm("kba,wkbd->wkad", prefix, right_side)
 
 
-def apply_terms(vector, right, ordered):
+def exchange(vector, right):
     products = mm("kab,wkbc->wkac", vector, right)
     from_left = shifted(products[0::3, 1], "sec", 1)
     from_right = shifted(products[2::3, 0], "sec", -1)
+    return products, from_left, from_right
+
+
+def combine(parts, ordered, factor=None):
+    products, from_left, from_right = parts
     lower = jnp.stack([from_left, products[0::3, 0]], axis=1)
     upper = jnp.stack([products[2::3, 1], from_right], axis=1)
     terms = jnp.concatenate([lower, products[1::3], upper], axis=0)
+    if factor is not None:
+        terms = terms * factor
     return mm("wkab,wkbc->kac", ordered, terms)
 
 
+def apply_terms(vector, right, ordered):
+    return combine(exchange(vector, right), ordered)
+
+
 def square_sums(normal, lifted):
-    return [jnp.sum(normal * normal), jnp.sum(lifted * lifted), jnp.sum(jnp.square(lifted * SHRINK))]
+    stacked = jnp.stack([normal, lifted, lifted * SHRINK], axis=0)
+    return jnp.sum(stacked * stacked, axis=(1, 2, 3))
 
 
 def scales(sums, cells):
@@ -79,12 +91,14 @@
     current = apply_terms(vector, right, ordered)
     for pair in range(ITERS // 2):
         lifted = apply_terms(current * LIFT, right, ordered)
+        more = 2 * pair + 2 < ITERS
+        if more:
+            parts = exchange(lifted * LIFT, right)
         first, second = scales(gathered_sums(square_sums(current, lifted), "sec"), cells)
-        current = lifted * (first / LIFT)
-        if 2 * pair + 2 < ITERS:
-            current = apply_terms(current * LIFT, right, ordered) * (second / LIFT)
+        if more:
+            current = combine(parts, ordered, first / LIFT) * (second / LIFT)
         else:
-            current = current * second
+            current = lifted * (first / LIFT) * second
     rows = lax.broadcasted_iota(jnp.int32, (blocks, width), 1) < ranks[0][:, None]
     trimmed = current * rows.astype(jnp.float32)[:, :, None]
     density = mm("kab,kcb->kac", trimmed, trimmed) / width

time: 126 us -> 119 us (0.944)
  blocking collectives: 20.6 us -> 0 us
  starting transfers between devices: 32.4 us -> 43.9 us
  waiting for transfers between devices: 33.4 us -> 38.8 us
  other arithmetic: 4.83 us -> 1.17 us
  local copies, waits for them, and re-layouts: 5.03 us -> 8.22 us
  matrix products: 22.3 us -> 20.2 us
    all_to_all x1 -> x0, blocking collectives: 20.6 us -> none  [gathered_sums(): return jnp.sum(lax.all_to_all(spread, axis, 0, 0, tiled=True), axis=0)]
    all_to_all x1 -> x2, starting transfers between devices: 9.43 us -> 19.6 us  [gathered_sums(): return jnp.sum(lax.all_to_all(spread, axis, 0, 0, tiled=True), axis=0)]
    all_to_all x1 -> x2, waiting for transfers between devices: 9.63 us -> 18.6 us  [gathered_sums(): return jnp.sum(lax.all_to_all(spread, axis, 0, 0, tiled=True), axis=0)]
    ppermute x8, waiting for transfers between devices: 17.2 us -> 13 us  [shifted(): return lax.ppermute(block, axis, route)]
    another operation x2, other arithmetic: 3.97 us -> 0.02 us  [square_sums(): stacked = jnp.stack([normal, lifted, lifted * SHRINK], axis=0)]
    dot_general x18, matrix products: 22.3 us -> 20.2 us  [mm(): return jnp.einsum(spec, a, b, precision=HIGH)]
    slice x4, local copies, waits for them, and re-layouts: 0.11 us -> 1.61 us  [combine(): terms = jnp.concatenate([lower, products[1::3], upper], axis=0)]
    ppermute x8, starting transfers between devices: 17.2 us -> 18.5 us  [shifted(): return lax.ppermute(block, axis, route)]
  transfers between devices with their start and end apart: 10 -> 11, of which waited for: 7 -> 7; matrix products, arithmetic and copies ran while one was open for 6% -> 8% of each run, Pallas kernels for 0% -> 0%
where the time goes in v6:
time: 119 us; the launch traced here: 118 us
  starting transfers between devices  43.9 us (37%)
  waiting for transfers between devices  38.8 us (33%)
  matrix products  20.2 us (17%)
  local copies, waits for them, and re-layouts  8.22 us (7%)
  between operations  6.25 us (5%)
    dot_general x18, matrix products, mm(): return jnp.einsum(spec, a, b, precision=HIGH)  20.2 us
    all_to_all x2, starting transfers between devices, gathered_sums(): return jnp.sum(lax.all_to_all(spread, axis, 0, 0, tiled=True), axis=0)  19.6 us
    all_to_all x2, waiting for transfers between devices, gathered_sums(): return jnp.sum(lax.all_to_all(spread, axis, 0, 0, tiled=True), axis=0)  18.6 us
    ppermute x8, starting transfers between devices, shifted(): return lax.ppermute(block, axis, route)  18.5 us
    ppermute x8, waiting for transfers between devices, shifted(): return lax.ppermute(block, axis, route)  13 us
    all_to_all x1, waiting for transfers between devices, left_environment(): every = lax.all_to_all(spread, 'seg', 0, 0, tiled=True)  7.23 us
    all_to_all x1, starting transfers between devices, left_environment(): every = lax.all_to_all(spread, 'seg', 0, 0, tiled=True)  5.78 us
  transfers between devices with their start and end apart: 11, of which 7 were waited for; matrix products, arithmetic and copies ran while one was open for 8% of the time, Pallas kernels for 0%

profile of v6, /device:TPU:8, one launch (start us, length us, event | category | flops | bytes accessed | tf_op | source)
XLA Modules:
  0.0 118.5 jit_solution(4445215237355181680)
XLA Ops:
  0.6 0.0 copy-start
  0.6 2.1 %broadcast_in_dim.34 = f32[8,2,128,128]{3,2,1,0:T(8,128)} broadcast(f32[2,128,128]{2,1,0:T(8,128)} %bitcast.164), dimensions={1,2,3} | broadcast | bytes 1179648 | tf_op jit(solution)/shard_map/broadcast_in_dim | solution.py:35
  2.7 5.8 %all-to-all-start = ((f32[8,2,128,128]{3,2,1,0:T(8,128)}), f32[8,2,128,128]{3,2,1,0:T(8,128)S(1)}, u32[]{:S(2)}, u32[]{:S(2)}) async-start(f32[8,2,128,128]{3,2,1,0:T(8,128)} %broadcast_in_dim.34), calls=%async_computation | async-start | bytes 2097152 | tf_op jit(solution)/shard_map/all_to_all | solution.py:36
  8.5 0.0 copy-done
  8.5 2.0 %convolution_bitcast_fusion.3 = f32[9,2,128,128]{2,3,0,1:T(8,128)S(1)} fusion(f32[1,2,128,128]{3,2,1,0:T(8,128)S(1)} %copy-done.3, f32[1,9,2,128,128]{4,3,2,1,0:T(8,128)S(1)} %copy-done), kind=kOutput, calls=%fused_computation.3 | convolution fusion | flops 452984832 | bytes 2490368 | tf_op jit(solution)/shard_map/kab,wkbc->wkac/dot_general | solution.py:29
  10.5 0.0 copy-start.4
  10.5 0.1 slice_bitcast_fusion.7
  10.6 3.1 %collective-permute-start = (f32[3,128,128]{1,2,0:T(8,128)S(1)}, f32[3,128,128]{1,2,0:T(8,128)S(1)}, u32[]{:S(2)}, u32[]{:S(2)}) collective-permute-start(f32[3,128,128]{1,2,0:T(8,128)S(1)} %get-tuple-element.17), channel_id=1, source_target_pairs={{0,1},{1,2},{2,3},{3,4},{4,5},{5,6},{6,7},{7,8},{8,9},{9,10},{10,1... | collective-permute-start | bytes 589832 | tf_op jit(solution)/shard_map/ppermute | solution.py:18
  13.7 1.3 %collective-permute-start.1 = (f32[3,128,128]{1,2,0:T(8,128)S(1)}, f32[3,128,128]{1,2,0:T(8,128)S(1)}, u32[]{:S(2)}, u32[]{:S(2)}) collective-permute-start(f32[3,128,128]{1,2,0:T(8,128)S(1)} %get-tuple-element.18), channel_id=1, source_target_pairs={{1,0},{2,1},{3,2},{4,3},{5,4},{6,5},{7,6},{8,7},{9,8},{10,9},{11,1... | collective-permute-start | bytes 589832 | tf_op jit(solution)/shard_map/ppermute | solution.py:18
  15.0 0.8 slice.122
  15.8 0.0 copy-done.4
  15.8 7.2 %all-to-all-done = f32[8,2,128,128]{3,2,1,0:T(8,128)S(1)} async-done(((f32[8,2,128,128]{3,2,1,0:T(8,128)}), f32[8,2,128,128]{3,2,1,0:T(8,128)S(1)}, u32[]{:S(2)}, u32[]{:S(2)}) %all-to-all-start) | async-done | bytes 1048608 | tf_op jit(solution)/shard_map/all_to_all | solution.py:36
  23.0 0.3 convolution_select_fusion.6
  23.3 0.0 copy-start.1
  23.3 0.3 convolution_select_fusion.5
  23.6 0.3 convolution_select_fusion.4
  23.9 0.3 convolution_select_fusion.3
  24.2 0.3 convolution_select_fusion.2
  24.4 0.3 convolution_select_fusion.1
  24.7 0.3 fusion.42
  25.0 1.3 %convolution_bitcast_fusion.5 = f32[9,2,128,128]{2,3,0,1:T(8,128)S(1)} fusion(f32[2,128,128,1]{2,1,3,0:T(8,128)S(1)} %fusion.42, f32[9,2,128,128]{3,2,1,0:T(8,128)S(1)} %copy-done.1), kind=kOutput, calls=%fused_computation.5 | convolution fusion | flops 452984832 | bytes 2490368 | tf_op jit(solution)/shard_map/wkbc,kcd->wkbd/dot_general | solution.py:29
  26.3 1.1 fusion
  27.4 0.1 fusion.78
  27.5 0.0 collective-permute-done
  27.5 0.0 collective-permute-done.1
  27.5 0.9 copy-done.2
  28.4 2.0 %fusion.1 = f32[2,128,128,1]{2,1,3,0:T(8,128)S(1)} fusion(f32[3,1,128,128]{2,3,0,1:T(8,128)S(1)} %bitcast.166, f32[3,1,128,128]{2,3,0,1:T(8,128)S(1)} %get-tuple-element.19, f32[3,2,128,128]{2,3,0,1:T(8,128)S(1)} %copy-done.2, f32[3,1,128,128]{2,3,0,1:T(8,128)S(1)} %get-tuple-element.20, f32[3,1,128,128]{2,3,0,1:T(8,128)S(1)} %bitcast.165, ...), kind=kOutput, calls=%fused_computation.8 | convolution fusion | flops 454754304 | bytes 2490368 | tf_op jit(solution)/shard_map/wkab,wkbc->kac/dot_general | solution.py:29
  30.4 1.1 convolution_bitcast_fusion.2
  31.5 0.1 slice_bitcast_fusion.5
  31.6 3.1 %collective-permute-start.2 = (f32[3,128,128]{2,1,0:T(8,128)S(1)}, f32[3,128,128]{2,1,0:T(8,128)S(1)}, u32[]{:S(2)}, u32[]{:S(2)}) collective-permute-start(f32[3,128,128]{2,1,0:T(8,128)S(1)} %get-tuple-element.10), channel_id=1, source_target_pairs={{0,1},{1,2},{2,3},{3,4},{4,5},{5,6},{6,7},{7,8},{8,9},{9,10},{10,1... | collective-permute-start | bytes 589832 | tf_op jit(solution)/shard_map/ppermute | solution.py:18
  34.7 1.5 %collective-permute-start.3 = (f32[3,128,128]{2,1,0:T(8,128)S(1)}, f32[3,128,128]{2,1,0:T(8,128)S(1)}, u32[]{:S(2)}, u32[]{:S(2)}) collective-permute-start(f32[3,128,128]{2,1,0:T(8,128)S(1)} %get-tuple-element.11), channel_id=1, source_target_pairs={{1,0},{2,1},{3,2},{4,3},{5,4},{6,5},{7,6},{8,7},{9,8},{10,9},{11,1... | collective-permute-start | bytes 589832 | tf_op jit(solution)/shard_map/ppermute | solution.py:18
  36.2 2.4 %collective-permute-done.2 = f32[3,128,128]{2,1,0:T(8,128)S(1)} collective-permute-done((f32[3,128,128]{2,1,0:T(8,128)S(1)}, f32[3,128,128]{2,1,0:T(8,128)S(1)}, u32[]{:S(2)}, u32[]{:S(2)}) %collective-permute-start.2) | collective-permute-done | bytes 196640 | tf_op jit(solution)/shard_map/ppermute | solution.py:18
  38.6 4.3 %collective-permute-done.3 = f32[3,128,128]{2,1,0:T(8,128)S(1)} collective-permute-done((f32[3,128,128]{2,1,0:T(8,128)S(1)}, f32[3,128,128]{2,1,0:T(8,128)S(1)}, u32[]{:S(2)}, u32[]{:S(2)}) %collective-permute-start.3) | collective-permute-done | bytes 196640 | tf_op jit(solution)/shard_map/ppermute | solution.py:18
  42.9 2.1 %fusion.11 = f32[2,128,128,1]{2,1,3,0:T(8,128)S(1)} fusion(f32[3,1,128,128]{3,2,0,1:T(8,128)S(1)} %bitcast.170, f32[3,1,128,128]{3,2,0,1:T(8,128)S(1)} %get-tuple-element.12, f32[3,2,128,128]{3,2,0,1:T(8,128)S(1)} %slice.127, f32[3,1,128,128]{3,2,0,1:T(8,128)S(1)} %get-tuple-element.13, f32[3,1,128,128]{3,2,0,1:T(8,128)S(1)} %bitcast.168, ...), kind=kOutput, calls=%fused_computation.18 | convolution fusion | flops 454754304 | bytes 2490368 | tf_op jit(solution)/shard_map/wkab,wkbc->kac/dot_general | solution.py:29
  45.0 1.1 convolution_bitcast_fusion.1
  46.1 0.9 slice_bitcast_fusion.3
  47.0 4.5 %collective-permute-start.4 = (f32[3,128,128]{2,1,0:T(8,128)}, f32[3,128,128]{2,1,0:T(8,128)}, u32[]{:S(2)}, u32[]{:S(2)}) collective-permute-start(f32[3,128,128]{2,1,0:T(8,128)} %get-tuple-element.6), channel_id=1, source_target_pairs={{0,1},{1,2},{2,3},{3,4},{4,5},{5,6},{6,7},{7,8},{8,9},{9,10},{10,1... | collective-permute-start | bytes 589832 | tf_op jit(solution)/shard_map/ppermute | solution.py:18
  51.5 1.3 %collective-permute-start.5 = (f32[3,128,128]{2,1,0:T(8,128)}, f32[3,128,128]{2,1,0:T(8,128)}, u32[]{:S(2)}, u32[]{:S(2)}) collective-permute-start(f32[3,128,128]{2,1,0:T(8,128)} %get-tuple-element.7), channel_id=1, source_target_pairs={{1,0},{2,1},{3,2},{4,3},{5,4},{6,5},{7,6},{8,7},{9,8},{10,9},{11,1... | collective-permute-start | bytes 589832 | tf_op jit(solution)/shard_map/ppermute | solution.py:18
  52.8 0.1 fusion.50
  52.9 0.6 broadcast_in_dim.35
  53.6 11.7 %all-to-all-start.1 = ((f32[32,1,3]{2,1,0:T(1,128)}), f32[32,1,3]{2,1,0:T(1,128)S(1)}, u32[]{:S(2)}, u32[]{:S(2)}) async-start(f32[32,1,3]{2,1,0:T(1,128)} %broadcast_in_dim.35), calls=%async_computation.1 | async-start | bytes 32768 | tf_op jit(solution)/shard_map/all_to_all | solution.py:25
  65.3 0.8 slice.132
  66.0 8.9 %all-to-all-done.1 = f32[32,1,3]{2,1,0:T(1,128)S(1)} async-done(((f32[32,1,3]{2,1,0:T(1,128)}), f32[32,1,3]{2,1,0:T(1,128)S(1)}, u32[]{:S(2)}, u32[]{:S(2)}) %all-to-all-start.1) | async-done | bytes 416 | tf_op jit(solution)/shard_map/all_to_all | solution.py:25
  75.0 0.1 reduce_sum.37
  75.0 0.6 fusion.80
  78.3 0.0 collective-permute-done.4
  78.3 0.0 collective-permute-done.5
  78.3 3.4 %fusion.44 = f32[2,128,128]{2,1,0:T(8,128)S(1)} fusion(f32[3,1,128,128]{3,2,0,1:T(8,128)} %bitcast.39, f32[3,1,128,128]{3,2,0,1:T(8,128)} %get-tuple-element.8, f32[3,2,128,128]{3,2,0,1:T(8,128)} %slice.132, f32[3,1,128,128]{3,2,0,1:T(8,128)} %get-tuple-element.9, f32[3,1,128,128]{3,2,0,1:T(8,128)} %bitcast.37, f32[]{:T(128)} %bitcast.43, ...), kind=kOutput, calls=%fused_computation.60 | convolution fusion | flops 455081984 | bytes 2490376 | tf_op jit(solution)/shard_map/wkab,wkbc->kac/dot_general | solution.py:29
  81.6 1.1 convolution_bitcast_fusion
  82.7 0.1 slice_bitcast_fusion.1
  82.8 2.5 %collective-permute-start.6 = (f32[3,128,128]{2,1,0:T(8,128)S(1)}, f32[3,128,128]{2,1,0:T(8,128)S(1)}, u32[]{:S(2)}, u32[]{:S(2)}) collective-permute-start(f32[3,128,128]{2,1,0:T(8,128)S(1)} %get-tuple-element.2), channel_id=1, source_target_pairs={{0,1},{1,2},{2,3},{3,4},{4,5},{5,6},{6,7},{7,8},{8,9},{9,10},{10,1... | collective-permute-start | bytes 589832 | tf_op jit(solution)/shard_map/ppermute | solution.py:18
  85.3 1.3 %collective-permute-start.7 = (f32[3,128,128]{2,1,0:T(8,128)S(1)}, f32[3,128,128]{2,1,0:T(8,128)S(1)}, u32[]{:S(2)}, u32[]{:S(2)}) collective-permute-start(f32[3,128,128]{2,1,0:T(8,128)S(1)} %get-tuple-element.3), channel_id=1, source_target_pairs={{1,0},{2,1},{3,2},{4,3},{5,4},{6,5},{7,6},{8,7},{9,8},{10,9},{11,1... | collective-permute-start | bytes 589832 | tf_op jit(solution)/shard_map/ppermute | solution.py:18
  86.7 1.8 %collective-permute-done.6 = f32[3,128,128]{2,1,0:T(8,128)S(1)} collective-permute-done((f32[3,128,128]{2,1,0:T(8,128)S(1)}, f32[3,128,128]{2,1,0:T(8,128)S(1)}, u32[]{:S(2)}, u32[]{:S(2)}) %collective-permute-start.6) | collective-permute-done | bytes 196640 | tf_op jit(solution)/shard_map/ppermute | solution.py:18
  88.5 4.4 %collective-permute-done.7 = f32[3,128,128]{2,1,0:T(8,128)S(1)} collective-permute-done((f32[3,128,128]{2,1,0:T(8,128)S(1)}, f32[3,128,128]{2,1,0:T(8,128)S(1)}, u32[]{:S(2)}, u32[]{:S(2)}) %collective-permute-start.7) | collective-permute-done | bytes 196640 | tf_op jit(solution)/shard_map/ppermute | solution.py:18
  92.9 2.0 %fusion.30 = f32[2,128,128,1]{2,1,3,0:T(8,128)S(1)} fusion(f32[3,1,128,128]{3,2,0,1:T(8,128)S(1)} %bitcast.169, f32[3,1,128,128]{3,2,0,1:T(8,128)S(1)} %get-tuple-element.4, f32[3,2,128,128]{3,2,0,1:T(8,128)S(1)} %slice.140, f32[3,1,128,128]{3,2,0,1:T(8,128)S(1)} %get-tuple-element.5, f32[3,1,128,128]{3,2,0,1:T(8,128)S(1)} %bitcast.167, ...), kind=kOutput, calls=%fused_computation.38 | convolution fusion | flops 454754304 | bytes 2490368 | tf_op jit(solution)/shard_map/wkab,wkbc->kac/dot_general | solution.py:29
  95.0 0.1 fusion.51
  95.1 0.6 broadcast_in_dim.36
  95.7 7.9 %all-to-all-start.2 = ((f32[32,1,3]{2,1,0:T(1,128)}), f32[32,1,3]{2,1,0:T(1,128)S(1)}, u32[]{:S(2)}, u32[]{:S(2)}) async-start(f32[32,1,3]{2,1,0:T(1,128)} %broadcast_in_dim.36), calls=%async_computation.2 | async-start | bytes 32768 | tf_op jit(solution)/shard_map/all_to_all | solution.py:25
  103.6 0.1 compare_convert_fusion
  103.7 9.6 %all-to-all-done.2 = f32[32,1,3]{2,1,0:T(1,128)S(1)} async-done(((f32[32,1,3]{2,1,0:T(1,128)}), f32[32,1,3]{2,1,0:T(1,128)S(1)}, u32[]{:S(2)}, u32[]{:S(2)}) %all-to-all-start.2) | async-done | bytes 416 | tf_op jit(solution)/shard_map/all_to_all | solution.py:25
  113.3 0.1 reduce_sum.39
  113.4 0.7 fusion.79
  116.7 0.7 fusion.62
  117.4 1.1 fusion.43
  (12 shorter events, 0.1 us)
Async XLA Ops:
  0.6 7.9 %copy-start = (f32[1,9,2,128,128]{4,3,2,1,0:T(8,128)S(1)}, f32[1,9,2,128,128]{4,3,2,1,0:T(8,128)}, u32[]{:S(2)}) copy-start(f32[1,9,2,128,128]{4,3,2,1,0:T(8,128)} %param.9) | copy-start | bytes 3538948
  2.7 5.8 %copy-start.3 = (f32[1,2,128,128]{3,2,1,0:T(8,128)S(1)}, f32[1,2,128,128]{3,2,1,0:T(8,128)}, u32[]{:S(2)}) copy-start(f32[1,2,128,128]{3,2,1,0:T(8,128)} %param.6) | copy-start | bytes 393220
  2.7 20.3 %all-to-all-start = ((f32[8,2,128,128]{3,2,1,0:T(8,128)}), f32[8,2,128,128]{3,2,1,0:T(8,128)S(1)}, u32[]{:S(2)}, u32[]{:S(2)}) async-start(f32[8,2,128,128]{3,2,1,0:T(8,128)} %broadcast_in_dim.34), calls=%async_computation | async-start | bytes 2097152 | tf_op jit(solution)/shard_map/all_to_all | solution.py:36
  10.5 5.3 %copy-start.4 = (s32[9,2]{0,1:T(2,128)S(1)}, s32[9,2]{0,1:T(2,128)}, u32[]{:S(2)}) copy-start(s32[9,2]{0,1:T(2,128)} %param.10) | copy-start | bytes 220
  10.6 16.9 %collective-permute-start = (f32[3,128,128]{1,2,0:T(8,128)S(1)}, f32[3,128,128]{1,2,0:T(8,128)S(1)}, u32[]{:S(2)}, u32[]{:S(2)}) collective-permute-start(f32[3,128,128]{1,2,0:T(8,128)S(1)} %get-tuple-element.17), channel_id=1, source_target_pairs={{0,1},{1,2},{2,3},{3,4},{4,5},{5,6},{6,7},{7,8},{8,9},{9,10},{10,1... | collective-permute-start | bytes 589832 | tf_op jit(solution)/shard_map/ppermute | solution.py:18
  13.7 13.8 %collective-permute-start.1 = (f32[3,128,128]{1,2,0:T(8,128)S(1)}, f32[3,128,128]{1,2,0:T(8,128)S(1)}, u32[]{:S(2)}, u32[]{:S(2)}) collective-permute-start(f32[3,128,128]{1,2,0:T(8,128)S(1)} %get-tuple-element.18), channel_id=1, source_target_pairs={{1,0},{2,1},{3,2},{4,3},{5,4},{6,5},{7,6},{8,7},{9,8},{10,9},{11,1... | collective-permute-start | bytes 589832 | tf_op jit(solution)/shard_map/ppermute | solution.py:18
  23.3 1.7 %copy-start.1 = (f32[9,2,128,128]{3,2,1,0:T(8,128)S(1)}, f32[9,2,128,128]{3,2,1,0:T(8,128)}, u32[]{:S(2)}) copy-start(f32[9,2,128,128]{3,2,1,0:T(8,128)} %param.7) | copy-start | bytes 3538948
  27.4 1.0 copy-start.2
  31.6 7.0 %collective-permute-start.2 = (f32[3,128,128]{2,1,0:T(8,128)S(1)}, f32[3,128,128]{2,1,0:T(8,128)S(1)}, u32[]{:S(2)}, u32[]{:S(2)}) collective-permute-start(f32[3,128,128]{2,1,0:T(8,128)S(1)} %get-tuple-element.10), channel_id=1, source_target_pairs={{0,1},{1,2},{2,3},{3,4},{4,5},{5,6},{6,7},{7,8},{8,9},{9,10},{10,1... | collective-permute-start | bytes 589832 | tf_op jit(solution)/shard_map/ppermute | solution.py:18
  34.7 8.2 %collective-permute-start.3 = (f32[3,128,128]{2,1,0:T(8,128)S(1)}, f32[3,128,128]{2,1,0:T(8,128)S(1)}, u32[]{:S(2)}, u32[]{:S(2)}) collective-permute-start(f32[3,128,128]{2,1,0:T(8,128)S(1)} %get-tuple-element.11), channel_id=1, source_target_pairs={{1,0},{2,1},{3,2},{4,3},{5,4},{6,5},{7,6},{8,7},{9,8},{10,9},{11,1... | collective-permute-start | bytes 589832 | tf_op jit(solution)/shard_map/ppermute | solution.py:18
  47.0 31.3 %collective-permute-start.4 = (f32[3,128,128]{2,1,0:T(8,128)}, f32[3,128,128]{2,1,0:T(8,128)}, u32[]{:S(2)}, u32[]{:S(2)}) collective-permute-start(f32[3,128,128]{2,1,0:T(8,128)} %get-tuple-element.6), channel_id=1, source_target_pairs={{0,1},{1,2},{2,3},{3,4},{4,5},{5,6},{6,7},{7,8},{8,9},{9,10},{10,1... | collective-permute-start | bytes 589832 | tf_op jit(solution)/shard_map/ppermute | solution.py:18
  51.5 26.8 %collective-permute-start.5 = (f32[3,128,128]{2,1,0:T(8,128)}, f32[3,128,128]{2,1,0:T(8,128)}, u32[]{:S(2)}, u32[]{:S(2)}) collective-permute-start(f32[3,128,128]{2,1,0:T(8,128)} %get-tuple-element.7), channel_id=1, source_target_pairs={{1,0},{2,1},{3,2},{4,3},{5,4},{6,5},{7,6},{8,7},{9,8},{10,9},{11,1... | collective-permute-start | bytes 589832 | tf_op jit(solution)/shard_map/ppermute | solution.py:18
  53.6 21.4 %all-to-all-start.1 = ((f32[32,1,3]{2,1,0:T(1,128)}), f32[32,1,3]{2,1,0:T(1,128)S(1)}, u32[]{:S(2)}, u32[]{:S(2)}) async-start(f32[32,1,3]{2,1,0:T(1,128)} %broadcast_in_dim.35), calls=%async_computation.1 | async-start | bytes 32768 | tf_op jit(solution)/shard_map/all_to_all | solution.py:25
  82.8 5.7 %collective-permute-start.6 = (f32[3,128,128]{2,1,0:T(8,128)S(1)}, f32[3,128,128]{2,1,0:T(8,128)S(1)}, u32[]{:S(2)}, u32[]{:S(2)}) collective-permute-start(f32[3,128,128]{2,1,0:T(8,128)S(1)} %get-tuple-element.2), channel_id=1, source_target_pairs={{0,1},{1,2},{2,3},{3,4},{4,5},{5,6},{6,7},{7,8},{8,9},{9,10},{10,1... | collective-permute-start | bytes 589832 | tf_op jit(solution)/shard_map/ppermute | solution.py:18
  85.3 7.6 %collective-permute-start.7 = (f32[3,128,128]{2,1,0:T(8,128)S(1)}, f32[3,128,128]{2,1,0:T(8,128)S(1)}, u32[]{:S(2)}, u32[]{:S(2)}) collective-permute-start(f32[3,128,128]{2,1,0:T(8,128)S(1)} %get-tuple-element.3), channel_id=1, source_target_pairs={{1,0},{2,1},{3,2},{4,3},{5,4},{6,5},{7,6},{8,7},{9,8},{10,9},{11,1... | collective-permute-start | bytes 589832 | tf_op jit(solution)/shard_map/ppermute | solution.py:18
  92.9 10.7 %copy-start.5 = (s32[1,2]{1,0:T(1,128)S(1)}, s32[1,2]{1,0:T(1,128)}, u32[]{:S(2)}) copy-start(s32[1,2]{1,0:T(1,128)} %param.11) | copy-start | bytes 28
  95.7 17.6 %all-to-all-start.2 = ((f32[32,1,3]{2,1,0:T(1,128)}), f32[32,1,3]{2,1,0:T(1,128)S(1)}, u32[]{:S(2)}, u32[]{:S(2)}) async-start(f32[32,1,3]{2,1,0:T(1,128)} %broadcast_in_dim.36), calls=%async_computation.2 | async-start | bytes 32768 | tf_op jit(solution)/shard_map/all_to_all | solution.py:25

commit v7 on v6

--- a/solution.py
+++ b/solution.py
@@ -20,8 +20,7 @@
 
 def gathered_sums(values, axis):
     count = lax.axis_size(axis)
-    row = values
-    spread = jnp.broadcast_to(row[None], (count, row.shape[0]))
+    spread = jnp.broadcast_to(values[None, :, None], (count, values.shape[0], 128))
     return jnp.sum(lax.all_to_all(spread, axis, 0, 0, tiled=True), axis=0)
 
 
@@ -89,19 +88,24 @@
     weighted = env * mpo_mask.astype(jnp.float32)[:, :, None, None]
     ordered = jnp.concatenate([weighted[0::3], weighted[1::3], weighted[2::3]], axis=0)
     current = apply_terms(vector, right, ordered)
+    rows = lax.broadcasted_iota(jnp.int32, (blocks, width), 1) < ranks[0][:, None]
     for pair in range(ITERS // 2):
         lifted = apply_terms(current * LIFT, right, ordered)
         more = 2 * pair + 2 < ITERS
         if more:
             parts = exchange(lifted * LIFT, right)
+        else:
+            trimmed = lifted * rows.astype(jnp.float32)[:, :, None]
+            peak = jnp.maximum(jnp.max(jnp.abs(trimmed)), jnp.finfo(jnp.float32).tiny)
+            unit = trimmed * (1.0 / peak)
+            gram, peak = lax.optimization_barrier((mm("kab,kcb->kac", unit, unit), peak))
         first, second = scales(gathered_sums(square_sums(current, lifted), "sec"), cells)
         if more:
             current = combine(parts, ordered, first / LIFT) * (second / LIFT)
         else:
-            current = lifted * (first / LIFT) * second
-    rows = lax.broadcasted_iota(jnp.int32, (blocks, width), 1) < ranks[0][:, None]
-    trimmed = current * rows.astype(jnp.float32)[:, :, None]
-    density = mm("kab,kcb->kac", trimmed, trimmed) / width
+            factor = (first / LIFT) * second
+            current = lifted * factor
+            density = gram * (jnp.square(factor * peak) / width)
     return (current[None], density[None])
 
 

time: 119 us -> 111 us (0.933)
  between operations: 6.25 us -> 1.68 us
  waiting for transfers between devices: 38.8 us -> 34.6 us
  other arithmetic: 1.17 us -> 2.78 us
    all_to_all x2, waiting for transfers between devices: 18.6 us -> 12.2 us  [gathered_sums(): return jnp.sum(lax.all_to_all(spread, axis, 0, 0, tiled=True), axis=0)]
    ppermute x8, waiting for transfers between devices: 13 us -> 15.2 us  [shifted(): return lax.ppermute(block, axis, route)]
    slice x2 -> x0, local copies, waits for them, and re-layouts: 1.25 us -> none  [scales(): shrunk = jnp.square(step / SHRINK) * sums[2]]
  transfers between devices with their start and end apart: 11 -> 11, of which waited for: 7 -> 8; matrix products, arithmetic and copies ran while one was open for 8% -> 9% of each run, Pallas kernels for 0% -> 0%
where the time goes in v7:
time: 111 us; the launch traced here: 110 us
  starting transfers between devices  44.8 us (40%)
  waiting for transfers between devices  34.6 us (31%)
  matrix products  19.4 us (17%)
  local copies, waits for them, and re-layouts  7.17 us (6%)
  other arithmetic  2.78 us (3%)
  between operations  1.68 us (2%)
    all_to_all x2, starting transfers between devices, gathered_sums(): return jnp.sum(lax.all_to_all(spread, axis, 0, 0, tiled=True), axis=0)  20.5 us
    dot_general x18, matrix products, mm(): return jnp.einsum(spec, a, b, precision=HIGH)  19.4 us
    ppermute x8, starting transfers between devices, shifted(): return lax.ppermute(block, axis, route)  18.5 us
    ppermute x8, waiting for transfers between devices, shifted(): return lax.ppermute(block, axis, route)  15.2 us
    all_to_all x2, waiting for transfers between devices, gathered_sums(): return jnp.sum(lax.all_to_all(spread, axis, 0, 0, tiled=True), axis=0)  12.2 us
    all_to_all x1, waiting for transfers between devices, left_environment(): every = lax.all_to_all(spread, 'seg', 0, 0, tiled=True)  7.22 us
    all_to_all x1, starting transfers between devices, left_environment(): every = lax.all_to_all(spread, 'seg', 0, 0, tiled=True)  5.78 us
  transfers between devices with their start and end apart: 11, of which 8 were waited for; matrix products, arithmetic and copies ran while one was open for 9% of the time, Pallas kernels for 0%

profile of v7, /device:TPU:8, one launch (start us, length us, event | category | flops | bytes accessed | tf_op | source)
XLA Modules:
  0.0 110.4 jit_solution(16187277980893115518)
XLA Ops:
  0.6 0.0 copy-start
  0.6 2.1 %broadcast_in_dim.18 = f32[8,2,128,128]{3,2,1,0:T(8,128)} broadcast(f32[2,128,128]{2,1,0:T(8,128)} %bitcast.197), dimensions={1,2,3} | broadcast | bytes 1179648 | tf_op jit(solution)/shard_map/broadcast_in_dim | solution.py:34
  2.7 5.8 %all-to-all-start = ((f32[8,2,128,128]{3,2,1,0:T(8,128)}), f32[8,2,128,128]{3,2,1,0:T(8,128)S(1)}, u32[]{:S(2)}, u32[]{:S(2)}) async-start(f32[8,2,128,128]{3,2,1,0:T(8,128)} %broadcast_in_dim.18), calls=%async_computation | async-start | bytes 2097152 | tf_op jit(solution)/shard_map/all_to_all | solution.py:35
  8.5 0.0 copy-done
  8.5 0.0 copy-done.3
  8.5 2.0 %convolution_bitcast_fusion.3 = f32[9,2,128,128]{2,3,0,1:T(8,128)S(1)} fusion(f32[1,2,128,128]{3,2,1,0:T(8,128)S(1)} %copy-done.3, f32[1,9,2,128,128]{4,3,2,1,0:T(8,128)S(1)} %copy-done), kind=kOutput, calls=%fused_computation.3 | convolution fusion | flops 452984832 | bytes 2490368 | tf_op jit(solution)/shard_map/kab,wkbc->wkac/dot_general | solution.py:28
  10.5 0.0 copy-start.4
  10.5 0.1 slice_bitcast_fusion.7
  10.6 3.1 %collective-permute-start = (f32[3,128,128]{1,2,0:T(8,128)S(1)}, f32[3,128,128]{1,2,0:T(8,128)S(1)}, u32[]{:S(2)}, u32[]{:S(2)}) collective-permute-start(f32[3,128,128]{1,2,0:T(8,128)S(1)} %get-tuple-element.23), channel_id=1, source_target_pairs={{0,1},{1,2},{2,3},{3,4},{4,5},{5,6},{6,7},{7,8},{8,9},{9,10},{10,1... | collective-permute-start | bytes 589832 | tf_op jit(solution)/shard_map/ppermute | solution.py:18
  13.7 1.3 %collective-permute-start.1 = (f32[3,128,128]{1,2,0:T(8,128)S(1)}, f32[3,128,128]{1,2,0:T(8,128)S(1)}, u32[]{:S(2)}, u32[]{:S(2)}) collective-permute-start(f32[3,128,128]{1,2,0:T(8,128)S(1)} %get-tuple-element.24), channel_id=1, source_target_pairs={{1,0},{2,1},{3,2},{4,3},{5,4},{6,5},{7,6},{8,7},{9,8},{10,9},{11,1... | collective-permute-start | bytes 589832 | tf_op jit(solution)/shard_map/ppermute | solution.py:18
  15.0 0.8 slice.122
  15.8 7.2 %all-to-all-done = f32[8,2,128,128]{3,2,1,0:T(8,128)S(1)} async-done(((f32[8,2,128,128]{3,2,1,0:T(8,128)}), f32[8,2,128,128]{3,2,1,0:T(8,128)S(1)}, u32[]{:S(2)}, u32[]{:S(2)}) %all-to-all-start) | async-done | bytes 1048608 | tf_op jit(solution)/shard_map/all_to_all | solution.py:35
  23.0 0.3 convolution_select_fusion.6
  23.3 0.0 copy-start.1
  23.3 0.3 convolution_select_fusion.5
  23.6 0.3 convolution_select_fusion.4
  23.9 0.3 convolution_select_fusion.3
  24.1 0.3 convolution_select_fusion.2
  24.4 0.3 convolution_select_fusion.1
  24.7 0.3 fusion.42
  25.0 1.3 %convolution_bitcast_fusion.5 = f32[9,2,128,128]{2,3,0,1:T(8,128)S(1)} fusion(f32[2,128,128,1]{2,1,3,0:T(8,128)S(1)} %fusion.42, f32[9,2,128,128]{3,2,1,0:T(8,128)S(1)} %copy-done.1), kind=kOutput, calls=%fused_computation.5 | convolution fusion | flops 452984832 | bytes 2490368 | tf_op jit(solution)/shard_map/wkbc,kcd->wkbd/dot_general | solution.py:28
  26.3 1.1 %fusion = f32[9,2,128,128]{2,3,0,1:T(8,128)S(1)} fusion(f32[9,2,128,128]{2,3,0,1:T(8,128)S(1)} %convolution_bitcast_fusion.5, f32[2,128,128,1]{2,1,3,0:T(8,128)S(1)} %fusion.42, f32[9,2]{0,1:T(2,128)S(1)} %convert_element_type.16), kind=kOutput, calls=%fused_computation.6 | convolution fusion | flops 453279744 | bytes 2490440 | tf_op jit(solution)/shard_map/kba,wkbd->wkad/dot_general | solution.py:28
  27.4 0.0 copy-start.2
  27.4 0.1 fusion.77
  27.5 0.0 collective-permute-done
  27.5 0.0 collective-permute-done.1
  27.5 0.9 copy-done.2
  28.4 2.0 %fusion.1 = f32[2,128,128,1]{2,1,3,0:T(8,128)S(1)} fusion(f32[3,1,128,128]{2,3,0,1:T(8,128)S(1)} %bitcast.199, f32[3,1,128,128]{2,3,0,1:T(8,128)S(1)} %get-tuple-element.25, f32[3,2,128,128]{2,3,0,1:T(8,128)S(1)} %copy-done.2, f32[3,1,128,128]{2,3,0,1:T(8,128)S(1)} %get-tuple-element.26, f32[3,1,128,128]{2,3,0,1:T(8,128)S(1)} %bitcast.198, ...), kind=kOutput, calls=%fused_computation.8 | convolution fusion | flops 454754304 | bytes 2490368 | tf_op jit(solution)/shard_map/wkab,wkbc->kac/dot_general | solution.py:28
  30.4 1.1 convolution_bitcast_fusion.2
  31.5 0.1 slice_bitcast_fusion.5
  31.6 3.1 %collective-permute-start.2 = (f32[3,128,128]{2,1,0:T(8,128)S(1)}, f32[3,128,128]{2,1,0:T(8,128)S(1)}, u32[]{:S(2)}, u32[]{:S(2)}) collective-permute-start(f32[3,128,128]{2,1,0:T(8,128)S(1)} %get-tuple-element.16), channel_id=1, source_target_pairs={{0,1},{1,2},{2,3},{3,4},{4,5},{5,6},{6,7},{7,8},{8,9},{9,10},{10,1... | collective-permute-start | bytes 589832 | tf_op jit(solution)/shard_map/ppermute | solution.py:18
  34.7 1.5 %collective-permute-start.3 = (f32[3,128,128]{2,1,0:T(8,128)S(1)}, f32[3,128,128]{2,1,0:T(8,128)S(1)}, u32[]{:S(2)}, u32[]{:S(2)}) collective-permute-start(f32[3,128,128]{2,1,0:T(8,128)S(1)} %get-tuple-element.17), channel_id=1, source_target_pairs={{1,0},{2,1},{3,2},{4,3},{5,4},{6,5},{7,6},{8,7},{9,8},{10,9},{11,1... | collective-permute-start | bytes 589832 | tf_op jit(solution)/shard_map/ppermute | solution.py:18
  36.2 2.4 %collective-permute-done.2 = f32[3,128,128]{2,1,0:T(8,128)S(1)} collective-permute-done((f32[3,128,128]{2,1,0:T(8,128)S(1)}, f32[3,128,128]{2,1,0:T(8,128)S(1)}, u32[]{:S(2)}, u32[]{:S(2)}) %collective-permute-start.2) | collective-permute-done | bytes 196640 | tf_op jit(solution)/shard_map/ppermute | solution.py:18
  38.6 4.3 %collective-permute-done.3 = f32[3,128,128]{2,1,0:T(8,128)S(1)} collective-permute-done((f32[3,128,128]{2,1,0:T(8,128)S(1)}, f32[3,128,128]{2,1,0:T(8,128)S(1)}, u32[]{:S(2)}, u32[]{:S(2)}) %collective-permute-start.3) | collective-permute-done | bytes 196640 | tf_op jit(solution)/shard_map/ppermute | solution.py:18
  42.9 2.1 %fusion.11 = f32[2,128,128,1]{2,1,3,0:T(8,128)S(1)} fusion(f32[3,1,128,128]{3,2,0,1:T(8,128)S(1)} %bitcast.205, f32[3,1,128,128]{3,2,0,1:T(8,128)S(1)} %get-tuple-element.18, f32[3,2,128,128]{3,2,0,1:T(8,128)S(1)} %slice.127, f32[3,1,128,128]{3,2,0,1:T(8,128)S(1)} %get-tuple-element.19, f32[3,1,128,128]{3,2,0,1:T(8,128)S(1)} %bitcast.204, ...), kind=kOutput, calls=%fused_computation.18 | convolution fusion | flops 454754304 | bytes 2490368 | tf_op jit(solution)/shard_map/wkab,wkbc->kac/dot_general | solution.py:28
  45.0 1.1 convolution_bitcast_fusion.1
  46.1 0.1 fusion.49
  46.2 0.7 broadcast_in_dim.19
  47.0 11.1 %all-to-all-start.1 = ((f32[32,3,128]{2,1,0:T(4,128)}), f32[32,3,128]{2,1,0:T(4,128)}, u32[]{:S(2)}, u32[]{:S(2)}) async-start(f32[32,3,128]{2,1,0:T(4,128)} %broadcast_in_dim.19), calls=%async_computation.1 | async-start | bytes 131072 | tf_op jit(solution)/shard_map/all_to_all | solution.py:24
  58.1 0.9 slice_bitcast_fusion.3
  59.0 0.8 slice.132
  59.8 3.6 %collective-permute-start.4 = (f32[3,128,128]{2,1,0:T(8,128)}, f32[3,128,128]{2,1,0:T(8,128)S(1)}, u32[]{:S(2)}, u32[]{:S(2)}) collective-permute-start(f32[3,128,128]{2,1,0:T(8,128)} %get-tuple-element.12), channel_id=1, source_target_pairs={{0,1},{1,2},{2,3},{3,4},{4,5},{5,6},{6,7},{7,8},{8,9},{9,10},{10,1... | collective-permute-start | bytes 589832 | tf_op jit(solution)/shard_map/ppermute | solution.py:18
  63.4 1.3 %collective-permute-start.5 = (f32[3,128,128]{2,1,0:T(8,128)}, f32[3,128,128]{2,1,0:T(8,128)S(1)}, u32[]{:S(2)}, u32[]{:S(2)}) collective-permute-start(f32[3,128,128]{2,1,0:T(8,128)} %get-tuple-element.13), channel_id=1, source_target_pairs={{1,0},{2,1},{3,2},{4,3},{5,4},{6,5},{7,6},{8,7},{9,8},{10,9},{11,1... | collective-permute-start | bytes 589832 | tf_op jit(solution)/shard_map/ppermute | solution.py:18
  64.7 3.4 %all-to-all-done.1 = f32[32,3,128]{2,1,0:T(4,128)} async-done(((f32[32,3,128]{2,1,0:T(4,128)}), f32[32,3,128]{2,1,0:T(4,128)}, u32[]{:S(2)}, u32[]{:S(2)}) %all-to-all-start.1) | async-done | bytes 49184 | tf_op jit(solution)/shard_map/all_to_all | solution.py:24
  68.1 0.9 reduce_sum.37
  69.0 0.0 collective-permute-done.4
  69.0 2.2 %collective-permute-done.5 = f32[3,128,128]{2,1,0:T(8,128)S(1)} collective-permute-done((f32[3,128,128]{2,1,0:T(8,128)}, f32[3,128,128]{2,1,0:T(8,128)S(1)}, u32[]{:S(2)}, u32[]{:S(2)}) %collective-permute-start.5) | collective-permute-done | bytes 196640 | tf_op jit(solution)/shard_map/ppermute | solution.py:18
  71.2 3.2 %fusion.43 = f32[2,128,128]{2,1,0:T(8,128)S(1)} fusion(f32[3,1,128,128]{3,2,0,1:T(8,128)S(1)} %bitcast.201, f32[3,1,128,128]{3,2,0,1:T(8,128)} %get-tuple-element.14, f32[3,2,128,128]{3,2,0,1:T(8,128)} %slice.132, f32[3,1,128,128]{3,2,0,1:T(8,128)} %get-tuple-element.15, f32[3,1,128,128]{3,2,0,1:T(8,128)S(1)} %bitcast.200, ...), kind=kOutput, calls=%fused_computation.58 | convolution fusion | flops 455081984 | bytes 2491392 | tf_op jit(solution)/shard_map/wkab,wkbc->kac/dot_general | solution.py:28
  74.4 1.1 convolution_bitcast_fusion
  75.5 0.0 copy-start.5
  75.5 0.1 slice_bitcast_fusion.1
  75.6 3.4 %collective-permute-start.6 = (f32[3,128,128]{2,1,0:T(8,128)S(1)}, f32[3,128,128]{2,1,0:T(8,128)S(1)}, u32[]{:S(2)}, u32[]{:S(2)}) collective-permute-start(f32[3,128,128]{2,1,0:T(8,128)S(1)} %get-tuple-element.8), channel_id=1, source_target_pairs={{0,1},{1,2},{2,3},{3,4},{4,5},{5,6},{6,7},{7,8},{8,9},{9,10},{10,1... | collective-permute-start | bytes 589832 | tf_op jit(solution)/shard_map/ppermute | solution.py:18
  78.9 1.3 %collective-permute-start.7 = (f32[3,128,128]{2,1,0:T(8,128)S(1)}, f32[3,128,128]{2,1,0:T(8,128)S(1)}, u32[]{:S(2)}, u32[]{:S(2)}) collective-permute-start(f32[3,128,128]{2,1,0:T(8,128)S(1)} %get-tuple-element.9), channel_id=1, source_target_pairs={{1,0},{2,1},{3,2},{4,3},{5,4},{6,5},{7,6},{8,7},{9,8},{10,9},{11,1... | collective-permute-start | bytes 589832 | tf_op jit(solution)/shard_map/ppermute | solution.py:18
  80.3 0.1 compare_convert_fusion
  80.4 1.7 %collective-permute-done.6 = f32[3,128,128]{2,1,0:T(8,128)S(1)} collective-permute-done((f32[3,128,128]{2,1,0:T(8,128)S(1)}, f32[3,128,128]{2,1,0:T(8,128)S(1)}, u32[]{:S(2)}, u32[]{:S(2)}) %collective-permute-start.6) | collective-permute-done | bytes 196640 | tf_op jit(solution)/shard_map/ppermute | solution.py:18
  82.1 4.5 %collective-permute-done.7 = f32[3,128,128]{2,1,0:T(8,128)S(1)} collective-permute-done((f32[3,128,128]{2,1,0:T(8,128)S(1)}, f32[3,128,128]{2,1,0:T(8,128)S(1)}, u32[]{:S(2)}, u32[]{:S(2)}) %collective-permute-start.7) | collective-permute-done | bytes 196640 | tf_op jit(solution)/shard_map/ppermute | solution.py:18
  86.6 2.0 %fusion.30 = f32[2,128,128,1]{2,1,3,0:T(8,128)S(1)} fusion(f32[3,1,128,128]{3,2,0,1:T(8,128)S(1)} %bitcast.203, f32[3,1,128,128]{3,2,0,1:T(8,128)S(1)} %get-tuple-element.10, f32[3,2,128,128]{3,2,0,1:T(8,128)S(1)} %slice.140, f32[3,1,128,128]{3,2,0,1:T(8,128)S(1)} %get-tuple-element.11, f32[3,1,128,128]{3,2,0,1:T(8,128)S(1)} %bitcast.202, ...), kind=kOutput, calls=%fused_computation.38 | convolution fusion | flops 454754304 | bytes 2490368 | tf_op jit(solution)/shard_map/wkab,wkbc->kac/dot_general | solution.py:28
  88.7 0.7 fusion.55
  89.4 0.1 fusion.50
  89.5 0.7 broadcast_in_dim.40
  90.2 9.4 %all-to-all-start.2 = ((f32[32,3,128]{2,1,0:T(4,128)}), f32[32,3,128]{2,1,0:T(4,128)S(1)}, u32[]{:S(2)}, u32[]{:S(2)}) async-start(f32[32,3,128]{2,1,0:T(4,128)} %broadcast_in_dim.40), calls=%async_computation.2 | async-start | bytes 131072 | tf_op jit(solution)/shard_map/all_to_all | solution.py:24
  100.3 0.5 fusion.58
  100.8 8.9 %all-to-all-done.2 = f32[32,3,128]{2,1,0:T(4,128)S(1)} async-done(((f32[32,3,128]{2,1,0:T(4,128)}), f32[32,3,128]{2,1,0:T(4,128)S(1)}, u32[]{:S(2)}, u32[]{:S(2)}) %all-to-all-start.2) | async-done | bytes 49184 | tf_op jit(solution)/shard_map/all_to_all | solution.py:24
  109.7 0.7 fusion.56
  (13 shorter events, 0.2 us)
Async XLA Ops:
  0.6 7.9 %copy-start = (f32[1,9,2,128,128]{4,3,2,1,0:T(8,128)S(1)}, f32[1,9,2,128,128]{4,3,2,1,0:T(8,128)}, u32[]{:S(2)}) copy-start(f32[1,9,2,128,128]{4,3,2,1,0:T(8,128)} %param.9) | copy-start | bytes 3538948
  2.7 5.8 %copy-start.3 = (f32[1,2,128,128]{3,2,1,0:T(8,128)S(1)}, f32[1,2,128,128]{3,2,1,0:T(8,128)}, u32[]{:S(2)}) copy-start(f32[1,2,128,128]{3,2,1,0:T(8,128)} %param.6) | copy-start | bytes 393220
  2.7 20.3 %all-to-all-start = ((f32[8,2,128,128]{3,2,1,0:T(8,128)}), f32[8,2,128,128]{3,2,1,0:T(8,128)S(1)}, u32[]{:S(2)}, u32[]{:S(2)}) async-start(f32[8,2,128,128]{3,2,1,0:T(8,128)} %broadcast_in_dim.18), calls=%async_computation | async-start | bytes 2097152 | tf_op jit(solution)/shard_map/all_to_all | solution.py:35
  10.5 5.3 %copy-start.4 = (s32[9,2]{0,1:T(2,128)S(1)}, s32[9,2]{0,1:T(2,128)}, u32[]{:S(2)}) copy-start(s32[9,2]{0,1:T(2,128)} %param.10) | copy-start | bytes 220
  10.6 16.9 %collective-permute-start = (f32[3,128,128]{1,2,0:T(8,128)S(1)}, f32[3,128,128]{1,2,0:T(8,128)S(1)}, u32[]{:S(2)}, u32[]{:S(2)}) collective-permute-start(f32[3,128,128]{1,2,0:T(8,128)S(1)} %get-tuple-element.23), channel_id=1, source_target_pairs={{0,1},{1,2},{2,3},{3,4},{4,5},{5,6},{6,7},{7,8},{8,9},{9,10},{10,1... | collective-permute-start | bytes 589832 | tf_op jit(solution)/shard_map/ppermute | solution.py:18
  13.7 13.8 %collective-permute-start.1 = (f32[3,128,128]{1,2,0:T(8,128)S(1)}, f32[3,128,128]{1,2,0:T(8,128)S(1)}, u32[]{:S(2)}, u32[]{:S(2)}) collective-permute-start(f32[3,128,128]{1,2,0:T(8,128)S(1)} %get-tuple-element.24), channel_id=1, source_target_pairs={{1,0},{2,1},{3,2},{4,3},{5,4},{6,5},{7,6},{8,7},{9,8},{10,9},{11,1... | collective-permute-start | bytes 589832 | tf_op jit(solution)/shard_map/ppermute | solution.py:18
  23.3 1.7 %copy-start.1 = (f32[9,2,128,128]{3,2,1,0:T(8,128)S(1)}, f32[9,2,128,128]{3,2,1,0:T(8,128)}, u32[]{:S(2)}) copy-start(f32[9,2,128,128]{3,2,1,0:T(8,128)} %param.7) | copy-start | bytes 3538948
  27.4 1.0 copy-start.2
  31.6 7.0 %collective-permute-start.2 = (f32[3,128,128]{2,1,0:T(8,128)S(1)}, f32[3,128,128]{2,1,0:T(8,128)S(1)}, u32[]{:S(2)}, u32[]{:S(2)}) collective-permute-start(f32[3,128,128]{2,1,0:T(8,128)S(1)} %get-tuple-element.16), channel_id=1, source_target_pairs={{0,1},{1,2},{2,3},{3,4},{4,5},{5,6},{6,7},{7,8},{8,9},{9,10},{10,1... | collective-permute-start | bytes 589832 | tf_op jit(solution)/shard_map/ppermute | solution.py:18
  34.7 8.2 %collective-permute-start.3 = (f32[3,128,128]{2,1,0:T(8,128)S(1)}, f32[3,128,128]{2,1,0:T(8,128)S(1)}, u32[]{:S(2)}, u32[]{:S(2)}) collective-permute-start(f32[3,128,128]{2,1,0:T(8,128)S(1)} %get-tuple-element.17), channel_id=1, source_target_pairs={{1,0},{2,1},{3,2},{4,3},{5,4},{6,5},{7,6},{8,7},{9,8},{10,9},{11,1... | collective-permute-start | bytes 589832 | tf_op jit(solution)/shard_map/ppermute | solution.py:18
  47.0 21.1 %all-to-all-start.1 = ((f32[32,3,128]{2,1,0:T(4,128)}), f32[32,3,128]{2,1,0:T(4,128)}, u32[]{:S(2)}, u32[]{:S(2)}) async-start(f32[32,3,128]{2,1,0:T(4,128)} %broadcast_in_dim.19), calls=%async_computation.1 | async-start | bytes 131072 | tf_op jit(solution)/shard_map/all_to_all | solution.py:24
  59.8 9.2 %collective-permute-start.4 = (f32[3,128,128]{2,1,0:T(8,128)}, f32[3,128,128]{2,1,0:T(8,128)S(1)}, u32[]{:S(2)}, u32[]{:S(2)}) collective-permute-start(f32[3,128,128]{2,1,0:T(8,128)} %get-tuple-element.12), channel_id=1, source_target_pairs={{0,1},{1,2},{2,3},{3,4},{4,5},{5,6},{6,7},{7,8},{8,9},{9,10},{10,1... | collective-permute-start | bytes 589832 | tf_op jit(solution)/shard_map/ppermute | solution.py:18
  63.4 7.8 %collective-permute-start.5 = (f32[3,128,128]{2,1,0:T(8,128)}, f32[3,128,128]{2,1,0:T(8,128)S(1)}, u32[]{:S(2)}, u32[]{:S(2)}) collective-permute-start(f32[3,128,128]{2,1,0:T(8,128)} %get-tuple-element.13), channel_id=1, source_target_pairs={{1,0},{2,1},{3,2},{4,3},{5,4},{6,5},{7,6},{8,7},{9,8},{10,9},{11,1... | collective-permute-start | bytes 589832 | tf_op jit(solution)/shard_map/ppermute | solution.py:18
  75.5 4.8 %copy-start.5 = (s32[1,2]{1,0:T(1,128)S(1)}, s32[1,2]{1,0:T(1,128)}, u32[]{:S(2)}) copy-start(s32[1,2]{1,0:T(1,128)} %param.11) | copy-start | bytes 28
  75.6 6.5 %collective-permute-start.6 = (f32[3,128,128]{2,1,0:T(8,128)S(1)}, f32[3,128,128]{2,1,0:T(8,128)S(1)}, u32[]{:S(2)}, u32[]{:S(2)}) collective-permute-start(f32[3,128,128]{2,1,0:T(8,128)S(1)} %get-tuple-element.8), channel_id=1, source_target_pairs={{0,1},{1,2},{2,3},{3,4},{4,5},{5,6},{6,7},{7,8},{8,9},{9,10},{10,1... | collective-permute-start | bytes 589832 | tf_op jit(solution)/shard_map/ppermute | solution.py:18
  78.9 7.7 %collective-permute-start.7 = (f32[3,128,128]{2,1,0:T(8,128)S(1)}, f32[3,128,128]{2,1,0:T(8,128)S(1)}, u32[]{:S(2)}, u32[]{:S(2)}) collective-permute-start(f32[3,128,128]{2,1,0:T(8,128)S(1)} %get-tuple-element.9), channel_id=1, source_target_pairs={{1,0},{2,1},{3,2},{4,3},{5,4},{6,5},{7,6},{8,7},{9,8},{10,9},{11,1... | collective-permute-start | bytes 589832 | tf_op jit(solution)/shard_map/ppermute | solution.py:18
  90.2 19.4 %all-to-all-start.2 = ((f32[32,3,128]{2,1,0:T(4,128)}), f32[32,3,128]{2,1,0:T(4,128)S(1)}, u32[]{:S(2)}, u32[]{:S(2)}) async-start(f32[32,3,128]{2,1,0:T(4,128)} %broadcast_in_dim.40), calls=%async_computation.2 | async-start | bytes 131072 | tf_op jit(solution)/shard_map/all_to_all | solution.py:24

commit v8 on v7

--- a/solution.py
+++ b/solution.py
@@ -6,7 +6,7 @@
 ITERS = 4
 
 
-HIGH = lax.Precision.HIGHEST
+HIGH = lax.Precision.HIGH
 EPS = 1e-06
 LIFT = 1024.0
 SHRINK = 2.0**-50

time: 111 us -> 105 us (0.946)
  matrix products: 19.4 us -> 11.8 us
  waiting for transfers between devices: 34.6 us -> 35.8 us
    dot_general x18, matrix products: 19.4 us -> 11.8 us  [mm(): return jnp.einsum(spec, a, b, precision=HIGH)]
  transfers between devices with their start and end apart: 11 -> 11, of which waited for: 8 -> 8; matrix products, arithmetic and copies ran while one was open for 9% -> 8% of each run, Pallas kernels for 0% -> 0%
where the time goes in v8:
time: 105 us; the launch traced here: 104 us
  starting transfers between devices  44.7 us (43%)
  waiting for transfers between devices  35.8 us (34%)
  matrix products  11.8 us (11%)
  local copies, waits for them, and re-layouts  7.18 us (7%)
  other arithmetic  2.78 us (3%)
  between operations  1.68 us (2%)
    all_to_all x2, starting transfers between devices, gathered_sums(): return jnp.sum(lax.all_to_all(spread, axis, 0, 0, tiled=True), axis=0)  20.5 us
    ppermute x8, starting transfers between devices, shifted(): return lax.ppermute(block, axis, route)  18.3 us
    ppermute x8, waiting for transfers between devices, shifted(): return lax.ppermute(block, axis, route)  15.3 us
    all_to_all x2, waiting for transfers between devices, gathered_sums(): return jnp.sum(lax.all_to_all(spread, axis, 0, 0, tiled=True), axis=0)  12.4 us
    dot_general x18, matrix products, mm(): return jnp.einsum(spec, a, b, precision=HIGH)  11.8 us
    all_to_all x1, waiting for transfers between devices, left_environment(): every = lax.all_to_all(spread, 'seg', 0, 0, tiled=True)  8.13 us
    all_to_all x1, starting transfers between devices, left_environment(): every = lax.all_to_all(spread, 'seg', 0, 0, tiled=True)  5.78 us
  transfers between devices with their start and end apart: 11, of which 8 were waited for; matrix products, arithmetic and copies ran while one was open for 8% of the time, Pallas kernels for 0%

profile of v8, /device:TPU:8, one launch (start us, length us, event | category | flops | bytes accessed | tf_op | source)
XLA Modules:
  0.0 103.9 jit_solution(3776341161680407671)
XLA Ops:
  0.6 0.0 copy-start
  0.6 2.1 %broadcast_in_dim.18 = f32[8,2,128,128]{3,2,1,0:T(8,128)} broadcast(f32[2,128,128]{2,1,0:T(8,128)} %bitcast.197), dimensions={1,2,3} | broadcast | bytes 1179648 | tf_op jit(solution)/shard_map/broadcast_in_dim | solution.py:34
  2.7 5.8 %all-to-all-start = ((f32[8,2,128,128]{3,2,1,0:T(8,128)}), f32[8,2,128,128]{3,2,1,0:T(8,128)S(1)}, u32[]{:S(2)}, u32[]{:S(2)}) async-start(f32[8,2,128,128]{3,2,1,0:T(8,128)} %broadcast_in_dim.18), calls=%async_computation | async-start | bytes 2097152 | tf_op jit(solution)/shard_map/all_to_all | solution.py:35
  8.5 0.0 copy-done
  8.5 0.0 copy-done.3
  8.5 1.1 %convolution_bitcast_fusion.3 = f32[9,2,128,128]{2,3,0,1:T(8,128)S(1)} fusion(f32[1,2,128,128]{3,2,1,0:T(8,128)S(1)} %copy-done.3, f32[1,9,2,128,128]{4,3,2,1,0:T(8,128)S(1)} %copy-done), kind=kOutput, calls=%fused_computation.3 | convolution fusion | flops 226492416 | bytes 2490368 | tf_op jit(solution)/shard_map/kab,wkbc->wkac/dot_general | solution.py:28
  9.6 0.0 copy-start.4
  9.6 0.1 slice_bitcast_fusion.7
  9.7 3.1 %collective-permute-start = (f32[3,128,128]{1,2,0:T(8,128)S(1)}, f32[3,128,128]{1,2,0:T(8,128)S(1)}, u32[]{:S(2)}, u32[]{:S(2)}) collective-permute-start(f32[3,128,128]{1,2,0:T(8,128)S(1)} %get-tuple-element.23), channel_id=1, source_target_pairs={{0,1},{1,2},{2,3},{3,4},{4,5},{5,6},{6,7},{7,8},{8,9},{9,10},{10,1... | collective-permute-start | bytes 589832 | tf_op jit(solution)/shard_map/ppermute | solution.py:18
  12.8 1.3 %collective-permute-start.1 = (f32[3,128,128]{1,2,0:T(8,128)S(1)}, f32[3,128,128]{1,2,0:T(8,128)S(1)}, u32[]{:S(2)}, u32[]{:S(2)}) collective-permute-start(f32[3,128,128]{1,2,0:T(8,128)S(1)} %get-tuple-element.24), channel_id=1, source_target_pairs={{1,0},{2,1},{3,2},{4,3},{5,4},{6,5},{7,6},{8,7},{9,8},{10,9},{11,1... | collective-permute-start | bytes 589832 | tf_op jit(solution)/shard_map/ppermute | solution.py:18
  14.1 0.8 slice.122
  14.9 8.1 %all-to-all-done = f32[8,2,128,128]{3,2,1,0:T(8,128)S(1)} async-done(((f32[8,2,128,128]{3,2,1,0:T(8,128)}), f32[8,2,128,128]{3,2,1,0:T(8,128)S(1)}, u32[]{:S(2)}, u32[]{:S(2)}) %all-to-all-start) | async-done | bytes 1048608 | tf_op jit(solution)/shard_map/all_to_all | solution.py:35
  23.0 0.2 convolution_select_fusion.6
  23.2 0.0 copy-start.1
  23.3 0.2 convolution_select_fusion.5
  23.5 0.2 convolution_select_fusion.4
  23.7 0.2 convolution_select_fusion.3
  23.9 0.2 convolution_select_fusion.2
  24.1 0.2 convolution_select_fusion.1
  24.3 0.2 fusion.42
  24.5 0.0 copy-done.1
  24.5 0.7 convolution_bitcast_fusion.5
  25.3 0.6 fusion
  25.9 0.1 fusion.77
  26.0 0.0 collective-permute-done
  26.0 0.0 collective-permute-done.1
  26.0 0.9 copy-done.2
  26.9 1.2 %fusion.1 = f32[2,128,128,1]{2,1,3,0:T(8,128)S(1)} fusion(f32[3,1,128,128]{2,3,0,1:T(8,128)S(1)} %bitcast.199, f32[3,1,128,128]{2,3,0,1:T(8,128)S(1)} %get-tuple-element.25, f32[3,2,128,128]{2,3,0,1:T(8,128)S(1)} %copy-done.2, f32[3,1,128,128]{2,3,0,1:T(8,128)S(1)} %get-tuple-element.26, f32[3,1,128,128]{2,3,0,1:T(8,128)S(1)} %bitcast.198, ...), kind=kOutput, calls=%fused_computation.8 | convolution fusion | flops 228261888 | bytes 2490368 | tf_op jit(solution)/shard_map/wkab,wkbc->kac/dot_general | solution.py:28
  28.0 0.6 convolution_bitcast_fusion.2
  28.7 0.1 slice_bitcast_fusion.5
  28.7 3.1 %collective-permute-start.2 = (f32[3,128,128]{2,1,0:T(8,128)S(1)}, f32[3,128,128]{2,1,0:T(8,128)S(1)}, u32[]{:S(2)}, u32[]{:S(2)}) collective-permute-start(f32[3,128,128]{2,1,0:T(8,128)S(1)} %get-tuple-element.16), channel_id=1, source_target_pairs={{0,1},{1,2},{2,3},{3,4},{4,5},{5,6},{6,7},{7,8},{8,9},{9,10},{10,1... | collective-permute-start | bytes 589832 | tf_op jit(solution)/shard_map/ppermute | solution.py:18
  31.8 1.3 %collective-permute-start.3 = (f32[3,128,128]{2,1,0:T(8,128)S(1)}, f32[3,128,128]{2,1,0:T(8,128)S(1)}, u32[]{:S(2)}, u32[]{:S(2)}) collective-permute-start(f32[3,128,128]{2,1,0:T(8,128)S(1)} %get-tuple-element.17), channel_id=1, source_target_pairs={{1,0},{2,1},{3,2},{4,3},{5,4},{6,5},{7,6},{8,7},{9,8},{10,9},{11,1... | collective-permute-start | bytes 589832 | tf_op jit(solution)/shard_map/ppermute | solution.py:18
  33.2 2.6 %collective-permute-done.2 = f32[3,128,128]{2,1,0:T(8,128)S(1)} collective-permute-done((f32[3,128,128]{2,1,0:T(8,128)S(1)}, f32[3,128,128]{2,1,0:T(8,128)S(1)}, u32[]{:S(2)}, u32[]{:S(2)}) %collective-permute-start.2) | collective-permute-done | bytes 196640 | tf_op jit(solution)/shard_map/ppermute | solution.py:18
  35.7 4.3 %collective-permute-done.3 = f32[3,128,128]{2,1,0:T(8,128)S(1)} collective-permute-done((f32[3,128,128]{2,1,0:T(8,128)S(1)}, f32[3,128,128]{2,1,0:T(8,128)S(1)}, u32[]{:S(2)}, u32[]{:S(2)}) %collective-permute-start.3) | collective-permute-done | bytes 196640 | tf_op jit(solution)/shard_map/ppermute | solution.py:18
  40.1 1.1 %fusion.11 = f32[2,128,128,1]{2,1,3,0:T(8,128)S(1)} fusion(f32[3,1,128,128]{3,2,0,1:T(8,128)S(1)} %bitcast.205, f32[3,1,128,128]{3,2,0,1:T(8,128)S(1)} %get-tuple-element.18, f32[3,2,128,128]{3,2,0,1:T(8,128)S(1)} %slice.127, f32[3,1,128,128]{3,2,0,1:T(8,128)S(1)} %get-tuple-element.19, f32[3,1,128,128]{3,2,0,1:T(8,128)S(1)} %bitcast.204, ...), kind=kOutput, calls=%fused_computation.18 | convolution fusion | flops 228261888 | bytes 2490368 | tf_op jit(solution)/shard_map/wkab,wkbc->kac/dot_general | solution.py:28
  41.2 0.6 convolution_bitcast_fusion.1
  41.9 0.1 fusion.49
  42.0 0.7 broadcast_in_dim.19
  42.7 11.1 %all-to-all-start.1 = ((f32[32,3,128]{2,1,0:T(4,128)}), f32[32,3,128]{2,1,0:T(4,128)}, u32[]{:S(2)}, u32[]{:S(2)}) async-start(f32[32,3,128]{2,1,0:T(4,128)} %broadcast_in_dim.19), calls=%async_computation.1 | async-start | bytes 131072 | tf_op jit(solution)/shard_map/all_to_all | solution.py:24
  53.8 0.9 slice_bitcast_fusion.3
  54.8 0.8 slice.132
  55.5 3.6 %collective-permute-start.4 = (f32[3,128,128]{2,1,0:T(8,128)}, f32[3,128,128]{2,1,0:T(8,128)S(1)}, u32[]{:S(2)}, u32[]{:S(2)}) collective-permute-start(f32[3,128,128]{2,1,0:T(8,128)} %get-tuple-element.12), channel_id=1, source_target_pairs={{0,1},{1,2},{2,3},{3,4},{4,5},{5,6},{6,7},{7,8},{8,9},{9,10},{10,1... | collective-permute-start | bytes 589832 | tf_op jit(solution)/shard_map/ppermute | solution.py:18
  59.2 1.3 %collective-permute-start.5 = (f32[3,128,128]{2,1,0:T(8,128)}, f32[3,128,128]{2,1,0:T(8,128)S(1)}, u32[]{:S(2)}, u32[]{:S(2)}) collective-permute-start(f32[3,128,128]{2,1,0:T(8,128)} %get-tuple-element.13), channel_id=1, source_target_pairs={{1,0},{2,1},{3,2},{4,3},{5,4},{6,5},{7,6},{8,7},{9,8},{10,9},{11,1... | collective-permute-start | bytes 589832 | tf_op jit(solution)/shard_map/ppermute | solution.py:18
  60.5 3.4 %all-to-all-done.1 = f32[32,3,128]{2,1,0:T(4,128)} async-done(((f32[32,3,128]{2,1,0:T(4,128)}), f32[32,3,128]{2,1,0:T(4,128)}, u32[]{:S(2)}, u32[]{:S(2)}) %all-to-all-start.1) | async-done | bytes 49184 | tf_op jit(solution)/shard_map/all_to_all | solution.py:24
  63.8 0.9 reduce_sum.37
  64.7 0.0 collective-permute-done.4
  64.8 2.2 %collective-permute-done.5 = f32[3,128,128]{2,1,0:T(8,128)S(1)} collective-permute-done((f32[3,128,128]{2,1,0:T(8,128)}, f32[3,128,128]{2,1,0:T(8,128)S(1)}, u32[]{:S(2)}, u32[]{:S(2)}) %collective-permute-start.5) | collective-permute-done | bytes 196640 | tf_op jit(solution)/shard_map/ppermute | solution.py:18
  66.9 2.3 %fusion.43 = f32[2,128,128]{2,1,0:T(8,128)S(1)} fusion(f32[3,1,128,128]{3,2,0,1:T(8,128)S(1)} %bitcast.201, f32[3,1,128,128]{3,2,0,1:T(8,128)} %get-tuple-element.14, f32[3,2,128,128]{3,2,0,1:T(8,128)} %slice.132, f32[3,1,128,128]{3,2,0,1:T(8,128)} %get-tuple-element.15, f32[3,1,128,128]{3,2,0,1:T(8,128)S(1)} %bitcast.200, ...), kind=kOutput, calls=%fused_computation.58 | convolution fusion | flops 228589568 | bytes 2491392 | tf_op jit(solution)/shard_map/wkab,wkbc->kac/dot_general | solution.py:28
  69.2 0.6 convolution_bitcast_fusion
  69.8 0.0 copy-start.5
  69.9 0.1 slice_bitcast_fusion.1
  69.9 3.4 %collective-permute-start.6 = (f32[3,128,128]{2,1,0:T(8,128)S(1)}, f32[3,128,128]{2,1,0:T(8,128)S(1)}, u32[]{:S(2)}, u32[]{:S(2)}) collective-permute-start(f32[3,128,128]{2,1,0:T(8,128)S(1)} %get-tuple-element.8), channel_id=1, source_target_pairs={{0,1},{1,2},{2,3},{3,4},{4,5},{5,6},{6,7},{7,8},{8,9},{9,10},{10,1... | collective-permute-start | bytes 589832 | tf_op jit(solution)/shard_map/ppermute | solution.py:18
  73.3 1.3 %collective-permute-start.7 = (f32[3,128,128]{2,1,0:T(8,128)S(1)}, f32[3,128,128]{2,1,0:T(8,128)S(1)}, u32[]{:S(2)}, u32[]{:S(2)}) collective-permute-start(f32[3,128,128]{2,1,0:T(8,128)S(1)} %get-tuple-element.9), channel_id=1, source_target_pairs={{1,0},{2,1},{3,2},{4,3},{5,4},{6,5},{7,6},{8,7},{9,8},{10,9},{11,1... | collective-permute-start | bytes 589832 | tf_op jit(solution)/shard_map/ppermute | solution.py:18
  74.6 0.1 compare_convert_fusion
  74.7 1.7 %collective-permute-done.6 = f32[3,128,128]{2,1,0:T(8,128)S(1)} collective-permute-done((f32[3,128,128]{2,1,0:T(8,128)S(1)}, f32[3,128,128]{2,1,0:T(8,128)S(1)}, u32[]{:S(2)}, u32[]{:S(2)}) %collective-permute-start.6) | collective-permute-done | bytes 196640 | tf_op jit(solution)/shard_map/ppermute | solution.py:18
  76.4 4.5 %collective-permute-done.7 = f32[3,128,128]{2,1,0:T(8,128)S(1)} collective-permute-done((f32[3,128,128]{2,1,0:T(8,128)S(1)}, f32[3,128,128]{2,1,0:T(8,128)S(1)}, u32[]{:S(2)}, u32[]{:S(2)}) %collective-permute-start.7) | collective-permute-done | bytes 196640 | tf_op jit(solution)/shard_map/ppermute | solution.py:18
  81.0 1.1 %fusion.30 = f32[2,128,128,1]{2,1,3,0:T(8,128)S(1)} fusion(f32[3,1,128,128]{3,2,0,1:T(8,128)S(1)} %bitcast.203, f32[3,1,128,128]{3,2,0,1:T(8,128)S(1)} %get-tuple-element.10, f32[3,2,128,128]{3,2,0,1:T(8,128)S(1)} %slice.140, f32[3,1,128,128]{3,2,0,1:T(8,128)S(1)} %get-tuple-element.11, f32[3,1,128,128]{3,2,0,1:T(8,128)S(1)} %bitcast.202, ...), kind=kOutput, calls=%fused_computation.38 | convolution fusion | flops 228261888 | bytes 2490368 | tf_op jit(solution)/shard_map/wkab,wkbc->kac/dot_general | solution.py:28
  82.1 0.7 fusion.55
  82.8 0.1 fusion.50
  82.9 0.7 broadcast_in_dim.40
  83.7 9.4 %all-to-all-start.2 = ((f32[32,3,128]{2,1,0:T(4,128)}), f32[32,3,128]{2,1,0:T(4,128)S(1)}, u32[]{:S(2)}, u32[]{:S(2)}) async-start(f32[32,3,128]{2,1,0:T(4,128)} %broadcast_in_dim.40), calls=%async_computation.2 | async-start | bytes 131072 | tf_op jit(solution)/shard_map/all_to_all | solution.py:24
  93.8 0.3 fusion.58
  94.1 9.0 %all-to-all-done.2 = f32[32,3,128]{2,1,0:T(4,128)S(1)} async-done(((f32[32,3,128]{2,1,0:T(4,128)}), f32[32,3,128]{2,1,0:T(4,128)S(1)}, u32[]{:S(2)}, u32[]{:S(2)}) %all-to-all-start.2) | async-done | bytes 49184 | tf_op jit(solution)/shard_map/all_to_all | solution.py:24
  103.2 0.7 fusion.56
  (13 shorter events, 0.2 us)
Async XLA Ops:
  0.6 7.9 %copy-start = (f32[1,9,2,128,128]{4,3,2,1,0:T(8,128)S(1)}, f32[1,9,2,128,128]{4,3,2,1,0:T(8,128)}, u32[]{:S(2)}) copy-start(f32[1,9,2,128,128]{4,3,2,1,0:T(8,128)} %param.9) | copy-start | bytes 3538948
  2.7 5.8 %copy-start.3 = (f32[1,2,128,128]{3,2,1,0:T(8,128)S(1)}, f32[1,2,128,128]{3,2,1,0:T(8,128)}, u32[]{:S(2)}) copy-start(f32[1,2,128,128]{3,2,1,0:T(8,128)} %param.6) | copy-start | bytes 393220
  2.7 20.3 %all-to-all-start = ((f32[8,2,128,128]{3,2,1,0:T(8,128)}), f32[8,2,128,128]{3,2,1,0:T(8,128)S(1)}, u32[]{:S(2)}, u32[]{:S(2)}) async-start(f32[8,2,128,128]{3,2,1,0:T(8,128)} %broadcast_in_dim.18), calls=%async_computation | async-start | bytes 2097152 | tf_op jit(solution)/shard_map/all_to_all | solution.py:35
  9.6 5.3 %copy-start.4 = (s32[9,2]{0,1:T(2,128)S(1)}, s32[9,2]{0,1:T(2,128)}, u32[]{:S(2)}) copy-start(s32[9,2]{0,1:T(2,128)} %param.10) | copy-start | bytes 220
  9.7 16.3 %collective-permute-start = (f32[3,128,128]{1,2,0:T(8,128)S(1)}, f32[3,128,128]{1,2,0:T(8,128)S(1)}, u32[]{:S(2)}, u32[]{:S(2)}) collective-permute-start(f32[3,128,128]{1,2,0:T(8,128)S(1)} %get-tuple-element.23), channel_id=1, source_target_pairs={{0,1},{1,2},{2,3},{3,4},{4,5},{5,6},{6,7},{7,8},{8,9},{9,10},{10,1... | collective-permute-start | bytes 589832 | tf_op jit(solution)/shard_map/ppermute | solution.py:18
  12.8 13.2 %collective-permute-start.1 = (f32[3,128,128]{1,2,0:T(8,128)S(1)}, f32[3,128,128]{1,2,0:T(8,128)S(1)}, u32[]{:S(2)}, u32[]{:S(2)}) collective-permute-start(f32[3,128,128]{1,2,0:T(8,128)S(1)} %get-tuple-element.24), channel_id=1, source_target_pairs={{1,0},{2,1},{3,2},{4,3},{5,4},{6,5},{7,6},{8,7},{9,8},{10,9},{11,1... | collective-permute-start | bytes 589832 | tf_op jit(solution)/shard_map/ppermute | solution.py:18
  23.2 1.3 %copy-start.1 = (f32[9,2,128,128]{3,2,1,0:T(8,128)S(1)}, f32[9,2,128,128]{3,2,1,0:T(8,128)}, u32[]{:S(2)}) copy-start(f32[9,2,128,128]{3,2,1,0:T(8,128)} %param.7) | copy-start | bytes 3538948
  25.9 1.0 copy-start.2
  28.7 7.0 %collective-permute-start.2 = (f32[3,128,128]{2,1,0:T(8,128)S(1)}, f32[3,128,128]{2,1,0:T(8,128)S(1)}, u32[]{:S(2)}, u32[]{:S(2)}) collective-permute-start(f32[3,128,128]{2,1,0:T(8,128)S(1)} %get-tuple-element.16), channel_id=1, source_target_pairs={{0,1},{1,2},{2,3},{3,4},{4,5},{5,6},{6,7},{7,8},{8,9},{9,10},{10,1... | collective-permute-start | bytes 589832 | tf_op jit(solution)/shard_map/ppermute | solution.py:18
  31.8 8.2 %collective-permute-start.3 = (f32[3,128,128]{2,1,0:T(8,128)S(1)}, f32[3,128,128]{2,1,0:T(8,128)S(1)}, u32[]{:S(2)}, u32[]{:S(2)}) collective-permute-start(f32[3,128,128]{2,1,0:T(8,128)S(1)} %get-tuple-element.17), channel_id=1, source_target_pairs={{1,0},{2,1},{3,2},{4,3},{5,4},{6,5},{7,6},{8,7},{9,8},{10,9},{11,1... | collective-permute-start | bytes 589832 | tf_op jit(solution)/shard_map/ppermute | solution.py:18
  42.7 21.1 %all-to-all-start.1 = ((f32[32,3,128]{2,1,0:T(4,128)}), f32[32,3,128]{2,1,0:T(4,128)}, u32[]{:S(2)}, u32[]{:S(2)}) async-start(f32[32,3,128]{2,1,0:T(4,128)} %broadcast_in_dim.19), calls=%async_computation.1 | async-start | bytes 131072 | tf_op jit(solution)/shard_map/all_to_all | solution.py:24
  55.5 9.2 %collective-permute-start.4 = (f32[3,128,128]{2,1,0:T(8,128)}, f32[3,128,128]{2,1,0:T(8,128)S(1)}, u32[]{:S(2)}, u32[]{:S(2)}) collective-permute-start(f32[3,128,128]{2,1,0:T(8,128)} %get-tuple-element.12), channel_id=1, source_target_pairs={{0,1},{1,2},{2,3},{3,4},{4,5},{5,6},{6,7},{7,8},{8,9},{9,10},{10,1... | collective-permute-start | bytes 589832 | tf_op jit(solution)/shard_map/ppermute | solution.py:18
  59.2 7.8 %collective-permute-start.5 = (f32[3,128,128]{2,1,0:T(8,128)}, f32[3,128,128]{2,1,0:T(8,128)S(1)}, u32[]{:S(2)}, u32[]{:S(2)}) collective-permute-start(f32[3,128,128]{2,1,0:T(8,128)} %get-tuple-element.13), channel_id=1, source_target_pairs={{1,0},{2,1},{3,2},{4,3},{5,4},{6,5},{7,6},{8,7},{9,8},{10,9},{11,1... | collective-permute-start | bytes 589832 | tf_op jit(solution)/shard_map/ppermute | solution.py:18
  69.8 4.7 %copy-start.5 = (s32[1,2]{1,0:T(1,128)S(1)}, s32[1,2]{1,0:T(1,128)}, u32[]{:S(2)}) copy-start(s32[1,2]{1,0:T(1,128)} %param.11) | copy-start | bytes 28
  69.9 6.5 %collective-permute-start.6 = (f32[3,128,128]{2,1,0:T(8,128)S(1)}, f32[3,128,128]{2,1,0:T(8,128)S(1)}, u32[]{:S(2)}, u32[]{:S(2)}) collective-permute-start(f32[3,128,128]{2,1,0:T(8,128)S(1)} %get-tuple-element.8), channel_id=1, source_target_pairs={{0,1},{1,2},{2,3},{3,4},{4,5},{5,6},{6,7},{7,8},{8,9},{9,10},{10,1... | collective-permute-start | bytes 589832 | tf_op jit(solution)/shard_map/ppermute | solution.py:18
  73.3 7.7 %collective-permute-start.7 = (f32[3,128,128]{2,1,0:T(8,128)S(1)}, f32[3,128,128]{2,1,0:T(8,128)S(1)}, u32[]{:S(2)}, u32[]{:S(2)}) collective-permute-start(f32[3,128,128]{2,1,0:T(8,128)S(1)} %get-tuple-element.9), channel_id=1, source_target_pairs={{1,0},{2,1},{3,2},{4,3},{5,4},{6,5},{7,6},{8,7},{9,8},{10,9},{11,1... | collective-permute-start | bytes 589832 | tf_op jit(solution)/shard_map/ppermute | solution.py:18
  83.7 19.4 %all-to-all-start.2 = ((f32[32,3,128]{2,1,0:T(4,128)}), f32[32,3,128]{2,1,0:T(4,128)S(1)}, u32[]{:S(2)}, u32[]{:S(2)}) async-start(f32[32,3,128]{2,1,0:T(4,128)} %broadcast_in_dim.40), calls=%async_computation.2 | async-start | bytes 131072 | tf_op jit(solution)/shard_map/all_to_all | solution.py:24

commit v9 on v8

--- a/solution.py
+++ b/solution.py
@@ -7,6 +7,7 @@
 
 
 HIGH = lax.Precision.HIGH
+EXACT = lax.Precision.HIGHEST
 EPS = 1e-06
 LIFT = 1024.0
 SHRINK = 2.0**-50
@@ -24,8 +25,8 @@
     return jnp.sum(lax.all_to_all(spread, axis, 0, 0, tiled=True), axis=0)
 
 
-def mm(spec, a, b):
-    return jnp.einsum(spec, a, b, precision=HIGH)
+def mm(spec, a, b, precision=HIGH):
+    return jnp.einsum(spec, a, b, precision=precision)
 
 
 def left_environment(left_env, maps):
@@ -36,10 +37,10 @@
     width = maps.shape[-1]
     prefix = jnp.broadcast_to(jnp.eye(width, dtype=jnp.float32), maps.shape)
     for step in range(segments - 1):
-        grown = mm("kab,kbc->kac", prefix, every[step])
+        grown = mm("kab,kbc->kac", prefix, every[step], EXACT)
         prefix = jnp.where(step < segment, grown, prefix)
-    right_side = mm("wkbc,kcd->wkbd", left_env, prefix)
-    return mm("kba,wkbd->wkad", prefix, right_side)
+    right_side = mm("wkbc,kcd->wkbd", left_env, prefix, EXACT)
+    return mm("kba,wkbd->wkad", prefix, right_side, EXACT)
 
 
 def exchange(vector, right):

time: 105 us -> 106 us (level)
  matrix products: 11.8 us -> 13.3 us
    dot_general x18, matrix products: 11.8 us -> 13.3 us  [mm(): return jnp.einsum(spec, a, b, precision=precision)]
  transfers between devices with their start and end apart: 11 -> 11, of which waited for: 8 -> 8; matrix products, arithmetic and copies ran while one was open for 8% -> 9% of each run, Pallas kernels for 0% -> 0%
where the time goes in v9:
time: 106 us; the launch traced here: 105 us
  starting transfers between devices  44.8 us (42%)
  waiting for transfers between devices  35.7 us (34%)
  matrix products  13.3 us (13%)
  local copies, waits for them, and re-layouts  7.17 us (7%)
  other arithmetic  2.78 us (3%)
  between operations  1.68 us (2%)
    all_to_all x2, starting transfers between devices, gathered_sums(): return jnp.sum(lax.all_to_all(spread, axis, 0, 0, tiled=True), axis=0)  20.5 us
    ppermute x8, starting transfers between devices, shifted(): return lax.ppermute(block, axis, route)  18.5 us
    ppermute x8, waiting for transfers between devices, shifted(): return lax.ppermute(block, axis, route)  15.3 us
    dot_general x18, matrix products, mm(): return jnp.einsum(spec, a, b, precision=precision)  13.3 us
    all_to_all x2, waiting for transfers between devices, gathered_sums(): return jnp.sum(lax.all_to_all(spread, axis, 0, 0, tiled=True), axis=0)  12.2 us
    all_to_all x1, waiting for transfers between devices, left_environment(): every = lax.all_to_all(spread, 'seg', 0, 0, tiled=True)  8.13 us
    all_to_all x1, starting transfers between devices, left_environment(): every = lax.all_to_all(spread, 'seg', 0, 0, tiled=True)  5.78 us
  transfers between devices with their start and end apart: 11, of which 8 were waited for; matrix products, arithmetic and copies ran while one was open for 9% of the time, Pallas kernels for 0%

profile of v9, /device:TPU:8, one launch (start us, length us, event | category | flops | bytes accessed | tf_op | source)
XLA Modules:
  0.0 105.4 jit_solution(14909150025752465624)
XLA Ops:
  0.6 0.0 copy-start
  0.6 2.1 %broadcast_in_dim.18 = f32[8,2,128,128]{3,2,1,0:T(8,128)} broadcast(f32[2,128,128]{2,1,0:T(8,128)} %bitcast.197), dimensions={1,2,3} | broadcast | bytes 1179648 | tf_op jit(solution)/shard_map/broadcast_in_dim | solution.py:35
  2.7 5.8 %all-to-all-start = ((f32[8,2,128,128]{3,2,1,0:T(8,128)}), f32[8,2,128,128]{3,2,1,0:T(8,128)S(1)}, u32[]{:S(2)}, u32[]{:S(2)}) async-start(f32[8,2,128,128]{3,2,1,0:T(8,128)} %broadcast_in_dim.18), calls=%async_computation | async-start | bytes 2097152 | tf_op jit(solution)/shard_map/all_to_all | solution.py:36
  8.5 0.0 copy-done
  8.5 1.1 %convolution_bitcast_fusion.3 = f32[9,2,128,128]{2,3,0,1:T(8,128)S(1)} fusion(f32[1,2,128,128]{3,2,1,0:T(8,128)S(1)} %copy-done.3, f32[1,9,2,128,128]{4,3,2,1,0:T(8,128)S(1)} %copy-done), kind=kOutput, calls=%fused_computation.3 | convolution fusion | flops 226492416 | bytes 2490368 | tf_op jit(solution)/shard_map/kab,wkbc->wkac/dot_general | solution.py:29
  9.6 0.0 copy-start.4
  9.6 0.1 slice_bitcast_fusion.7
  9.7 3.1 %collective-permute-start = (f32[3,128,128]{1,2,0:T(8,128)S(1)}, f32[3,128,128]{1,2,0:T(8,128)S(1)}, u32[]{:S(2)}, u32[]{:S(2)}) collective-permute-start(f32[3,128,128]{1,2,0:T(8,128)S(1)} %get-tuple-element.23), channel_id=1, source_target_pairs={{0,1},{1,2},{2,3},{3,4},{4,5},{5,6},{6,7},{7,8},{8,9},{9,10},{10,1... | collective-permute-start | bytes 589832 | tf_op jit(solution)/shard_map/ppermute | solution.py:19
  12.8 1.3 %collective-permute-start.1 = (f32[3,128,128]{1,2,0:T(8,128)S(1)}, f32[3,128,128]{1,2,0:T(8,128)S(1)}, u32[]{:S(2)}, u32[]{:S(2)}) collective-permute-start(f32[3,128,128]{1,2,0:T(8,128)S(1)} %get-tuple-element.24), channel_id=1, source_target_pairs={{1,0},{2,1},{3,2},{4,3},{5,4},{6,5},{7,6},{8,7},{9,8},{10,9},{11,1... | collective-permute-start | bytes 589832 | tf_op jit(solution)/shard_map/ppermute | solution.py:19
  14.1 0.8 slice.122
  14.9 0.0 copy-done.4
  14.9 8.1 %all-to-all-done = f32[8,2,128,128]{3,2,1,0:T(8,128)S(1)} async-done(((f32[8,2,128,128]{3,2,1,0:T(8,128)}), f32[8,2,128,128]{3,2,1,0:T(8,128)S(1)}, u32[]{:S(2)}, u32[]{:S(2)}) %all-to-all-start) | async-done | bytes 1048608 | tf_op jit(solution)/shard_map/all_to_all | solution.py:36
  23.0 0.3 convolution_select_fusion.6
  23.3 0.0 copy-start.1
  23.3 0.3 convolution_select_fusion.5
  23.6 0.3 convolution_select_fusion.4
  23.9 0.3 convolution_select_fusion.3
  24.1 0.3 convolution_select_fusion.2
  24.4 0.3 convolution_select_fusion.1
  24.7 0.3 fusion.42
  25.0 1.3 %convolution_bitcast_fusion.5 = f32[9,2,128,128]{2,3,0,1:T(8,128)S(1)} fusion(f32[2,128,128,1]{2,1,3,0:T(8,128)S(1)} %fusion.42, f32[9,2,128,128]{3,2,1,0:T(8,128)S(1)} %copy-done.1), kind=kOutput, calls=%fused_computation.5 | convolution fusion | flops 452984832 | bytes 2490368 | tf_op jit(solution)/shard_map/wkbc,kcd->wkbd/dot_general | solution.py:29
  26.3 1.1 %fusion = f32[9,2,128,128]{2,3,0,1:T(8,128)S(1)} fusion(f32[9,2,128,128]{2,3,0,1:T(8,128)S(1)} %convolution_bitcast_fusion.5, f32[2,128,128,1]{2,1,3,0:T(8,128)S(1)} %fusion.42, f32[9,2]{0,1:T(2,128)S(1)} %convert_element_type.16), kind=kOutput, calls=%fused_computation.6 | convolution fusion | flops 453279744 | bytes 2490440 | tf_op jit(solution)/shard_map/kba,wkbd->wkad/dot_general | solution.py:29
  27.4 0.0 copy-start.2
  27.4 0.1 fusion.77
  27.5 0.0 collective-permute-done
  27.5 0.0 collective-permute-done.1
  27.5 0.9 copy-done.2
  28.4 1.2 %fusion.1 = f32[2,128,128,1]{2,1,3,0:T(8,128)S(1)} fusion(f32[3,1,128,128]{2,3,0,1:T(8,128)S(1)} %bitcast.199, f32[3,1,128,128]{2,3,0,1:T(8,128)S(1)} %get-tuple-element.25, f32[3,2,128,128]{2,3,0,1:T(8,128)S(1)} %copy-done.2, f32[3,1,128,128]{2,3,0,1:T(8,128)S(1)} %get-tuple-element.26, f32[3,1,128,128]{2,3,0,1:T(8,128)S(1)} %bitcast.198, ...), kind=kOutput, calls=%fused_computation.8 | convolution fusion | flops 228261888 | bytes 2490368 | tf_op jit(solution)/shard_map/wkab,wkbc->kac/dot_general | solution.py:29
  29.5 0.6 convolution_bitcast_fusion.2
  30.2 0.1 slice_bitcast_fusion.5
  30.2 3.1 %collective-permute-start.2 = (f32[3,128,128]{2,1,0:T(8,128)S(1)}, f32[3,128,128]{2,1,0:T(8,128)S(1)}, u32[]{:S(2)}, u32[]{:S(2)}) collective-permute-start(f32[3,128,128]{2,1,0:T(8,128)S(1)} %get-tuple-element.16), channel_id=1, source_target_pairs={{0,1},{1,2},{2,3},{3,4},{4,5},{5,6},{6,7},{7,8},{8,9},{9,10},{10,1... | collective-permute-start | bytes 589832 | tf_op jit(solution)/shard_map/ppermute | solution.py:19
  33.3 1.3 %collective-permute-start.3 = (f32[3,128,128]{2,1,0:T(8,128)S(1)}, f32[3,128,128]{2,1,0:T(8,128)S(1)}, u32[]{:S(2)}, u32[]{:S(2)}) collective-permute-start(f32[3,128,128]{2,1,0:T(8,128)S(1)} %get-tuple-element.17), channel_id=1, source_target_pairs={{1,0},{2,1},{3,2},{4,3},{5,4},{6,5},{7,6},{8,7},{9,8},{10,9},{11,1... | collective-permute-start | bytes 589832 | tf_op jit(solution)/shard_map/ppermute | solution.py:19
  34.6 2.6 %collective-permute-done.2 = f32[3,128,128]{2,1,0:T(8,128)S(1)} collective-permute-done((f32[3,128,128]{2,1,0:T(8,128)S(1)}, f32[3,128,128]{2,1,0:T(8,128)S(1)}, u32[]{:S(2)}, u32[]{:S(2)}) %collective-permute-start.2) | collective-permute-done | bytes 196640 | tf_op jit(solution)/shard_map/ppermute | solution.py:19
  37.2 4.3 %collective-permute-done.3 = f32[3,128,128]{2,1,0:T(8,128)S(1)} collective-permute-done((f32[3,128,128]{2,1,0:T(8,128)S(1)}, f32[3,128,128]{2,1,0:T(8,128)S(1)}, u32[]{:S(2)}, u32[]{:S(2)}) %collective-permute-start.3) | collective-permute-done | bytes 196640 | tf_op jit(solution)/shard_map/ppermute | solution.py:19
  41.6 1.1 %fusion.11 = f32[2,128,128,1]{2,1,3,0:T(8,128)S(1)} fusion(f32[3,1,128,128]{3,2,0,1:T(8,128)S(1)} %bitcast.205, f32[3,1,128,128]{3,2,0,1:T(8,128)S(1)} %get-tuple-element.18, f32[3,2,128,128]{3,2,0,1:T(8,128)S(1)} %slice.127, f32[3,1,128,128]{3,2,0,1:T(8,128)S(1)} %get-tuple-element.19, f32[3,1,128,128]{3,2,0,1:T(8,128)S(1)} %bitcast.204, ...), kind=kOutput, calls=%fused_computation.18 | convolution fusion | flops 228261888 | bytes 2490368 | tf_op jit(solution)/shard_map/wkab,wkbc->kac/dot_general | solution.py:29
  42.7 0.6 convolution_bitcast_fusion.1
  43.4 0.1 fusion.49
  43.5 0.7 broadcast_in_dim.19
  44.2 11.1 %all-to-all-start.1 = ((f32[32,3,128]{2,1,0:T(4,128)}), f32[32,3,128]{2,1,0:T(4,128)}, u32[]{:S(2)}, u32[]{:S(2)}) async-start(f32[32,3,128]{2,1,0:T(4,128)} %broadcast_in_dim.19), calls=%async_computation.1 | async-start | bytes 131072 | tf_op jit(solution)/shard_map/all_to_all | solution.py:25
  55.3 0.9 slice_bitcast_fusion.3
  56.3 0.8 slice.132
  57.0 3.6 %collective-permute-start.4 = (f32[3,128,128]{2,1,0:T(8,128)}, f32[3,128,128]{2,1,0:T(8,128)S(1)}, u32[]{:S(2)}, u32[]{:S(2)}) collective-permute-start(f32[3,128,128]{2,1,0:T(8,128)} %get-tuple-element.12), channel_id=1, source_target_pairs={{0,1},{1,2},{2,3},{3,4},{4,5},{5,6},{6,7},{7,8},{8,9},{9,10},{10,1... | collective-permute-start | bytes 589832 | tf_op jit(solution)/shard_map/ppermute | solution.py:19
  60.7 1.5 %collective-permute-start.5 = (f32[3,128,128]{2,1,0:T(8,128)}, f32[3,128,128]{2,1,0:T(8,128)S(1)}, u32[]{:S(2)}, u32[]{:S(2)}) collective-permute-start(f32[3,128,128]{2,1,0:T(8,128)} %get-tuple-element.13), channel_id=1, source_target_pairs={{1,0},{2,1},{3,2},{4,3},{5,4},{6,5},{7,6},{8,7},{9,8},{10,9},{11,1... | collective-permute-start | bytes 589832 | tf_op jit(solution)/shard_map/ppermute | solution.py:19
  62.1 3.2 %all-to-all-done.1 = f32[32,3,128]{2,1,0:T(4,128)} async-done(((f32[32,3,128]{2,1,0:T(4,128)}), f32[32,3,128]{2,1,0:T(4,128)}, u32[]{:S(2)}, u32[]{:S(2)}) %all-to-all-start.1) | async-done | bytes 49184 | tf_op jit(solution)/shard_map/all_to_all | solution.py:25
  65.3 0.9 reduce_sum.37
  66.2 0.0 collective-permute-done.4
  66.3 2.2 %collective-permute-done.5 = f32[3,128,128]{2,1,0:T(8,128)S(1)} collective-permute-done((f32[3,128,128]{2,1,0:T(8,128)}, f32[3,128,128]{2,1,0:T(8,128)S(1)}, u32[]{:S(2)}, u32[]{:S(2)}) %collective-permute-start.5) | collective-permute-done | bytes 196640 | tf_op jit(solution)/shard_map/ppermute | solution.py:19
  68.4 2.3 %fusion.43 = f32[2,128,128]{2,1,0:T(8,128)S(1)} fusion(f32[3,1,128,128]{3,2,0,1:T(8,128)S(1)} %bitcast.201, f32[3,1,128,128]{3,2,0,1:T(8,128)} %get-tuple-element.14, f32[3,2,128,128]{3,2,0,1:T(8,128)} %slice.132, f32[3,1,128,128]{3,2,0,1:T(8,128)} %get-tuple-element.15, f32[3,1,128,128]{3,2,0,1:T(8,128)S(1)} %bitcast.200, ...), kind=kOutput, calls=%fused_computation.58 | convolution fusion | flops 228589568 | bytes 2491392 | tf_op jit(solution)/shard_map/wkab,wkbc->kac/dot_general | solution.py:29
  70.7 0.6 convolution_bitcast_fusion
  71.3 0.0 copy-start.5
  71.3 0.1 slice_bitcast_fusion.1
  71.4 3.4 %collective-permute-start.6 = (f32[3,128,128]{2,1,0:T(8,128)S(1)}, f32[3,128,128]{2,1,0:T(8,128)S(1)}, u32[]{:S(2)}, u32[]{:S(2)}) collective-permute-start(f32[3,128,128]{2,1,0:T(8,128)S(1)} %get-tuple-element.8), channel_id=1, source_target_pairs={{0,1},{1,2},{2,3},{3,4},{4,5},{5,6},{6,7},{7,8},{8,9},{9,10},{10,1... | collective-permute-start | bytes 589832 | tf_op jit(solution)/shard_map/ppermute | solution.py:19
  74.8 1.3 %collective-permute-start.7 = (f32[3,128,128]{2,1,0:T(8,128)S(1)}, f32[3,128,128]{2,1,0:T(8,128)S(1)}, u32[]{:S(2)}, u32[]{:S(2)}) collective-permute-start(f32[3,128,128]{2,1,0:T(8,128)S(1)} %get-tuple-element.9), channel_id=1, source_target_pairs={{1,0},{2,1},{3,2},{4,3},{5,4},{6,5},{7,6},{8,7},{9,8},{10,9},{11,1... | collective-permute-start | bytes 589832 | tf_op jit(solution)/shard_map/ppermute | solution.py:19
  76.1 0.1 compare_convert_fusion
  76.2 1.7 %collective-permute-done.6 = f32[3,128,128]{2,1,0:T(8,128)S(1)} collective-permute-done((f32[3,128,128]{2,1,0:T(8,128)S(1)}, f32[3,128,128]{2,1,0:T(8,128)S(1)}, u32[]{:S(2)}, u32[]{:S(2)}) %collective-permute-start.6) | collective-permute-done | bytes 196640 | tf_op jit(solution)/shard_map/ppermute | solution.py:19
  78.0 4.5 %collective-permute-done.7 = f32[3,128,128]{2,1,0:T(8,128)S(1)} collective-permute-done((f32[3,128,128]{2,1,0:T(8,128)S(1)}, f32[3,128,128]{2,1,0:T(8,128)S(1)}, u32[]{:S(2)}, u32[]{:S(2)}) %collective-permute-start.7) | collective-permute-done | bytes 196640 | tf_op jit(solution)/shard_map/ppermute | solution.py:19
  82.5 1.1 %fusion.30 = f32[2,128,128,1]{2,1,3,0:T(8,128)S(1)} fusion(f32[3,1,128,128]{3,2,0,1:T(8,128)S(1)} %bitcast.203, f32[3,1,128,128]{3,2,0,1:T(8,128)S(1)} %get-tuple-element.10, f32[3,2,128,128]{3,2,0,1:T(8,128)S(1)} %slice.140, f32[3,1,128,128]{3,2,0,1:T(8,128)S(1)} %get-tuple-element.11, f32[3,1,128,128]{3,2,0,1:T(8,128)S(1)} %bitcast.202, ...), kind=kOutput, calls=%fused_computation.38 | convolution fusion | flops 228261888 | bytes 2490368 | tf_op jit(solution)/shard_map/wkab,wkbc->kac/dot_general | solution.py:29
  83.6 0.7 fusion.55
  84.3 0.1 fusion.50
  84.5 0.7 broadcast_in_dim.40
  85.2 9.4 %all-to-all-start.2 = ((f32[32,3,128]{2,1,0:T(4,128)}), f32[32,3,128]{2,1,0:T(4,128)S(1)}, u32[]{:S(2)}, u32[]{:S(2)}) async-start(f32[32,3,128]{2,1,0:T(4,128)} %broadcast_in_dim.40), calls=%async_computation.2 | async-start | bytes 131072 | tf_op jit(solution)/shard_map/all_to_all | solution.py:25
  95.3 0.3 fusion.58
  95.6 9.0 %all-to-all-done.2 = f32[32,3,128]{2,1,0:T(4,128)S(1)} async-done(((f32[32,3,128]{2,1,0:T(4,128)}), f32[32,3,128]{2,1,0:T(4,128)S(1)}, u32[]{:S(2)}, u32[]{:S(2)}) %all-to-all-start.2) | async-done | bytes 49184 | tf_op jit(solution)/shard_map/all_to_all | solution.py:25
  104.7 0.7 fusion.56
  (13 shorter events, 0.2 us)
Async XLA Ops:
  0.6 7.9 %copy-start = (f32[1,9,2,128,128]{4,3,2,1,0:T(8,128)S(1)}, f32[1,9,2,128,128]{4,3,2,1,0:T(8,128)}, u32[]{:S(2)}) copy-start(f32[1,9,2,128,128]{4,3,2,1,0:T(8,128)} %param.9) | copy-start | bytes 3538948
  2.7 5.8 %copy-start.3 = (f32[1,2,128,128]{3,2,1,0:T(8,128)S(1)}, f32[1,2,128,128]{3,2,1,0:T(8,128)}, u32[]{:S(2)}) copy-start(f32[1,2,128,128]{3,2,1,0:T(8,128)} %param.6) | copy-start | bytes 393220
  2.7 20.3 %all-to-all-start = ((f32[8,2,128,128]{3,2,1,0:T(8,128)}), f32[8,2,128,128]{3,2,1,0:T(8,128)S(1)}, u32[]{:S(2)}, u32[]{:S(2)}) async-start(f32[8,2,128,128]{3,2,1,0:T(8,128)} %broadcast_in_dim.18), calls=%async_computation | async-start | bytes 2097152 | tf_op jit(solution)/shard_map/all_to_all | solution.py:36
  9.6 5.3 %copy-start.4 = (s32[9,2]{0,1:T(2,128)S(1)}, s32[9,2]{0,1:T(2,128)}, u32[]{:S(2)}) copy-start(s32[9,2]{0,1:T(2,128)} %param.10) | copy-start | bytes 220
  9.7 17.8 %collective-permute-start = (f32[3,128,128]{1,2,0:T(8,128)S(1)}, f32[3,128,128]{1,2,0:T(8,128)S(1)}, u32[]{:S(2)}, u32[]{:S(2)}) collective-permute-start(f32[3,128,128]{1,2,0:T(8,128)S(1)} %get-tuple-element.23), channel_id=1, source_target_pairs={{0,1},{1,2},{2,3},{3,4},{4,5},{5,6},{6,7},{7,8},{8,9},{9,10},{10,1... | collective-permute-start | bytes 589832 | tf_op jit(solution)/shard_map/ppermute | solution.py:19
  12.8 14.7 %collective-permute-start.1 = (f32[3,128,128]{1,2,0:T(8,128)S(1)}, f32[3,128,128]{1,2,0:T(8,128)S(1)}, u32[]{:S(2)}, u32[]{:S(2)}) collective-permute-start(f32[3,128,128]{1,2,0:T(8,128)S(1)} %get-tuple-element.24), channel_id=1, source_target_pairs={{1,0},{2,1},{3,2},{4,3},{5,4},{6,5},{7,6},{8,7},{9,8},{10,9},{11,1... | collective-permute-start | bytes 589832 | tf_op jit(solution)/shard_map/ppermute | solution.py:19
  23.3 1.7 %copy-start.1 = (f32[9,2,128,128]{3,2,1,0:T(8,128)S(1)}, f32[9,2,128,128]{3,2,1,0:T(8,128)}, u32[]{:S(2)}) copy-start(f32[9,2,128,128]{3,2,1,0:T(8,128)} %param.7) | copy-start | bytes 3538948
  27.4 1.0 copy-start.2
  30.2 7.0 %collective-permute-start.2 = (f32[3,128,128]{2,1,0:T(8,128)S(1)}, f32[3,128,128]{2,1,0:T(8,128)S(1)}, u32[]{:S(2)}, u32[]{:S(2)}) collective-permute-start(f32[3,128,128]{2,1,0:T(8,128)S(1)} %get-tuple-element.16), channel_id=1, source_target_pairs={{0,1},{1,2},{2,3},{3,4},{4,5},{5,6},{6,7},{7,8},{8,9},{9,10},{10,1... | collective-permute-start | bytes 589832 | tf_op jit(solution)/shard_map/ppermute | solution.py:19
  33.3 8.2 %collective-permute-start.3 = (f32[3,128,128]{2,1,0:T(8,128)S(1)}, f32[3,128,128]{2,1,0:T(8,128)S(1)}, u32[]{:S(2)}, u32[]{:S(2)}) collective-permute-start(f32[3,128,128]{2,1,0:T(8,128)S(1)} %get-tuple-element.17), channel_id=1, source_target_pairs={{1,0},{2,1},{3,2},{4,3},{5,4},{6,5},{7,6},{8,7},{9,8},{10,9},{11,1... | collective-permute-start | bytes 589832 | tf_op jit(solution)/shard_map/ppermute | solution.py:19
  44.2 21.1 %all-to-all-start.1 = ((f32[32,3,128]{2,1,0:T(4,128)}), f32[32,3,128]{2,1,0:T(4,128)}, u32[]{:S(2)}, u32[]{:S(2)}) async-start(f32[32,3,128]{2,1,0:T(4,128)} %broadcast_in_dim.19), calls=%async_computation.1 | async-start | bytes 131072 | tf_op jit(solution)/shard_map/all_to_all | solution.py:25
  57.0 9.2 %collective-permute-start.4 = (f32[3,128,128]{2,1,0:T(8,128)}, f32[3,128,128]{2,1,0:T(8,128)S(1)}, u32[]{:S(2)}, u32[]{:S(2)}) collective-permute-start(f32[3,128,128]{2,1,0:T(8,128)} %get-tuple-element.12), channel_id=1, source_target_pairs={{0,1},{1,2},{2,3},{3,4},{4,5},{5,6},{6,7},{7,8},{8,9},{9,10},{10,1... | collective-permute-start | bytes 589832 | tf_op jit(solution)/shard_map/ppermute | solution.py:19
  60.7 7.8 %collective-permute-start.5 = (f32[3,128,128]{2,1,0:T(8,128)}, f32[3,128,128]{2,1,0:T(8,128)S(1)}, u32[]{:S(2)}, u32[]{:S(2)}) collective-permute-start(f32[3,128,128]{2,1,0:T(8,128)} %get-tuple-element.13), channel_id=1, source_target_pairs={{1,0},{2,1},{3,2},{4,3},{5,4},{6,5},{7,6},{8,7},{9,8},{10,9},{11,1... | collective-permute-start | bytes 589832 | tf_op jit(solution)/shard_map/ppermute | solution.py:19
  71.3 4.8 %copy-start.5 = (s32[1,2]{1,0:T(1,128)S(1)}, s32[1,2]{1,0:T(1,128)}, u32[]{:S(2)}) copy-start(s32[1,2]{1,0:T(1,128)} %param.11) | copy-start | bytes 28
  71.4 6.5 %collective-permute-start.6 = (f32[3,128,128]{2,1,0:T(8,128)S(1)}, f32[3,128,128]{2,1,0:T(8,128)S(1)}, u32[]{:S(2)}, u32[]{:S(2)}) collective-permute-start(f32[3,128,128]{2,1,0:T(8,128)S(1)} %get-tuple-element.8), channel_id=1, source_target_pairs={{0,1},{1,2},{2,3},{3,4},{4,5},{5,6},{6,7},{7,8},{8,9},{9,10},{10,1... | collective-permute-start | bytes 589832 | tf_op jit(solution)/shard_map/ppermute | solution.py:19
  74.8 7.7 %collective-permute-start.7 = (f32[3,128,128]{2,1,0:T(8,128)S(1)}, f32[3,128,128]{2,1,0:T(8,128)S(1)}, u32[]{:S(2)}, u32[]{:S(2)}) collective-permute-start(f32[3,128,128]{2,1,0:T(8,128)S(1)} %get-tuple-element.9), channel_id=1, source_target_pairs={{1,0},{2,1},{3,2},{4,3},{5,4},{6,5},{7,6},{8,7},{9,8},{10,9},{11,1... | collective-permute-start | bytes 589832 | tf_op jit(solution)/shard_map/ppermute | solution.py:19
  85.2 19.4 %all-to-all-start.2 = ((f32[32,3,128]{2,1,0:T(4,128)}), f32[32,3,128]{2,1,0:T(4,128)S(1)}, u32[]{:S(2)}, u32[]{:S(2)}) async-start(f32[32,3,128]{2,1,0:T(4,128)} %broadcast_in_dim.40), calls=%async_computation.2 | async-start | bytes 131072 | tf_op jit(solution)/shard_map/all_to_all | solution.py:25

commit v10 on v9

--- a/solution.py
+++ b/solution.py
@@ -34,19 +34,24 @@
     segment = lax.axis_index("seg")
     spread = jnp.broadcast_to(maps[None], (segments,) + maps.shape)
     every = lax.all_to_all(spread, "seg", 0, 0, tiled=True)
+    scan = every[: segments - 1]
+    reach = 1
+    while reach < segments - 1:
+        joined = mm("tkab,tkbc->tkac", scan[:-reach], scan[reach:], EXACT)
+        scan = jnp.concatenate([scan[:reach], joined], axis=0)
+        reach *= 2
     width = maps.shape[-1]
-    prefix = jnp.broadcast_to(jnp.eye(width, dtype=jnp.float32), maps.shape)
-    for step in range(segments - 1):
-        grown = mm("kab,kbc->kac", prefix, every[step], EXACT)
-        prefix = jnp.where(step < segment, grown, prefix)
+    eye = jnp.broadcast_to(jnp.eye(width, dtype=jnp.float32), maps.shape)
+    before = lax.dynamic_index_in_dim(scan, jnp.maximum(segment - 1, 0), 0, keepdims=False)
+    prefix = jnp.where(segment > 0, before, eye)
     right_side = mm("wkbc,kcd->wkbd", left_env, prefix, EXACT)
     return mm("kba,wkbd->wkad", prefix, right_side, EXACT)
 
 
 def exchange(vector, right):
     products = mm("kab,wkbc->wkac", vector, right)
-    from_left = shifted(products[0::3, 1], "sec", 1)
-    from_right = shifted(products[2::3, 0], "sec", -1)
+    from_left = shifted(mm("ab,wbc->wac", vector[1], right[0::3, 1]), "sec", 1)
+    from_right = shifted(mm("ab,wbc->wac", vector[0], right[2::3, 0]), "sec", -1)
     return products, from_left, from_right
 
 
@@ -61,7 +66,10 @@
 
 
 def apply_terms(vector, right, ordered):
-    return combine(exchange(vector, right), ordered)
+    products = mm("kab,wkbc->wkac", vector, right)
+    from_left = shifted(products[0::3, 1], "sec", 1)
+    from_right = shifted(products[2::3, 0], "sec", -1)
+    return combine((products, from_left, from_right), ordered)
 
 
 def square_sums(normal, lifted):

time: 106 us -> 113 us (1.066)
  matrix products: 13.3 us -> 18.6 us
  waiting for transfers between devices: 35.7 us -> 33.1 us
  local copies, waits for them, and re-layouts: 7.17 us -> 9.55 us
    dot_general x18 -> x16, matrix products: 13.3 us -> 18.6 us  [mm(): return jnp.einsum(spec, a, b, precision=precision)]
    all_to_all x2, waiting for transfers between devices: 12.2 us -> 9 us  [gathered_sums(): return jnp.sum(lax.all_to_all(spread, axis, 0, 0, tiled=True), axis=0)]
    ppermute x8, waiting for transfers between devices: 15.3 us -> 17.4 us  [shifted(): return lax.ppermute(block, axis, route)]
    unnamed x12 -> x31, local copies, waits for them, and re-layouts: 0.89 us -> 2.5 us
    all_to_all x1, waiting for transfers between devices: 8.13 us -> 6.65 us  [left_environment(): every = lax.all_to_all(spread, 'seg', 0, 0, tiled=True)]
  transfers between devices with their start and end apart: 11 -> 11, of which waited for: 8 -> 8; matrix products, arithmetic and copies ran while one was open for 9% -> 14% of each run, Pallas kernels for 0% -> 0%
where the time goes in v10:
time: 113 us; the launch traced here: 112 us
  starting transfers between devices  45.6 us (40%)
  waiting for transfers between devices  33.1 us (29%)
  matrix products  18.6 us (16%)
  local copies, waits for them, and re-layouts  9.55 us (8%)
  other arithmetic  3.52 us (3%)
  between operations  1.72 us (2%)
    all_to_all x2, starting transfers between devices, gathered_sums(): return jnp.sum(lax.all_to_all(spread, axis, 0, 0, tiled=True), axis=0)  20.5 us
    ppermute x8, starting transfers between devices, shifted(): return lax.ppermute(block, axis, route)  19.3 us
    dot_general x16, matrix products, mm(): return jnp.einsum(spec, a, b, precision=precision)  18.6 us
    ppermute x8, waiting for transfers between devices, shifted(): return lax.ppermute(block, axis, route)  17.4 us
    all_to_all x2, waiting for transfers between devices, gathered_sums(): return jnp.sum(lax.all_to_all(spread, axis, 0, 0, tiled=True), axis=0)  9 us
    all_to_all x1, waiting for transfers between devices, left_environment(): every = lax.all_to_all(spread, 'seg', 0, 0, tiled=True)  6.65 us
    all_to_all x1, starting transfers between devices, left_environment(): every = lax.all_to_all(spread, 'seg', 0, 0, tiled=True)  5.78 us
    unnamed x31, local copies, waits for them, and re-layouts  2.5 us
  transfers between devices with their start and end apart: 11, of which 8 were waited for; matrix products, arithmetic and copies ran while one was open for 14% of the time, Pallas kernels for 0%

profile of v10, /device:TPU:8, one launch (start us, length us, event | category | flops | bytes accessed | tf_op | source)
XLA Modules:
  0.0 112.1 jit_solution(9474440647021368539)
XLA Ops:
  0.6 0.0 copy-start
  0.6 2.1 %broadcast_in_dim.15 = f32[8,2,128,128]{3,2,1,0:T(8,128)} broadcast(f32[2,128,128]{2,1,0:T(8,128)} %bitcast.193), dimensions={1,2,3} | broadcast | bytes 1179648 | tf_op jit(solution)/shard_map/broadcast_in_dim | solution.py:35
  2.8 5.8 %all-to-all-start = ((f32[8,2,128,128]{3,2,1,0:T(8,128)}), f32[8,2,128,128]{3,2,1,0:T(8,128)S(1)}, u32[]{:S(2)}, u32[]{:S(2)}) async-start(f32[8,2,128,128]{3,2,1,0:T(8,128)} %broadcast_in_dim.15), calls=%async_computation | async-start | bytes 2097152 | tf_op jit(solution)/shard_map/all_to_all | solution.py:36
  8.5 1.1 convolution_bitcast_fusion.3
  9.6 0.0 copy-start.13
  9.7 0.9 slice_bitcast_fusion.5
  10.5 3.8 %collective-permute-start = (f32[3,128,128]{1,2,0:T(8,128)}, f32[3,128,128]{1,2,0:T(8,128)}, u32[]{:S(2)}, u32[]{:S(2)}) collective-permute-start(f32[3,128,128]{1,2,0:T(8,128)} %get-tuple-element.21), channel_id=1, source_target_pairs={{0,1},{1,2},{2,3},{3,4},{4,5},{5,6},{6,7},{7,8},{8,9},{9,10},{10,1... | collective-permute-start | bytes 589832 | tf_op jit(solution)/shard_map/ppermute | solution.py:19
  14.3 1.3 %collective-permute-start.1 = (f32[3,128,128]{1,2,0:T(8,128)}, f32[3,128,128]{1,2,0:T(8,128)}, u32[]{:S(2)}, u32[]{:S(2)}) collective-permute-start(f32[3,128,128]{1,2,0:T(8,128)} %get-tuple-element.22), channel_id=1, source_target_pairs={{1,0},{2,1},{3,2},{4,3},{5,4},{6,5},{7,6},{8,7},{9,8},{10,9},{11,1... | collective-permute-start | bytes 589832 | tf_op jit(solution)/shard_map/ppermute | solution.py:19
  15.6 0.8 slice.140
  16.4 6.7 %all-to-all-done = f32[8,2,128,128]{3,2,1,0:T(8,128)S(1)} async-done(((f32[8,2,128,128]{3,2,1,0:T(8,128)}), f32[8,2,128,128]{3,2,1,0:T(8,128)S(1)}, u32[]{:S(2)}, u32[]{:S(2)}) %all-to-all-start) | async-done | bytes 1048608 | tf_op jit(solution)/shard_map/all_to_all | solution.py:36
  23.1 0.9 fusion.46
  24.0 0.8 fusion.45
  24.7 0.1 fusion.44
  24.8 0.5 fusion.50
  25.4 1.3 %convolution_bitcast_fusion.5 = f32[9,2,128,128]{2,3,0,1:T(8,128)S(1)} fusion(f32[9,2,128,128]{3,2,1,0:T(8,128)S(1)} %copy-done, s32[]{:T(128)S(6)} %max.6, f32[4,2,128,128]{3,2,1,0:T(8,128)S(1)} %slice.169, f32[3,2,128,128]{3,2,1,0:T(8,128)S(1)} %fusion.50, f32[128,128]{1,0:T(8,128)S(1)} %fusion.76, pred[]{:T(512)S(6)} %gt.3), kind=kOutput, calls=%fused_computation.5 | convolution fusion | flops 453050368 | bytes 3342341 | tf_op jit(solution)/shard_map/wkbc,kcd->wkbd/dot_general | solution.py:29
  26.7 1.1 %fusion = f32[9,2,128,128]{2,3,0,1:T(8,128)S(1)} fusion(f32[9,2,128,128]{2,3,0,1:T(8,128)S(1)} %convolution_bitcast_fusion.5, f32[9,2]{0,1:T(2,128)S(1)} %convert_element_type.14, s32[]{:T(128)S(6)} %max.6, f32[4,2,128,128]{3,2,1,0:T(8,128)S(1)} %slice.169, f32[3,2,128,128]{3,2,1,0:T(8,128)S(1)} %fusion.50, f32[128,128]{1,0:T(8,128)S(1)} %fusion.76, pred[]{:T(512)S(6)} %gt.3), kind=kOutput, calls=%fused_computation.6 | convolution fusion | flops 453345280 | bytes 3342413 | tf_op jit(solution)/shard_map/kba,wkbd->wkad/dot_general | solution.py:29
  27.8 0.1 fusion.89
  28.0 0.0 collective-permute-done
  28.0 0.0 collective-permute-done.1
  28.0 0.8 copy-done.9
  28.8 0.2 copy-done.10
  29.0 0.2 copy-done.11
  29.3 2.2 %fusion.1 = f32[2,128,128,1]{2,1,3,0:T(8,128)S(1)} fusion(f32[3,1,128,128]{2,3,0,1:T(8,128)} %bitcast.16, f32[3,1,128,128]{2,3,0,1:T(8,128)S(1)} %copy-done.10, f32[3,2,128,128]{2,3,0,1:T(8,128)S(1)} %copy-done.9, f32[3,1,128,128]{2,3,0,1:T(8,128)S(1)} %copy-done.11, f32[3,1,128,128]{2,3,0,1:T(8,128)} %bitcast.14, ...), kind=kOutput, calls=%fused_computation.10 | convolution fusion | flops 228261888 | bytes 2490368 | tf_op jit(solution)/shard_map/wkab,wkbc->kac/dot_general | solution.py:29
  31.5 0.6 convolution_bitcast_fusion.2
  32.1 0.1 slice_bitcast_fusion.3
  32.2 3.1 %collective-permute-start.2 = (f32[3,128,128]{2,1,0:T(8,128)S(1)}, f32[3,128,128]{2,1,0:T(8,128)S(1)}, u32[]{:S(2)}, u32[]{:S(2)}) collective-permute-start(f32[3,128,128]{2,1,0:T(8,128)S(1)} %get-tuple-element.14), channel_id=1, source_target_pairs={{0,1},{1,2},{2,3},{3,4},{4,5},{5,6},{6,7},{7,8},{8,9},{9,10},{10,1... | collective-permute-start | bytes 589832 | tf_op jit(solution)/shard_map/ppermute | solution.py:19
  35.2 1.3 %collective-permute-start.3 = (f32[3,128,128]{2,1,0:T(8,128)S(1)}, f32[3,128,128]{2,1,0:T(8,128)S(1)}, u32[]{:S(2)}, u32[]{:S(2)}) collective-permute-start(f32[3,128,128]{2,1,0:T(8,128)S(1)} %get-tuple-element.15), channel_id=1, source_target_pairs={{1,0},{2,1},{3,2},{4,3},{5,4},{6,5},{7,6},{8,7},{9,8},{10,9},{11,1... | collective-permute-start | bytes 589832 | tf_op jit(solution)/shard_map/ppermute | solution.py:19
  36.5 1.1 %copy.69 = f32[1,9,2,128,128]{4,3,1,2,0:T(8,128)} copy(f32[1,9,2,128,128]{4,3,2,1,0:T(8,128)S(1)} %copy-done.1) | data formatting | bytes 2359296 | tf_op args[3]
  37.7 1.5 %collective-permute-done.2 = f32[3,128,128]{2,1,0:T(8,128)S(1)} collective-permute-done((f32[3,128,128]{2,1,0:T(8,128)S(1)}, f32[3,128,128]{2,1,0:T(8,128)S(1)}, u32[]{:S(2)}, u32[]{:S(2)}) %collective-permute-start.2) | collective-permute-done | bytes 196640 | tf_op jit(solution)/shard_map/ppermute | solution.py:19
  39.2 4.3 %collective-permute-done.3 = f32[3,128,128]{2,1,0:T(8,128)S(1)} collective-permute-done((f32[3,128,128]{2,1,0:T(8,128)S(1)}, f32[3,128,128]{2,1,0:T(8,128)S(1)}, u32[]{:S(2)}, u32[]{:S(2)}) %collective-permute-start.3) | collective-permute-done | bytes 196640 | tf_op jit(solution)/shard_map/ppermute | solution.py:19
  43.5 1.1 %fusion.11 = f32[2,128,128,1]{2,1,3,0:T(8,128)S(1)} fusion(f32[3,1,128,128]{3,2,0,1:T(8,128)S(1)} %bitcast.199, f32[3,1,128,128]{3,2,0,1:T(8,128)S(1)} %get-tuple-element.16, f32[3,2,128,128]{3,2,0,1:T(8,128)S(1)} %slice.145, f32[3,1,128,128]{3,2,0,1:T(8,128)S(1)} %get-tuple-element.17, f32[3,1,128,128]{3,2,0,1:T(8,128)S(1)} %bitcast.197, ...), kind=kOutput, calls=%fused_computation.20 | convolution fusion | flops 228261888 | bytes 2490368 | tf_op jit(solution)/shard_map/wkab,wkbc->kac/dot_general | solution.py:29
  44.6 0.7 fusion.68
  45.3 0.6 convolution_bitcast_fusion.1
  46.0 0.1 fusion.52
  46.1 0.7 broadcast_in_dim.17
  46.8 11.1 %all-to-all-start.1 = ((f32[32,3,128]{2,1,0:T(4,128)}), f32[32,3,128]{2,1,0:T(4,128)}, u32[]{:S(2)}, u32[]{:S(2)}) async-start(f32[32,3,128]{2,1,0:T(4,128)} %broadcast_in_dim.17), calls=%async_computation.1 | async-start | bytes 131072 | tf_op jit(solution)/shard_map/all_to_all | solution.py:25
  57.9 0.0 copy-start.2
  57.9 0.8 fusion.88
  58.7 1.9 %convolution_bitcast_fusion.6 = f32[3,128,128]{2,1,0:T(8,128)} fusion(f32[9,2,128,128]{3,2,0,1:T(8,128)} %bitcast.187, f32[2,128,128]{2,1,0:T(8,128)} %get-tuple-element.28), kind=kOutput, calls=%fused_computation.53 | convolution fusion | flops 37748736 | bytes 458752 | tf_op jit(solution)/shard_map/ab,wbc->wac/dot_general | solution.py:29
  60.6 1.8 %convolution_bitcast_fusion.7 = f32[3,128,128]{2,1,0:T(8,128)} fusion(f32[9,2,128,128]{3,2,0,1:T(8,128)} %bitcast.188, f32[2,128,128]{2,1,0:T(8,128)S(1)} %copy-done.2), kind=kOutput, calls=%fused_computation.54 | convolution fusion | flops 37748736 | bytes 458752 | tf_op jit(solution)/shard_map/ab,wbc->wac/dot_general | solution.py:29
  62.4 0.8 slice.151
  63.2 3.6 %collective-permute-start.4 = (f32[3,128,128]{2,1,0:T(8,128)}, f32[3,128,128]{2,1,0:T(8,128)S(1)}, u32[]{:S(2)}, u32[]{:S(2)}) collective-permute-start(f32[3,128,128]{2,1,0:T(8,128)} %convolution_bitcast_fusion.7), channel_id=1, source_target_pairs={{0,1},{1,2},{2,3},{3,4},{4,5},{5,6},{6,7},{7,8},{8,9},{9,10},{10,1... | collective-permute-start | bytes 589832 | tf_op jit(solution)/shard_map/ppermute | solution.py:19
  66.8 1.5 %collective-permute-start.5 = (f32[3,128,128]{2,1,0:T(8,128)}, f32[3,128,128]{2,1,0:T(8,128)S(1)}, u32[]{:S(2)}, u32[]{:S(2)}) collective-permute-start(f32[3,128,128]{2,1,0:T(8,128)} %convolution_bitcast_fusion.6), channel_id=1, source_target_pairs={{1,0},{2,1},{3,2},{4,3},{5,4},{6,5},{7,6},{8,7},{9,8},{10,9},{11,1... | collective-permute-start | bytes 589832 | tf_op jit(solution)/shard_map/ppermute | solution.py:19
  68.3 0.0 all-to-all-done.1
  68.3 0.9 reduce_sum.37
  69.3 1.1 collective-permute-done.4
  70.3 4.3 %collective-permute-done.5 = f32[3,128,128]{2,1,0:T(8,128)S(1)} collective-permute-done((f32[3,128,128]{2,1,0:T(8,128)}, f32[3,128,128]{2,1,0:T(8,128)S(1)}, u32[]{:S(2)}, u32[]{:S(2)}) %collective-permute-start.5) | collective-permute-done | bytes 196640 | tf_op jit(solution)/shard_map/ppermute | solution.py:19
  74.6 2.6 %fusion.43 = f32[2,128,128]{2,1,0:T(8,128)S(1)} fusion(f32[3,1,128,128]{3,2,0,1:T(8,128)S(1)} %bitcast.195, f32[3,1,128,128]{3,2,0,1:T(8,128)} %get-tuple-element.13, f32[3,2,128,128]{3,2,0,1:T(8,128)} %slice.151, f32[3,1,128,128]{3,2,0,1:T(8,128)} %get-tuple-element.12, f32[3,1,128,128]{3,2,0,1:T(8,128)S(1)} %bitcast.194, ...), kind=kOutput, calls=%fused_computation.56 | convolution fusion | flops 228589568 | bytes 2491392 | tf_op jit(solution)/shard_map/wkab,wkbc->kac/dot_general | solution.py:29
  77.2 0.6 convolution_bitcast_fusion
  77.8 0.0 copy-start.14
  77.9 0.1 slice_bitcast_fusion.1
  77.9 3.5 %collective-permute-start.6 = (f32[3,128,128]{2,1,0:T(8,128)S(1)}, f32[3,128,128]{2,1,0:T(8,128)S(1)}, u32[]{:S(2)}, u32[]{:S(2)}) collective-permute-start(f32[3,128,128]{2,1,0:T(8,128)S(1)} %get-tuple-element.8), channel_id=1, source_target_pairs={{0,1},{1,2},{2,3},{3,4},{4,5},{5,6},{6,7},{7,8},{8,9},{9,10},{10,1... | collective-permute-start | bytes 589832 | tf_op jit(solution)/shard_map/ppermute | solution.py:19
  81.5 1.3 %collective-permute-start.7 = (f32[3,128,128]{2,1,0:T(8,128)S(1)}, f32[3,128,128]{2,1,0:T(8,128)S(1)}, u32[]{:S(2)}, u32[]{:S(2)}) collective-permute-start(f32[3,128,128]{2,1,0:T(8,128)S(1)} %get-tuple-element.9), channel_id=1, source_target_pairs={{1,0},{2,1},{3,2},{4,3},{5,4},{6,5},{7,6},{8,7},{9,8},{10,9},{11,1... | collective-permute-start | bytes 589832 | tf_op jit(solution)/shard_map/ppermute | solution.py:19
  82.8 0.1 compare_convert_fusion
  82.9 1.7 %collective-permute-done.6 = f32[3,128,128]{2,1,0:T(8,128)S(1)} collective-permute-done((f32[3,128,128]{2,1,0:T(8,128)S(1)}, f32[3,128,128]{2,1,0:T(8,128)S(1)}, u32[]{:S(2)}, u32[]{:S(2)}) %collective-permute-start.6) | collective-permute-done | bytes 196640 | tf_op jit(solution)/shard_map/ppermute | solution.py:19
  84.6 4.5 %collective-permute-done.7 = f32[3,128,128]{2,1,0:T(8,128)S(1)} collective-permute-done((f32[3,128,128]{2,1,0:T(8,128)S(1)}, f32[3,128,128]{2,1,0:T(8,128)S(1)}, u32[]{:S(2)}, u32[]{:S(2)}) %collective-permute-start.7) | collective-permute-done | bytes 196640 | tf_op jit(solution)/shard_map/ppermute | solution.py:19
  89.1 1.2 %fusion.30 = f32[2,128,128,1]{2,1,3,0:T(8,128)S(1)} fusion(f32[3,1,128,128]{3,2,0,1:T(8,128)S(1)} %bitcast.198, f32[3,1,128,128]{3,2,0,1:T(8,128)S(1)} %get-tuple-element.10, f32[3,2,128,128]{3,2,0,1:T(8,128)S(1)} %slice.160, f32[3,1,128,128]{3,2,0,1:T(8,128)S(1)} %get-tuple-element.11, f32[3,1,128,128]{3,2,0,1:T(8,128)S(1)} %bitcast.196, ...), kind=kOutput, calls=%fused_computation.40 | convolution fusion | flops 228261888 | bytes 2490368 | tf_op jit(solution)/shard_map/wkab,wkbc->kac/dot_general | solution.py:29
  90.3 0.7 fusion.66
  91.0 0.1 fusion.53
  91.1 0.7 broadcast_in_dim.18
  91.9 9.4 %all-to-all-start.2 = ((f32[32,3,128]{2,1,0:T(4,128)}), f32[32,3,128]{2,1,0:T(4,128)S(1)}, u32[]{:S(2)}, u32[]{:S(2)}) async-start(f32[32,3,128]{2,1,0:T(4,128)} %broadcast_in_dim.18), calls=%async_computation.2 | async-start | bytes 131072 | tf_op jit(solution)/shard_map/all_to_all | solution.py:25
  102.0 0.3 fusion.69
  102.3 9.0 %all-to-all-done.2 = f32[32,3,128]{2,1,0:T(4,128)S(1)} async-done(((f32[32,3,128]{2,1,0:T(4,128)}), f32[32,3,128]{2,1,0:T(4,128)S(1)}, u32[]{:S(2)}, u32[]{:S(2)}) %all-to-all-start.2) | async-done | bytes 49184 | tf_op jit(solution)/shard_map/all_to_all | solution.py:25
  111.4 0.7 fusion.67
  (33 shorter events, 0.2 us)
Async XLA Ops:
  0.6 24.8 %copy-start = (f32[9,2,128,128]{3,2,1,0:T(8,128)S(1)}, f32[9,2,128,128]{3,2,1,0:T(8,128)}, u32[]{:S(2)}) copy-start(f32[9,2,128,128]{3,2,1,0:T(8,128)} %param.7) | copy-start | bytes 3538948
  2.7 5.8 %copy-start.1 = (f32[1,9,2,128,128]{4,3,2,1,0:T(8,128)S(1)}, f32[1,9,2,128,128]{4,3,2,1,0:T(8,128)}, u32[]{:S(2)}) copy-start(f32[1,9,2,128,128]{4,3,2,1,0:T(8,128)} %param.9) | copy-start | bytes 3538948
  2.7 5.8 %copy-start.12 = (f32[1,2,128,128]{3,2,1,0:T(8,128)S(1)}, f32[1,2,128,128]{3,2,1,0:T(8,128)}, u32[]{:S(2)}) copy-start(f32[1,2,128,128]{3,2,1,0:T(8,128)} %param.6) | copy-start | bytes 393220
  2.8 20.3 %all-to-all-start = ((f32[8,2,128,128]{3,2,1,0:T(8,128)}), f32[8,2,128,128]{3,2,1,0:T(8,128)S(1)}, u32[]{:S(2)}, u32[]{:S(2)}) async-start(f32[8,2,128,128]{3,2,1,0:T(8,128)} %broadcast_in_dim.15), calls=%async_computation | async-start | bytes 2097152 | tf_op jit(solution)/shard_map/all_to_all | solution.py:36
  9.6 6.8 %copy-start.13 = (s32[9,2]{0,1:T(2,128)S(1)}, s32[9,2]{0,1:T(2,128)}, u32[]{:S(2)}) copy-start(s32[9,2]{0,1:T(2,128)} %param.10) | copy-start | bytes 220
  10.5 17.4 %collective-permute-start = (f32[3,128,128]{1,2,0:T(8,128)}, f32[3,128,128]{1,2,0:T(8,128)}, u32[]{:S(2)}, u32[]{:S(2)}) collective-permute-start(f32[3,128,128]{1,2,0:T(8,128)} %get-tuple-element.21), channel_id=1, source_target_pairs={{0,1},{1,2},{2,3},{3,4},{4,5},{5,6},{6,7},{7,8},{8,9},{9,10},{10,1... | collective-permute-start | bytes 589832 | tf_op jit(solution)/shard_map/ppermute | solution.py:19
  14.3 13.7 %collective-permute-start.1 = (f32[3,128,128]{1,2,0:T(8,128)}, f32[3,128,128]{1,2,0:T(8,128)}, u32[]{:S(2)}, u32[]{:S(2)}) collective-permute-start(f32[3,128,128]{1,2,0:T(8,128)} %get-tuple-element.22), channel_id=1, source_target_pairs={{1,0},{2,1},{3,2},{4,3},{5,4},{6,5},{7,6},{8,7},{9,8},{10,9},{11,1... | collective-permute-start | bytes 589832 | tf_op jit(solution)/shard_map/ppermute | solution.py:19
  27.8 1.0 copy-start.9
  27.8 1.2 %copy-start.10 = (f32[3,1,128,128]{2,3,0,1:T(8,128)S(1)}, f32[3,1,128,128]{2,3,0,1:T(8,128)}, u32[]{:S(2)}) copy-start(f32[3,1,128,128]{2,3,0,1:T(8,128)} %get-tuple-element.23) | copy-start | bytes 589828
  27.8 1.5 %copy-start.11 = (f32[3,1,128,128]{2,3,0,1:T(8,128)S(1)}, f32[3,1,128,128]{2,3,0,1:T(8,128)}, u32[]{:S(2)}) copy-start(f32[3,1,128,128]{2,3,0,1:T(8,128)} %get-tuple-element.24) | copy-start | bytes 589828
  27.9 15.6 %copy-start.3 = (f32[3,2,128,128]{2,3,0,1:T(8,128)}, f32[3,2,128,128]{2,3,0,1:T(8,128)S(1)}, u32[]{:S(2)}) copy-start(f32[3,2,128,128]{2,3,0,1:T(8,128)S(1)} %get-tuple-element.18) | copy-start | bytes 1179652
  27.9 15.5 %copy-start.5 = (f32[3,2,128,128]{2,3,0,1:T(8,128)}, f32[3,2,128,128]{2,3,0,1:T(8,128)S(1)}, u32[]{:S(2)}) copy-start(f32[3,2,128,128]{2,3,0,1:T(8,128)S(1)} %get-tuple-element.19) | copy-start | bytes 1179652
  27.9 15.5 %copy-start.7 = (f32[3,2,128,128]{2,3,0,1:T(8,128)}, f32[3,2,128,128]{2,3,0,1:T(8,128)S(1)}, u32[]{:S(2)}) copy-start(f32[3,2,128,128]{2,3,0,1:T(8,128)S(1)} %get-tuple-element.20) | copy-start | bytes 1179652
  32.2 7.0 %collective-permute-start.2 = (f32[3,128,128]{2,1,0:T(8,128)S(1)}, f32[3,128,128]{2,1,0:T(8,128)S(1)}, u32[]{:S(2)}, u32[]{:S(2)}) collective-permute-start(f32[3,128,128]{2,1,0:T(8,128)S(1)} %get-tuple-element.14), channel_id=1, source_target_pairs={{0,1},{1,2},{2,3},{3,4},{4,5},{5,6},{6,7},{7,8},{8,9},{9,10},{10,1... | collective-permute-start | bytes 589832 | tf_op jit(solution)/shard_map/ppermute | solution.py:19
  35.2 8.2 %collective-permute-start.3 = (f32[3,128,128]{2,1,0:T(8,128)S(1)}, f32[3,128,128]{2,1,0:T(8,128)S(1)}, u32[]{:S(2)}, u32[]{:S(2)}) collective-permute-start(f32[3,128,128]{2,1,0:T(8,128)S(1)} %get-tuple-element.15), channel_id=1, source_target_pairs={{1,0},{2,1},{3,2},{4,3},{5,4},{6,5},{7,6},{8,7},{9,8},{10,9},{11,1... | collective-permute-start | bytes 589832 | tf_op jit(solution)/shard_map/ppermute | solution.py:19
  46.8 21.5 %all-to-all-start.1 = ((f32[32,3,128]{2,1,0:T(4,128)}), f32[32,3,128]{2,1,0:T(4,128)}, u32[]{:S(2)}, u32[]{:S(2)}) async-start(f32[32,3,128]{2,1,0:T(4,128)} %broadcast_in_dim.17), calls=%async_computation.1 | async-start | bytes 131072 | tf_op jit(solution)/shard_map/all_to_all | solution.py:25
  57.9 2.7 %copy-start.2 = (f32[2,128,128]{2,1,0:T(8,128)S(1)}, f32[2,128,128]{2,1,0:T(8,128)}, u32[]{:S(2)}) copy-start(f32[2,128,128]{2,1,0:T(8,128)} %get-tuple-element.28) | copy-start | bytes 393220
  63.2 7.1 %collective-permute-start.4 = (f32[3,128,128]{2,1,0:T(8,128)}, f32[3,128,128]{2,1,0:T(8,128)S(1)}, u32[]{:S(2)}, u32[]{:S(2)}) collective-permute-start(f32[3,128,128]{2,1,0:T(8,128)} %convolution_bitcast_fusion.7), channel_id=1, source_target_pairs={{0,1},{1,2},{2,3},{3,4},{4,5},{5,6},{6,7},{7,8},{8,9},{9,10},{10,1... | collective-permute-start | bytes 589832 | tf_op jit(solution)/shard_map/ppermute | solution.py:19
  66.8 7.8 %collective-permute-start.5 = (f32[3,128,128]{2,1,0:T(8,128)}, f32[3,128,128]{2,1,0:T(8,128)S(1)}, u32[]{:S(2)}, u32[]{:S(2)}) collective-permute-start(f32[3,128,128]{2,1,0:T(8,128)} %convolution_bitcast_fusion.6), channel_id=1, source_target_pairs={{1,0},{2,1},{3,2},{4,3},{5,4},{6,5},{7,6},{8,7},{9,8},{10,9},{11,1... | collective-permute-start | bytes 589832 | tf_op jit(solution)/shard_map/ppermute | solution.py:19
  77.8 4.9 %copy-start.14 = (s32[1,2]{1,0:T(1,128)S(1)}, s32[1,2]{1,0:T(1,128)}, u32[]{:S(2)}) copy-start(s32[1,2]{1,0:T(1,128)} %param.11) | copy-start | bytes 28
  77.9 11.3 %copy-start.4 = (f32[3,2,128,128]{2,3,0,1:T(8,128)S(1)}, f32[3,2,128,128]{2,3,0,1:T(8,128)}, u32[]{:S(2)}) copy-start(f32[3,2,128,128]{2,3,0,1:T(8,128)} %copy-done.3) | copy-start | bytes 1179652
  77.9 11.3 %copy-start.6 = (f32[3,2,128,128]{2,3,0,1:T(8,128)S(1)}, f32[3,2,128,128]{2,3,0,1:T(8,128)}, u32[]{:S(2)}) copy-start(f32[3,2,128,128]{2,3,0,1:T(8,128)} %copy-done.5) | copy-start | bytes 1179652
  77.9 11.3 %copy-start.8 = (f32[3,2,128,128]{2,3,0,1:T(8,128)S(1)}, f32[3,2,128,128]{2,3,0,1:T(8,128)}, u32[]{:S(2)}) copy-start(f32[3,2,128,128]{2,3,0,1:T(8,128)} %copy-done.7) | copy-start | bytes 1179652
  77.9 6.7 %collective-permute-start.6 = (f32[3,128,128]{2,1,0:T(8,128)S(1)}, f32[3,128,128]{2,1,0:T(8,128)S(1)}, u32[]{:S(2)}, u32[]{:S(2)}) collective-permute-start(f32[3,128,128]{2,1,0:T(8,128)S(1)} %get-tuple-element.8), channel_id=1, source_target_pairs={{0,1},{1,2},{2,3},{3,4},{4,5},{5,6},{6,7},{7,8},{8,9},{9,10},{10,1... | collective-permute-start | bytes 589832 | tf_op jit(solution)/shard_map/ppermute | solution.py:19
  81.5 7.7 %collective-permute-start.7 = (f32[3,128,128]{2,1,0:T(8,128)S(1)}, f32[3,128,128]{2,1,0:T(8,128)S(1)}, u32[]{:S(2)}, u32[]{:S(2)}) collective-permute-start(f32[3,128,128]{2,1,0:T(8,128)S(1)} %get-tuple-element.9), channel_id=1, source_target_pairs={{1,0},{2,1},{3,2},{4,3},{5,4},{6,5},{7,6},{8,7},{9,8},{10,9},{11,1... | collective-permute-start | bytes 589832 | tf_op jit(solution)/shard_map/ppermute | solution.py:19
  91.9 19.4 %all-to-all-start.2 = ((f32[32,3,128]{2,1,0:T(4,128)}), f32[32,3,128]{2,1,0:T(4,128)S(1)}, u32[]{:S(2)}, u32[]{:S(2)}) async-start(f32[32,3,128]{2,1,0:T(4,128)} %broadcast_in_dim.18), calls=%async_computation.2 | async-start | bytes 131072 | tf_op jit(solution)/shard_map/all_to_all | solution.py:25

commit v11 on v9

--- a/solution.py
+++ b/solution.py
@@ -39,8 +39,8 @@
     for step in range(segments - 1):
         grown = mm("kab,kbc->kac", prefix, every[step], EXACT)
         prefix = jnp.where(step < segment, grown, prefix)
-    right_side = mm("wkbc,kcd->wkbd", left_env, prefix, EXACT)
-    return mm("kba,wkbd->wkad", prefix, right_side, EXACT)
+    right_side = mm("wkbc,kcd->wkbd", left_env, prefix)
+    return mm("kba,wkbd->wkad", prefix, right_side)
 
 
 def exchange(vector, right):
@@ -50,13 +50,11 @@
     return products, from_left, from_right
 
 
-def combine(parts, ordered, factor=None):
+def combine(parts, ordered):
     products, from_left, from_right = parts
     lower = jnp.stack([from_left, products[0::3, 0]], axis=1)
     upper = jnp.stack([products[2::3, 1], from_right], axis=1)
     terms = jnp.concatenate([lower, products[1::3], upper], axis=0)
-    if factor is not None:
-        terms = terms * factor
     return mm("wkab,wkbc->kac", ordered, terms)
 
 
@@ -102,7 +100,7 @@
             gram, peak = lax.optimization_barrier((mm("kab,kcb->kac", unit, unit), peak))
         first, second = scales(gathered_sums(square_sums(current, lifted), "sec"), cells)
         if more:
-            current = combine(parts, ordered, first / LIFT) * (second / LIFT)
+            current = combine(parts, ordered * (first / LIFT)) * (second / LIFT)
         else:
             factor = (first / LIFT) * second
             current = lifted * factor

time: 106 us -> 105 us (level)
  transfers between devices with their start and end apart: 11 -> 11, of which waited for: 8 -> 8; matrix products, arithmetic and copies ran while one was open for 9% -> 8% of each run, Pallas kernels for 0% -> 0%
where the time goes in v11:
time: 105 us; the launch traced here: 104 us
  starting transfers between devices  44.6 us (42%)
  waiting for transfers between devices  35.9 us (34%)
  matrix products  12.3 us (12%)
  local copies, waits for them, and re-layouts  7.17 us (7%)
  other arithmetic  2.78 us (3%)
  between operations  1.68 us (2%)
    all_to_all x2, starting transfers between devices, gathered_sums(): return jnp.sum(lax.all_to_all(spread, axis, 0, 0, tiled=True), axis=0)  20.5 us
    ppermute x8, starting transfers between devices, shifted(): return lax.ppermute(block, axis, route)  18.3 us
    ppermute x8, waiting for transfers between devices, shifted(): return lax.ppermute(block, axis, route)  15.3 us
    all_to_all x2, waiting for transfers between devices, gathered_sums(): return jnp.sum(lax.all_to_all(spread, axis, 0, 0, tiled=True), axis=0)  12.4 us
    dot_general x18, matrix products, mm(): return jnp.einsum(spec, a, b, precision=precision)  12.3 us
    all_to_all x1, waiting for transfers between devices, left_environment(): every = lax.all_to_all(spread, 'seg', 0, 0, tiled=True)  8.13 us
    all_to_all x1, starting transfers between devices, left_environment(): every = lax.all_to_all(spread, 'seg', 0, 0, tiled=True)  5.78 us
  transfers between devices with their start and end apart: 11, of which 8 were waited for; matrix products, arithmetic and copies ran while one was open for 8% of the time, Pallas kernels for 0%

profile of v11, /device:TPU:8, one launch (start us, length us, event | category | flops | bytes accessed | tf_op | source)
XLA Modules:
  0.0 104.4 jit_solution(1400225359766987156)
XLA Ops:
  0.6 0.0 copy-start
  0.6 2.1 %broadcast_in_dim.18 = f32[8,2,128,128]{3,2,1,0:T(8,128)} broadcast(f32[2,128,128]{2,1,0:T(8,128)} %bitcast.197), dimensions={1,2,3} | broadcast | bytes 1179648 | tf_op jit(solution)/shard_map/broadcast_in_dim | solution.py:35
  2.7 5.8 %all-to-all-start = ((f32[8,2,128,128]{3,2,1,0:T(8,128)}), f32[8,2,128,128]{3,2,1,0:T(8,128)S(1)}, u32[]{:S(2)}, u32[]{:S(2)}) async-start(f32[8,2,128,128]{3,2,1,0:T(8,128)} %broadcast_in_dim.18), calls=%async_computation | async-start | bytes 2097152 | tf_op jit(solution)/shard_map/all_to_all | solution.py:36
  8.5 0.0 copy-done
  8.5 0.0 copy-done.3
  8.5 1.1 %convolution_bitcast_fusion.3 = f32[9,2,128,128]{2,3,0,1:T(8,128)S(1)} fusion(f32[1,2,128,128]{3,2,1,0:T(8,128)S(1)} %copy-done.3, f32[1,9,2,128,128]{4,3,2,1,0:T(8,128)S(1)} %copy-done), kind=kOutput, calls=%fused_computation.3 | convolution fusion | flops 226492416 | bytes 2490368 | tf_op jit(solution)/shard_map/kab,wkbc->wkac/dot_general | solution.py:29
  9.6 0.0 copy-start.4
  9.6 0.1 slice_bitcast_fusion.7
  9.7 3.1 %collective-permute-start = (f32[3,128,128]{1,2,0:T(8,128)S(1)}, f32[3,128,128]{1,2,0:T(8,128)S(1)}, u32[]{:S(2)}, u32[]{:S(2)}) collective-permute-start(f32[3,128,128]{1,2,0:T(8,128)S(1)} %get-tuple-element.23), channel_id=1, source_target_pairs={{0,1},{1,2},{2,3},{3,4},{4,5},{5,6},{6,7},{7,8},{8,9},{9,10},{10,1... | collective-permute-start | bytes 589832 | tf_op jit(solution)/shard_map/ppermute | solution.py:19
  12.8 1.3 %collective-permute-start.1 = (f32[3,128,128]{1,2,0:T(8,128)S(1)}, f32[3,128,128]{1,2,0:T(8,128)S(1)}, u32[]{:S(2)}, u32[]{:S(2)}) collective-permute-start(f32[3,128,128]{1,2,0:T(8,128)S(1)} %get-tuple-element.24), channel_id=1, source_target_pairs={{1,0},{2,1},{3,2},{4,3},{5,4},{6,5},{7,6},{8,7},{9,8},{10,9},{11,1... | collective-permute-start | bytes 589832 | tf_op jit(solution)/shard_map/ppermute | solution.py:19
  14.1 0.8 slice.122
  14.9 0.0 copy-done.4
  14.9 8.1 %all-to-all-done = f32[8,2,128,128]{3,2,1,0:T(8,128)S(1)} async-done(((f32[8,2,128,128]{3,2,1,0:T(8,128)}), f32[8,2,128,128]{3,2,1,0:T(8,128)S(1)}, u32[]{:S(2)}, u32[]{:S(2)}) %all-to-all-start) | async-done | bytes 1048608 | tf_op jit(solution)/shard_map/all_to_all | solution.py:36
  23.0 0.3 convolution_select_fusion.6
  23.3 0.0 copy-start.1
  23.3 0.3 convolution_select_fusion.5
  23.6 0.3 convolution_select_fusion.4
  23.9 0.3 convolution_select_fusion.3
  24.2 0.3 convolution_select_fusion.2
  24.4 0.3 convolution_select_fusion.1
  24.7 0.3 fusion.48
  25.0 0.7 convolution_bitcast_fusion.5
  25.7 0.6 fusion
  26.4 0.1 fusion.87
  26.5 0.0 collective-permute-done
  26.5 0.0 collective-permute-done.1
  26.5 0.9 copy-done.2
  27.3 1.2 %fusion.1 = f32[2,128,128,1]{2,1,3,0:T(8,128)S(1)} fusion(f32[3,1,128,128]{2,3,0,1:T(8,128)S(1)} %bitcast.199, f32[3,1,128,128]{2,3,0,1:T(8,128)S(1)} %get-tuple-element.25, f32[3,2,128,128]{2,3,0,1:T(8,128)S(1)} %copy-done.2, f32[3,1,128,128]{2,3,0,1:T(8,128)S(1)} %get-tuple-element.26, f32[3,1,128,128]{2,3,0,1:T(8,128)S(1)} %bitcast.198, ...), kind=kOutput, calls=%fused_computation.8 | convolution fusion | flops 228261888 | bytes 2490368 | tf_op jit(solution)/shard_map/wkab,wkbc->kac/dot_general | solution.py:29
  28.5 0.6 convolution_bitcast_fusion.2
  29.1 0.1 slice_bitcast_fusion.5
  29.2 3.1 %collective-permute-start.2 = (f32[3,128,128]{2,1,0:T(8,128)S(1)}, f32[3,128,128]{2,1,0:T(8,128)S(1)}, u32[]{:S(2)}, u32[]{:S(2)}) collective-permute-start(f32[3,128,128]{2,1,0:T(8,128)S(1)} %get-tuple-element.16), channel_id=1, source_target_pairs={{0,1},{1,2},{2,3},{3,4},{4,5},{5,6},{6,7},{7,8},{8,9},{9,10},{10,1... | collective-permute-start | bytes 589832 | tf_op jit(solution)/shard_map/ppermute | solution.py:19
  32.3 1.3 %collective-permute-start.3 = (f32[3,128,128]{2,1,0:T(8,128)S(1)}, f32[3,128,128]{2,1,0:T(8,128)S(1)}, u32[]{:S(2)}, u32[]{:S(2)}) collective-permute-start(f32[3,128,128]{2,1,0:T(8,128)S(1)} %get-tuple-element.17), channel_id=1, source_target_pairs={{1,0},{2,1},{3,2},{4,3},{5,4},{6,5},{7,6},{8,7},{9,8},{10,9},{11,1... | collective-permute-start | bytes 589832 | tf_op jit(solution)/shard_map/ppermute | solution.py:19
  33.6 2.6 %collective-permute-done.2 = f32[3,128,128]{2,1,0:T(8,128)S(1)} collective-permute-done((f32[3,128,128]{2,1,0:T(8,128)S(1)}, f32[3,128,128]{2,1,0:T(8,128)S(1)}, u32[]{:S(2)}, u32[]{:S(2)}) %collective-permute-start.2) | collective-permute-done | bytes 196640 | tf_op jit(solution)/shard_map/ppermute | solution.py:19
  36.2 4.3 %collective-permute-done.3 = f32[3,128,128]{2,1,0:T(8,128)S(1)} collective-permute-done((f32[3,128,128]{2,1,0:T(8,128)S(1)}, f32[3,128,128]{2,1,0:T(8,128)S(1)}, u32[]{:S(2)}, u32[]{:S(2)}) %collective-permute-start.3) | collective-permute-done | bytes 196640 | tf_op jit(solution)/shard_map/ppermute | solution.py:19
  40.5 1.1 %fusion.11 = f32[2,128,128,1]{2,1,3,0:T(8,128)S(1)} fusion(f32[3,1,128,128]{3,2,0,1:T(8,128)S(1)} %bitcast.205, f32[3,1,128,128]{3,2,0,1:T(8,128)S(1)} %get-tuple-element.18, f32[3,2,128,128]{3,2,0,1:T(8,128)S(1)} %slice.127, f32[3,1,128,128]{3,2,0,1:T(8,128)S(1)} %get-tuple-element.19, f32[3,1,128,128]{3,2,0,1:T(8,128)S(1)} %bitcast.204, ...), kind=kOutput, calls=%fused_computation.18 | convolution fusion | flops 228261888 | bytes 2490368 | tf_op jit(solution)/shard_map/wkab,wkbc->kac/dot_general | solution.py:29
  41.7 0.6 convolution_bitcast_fusion.1
  42.3 0.1 fusion.59
  42.5 0.7 broadcast_in_dim.19
  43.2 11.1 %all-to-all-start.1 = ((f32[32,3,128]{2,1,0:T(4,128)}), f32[32,3,128]{2,1,0:T(4,128)}, u32[]{:S(2)}, u32[]{:S(2)}) async-start(f32[32,3,128]{2,1,0:T(4,128)} %broadcast_in_dim.19), calls=%async_computation.1 | async-start | bytes 131072 | tf_op jit(solution)/shard_map/all_to_all | solution.py:25
  54.3 0.9 slice_bitcast_fusion.3
  55.2 0.8 slice.133
  56.0 3.6 %collective-permute-start.4 = (f32[3,128,128]{2,1,0:T(8,128)}, f32[3,128,128]{2,1,0:T(8,128)S(1)}, u32[]{:S(2)}, u32[]{:S(2)}) collective-permute-start(f32[3,128,128]{2,1,0:T(8,128)} %get-tuple-element.12), channel_id=1, source_target_pairs={{0,1},{1,2},{2,3},{3,4},{4,5},{5,6},{6,7},{7,8},{8,9},{9,10},{10,1... | collective-permute-start | bytes 589832 | tf_op jit(solution)/shard_map/ppermute | solution.py:19
  59.6 1.3 %collective-permute-start.5 = (f32[3,128,128]{2,1,0:T(8,128)}, f32[3,128,128]{2,1,0:T(8,128)S(1)}, u32[]{:S(2)}, u32[]{:S(2)}) collective-permute-start(f32[3,128,128]{2,1,0:T(8,128)} %get-tuple-element.13), channel_id=1, source_target_pairs={{1,0},{2,1},{3,2},{4,3},{5,4},{6,5},{7,6},{8,7},{9,8},{10,9},{11,1... | collective-permute-start | bytes 589832 | tf_op jit(solution)/shard_map/ppermute | solution.py:19
  60.9 3.4 %all-to-all-done.1 = f32[32,3,128]{2,1,0:T(4,128)} async-done(((f32[32,3,128]{2,1,0:T(4,128)}), f32[32,3,128]{2,1,0:T(4,128)}, u32[]{:S(2)}, u32[]{:S(2)}) %all-to-all-start.1) | async-done | bytes 49184 | tf_op jit(solution)/shard_map/all_to_all | solution.py:25
  64.3 0.9 reduce_sum.37
  65.2 0.0 collective-permute-done.4
  65.2 2.2 %collective-permute-done.5 = f32[3,128,128]{2,1,0:T(8,128)S(1)} collective-permute-done((f32[3,128,128]{2,1,0:T(8,128)}, f32[3,128,128]{2,1,0:T(8,128)S(1)}, u32[]{:S(2)}, u32[]{:S(2)}) %collective-permute-start.5) | collective-permute-done | bytes 196640 | tf_op jit(solution)/shard_map/ppermute | solution.py:19
  67.4 2.3 %fusion.49 = f32[2,128,128]{2,1,0:T(8,128)S(1)} fusion(f32[3,1,128,128]{3,2,0,1:T(8,128)S(1)} %bitcast.201, f32[3,1,128,128]{3,2,0,1:T(8,128)} %get-tuple-element.14, f32[3,2,128,128]{3,2,0,1:T(8,128)} %slice.133, f32[3,1,128,128]{3,2,0,1:T(8,128)} %get-tuple-element.15, f32[3,1,128,128]{3,2,0,1:T(8,128)S(1)} %bitcast.200, ...), kind=kOutput, calls=%fused_computation.59 | convolution fusion | flops 228589568 | bytes 2491392 | tf_op jit(solution)/shard_map/wkab,wkbc->kac/dot_general | solution.py:29
  69.7 0.6 convolution_bitcast_fusion
  70.4 0.0 copy-start.5
  70.4 0.1 slice_bitcast_fusion.1
  70.4 3.4 %collective-permute-start.6 = (f32[3,128,128]{2,1,0:T(8,128)S(1)}, f32[3,128,128]{2,1,0:T(8,128)S(1)}, u32[]{:S(2)}, u32[]{:S(2)}) collective-permute-start(f32[3,128,128]{2,1,0:T(8,128)S(1)} %get-tuple-element.8), channel_id=1, source_target_pairs={{0,1},{1,2},{2,3},{3,4},{4,5},{5,6},{6,7},{7,8},{8,9},{9,10},{10,1... | collective-permute-start | bytes 589832 | tf_op jit(solution)/shard_map/ppermute | solution.py:19
  73.8 1.3 %collective-permute-start.7 = (f32[3,128,128]{2,1,0:T(8,128)S(1)}, f32[3,128,128]{2,1,0:T(8,128)S(1)}, u32[]{:S(2)}, u32[]{:S(2)}) collective-permute-start(f32[3,128,128]{2,1,0:T(8,128)S(1)} %get-tuple-element.9), channel_id=1, source_target_pairs={{1,0},{2,1},{3,2},{4,3},{5,4},{6,5},{7,6},{8,7},{9,8},{10,9},{11,1... | collective-permute-start | bytes 589832 | tf_op jit(solution)/shard_map/ppermute | solution.py:19
  75.1 0.1 compare_convert_fusion
  75.2 1.7 %collective-permute-done.6 = f32[3,128,128]{2,1,0:T(8,128)S(1)} collective-permute-done((f32[3,128,128]{2,1,0:T(8,128)S(1)}, f32[3,128,128]{2,1,0:T(8,128)S(1)}, u32[]{:S(2)}, u32[]{:S(2)}) %collective-permute-start.6) | collective-permute-done | bytes 196640 | tf_op jit(solution)/shard_map/ppermute | solution.py:19
  77.0 4.5 %collective-permute-done.7 = f32[3,128,128]{2,1,0:T(8,128)S(1)} collective-permute-done((f32[3,128,128]{2,1,0:T(8,128)S(1)}, f32[3,128,128]{2,1,0:T(8,128)S(1)}, u32[]{:S(2)}, u32[]{:S(2)}) %collective-permute-start.7) | collective-permute-done | bytes 196640 | tf_op jit(solution)/shard_map/ppermute | solution.py:19
  81.5 1.1 %fusion.31 = f32[2,128,128,1]{2,1,3,0:T(8,128)S(1)} fusion(f32[3,1,128,128]{3,2,0,1:T(8,128)S(1)} %bitcast.203, f32[3,1,128,128]{3,2,0,1:T(8,128)S(1)} %get-tuple-element.10, f32[3,2,128,128]{3,2,0,1:T(8,128)S(1)} %slice.140, f32[3,1,128,128]{3,2,0,1:T(8,128)S(1)} %get-tuple-element.11, f32[3,1,128,128]{3,2,0,1:T(8,128)S(1)} %bitcast.202, ...), kind=kOutput, calls=%fused_computation.38 | convolution fusion | flops 228261888 | bytes 2490368 | tf_op jit(solution)/shard_map/wkab,wkbc->kac/dot_general | solution.py:29
  82.6 0.7 fusion.65
  83.3 0.1 fusion.60
  83.5 0.7 broadcast_in_dim.40
  84.2 9.4 %all-to-all-start.2 = ((f32[32,3,128]{2,1,0:T(4,128)}), f32[32,3,128]{2,1,0:T(4,128)S(1)}, u32[]{:S(2)}, u32[]{:S(2)}) async-start(f32[32,3,128]{2,1,0:T(4,128)} %broadcast_in_dim.40), calls=%async_computation.2 | async-start | bytes 131072 | tf_op jit(solution)/shard_map/all_to_all | solution.py:25
  94.3 0.3 fusion.68
  94.6 9.0 %all-to-all-done.2 = f32[32,3,128]{2,1,0:T(4,128)S(1)} async-done(((f32[32,3,128]{2,1,0:T(4,128)}), f32[32,3,128]{2,1,0:T(4,128)S(1)}, u32[]{:S(2)}, u32[]{:S(2)}) %all-to-all-start.2) | async-done | bytes 49184 | tf_op jit(solution)/shard_map/all_to_all | solution.py:25
  103.7 0.7 fusion.66
  (13 shorter events, 0.2 us)
Async XLA Ops:
  0.6 7.9 %copy-start = (f32[1,9,2,128,128]{4,3,2,1,0:T(8,128)S(1)}, f32[1,9,2,128,128]{4,3,2,1,0:T(8,128)}, u32[]{:S(2)}) copy-start(f32[1,9,2,128,128]{4,3,2,1,0:T(8,128)} %param.9) | copy-start | bytes 3538948
  2.7 5.8 %copy-start.3 = (f32[1,2,128,128]{3,2,1,0:T(8,128)S(1)}, f32[1,2,128,128]{3,2,1,0:T(8,128)}, u32[]{:S(2)}) copy-start(f32[1,2,128,128]{3,2,1,0:T(8,128)} %param.6) | copy-start | bytes 393220
  2.7 20.3 %all-to-all-start = ((f32[8,2,128,128]{3,2,1,0:T(8,128)}), f32[8,2,128,128]{3,2,1,0:T(8,128)S(1)}, u32[]{:S(2)}, u32[]{:S(2)}) async-start(f32[8,2,128,128]{3,2,1,0:T(8,128)} %broadcast_in_dim.18), calls=%async_computation | async-start | bytes 2097152 | tf_op jit(solution)/shard_map/all_to_all | solution.py:36
  9.6 5.3 %copy-start.4 = (s32[9,2]{0,1:T(2,128)S(1)}, s32[9,2]{0,1:T(2,128)}, u32[]{:S(2)}) copy-start(s32[9,2]{0,1:T(2,128)} %param.10) | copy-start | bytes 220
  9.7 16.8 %collective-permute-start = (f32[3,128,128]{1,2,0:T(8,128)S(1)}, f32[3,128,128]{1,2,0:T(8,128)S(1)}, u32[]{:S(2)}, u32[]{:S(2)}) collective-permute-start(f32[3,128,128]{1,2,0:T(8,128)S(1)} %get-tuple-element.23), channel_id=1, source_target_pairs={{0,1},{1,2},{2,3},{3,4},{4,5},{5,6},{6,7},{7,8},{8,9},{9,10},{10,1... | collective-permute-start | bytes 589832 | tf_op jit(solution)/shard_map/ppermute | solution.py:19
  12.8 13.7 %collective-permute-start.1 = (f32[3,128,128]{1,2,0:T(8,128)S(1)}, f32[3,128,128]{1,2,0:T(8,128)S(1)}, u32[]{:S(2)}, u32[]{:S(2)}) collective-permute-start(f32[3,128,128]{1,2,0:T(8,128)S(1)} %get-tuple-element.24), channel_id=1, source_target_pairs={{1,0},{2,1},{3,2},{4,3},{5,4},{6,5},{7,6},{8,7},{9,8},{10,9},{11,1... | collective-permute-start | bytes 589832 | tf_op jit(solution)/shard_map/ppermute | solution.py:19
  23.3 1.7 %copy-start.1 = (f32[9,2,128,128]{3,2,1,0:T(8,128)S(1)}, f32[9,2,128,128]{3,2,1,0:T(8,128)}, u32[]{:S(2)}) copy-start(f32[9,2,128,128]{3,2,1,0:T(8,128)} %param.7) | copy-start | bytes 3538948
  26.3 1.0 copy-start.2
  29.2 7.0 %collective-permute-start.2 = (f32[3,128,128]{2,1,0:T(8,128)S(1)}, f32[3,128,128]{2,1,0:T(8,128)S(1)}, u32[]{:S(2)}, u32[]{:S(2)}) collective-permute-start(f32[3,128,128]{2,1,0:T(8,128)S(1)} %get-tuple-element.16), channel_id=1, source_target_pairs={{0,1},{1,2},{2,3},{3,4},{4,5},{5,6},{6,7},{7,8},{8,9},{9,10},{10,1... | collective-permute-start | bytes 589832 | tf_op jit(solution)/shard_map/ppermute | solution.py:19
  32.3 8.2 %collective-permute-start.3 = (f32[3,128,128]{2,1,0:T(8,128)S(1)}, f32[3,128,128]{2,1,0:T(8,128)S(1)}, u32[]{:S(2)}, u32[]{:S(2)}) collective-permute-start(f32[3,128,128]{2,1,0:T(8,128)S(1)} %get-tuple-element.17), channel_id=1, source_target_pairs={{1,0},{2,1},{3,2},{4,3},{5,4},{6,5},{7,6},{8,7},{9,8},{10,9},{11,1... | collective-permute-start | bytes 589832 | tf_op jit(solution)/shard_map/ppermute | solution.py:19
  43.2 21.1 %all-to-all-start.1 = ((f32[32,3,128]{2,1,0:T(4,128)}), f32[32,3,128]{2,1,0:T(4,128)}, u32[]{:S(2)}, u32[]{:S(2)}) async-start(f32[32,3,128]{2,1,0:T(4,128)} %broadcast_in_dim.19), calls=%async_computation.1 | async-start | bytes 131072 | tf_op jit(solution)/shard_map/all_to_all | solution.py:25
  56.0 9.2 %collective-permute-start.4 = (f32[3,128,128]{2,1,0:T(8,128)}, f32[3,128,128]{2,1,0:T(8,128)S(1)}, u32[]{:S(2)}, u32[]{:S(2)}) collective-permute-start(f32[3,128,128]{2,1,0:T(8,128)} %get-tuple-element.12), channel_id=1, source_target_pairs={{0,1},{1,2},{2,3},{3,4},{4,5},{5,6},{6,7},{7,8},{8,9},{9,10},{10,1... | collective-permute-start | bytes 589832 | tf_op jit(solution)/shard_map/ppermute | solution.py:19
  59.6 7.8 %collective-permute-start.5 = (f32[3,128,128]{2,1,0:T(8,128)}, f32[3,128,128]{2,1,0:T(8,128)S(1)}, u32[]{:S(2)}, u32[]{:S(2)}) collective-permute-start(f32[3,128,128]{2,1,0:T(8,128)} %get-tuple-element.13), channel_id=1, source_target_pairs={{1,0},{2,1},{3,2},{4,3},{5,4},{6,5},{7,6},{8,7},{9,8},{10,9},{11,1... | collective-permute-start | bytes 589832 | tf_op jit(solution)/shard_map/ppermute | solution.py:19
  70.4 4.8 %copy-start.5 = (s32[1,2]{1,0:T(1,128)S(1)}, s32[1,2]{1,0:T(1,128)}, u32[]{:S(2)}) copy-start(s32[1,2]{1,0:T(1,128)} %param.11) | copy-start | bytes 28
  70.4 6.5 %collective-permute-start.6 = (f32[3,128,128]{2,1,0:T(8,128)S(1)}, f32[3,128,128]{2,1,0:T(8,128)S(1)}, u32[]{:S(2)}, u32[]{:S(2)}) collective-permute-start(f32[3,128,128]{2,1,0:T(8,128)S(1)} %get-tuple-element.8), channel_id=1, source_target_pairs={{0,1},{1,2},{2,3},{3,4},{4,5},{5,6},{6,7},{7,8},{8,9},{9,10},{10,1... | collective-permute-start | bytes 589832 | tf_op jit(solution)/shard_map/ppermute | solution.py:19
  73.8 7.7 %collective-permute-start.7 = (f32[3,128,128]{2,1,0:T(8,128)S(1)}, f32[3,128,128]{2,1,0:T(8,128)S(1)}, u32[]{:S(2)}, u32[]{:S(2)}) collective-permute-start(f32[3,128,128]{2,1,0:T(8,128)S(1)} %get-tuple-element.9), channel_id=1, source_target_pairs={{1,0},{2,1},{3,2},{4,3},{5,4},{6,5},{7,6},{8,7},{9,8},{10,9},{11,1... | collective-permute-start | bytes 589832 | tf_op jit(solution)/shard_map/ppermute | solution.py:19
  84.2 19.4 %all-to-all-start.2 = ((f32[32,3,128]{2,1,0:T(4,128)}), f32[32,3,128]{2,1,0:T(4,128)S(1)}, u32[]{:S(2)}, u32[]{:S(2)}) async-start(f32[32,3,128]{2,1,0:T(4,128)} %broadcast_in_dim.40), calls=%async_computation.2 | async-start | bytes 131072 | tf_op jit(solution)/shard_map/all_to_all | solution.py:25

commit v12 on v11

--- a/solution.py
+++ b/solution.py
@@ -29,7 +29,7 @@
     return jnp.einsum(spec, a, b, precision=precision)
 
 
-def left_environment(left_env, maps):
+def prefix_products(maps):
     segments = lax.axis_size("seg")
     segment = lax.axis_index("seg")
     spread = jnp.broadcast_to(maps[None], (segments,) + maps.shape)
@@ -39,8 +39,11 @@
     for step in range(segments - 1):
         grown = mm("kab,kbc->kac", prefix, every[step], EXACT)
         prefix = jnp.where(step < segment, grown, prefix)
-    right_side = mm("wkbc,kcd->wkbd", left_env, prefix)
-    return mm("kba,wkbd->wkad", prefix, right_side)
+    return prefix
+
+
+def sandwich(prefix, terms):
+    return mm("kba,wkbd->wkad", prefix, mm("wkbc,kcd->wkbd", terms, prefix))
 
 
 def exchange(vector, right):
@@ -50,12 +53,15 @@
     return products, from_left, from_right
 
 
-def combine(parts, ordered):
+def gathered(parts):
     products, from_left, from_right = parts
     lower = jnp.stack([from_left, products[0::3, 0]], axis=1)
     upper = jnp.stack([products[2::3, 1], from_right], axis=1)
-    terms = jnp.concatenate([lower, products[1::3], upper], axis=0)
-    return mm("wkab,wkbc->kac", ordered, terms)
+    return jnp.concatenate([lower, products[1::3], upper], axis=0)
+
+
+def combine(parts, ordered):
+    return mm("wkab,wkbc->kac", ordered, gathered(parts))
 
 
 def apply_terms(vector, right, ordered):
@@ -83,10 +89,13 @@
     blocks = vector.shape[0]
     width = vector.shape[1]
     cells = lax.axis_size("sec") * blocks * width * width
-    env = left_environment(left_env, maps)
-    weighted = env * mpo_mask.astype(jnp.float32)[:, :, None, None]
-    ordered = jnp.concatenate([weighted[0::3], weighted[1::3], weighted[2::3]], axis=0)
-    current = apply_terms(vector, right, ordered)
+    prefix = prefix_products(maps)
+    masked = left_env * mpo_mask.astype(jnp.float32)[:, :, None, None]
+    start = jnp.concatenate([masked[0::3], masked[1::3], masked[2::3]], axis=0)
+    parts = exchange(vector, right)
+    moved = mm("kab,wkbc->wkac", prefix, gathered(parts))
+    current = mm("kba,kbc->kac", prefix, mm("wkab,wkbc->kac", start, moved))
+    ordered = sandwich(prefix, start)
     rows = lax.broadcasted_iota(jnp.int32, (blocks, width), 1) < ranks[0][:, None]
     for pair in range(ITERS // 2):
         lifted = apply_terms(current * LIFT, right, ordered)

time: 105 us -> 106 us (level)
  waiting for transfers between devices: 35.9 us -> 33.4 us
  matrix products: 12.3 us -> 13.9 us
    all_to_all x1, waiting for transfers between devices: 8.13 us -> 6.32 us  [prefix_products(): every = lax.all_to_all(spread, 'seg', 0, 0, tiled=True)]
    dot_general x18 -> x20, matrix products: 12.3 us -> 13.9 us  [mm(): return jnp.einsum(spec, a, b, precision=precision)]
  transfers between devices with their start and end apart: 11 -> 11, of which waited for: 8 -> 8; matrix products, arithmetic and copies ran while one was open for 8% -> 9% of each run, Pallas kernels for 0% -> 0%
where the time goes in v12:
time: 106 us; the launch traced here: 105 us
  starting transfers between devices  45.3 us (43%)
  waiting for transfers between devices  33.4 us (32%)
  matrix products  13.9 us (13%)
  local copies, waits for them, and re-layouts  7.54 us (7%)
  other arithmetic  2.92 us (3%)
  between operations  1.7 us (2%)
    all_to_all x2, starting transfers between devices, gathered_sums(): return jnp.sum(lax.all_to_all(spread, axis, 0, 0, tiled=True), axis=0)  20.5 us
    ppermute x8, starting transfers between devices, shifted(): return lax.ppermute(block, axis, route)  19 us
    ppermute x8, waiting for transfers between devices, shifted(): return lax.ppermute(block, axis, route)  14.7 us
    dot_general x20, matrix products, mm(): return jnp.einsum(spec, a, b, precision=precision)  13.9 us
    all_to_all x2, waiting for transfers between devices, gathered_sums(): return jnp.sum(lax.all_to_all(spread, axis, 0, 0, tiled=True), axis=0)  12.4 us
    all_to_all x1, waiting for transfers between devices, prefix_products(): every = lax.all_to_all(spread, 'seg', 0, 0, tiled=True)  6.32 us
    all_to_all x1, starting transfers between devices, prefix_products(): every = lax.all_to_all(spread, 'seg', 0, 0, tiled=True)  5.78 us
  transfers between devices with their start and end apart: 11, of which 8 were waited for; matrix products, arithmetic and copies ran while one was open for 9% of the time, Pallas kernels for 0%

profile of v12, /device:TPU:8, one launch (start us, length us, event | category | flops | bytes accessed | tf_op | source)
XLA Modules:
  0.0 104.8 jit_solution(6238846466816435719)
XLA Ops:
  0.6 0.0 copy-start
  0.6 2.1 %broadcast_in_dim.18 = f32[8,2,128,128]{3,2,1,0:T(8,128)} broadcast(f32[2,128,128]{2,1,0:T(8,128)} %bitcast.202), dimensions={1,2,3} | broadcast | bytes 1179648 | tf_op jit(solution)/shard_map/broadcast_in_dim | solution.py:35
  2.7 5.8 %all-to-all-start = ((f32[8,2,128,128]{3,2,1,0:T(8,128)}), f32[8,2,128,128]{3,2,1,0:T(8,128)S(1)}, u32[]{:S(2)}, u32[]{:S(2)}) async-start(f32[8,2,128,128]{3,2,1,0:T(8,128)} %broadcast_in_dim.18), calls=%async_computation | async-start | bytes 2097152 | tf_op jit(solution)/shard_map/all_to_all | solution.py:36
  8.5 1.1 %convolution_bitcast_fusion.4 = f32[9,2,128,128]{2,3,0,1:T(8,128)S(1)} fusion(f32[1,2,128,128]{3,2,1,0:T(8,128)S(1)} %copy-done.5, f32[1,9,2,128,128]{4,3,2,1,0:T(8,128)S(1)} %copy-done), kind=kOutput, calls=%fused_computation.4 | convolution fusion | flops 226492416 | bytes 2490368 | tf_op jit(solution)/shard_map/kab,wkbc->wkac/dot_general | solution.py:29
  9.6 0.0 copy-start.6
  9.6 0.0 copy-start.1
  9.6 1.0 slice_bitcast_fusion.7
  10.6 3.8 %collective-permute-start = (f32[3,128,128]{1,2,0:T(8,128)}, f32[3,128,128]{1,2,0:T(8,128)}, u32[]{:S(2)}, u32[]{:S(2)}) collective-permute-start(f32[3,128,128]{1,2,0:T(8,128)} %get-tuple-element.20), channel_id=1, source_target_pairs={{0,1},{1,2},{2,3},{3,4},{4,5},{5,6},{6,7},{7,8},{8,9},{9,10},{10,1... | collective-permute-start | bytes 589832 | tf_op jit(solution)/shard_map/ppermute | solution.py:19
  14.4 1.3 %collective-permute-start.1 = (f32[3,128,128]{1,2,0:T(8,128)}, f32[3,128,128]{1,2,0:T(8,128)}, u32[]{:S(2)}, u32[]{:S(2)}) collective-permute-start(f32[3,128,128]{1,2,0:T(8,128)} %get-tuple-element.21), channel_id=1, source_target_pairs={{1,0},{2,1},{3,2},{4,3},{5,4},{6,5},{7,6},{8,7},{9,8},{10,9},{11,1... | collective-permute-start | bytes 589832 | tf_op jit(solution)/shard_map/ppermute | solution.py:19
  15.7 0.8 slice.122
  16.5 0.1 copy_multiply_fusion
  16.6 0.1 fusion.89
  16.7 6.3 %all-to-all-done = f32[8,2,128,128]{3,2,1,0:T(8,128)S(1)} async-done(((f32[8,2,128,128]{3,2,1,0:T(8,128)}), f32[8,2,128,128]{3,2,1,0:T(8,128)S(1)}, u32[]{:S(2)}, u32[]{:S(2)}) %all-to-all-start) | async-done | bytes 1048608 | tf_op jit(solution)/shard_map/all_to_all | solution.py:36
  23.0 0.3 convolution_select_fusion.6
  23.3 0.3 convolution_select_fusion.5
  23.6 0.3 convolution_select_fusion.4
  23.9 0.3 convolution_select_fusion.3
  24.1 0.3 convolution_select_fusion.2
  24.4 0.3 convolution_select_fusion.1
  24.7 0.3 convolution_select_fusion
  25.0 0.7 convolution_bitcast_fusion.6
  25.8 0.0 collective-permute-done
  25.8 0.2 copy-done.2
  26.0 0.0 copy-done.3
  26.0 0.1 copy-done.4
  26.1 1.7 %convolution_bitcast_fusion.3 = f32[9,2,128,128]{2,3,0,1:T(8,128)S(1)} fusion(f32[3,1,128,128]{2,3,0,1:T(8,128)} %bitcast.21, f32[3,1,128,128]{2,3,0,1:T(8,128)S(1)} %copy-done.3, f32[3,2,128,128]{2,3,0,1:T(8,128)S(1)} %copy-done.2, f32[3,1,128,128]{2,3,0,1:T(8,128)S(1)} %copy-done.4, f32[3,1,128,128]{2,3,0,1:T(8,128)} %bitcast.19, ...), kind=kOutput, calls=%fused_computation.3 | convolution fusion | flops 227672064 | bytes 2490368 | tf_op jit(solution)/shard_map/kab,wkbc->wkac/dot_general | solution.py:29
  27.8 0.8 convolution_bitcast_fusion.7
  28.6 0.3 fusion.90
  28.9 0.6 convolution_bitcast_fusion.2
  29.5 0.1 slice_bitcast_fusion.5
  29.6 3.1 %collective-permute-start.2 = (f32[3,128,128]{2,1,0:T(8,128)S(1)}, f32[3,128,128]{2,1,0:T(8,128)S(1)}, u32[]{:S(2)}, u32[]{:S(2)}) collective-permute-start(f32[3,128,128]{2,1,0:T(8,128)S(1)} %get-tuple-element.16), channel_id=1, source_target_pairs={{0,1},{1,2},{2,3},{3,4},{4,5},{5,6},{6,7},{7,8},{8,9},{9,10},{10,1... | collective-permute-start | bytes 589832 | tf_op jit(solution)/shard_map/ppermute | solution.py:19
  32.7 1.3 %collective-permute-start.3 = (f32[3,128,128]{2,1,0:T(8,128)S(1)}, f32[3,128,128]{2,1,0:T(8,128)S(1)}, u32[]{:S(2)}, u32[]{:S(2)}) collective-permute-start(f32[3,128,128]{2,1,0:T(8,128)S(1)} %get-tuple-element.17), channel_id=1, source_target_pairs={{1,0},{2,1},{3,2},{4,3},{5,4},{6,5},{7,6},{8,7},{9,8},{10,9},{11,1... | collective-permute-start | bytes 589832 | tf_op jit(solution)/shard_map/ppermute | solution.py:19
  34.0 0.6 convolution_bitcast_fusion.5
  34.6 2.0 %collective-permute-done.2 = f32[3,128,128]{2,1,0:T(8,128)S(1)} collective-permute-done((f32[3,128,128]{2,1,0:T(8,128)S(1)}, f32[3,128,128]{2,1,0:T(8,128)S(1)}, u32[]{:S(2)}, u32[]{:S(2)}) %collective-permute-start.2) | collective-permute-done | bytes 196640 | tf_op jit(solution)/shard_map/ppermute | solution.py:19
  36.6 4.3 %collective-permute-done.3 = f32[3,128,128]{2,1,0:T(8,128)S(1)} collective-permute-done((f32[3,128,128]{2,1,0:T(8,128)S(1)}, f32[3,128,128]{2,1,0:T(8,128)S(1)}, u32[]{:S(2)}, u32[]{:S(2)}) %collective-permute-start.3) | collective-permute-done | bytes 196640 | tf_op jit(solution)/shard_map/ppermute | solution.py:19
  40.9 1.2 %fusion.9 = f32[2,128,128,1]{2,1,3,0:T(8,128)S(1)} fusion(f32[9,2,128,128]{2,3,0,1:T(8,128)S(1)} %convolution_bitcast_fusion.5, f32[3,1,128,128]{3,2,0,1:T(8,128)S(1)} %bitcast.207, f32[3,1,128,128]{3,2,0,1:T(8,128)S(1)} %get-tuple-element.18, f32[3,2,128,128]{3,2,0,1:T(8,128)S(1)} %slice.127, f32[3,1,128,128]{3,2,0,1:T(8,128)S(1)} %get-tuple-element.19, ...), kind=kOutput, calls=%fused_computation.17 | convolution fusion | flops 227672064 | bytes 2490368 | tf_op jit(solution)/shard_map/wkab,wkbc->kac/dot_general | solution.py:29
  42.1 0.6 convolution_bitcast_fusion.1
  42.7 0.1 fusion.55
  42.9 0.7 broadcast_in_dim.19
  43.6 11.1 %all-to-all-start.1 = ((f32[32,3,128]{2,1,0:T(4,128)}), f32[32,3,128]{2,1,0:T(4,128)}, u32[]{:S(2)}, u32[]{:S(2)}) async-start(f32[32,3,128]{2,1,0:T(4,128)} %broadcast_in_dim.19), calls=%async_computation.1 | async-start | bytes 131072 | tf_op jit(solution)/shard_map/all_to_all | solution.py:25
  54.7 0.9 slice_bitcast_fusion.3
  55.6 0.8 slice.133
  56.4 3.6 %collective-permute-start.4 = (f32[3,128,128]{2,1,0:T(8,128)}, f32[3,128,128]{2,1,0:T(8,128)S(1)}, u32[]{:S(2)}, u32[]{:S(2)}) collective-permute-start(f32[3,128,128]{2,1,0:T(8,128)} %get-tuple-element.12), channel_id=1, source_target_pairs={{0,1},{1,2},{2,3},{3,4},{4,5},{5,6},{6,7},{7,8},{8,9},{9,10},{10,1... | collective-permute-start | bytes 589832 | tf_op jit(solution)/shard_map/ppermute | solution.py:19
  60.0 1.3 %collective-permute-start.5 = (f32[3,128,128]{2,1,0:T(8,128)}, f32[3,128,128]{2,1,0:T(8,128)S(1)}, u32[]{:S(2)}, u32[]{:S(2)}) collective-permute-start(f32[3,128,128]{2,1,0:T(8,128)} %get-tuple-element.13), channel_id=1, source_target_pairs={{1,0},{2,1},{3,2},{4,3},{5,4},{6,5},{7,6},{8,7},{9,8},{10,9},{11,1... | collective-permute-start | bytes 589832 | tf_op jit(solution)/shard_map/ppermute | solution.py:19
  61.3 3.4 %all-to-all-done.1 = f32[32,3,128]{2,1,0:T(4,128)} async-done(((f32[32,3,128]{2,1,0:T(4,128)}), f32[32,3,128]{2,1,0:T(4,128)}, u32[]{:S(2)}, u32[]{:S(2)}) %all-to-all-start.1) | async-done | bytes 49184 | tf_op jit(solution)/shard_map/all_to_all | solution.py:25
  64.7 0.9 reduce_sum.37
  65.6 2.2 %collective-permute-done.5 = f32[3,128,128]{2,1,0:T(8,128)S(1)} collective-permute-done((f32[3,128,128]{2,1,0:T(8,128)}, f32[3,128,128]{2,1,0:T(8,128)S(1)}, u32[]{:S(2)}, u32[]{:S(2)}) %collective-permute-start.5) | collective-permute-done | bytes 196640 | tf_op jit(solution)/shard_map/ppermute | solution.py:19
  67.8 2.3 %fusion.45 = f32[2,128,128]{2,1,0:T(8,128)S(1)} fusion(f32[3,1,128,128]{3,2,0,1:T(8,128)S(1)} %bitcast.204, f32[3,1,128,128]{3,2,0,1:T(8,128)} %get-tuple-element.14, f32[3,2,128,128]{3,2,0,1:T(8,128)} %slice.133, f32[3,1,128,128]{3,2,0,1:T(8,128)} %get-tuple-element.15, f32[3,1,128,128]{3,2,0,1:T(8,128)S(1)} %bitcast.203, ...), kind=kOutput, calls=%fused_computation.58 | convolution fusion | flops 227999744 | bytes 2491392 | tf_op jit(solution)/shard_map/wkab,wkbc->kac/dot_general | solution.py:29
  70.1 0.6 convolution_bitcast_fusion
  70.8 0.0 copy-start.7
  70.8 0.1 slice_bitcast_fusion.1
  70.8 3.4 %collective-permute-start.6 = (f32[3,128,128]{2,1,0:T(8,128)S(1)}, f32[3,128,128]{2,1,0:T(8,128)S(1)}, u32[]{:S(2)}, u32[]{:S(2)}) collective-permute-start(f32[3,128,128]{2,1,0:T(8,128)S(1)} %get-tuple-element.8), channel_id=1, source_target_pairs={{0,1},{1,2},{2,3},{3,4},{4,5},{5,6},{6,7},{7,8},{8,9},{9,10},{10,1... | collective-permute-start | bytes 589832 | tf_op jit(solution)/shard_map/ppermute | solution.py:19
  74.2 1.3 %collective-permute-start.7 = (f32[3,128,128]{2,1,0:T(8,128)S(1)}, f32[3,128,128]{2,1,0:T(8,128)S(1)}, u32[]{:S(2)}, u32[]{:S(2)}) collective-permute-start(f32[3,128,128]{2,1,0:T(8,128)S(1)} %get-tuple-element.9), channel_id=1, source_target_pairs={{1,0},{2,1},{3,2},{4,3},{5,4},{6,5},{7,6},{8,7},{9,8},{10,9},{11,1... | collective-permute-start | bytes 589832 | tf_op jit(solution)/shard_map/ppermute | solution.py:19
  75.5 0.1 compare_convert_fusion
  75.6 1.7 %collective-permute-done.6 = f32[3,128,128]{2,1,0:T(8,128)S(1)} collective-permute-done((f32[3,128,128]{2,1,0:T(8,128)S(1)}, f32[3,128,128]{2,1,0:T(8,128)S(1)}, u32[]{:S(2)}, u32[]{:S(2)}) %collective-permute-start.6) | collective-permute-done | bytes 196640 | tf_op jit(solution)/shard_map/ppermute | solution.py:19
  77.4 4.5 %collective-permute-done.7 = f32[3,128,128]{2,1,0:T(8,128)S(1)} collective-permute-done((f32[3,128,128]{2,1,0:T(8,128)S(1)}, f32[3,128,128]{2,1,0:T(8,128)S(1)}, u32[]{:S(2)}, u32[]{:S(2)}) %collective-permute-start.7) | collective-permute-done | bytes 196640 | tf_op jit(solution)/shard_map/ppermute | solution.py:19
  81.9 1.2 %fusion.29 = f32[2,128,128,1]{2,1,3,0:T(8,128)S(1)} fusion(f32[9,2,128,128]{2,3,0,1:T(8,128)S(1)} %convolution_bitcast_fusion.5, f32[3,1,128,128]{3,2,0,1:T(8,128)S(1)} %bitcast.208, f32[3,1,128,128]{3,2,0,1:T(8,128)S(1)} %get-tuple-element.10, f32[3,2,128,128]{3,2,0,1:T(8,128)S(1)} %slice.140, f32[3,1,128,128]{3,2,0,1:T(8,128)S(1)} %get-tuple-element.11, ...), kind=kOutput, calls=%fused_computation.37 | convolution fusion | flops 227672064 | bytes 2490368 | tf_op jit(solution)/shard_map/wkab,wkbc->kac/dot_general | solution.py:29
  83.0 0.7 fusion.64
  83.7 0.1 fusion.56
  83.9 0.7 broadcast_in_dim.40
  84.6 9.4 %all-to-all-start.2 = ((f32[32,3,128]{2,1,0:T(4,128)}), f32[32,3,128]{2,1,0:T(4,128)S(1)}, u32[]{:S(2)}, u32[]{:S(2)}) async-start(f32[32,3,128]{2,1,0:T(4,128)} %broadcast_in_dim.40), calls=%async_computation.2 | async-start | bytes 131072 | tf_op jit(solution)/shard_map/all_to_all | solution.py:25
  94.7 0.3 fusion.67
  95.0 9.0 %all-to-all-done.2 = f32[32,3,128]{2,1,0:T(4,128)S(1)} async-done(((f32[32,3,128]{2,1,0:T(4,128)}), f32[32,3,128]{2,1,0:T(4,128)S(1)}, u32[]{:S(2)}, u32[]{:S(2)}) %all-to-all-start.2) | async-done | bytes 49184 | tf_op jit(solution)/shard_map/all_to_all | solution.py:25
  104.1 0.7 fusion.65
  (20 shorter events, 0.2 us)
Async XLA Ops:
  0.6 7.9 %copy-start = (f32[1,9,2,128,128]{4,3,2,1,0:T(8,128)S(1)}, f32[1,9,2,128,128]{4,3,2,1,0:T(8,128)}, u32[]{:S(2)}) copy-start(f32[1,9,2,128,128]{4,3,2,1,0:T(8,128)} %param.9) | copy-start | bytes 3538948
  2.7 5.8 %copy-start.5 = (f32[1,2,128,128]{3,2,1,0:T(8,128)S(1)}, f32[1,2,128,128]{3,2,1,0:T(8,128)}, u32[]{:S(2)}) copy-start(f32[1,2,128,128]{3,2,1,0:T(8,128)} %param.6) | copy-start | bytes 393220
  2.7 20.3 %all-to-all-start = ((f32[8,2,128,128]{3,2,1,0:T(8,128)}), f32[8,2,128,128]{3,2,1,0:T(8,128)S(1)}, u32[]{:S(2)}, u32[]{:S(2)}) async-start(f32[8,2,128,128]{3,2,1,0:T(8,128)} %broadcast_in_dim.18), calls=%async_computation | async-start | bytes 2097152 | tf_op jit(solution)/shard_map/all_to_all | solution.py:36
  9.6 6.8 %copy-start.6 = (s32[9,2]{0,1:T(2,128)S(1)}, s32[9,2]{0,1:T(2,128)}, u32[]{:S(2)}) copy-start(s32[9,2]{0,1:T(2,128)} %param.10) | copy-start | bytes 220
  9.6 6.8 %copy-start.1 = (f32[9,2,128,128]{3,2,1,0:T(8,128)S(1)}, f32[9,2,128,128]{3,2,1,0:T(8,128)}, u32[]{:S(2)}) copy-start(f32[9,2,128,128]{3,2,1,0:T(8,128)} %param.7) | copy-start | bytes 3538948
  10.6 15.2 %collective-permute-start = (f32[3,128,128]{1,2,0:T(8,128)}, f32[3,128,128]{1,2,0:T(8,128)}, u32[]{:S(2)}, u32[]{:S(2)}) collective-permute-start(f32[3,128,128]{1,2,0:T(8,128)} %get-tuple-element.20), channel_id=1, source_target_pairs={{0,1},{1,2},{2,3},{3,4},{4,5},{5,6},{6,7},{7,8},{8,9},{9,10},{10,1... | collective-permute-start | bytes 589832 | tf_op jit(solution)/shard_map/ppermute | solution.py:19
  14.4 11.4 %collective-permute-start.1 = (f32[3,128,128]{1,2,0:T(8,128)}, f32[3,128,128]{1,2,0:T(8,128)}, u32[]{:S(2)}, u32[]{:S(2)}) collective-permute-start(f32[3,128,128]{1,2,0:T(8,128)} %get-tuple-element.21), channel_id=1, source_target_pairs={{1,0},{2,1},{3,2},{4,3},{5,4},{6,5},{7,6},{8,7},{9,8},{10,9},{11,1... | collective-permute-start | bytes 589832 | tf_op jit(solution)/shard_map/ppermute | solution.py:19
  25.0 1.0 copy-start.2
  25.0 1.0 copy-start.3
  25.0 1.1 %copy-start.4 = (f32[3,1,128,128]{2,3,0,1:T(8,128)S(1)}, f32[3,1,128,128]{2,3,0,1:T(8,128)}, u32[]{:S(2)}) copy-start(f32[3,1,128,128]{2,3,0,1:T(8,128)} %get-tuple-element.23) | copy-start | bytes 589828
  29.6 7.0 %collective-permute-start.2 = (f32[3,128,128]{2,1,0:T(8,128)S(1)}, f32[3,128,128]{2,1,0:T(8,128)S(1)}, u32[]{:S(2)}, u32[]{:S(2)}) collective-permute-start(f32[3,128,128]{2,1,0:T(8,128)S(1)} %get-tuple-element.16), channel_id=1, source_target_pairs={{0,1},{1,2},{2,3},{3,4},{4,5},{5,6},{6,7},{7,8},{8,9},{9,10},{10,1... | collective-permute-start | bytes 589832 | tf_op jit(solution)/shard_map/ppermute | solution.py:19
  32.7 8.2 %collective-permute-start.3 = (f32[3,128,128]{2,1,0:T(8,128)S(1)}, f32[3,128,128]{2,1,0:T(8,128)S(1)}, u32[]{:S(2)}, u32[]{:S(2)}) collective-permute-start(f32[3,128,128]{2,1,0:T(8,128)S(1)} %get-tuple-element.17), channel_id=1, source_target_pairs={{1,0},{2,1},{3,2},{4,3},{5,4},{6,5},{7,6},{8,7},{9,8},{10,9},{11,1... | collective-permute-start | bytes 589832 | tf_op jit(solution)/shard_map/ppermute | solution.py:19
  43.6 21.1 %all-to-all-start.1 = ((f32[32,3,128]{2,1,0:T(4,128)}), f32[32,3,128]{2,1,0:T(4,128)}, u32[]{:S(2)}, u32[]{:S(2)}) async-start(f32[32,3,128]{2,1,0:T(4,128)} %broadcast_in_dim.19), calls=%async_computation.1 | async-start | bytes 131072 | tf_op jit(solution)/shard_map/all_to_all | solution.py:25
  56.4 9.2 %collective-permute-start.4 = (f32[3,128,128]{2,1,0:T(8,128)}, f32[3,128,128]{2,1,0:T(8,128)S(1)}, u32[]{:S(2)}, u32[]{:S(2)}) collective-permute-start(f32[3,128,128]{2,1,0:T(8,128)} %get-tuple-element.12), channel_id=1, source_target_pairs={{0,1},{1,2},{2,3},{3,4},{4,5},{5,6},{6,7},{7,8},{8,9},{9,10},{10,1... | collective-permute-start | bytes 589832 | tf_op jit(solution)/shard_map/ppermute | solution.py:19
  60.0 7.8 %collective-permute-start.5 = (f32[3,128,128]{2,1,0:T(8,128)}, f32[3,128,128]{2,1,0:T(8,128)S(1)}, u32[]{:S(2)}, u32[]{:S(2)}) collective-permute-start(f32[3,128,128]{2,1,0:T(8,128)} %get-tuple-element.13), channel_id=1, source_target_pairs={{1,0},{2,1},{3,2},{4,3},{5,4},{6,5},{7,6},{8,7},{9,8},{10,9},{11,1... | collective-permute-start | bytes 589832 | tf_op jit(solution)/shard_map/ppermute | solution.py:19
  70.8 4.8 %copy-start.7 = (s32[1,2]{1,0:T(1,128)S(1)}, s32[1,2]{1,0:T(1,128)}, u32[]{:S(2)}) copy-start(s32[1,2]{1,0:T(1,128)} %param.11) | copy-start | bytes 28
  70.8 6.5 %collective-permute-start.6 = (f32[3,128,128]{2,1,0:T(8,128)S(1)}, f32[3,128,128]{2,1,0:T(8,128)S(1)}, u32[]{:S(2)}, u32[]{:S(2)}) collective-permute-start(f32[3,128,128]{2,1,0:T(8,128)S(1)} %get-tuple-element.8), channel_id=1, source_target_pairs={{0,1},{1,2},{2,3},{3,4},{4,5},{5,6},{6,7},{7,8},{8,9},{9,10},{10,1... | collective-permute-start | bytes 589832 | tf_op jit(solution)/shard_map/ppermute | solution.py:19
  74.2 7.7 %collective-permute-start.7 = (f32[3,128,128]{2,1,0:T(8,128)S(1)}, f32[3,128,128]{2,1,0:T(8,128)S(1)}, u32[]{:S(2)}, u32[]{:S(2)}) collective-permute-start(f32[3,128,128]{2,1,0:T(8,128)S(1)} %get-tuple-element.9), channel_id=1, source_target_pairs={{1,0},{2,1},{3,2},{4,3},{5,4},{6,5},{7,6},{8,7},{9,8},{10,9},{11,1... | collective-permute-start | bytes 589832 | tf_op jit(solution)/shard_map/ppermute | solution.py:19
  84.6 19.4 %all-to-all-start.2 = ((f32[32,3,128]{2,1,0:T(4,128)}), f32[32,3,128]{2,1,0:T(4,128)S(1)}, u32[]{:S(2)}, u32[]{:S(2)}) async-start(f32[32,3,128]{2,1,0:T(4,128)} %broadcast_in_dim.40), calls=%async_computation.2 | async-start | bytes 131072 | tf_op jit(solution)/shard_map/all_to_all | solution.py:25

commit v13 on v11

--- a/solution.py
+++ b/solution.py
@@ -58,8 +58,16 @@
     return mm("wkab,wkbc->kac", ordered, terms)
 
 
-def apply_terms(vector, right, ordered):
-    return combine(exchange(vector, right), ordered)
+def apply_terms(vector, right, ordered, split=False):
+    if not split:
+        return combine(exchange(vector, right), ordered)
+    products, from_left, from_right = exchange(vector, right)
+    group = ordered.shape[0] // 3
+    blank = jnp.zeros_like(from_left)
+    inner = combine((products, blank, blank), ordered)
+    lower = inner[0] + mm("wab,wbc->ac", ordered[:group, 0], from_left)
+    upper = inner[1] + mm("wab,wbc->ac", ordered[2 * group :, 1], from_right)
+    return jnp.stack([lower, upper], axis=0)
 
 
 def square_sums(normal, lifted):
@@ -89,7 +97,7 @@
     current = apply_terms(vector, right, ordered)
     rows = lax.broadcasted_iota(jnp.int32, (blocks, width), 1) < ranks[0][:, None]
     for pair in range(ITERS // 2):
-        lifted = apply_terms(current * LIFT, right, ordered)
+        lifted = apply_terms(current * LIFT, right, ordered, split=True)
         more = 2 * pair + 2 < ITERS
         if more:
             parts = exchange(lifted * LIFT, right)

time: 105 us -> 104 us (level)
  waiting for transfers between devices: 35.9 us -> 32.8 us
  matrix products: 12.3 us -> 13.7 us
    ppermute x8, waiting for transfers between devices: 15.3 us -> 12.3 us  [shifted(): return lax.ppermute(block, axis, route)]
    dot_general x18 -> x22, matrix products: 12.3 us -> 13.7 us  [mm(): return jnp.einsum(spec, a, b, precision=precision)]
  transfers between devices with their start and end apart: 11 -> 11, of which waited for: 8 -> 8; matrix products, arithmetic and copies ran while one was open for 8% -> 11% of each run, Pallas kernels for 0% -> 0%
where the time goes in v13:
time: 104 us
  starting transfers between devices  44.8 us (43%)
  waiting for transfers between devices  32.8 us (32%)
  matrix products  13.7 us (13%)
  local copies, waits for them, and re-layouts  7.17 us (7%)
  other arithmetic  3.42 us (3%)
  between operations  1.72 us (2%)
    all_to_all x2, starting transfers between devices, gathered_sums(): return jnp.sum(lax.all_to_all(spread, axis, 0, 0, tiled=True), axis=0)  20.5 us
    ppermute x8, starting transfers between devices, shifted(): return lax.ppermute(block, axis, route)  18.5 us
    dot_general x22, matrix products, mm(): return jnp.einsum(spec, a, b, precision=precision)  13.7 us
    all_to_all x2, waiting for transfers between devices, gathered_sums(): return jnp.sum(lax.all_to_all(spread, axis, 0, 0, tiled=True), axis=0)  12.4 us
    ppermute x8, waiting for transfers between devices, shifted(): return lax.ppermute(block, axis, route)  12.3 us
    all_to_all x1, waiting for transfers between devices, left_environment(): every = lax.all_to_all(spread, 'seg', 0, 0, tiled=True)  8.13 us
    all_to_all x1, starting transfers between devices, left_environment(): every = lax.all_to_all(spread, 'seg', 0, 0, tiled=True)  5.78 us
  transfers between devices with their start and end apart: 11, of which 8 were waited for; matrix products, arithmetic and copies ran while one was open for 11% of the time, Pallas kernels for 0%

profile of v13, /device:TPU:8, one launch (start us, length us, event | category | flops | bytes accessed | tf_op | source)
XLA Modules:
  0.0 103.6 jit_solution(13716950307164378708)
XLA Ops:
  0.6 0.0 copy-start
  0.6 2.1 %broadcast_in_dim.16 = f32[8,2,128,128]{3,2,1,0:T(8,128)} broadcast(f32[2,128,128]{2,1,0:T(8,128)} %bitcast.236), dimensions={1,2,3} | broadcast | bytes 1179648 | tf_op jit(solution)/shard_map/broadcast_in_dim | solution.py:35
  2.7 5.8 %all-to-all-start = ((f32[8,2,128,128]{3,2,1,0:T(8,128)}), f32[8,2,128,128]{3,2,1,0:T(8,128)S(1)}, u32[]{:S(2)}, u32[]{:S(2)}) async-start(f32[8,2,128,128]{3,2,1,0:T(8,128)} %broadcast_in_dim.16), calls=%async_computation | async-start | bytes 2097152 | tf_op jit(solution)/shard_map/all_to_all | solution.py:36
  8.5 1.1 %convolution_bitcast_fusion.3 = f32[9,2,128,128]{2,3,0,1:T(8,128)S(1)} fusion(f32[1,2,128,128]{3,2,1,0:T(8,128)S(1)} %copy-done.3, f32[1,9,2,128,128]{4,3,2,1,0:T(8,128)S(1)} %copy-done), kind=kOutput, calls=%fused_computation.3 | convolution fusion | flops 226492416 | bytes 2490368 | tf_op jit(solution)/shard_map/kab,wkbc->wkac/dot_general | solution.py:29
  9.6 0.0 copy-start.4
  9.6 0.1 slice_bitcast_fusion.9
  9.7 3.1 %collective-permute-start = (f32[3,128,128]{1,2,0:T(8,128)S(1)}, f32[3,128,128]{1,2,0:T(8,128)S(1)}, u32[]{:S(2)}, u32[]{:S(2)}) collective-permute-start(f32[3,128,128]{1,2,0:T(8,128)S(1)} %get-tuple-element.23), channel_id=1, source_target_pairs={{0,1},{1,2},{2,3},{3,4},{4,5},{5,6},{6,7},{7,8},{8,9},{9,10},{10,1... | collective-permute-start | bytes 589832 | tf_op jit(solution)/shard_map/ppermute | solution.py:19
  12.8 1.3 %collective-permute-start.1 = (f32[3,128,128]{1,2,0:T(8,128)S(1)}, f32[3,128,128]{1,2,0:T(8,128)S(1)}, u32[]{:S(2)}, u32[]{:S(2)}) collective-permute-start(f32[3,128,128]{1,2,0:T(8,128)S(1)} %get-tuple-element.24), channel_id=1, source_target_pairs={{1,0},{2,1},{3,2},{4,3},{5,4},{6,5},{7,6},{8,7},{9,8},{10,9},{11,1... | collective-permute-start | bytes 589832 | tf_op jit(solution)/shard_map/ppermute | solution.py:19
  14.1 0.8 slice.142
  14.9 8.1 %all-to-all-done = f32[8,2,128,128]{3,2,1,0:T(8,128)S(1)} async-done(((f32[8,2,128,128]{3,2,1,0:T(8,128)}), f32[8,2,128,128]{3,2,1,0:T(8,128)S(1)}, u32[]{:S(2)}, u32[]{:S(2)}) %all-to-all-start) | async-done | bytes 1048608 | tf_op jit(solution)/shard_map/all_to_all | solution.py:36
  23.0 0.3 convolution_select_fusion.6
  23.3 0.0 copy-start.1
  23.3 0.3 convolution_select_fusion.5
  23.6 0.3 convolution_select_fusion.4
  23.9 0.3 convolution_select_fusion.3
  24.1 0.3 convolution_select_fusion.2
  24.4 0.3 convolution_select_fusion.1
  24.7 0.3 fusion.45
  25.0 0.7 convolution_bitcast_fusion.5
  25.7 0.6 fusion
  26.3 0.1 fusion.105
  26.5 0.0 collective-permute-done
  26.5 0.9 copy-done.2
  27.3 1.2 %fusion.12 = f32[2,128,128,1]{2,1,3,0:T(8,128)S(1)} fusion(f32[3,1,128,128]{2,3,0,1:T(8,128)S(1)} %bitcast.238, f32[3,1,128,128]{2,3,0,1:T(8,128)S(1)} %get-tuple-element.25, f32[3,2,128,128]{2,3,0,1:T(8,128)S(1)} %copy-done.2, f32[3,1,128,128]{2,3,0,1:T(8,128)S(1)} %get-tuple-element.26, f32[3,1,128,128]{2,3,0,1:T(8,128)S(1)} %bitcast.237, ...), kind=kOutput, calls=%fused_computation.22 | convolution fusion | flops 228261888 | bytes 2490368 | tf_op jit(solution)/shard_map/wkab,wkbc->kac/dot_general | solution.py:29
  28.5 0.6 convolution_bitcast_fusion.2
  29.1 0.1 slice_bitcast_fusion.7
  29.2 3.1 %collective-permute-start.2 = (f32[3,128,128]{2,1,0:T(8,128)S(1)}, f32[3,128,128]{2,1,0:T(8,128)S(1)}, u32[]{:S(2)}, u32[]{:S(2)}) collective-permute-start(f32[3,128,128]{2,1,0:T(8,128)S(1)} %get-tuple-element.16), channel_id=1, source_target_pairs={{0,1},{1,2},{2,3},{3,4},{4,5},{5,6},{6,7},{7,8},{8,9},{9,10},{10,1... | collective-permute-start | bytes 589832 | tf_op jit(solution)/shard_map/ppermute | solution.py:19
  32.3 1.3 %collective-permute-start.3 = (f32[3,128,128]{2,1,0:T(8,128)S(1)}, f32[3,128,128]{2,1,0:T(8,128)S(1)}, u32[]{:S(2)}, u32[]{:S(2)}) collective-permute-start(f32[3,128,128]{2,1,0:T(8,128)S(1)} %get-tuple-element.17), channel_id=1, source_target_pairs={{1,0},{2,1},{3,2},{4,3},{5,4},{6,5},{7,6},{8,7},{9,8},{10,9},{11,1... | collective-permute-start | bytes 589832 | tf_op jit(solution)/shard_map/ppermute | solution.py:19
  33.6 1.1 %fusion.41 = f32[2,128,128]{2,1,0:T(8,128)S(1)} fusion(f32[3,1,128,128]{3,2,0,1:T(8,128)S(1)} %get-tuple-element.18, f32[3,1,128,128]{3,2,0,1:T(8,128)S(1)} %get-tuple-element.19, f32[3,2,128,128]{3,2,0,1:T(8,128)S(1)} %slice.146, f32[3,2,128,128]{2,3,0,1:T(8,128)S(1)} %get-tuple-element.21, f32[3,2,128,128]{2,3,0,1:T(8,128)S(1)} %get-tuple-element.22, ...), kind=kOutput, calls=%fused_computation.54 | convolution fusion | flops 228851712 | bytes 2097152 | tf_op jit(solution)/shard_map/wkab,wkbc->kac/dot_general | solution.py:29
  34.7 1.5 %collective-permute-done.2 = f32[3,128,128]{2,1,0:T(8,128)S(1)} collective-permute-done((f32[3,128,128]{2,1,0:T(8,128)S(1)}, f32[3,128,128]{2,1,0:T(8,128)S(1)}, u32[]{:S(2)}, u32[]{:S(2)}) %collective-permute-start.2) | collective-permute-done | bytes 196640 | tf_op jit(solution)/shard_map/ppermute | solution.py:19
  36.2 0.4 fusion.51
  36.6 4.0 %collective-permute-done.3 = f32[3,128,128]{2,1,0:T(8,128)S(1)} collective-permute-done((f32[3,128,128]{2,1,0:T(8,128)S(1)}, f32[3,128,128]{2,1,0:T(8,128)S(1)}, u32[]{:S(2)}, u32[]{:S(2)}) %collective-permute-start.3) | collective-permute-done | bytes 196640 | tf_op jit(solution)/shard_map/ppermute | solution.py:19
  40.5 0.4 fusion.52
  40.9 0.6 convolution_bitcast_fusion.1
  41.6 0.1 fusion.66
  41.7 0.7 broadcast_in_dim.17
  42.4 11.1 %all-to-all-start.1 = ((f32[32,3,128]{2,1,0:T(4,128)}), f32[32,3,128]{2,1,0:T(4,128)}, u32[]{:S(2)}, u32[]{:S(2)}) async-start(f32[32,3,128]{2,1,0:T(4,128)} %broadcast_in_dim.17), calls=%async_computation.1 | async-start | bytes 131072 | tf_op jit(solution)/shard_map/all_to_all | solution.py:25
  53.5 0.9 slice_bitcast_fusion.5
  54.5 0.8 slice.157
  55.2 3.6 %collective-permute-start.4 = (f32[3,128,128]{2,1,0:T(8,128)}, f32[3,128,128]{2,1,0:T(8,128)S(1)}, u32[]{:S(2)}, u32[]{:S(2)}) collective-permute-start(f32[3,128,128]{2,1,0:T(8,128)} %get-tuple-element.12), channel_id=1, source_target_pairs={{0,1},{1,2},{2,3},{3,4},{4,5},{5,6},{6,7},{7,8},{8,9},{9,10},{10,1... | collective-permute-start | bytes 589832 | tf_op jit(solution)/shard_map/ppermute | solution.py:19
  58.9 1.3 %collective-permute-start.5 = (f32[3,128,128]{2,1,0:T(8,128)}, f32[3,128,128]{2,1,0:T(8,128)S(1)}, u32[]{:S(2)}, u32[]{:S(2)}) collective-permute-start(f32[3,128,128]{2,1,0:T(8,128)} %get-tuple-element.13), channel_id=1, source_target_pairs={{1,0},{2,1},{3,2},{4,3},{5,4},{6,5},{7,6},{8,7},{9,8},{10,9},{11,1... | collective-permute-start | bytes 589832 | tf_op jit(solution)/shard_map/ppermute | solution.py:19
  60.2 3.4 %all-to-all-done.1 = f32[32,3,128]{2,1,0:T(4,128)} async-done(((f32[32,3,128]{2,1,0:T(4,128)}), f32[32,3,128]{2,1,0:T(4,128)}, u32[]{:S(2)}, u32[]{:S(2)}) %all-to-all-start.1) | async-done | bytes 49184 | tf_op jit(solution)/shard_map/all_to_all | solution.py:25
  63.5 0.9 reduce_sum.37
  64.5 2.2 %collective-permute-done.5 = f32[3,128,128]{2,1,0:T(8,128)S(1)} collective-permute-done((f32[3,128,128]{2,1,0:T(8,128)}, f32[3,128,128]{2,1,0:T(8,128)S(1)}, u32[]{:S(2)}, u32[]{:S(2)}) %collective-permute-start.5) | collective-permute-done | bytes 196640 | tf_op jit(solution)/shard_map/ppermute | solution.py:19
  66.6 2.3 %fusion.46 = f32[2,128,128]{2,1,0:T(8,128)S(1)} fusion(f32[3,1,128,128]{3,2,0,1:T(8,128)S(1)} %bitcast.240, f32[3,1,128,128]{3,2,0,1:T(8,128)} %get-tuple-element.14, f32[3,2,128,128]{3,2,0,1:T(8,128)} %slice.157, f32[3,1,128,128]{3,2,0,1:T(8,128)} %get-tuple-element.15, f32[3,1,128,128]{3,2,0,1:T(8,128)S(1)} %bitcast.239, ...), kind=kOutput, calls=%fused_computation.57 | convolution fusion | flops 228589568 | bytes 2491392 | tf_op jit(solution)/shard_map/wkab,wkbc->kac/dot_general | solution.py:29
  69.0 0.6 convolution_bitcast_fusion
  69.6 0.0 copy-start.5
  69.6 0.1 slice_bitcast_fusion.3
  69.7 3.4 %collective-permute-start.6 = (f32[3,128,128]{2,1,0:T(8,128)S(1)}, f32[3,128,128]{2,1,0:T(8,128)S(1)}, u32[]{:S(2)}, u32[]{:S(2)}) collective-permute-start(f32[3,128,128]{2,1,0:T(8,128)S(1)} %get-tuple-element.8), channel_id=1, source_target_pairs={{0,1},{1,2},{2,3},{3,4},{4,5},{5,6},{6,7},{7,8},{8,9},{9,10},{10,1... | collective-permute-start | bytes 589832 | tf_op jit(solution)/shard_map/ppermute | solution.py:19
  73.1 0.1 compare_convert_fusion
  73.2 1.5 %collective-permute-start.7 = (f32[3,128,128]{2,1,0:T(8,128)S(1)}, f32[3,128,128]{2,1,0:T(8,128)S(1)}, u32[]{:S(2)}, u32[]{:S(2)}) collective-permute-start(f32[3,128,128]{2,1,0:T(8,128)S(1)} %get-tuple-element.9), channel_id=1, source_target_pairs={{1,0},{2,1},{3,2},{4,3},{5,4},{6,5},{7,6},{8,7},{9,8},{10,9},{11,1... | collective-permute-start | bytes 589832 | tf_op jit(solution)/shard_map/ppermute | solution.py:19
  74.7 1.1 %fusion.44 = f32[2,128,128]{2,1,0:T(8,128)S(1)} fusion(f32[3,1,128,128]{3,2,0,1:T(8,128)S(1)} %get-tuple-element.10, f32[3,1,128,128]{3,2,0,1:T(8,128)S(1)} %get-tuple-element.11, f32[3,2,128,128]{3,2,0,1:T(8,128)S(1)} %slice.163, f32[3,2,128,128]{2,3,0,1:T(8,128)S(1)} %get-tuple-element.21, f32[3,2,128,128]{2,3,0,1:T(8,128)S(1)} %get-tuple-element.22, ...), kind=kOutput, calls=%fused_computation.55 | convolution fusion | flops 228851712 | bytes 2097152 | tf_op jit(solution)/shard_map/wkab,wkbc->kac/dot_general | solution.py:29
  75.8 0.4 collective-permute-done.6
  76.2 0.4 fusion.53
  76.6 4.3 %collective-permute-done.7 = f32[3,128,128]{2,1,0:T(8,128)S(1)} collective-permute-done((f32[3,128,128]{2,1,0:T(8,128)S(1)}, f32[3,128,128]{2,1,0:T(8,128)S(1)}, u32[]{:S(2)}, u32[]{:S(2)}) %collective-permute-start.7) | collective-permute-done | bytes 196640 | tf_op jit(solution)/shard_map/ppermute | solution.py:19
  80.8 0.4 fusion.54
  81.2 0.7 fusion.80
  81.9 0.1 fusion.67
  82.1 0.7 broadcast_in_dim.18
  82.8 9.4 %all-to-all-start.2 = ((f32[32,3,128]{2,1,0:T(4,128)}), f32[32,3,128]{2,1,0:T(4,128)S(1)}, u32[]{:S(2)}, u32[]{:S(2)}) async-start(f32[32,3,128]{2,1,0:T(4,128)} %broadcast_in_dim.18), calls=%async_computation.2 | async-start | bytes 131072 | tf_op jit(solution)/shard_map/all_to_all | solution.py:25
  92.9 0.3 fusion.72
  93.2 9.0 %all-to-all-done.2 = f32[32,3,128]{2,1,0:T(4,128)S(1)} async-done(((f32[32,3,128]{2,1,0:T(4,128)}), f32[32,3,128]{2,1,0:T(4,128)S(1)}, u32[]{:S(2)}, u32[]{:S(2)}) %all-to-all-start.2) | async-done | bytes 49184 | tf_op jit(solution)/shard_map/all_to_all | solution.py:25
  102.3 0.7 fusion.77
  103.0 0.7 multiply_bitcast_fusion
  (20 shorter events, 0.2 us)
Async XLA Ops:
  0.6 7.9 %copy-start = (f32[1,9,2,128,128]{4,3,2,1,0:T(8,128)S(1)}, f32[1,9,2,128,128]{4,3,2,1,0:T(8,128)}, u32[]{:S(2)}) copy-start(f32[1,9,2,128,128]{4,3,2,1,0:T(8,128)} %param.9) | copy-start | bytes 3538948
  2.7 5.8 %copy-start.3 = (f32[1,2,128,128]{3,2,1,0:T(8,128)S(1)}, f32[1,2,128,128]{3,2,1,0:T(8,128)}, u32[]{:S(2)}) copy-start(f32[1,2,128,128]{3,2,1,0:T(8,128)} %param.6) | copy-start | bytes 393220
  2.7 20.3 %all-to-all-start = ((f32[8,2,128,128]{3,2,1,0:T(8,128)}), f32[8,2,128,128]{3,2,1,0:T(8,128)S(1)}, u32[]{:S(2)}, u32[]{:S(2)}) async-start(f32[8,2,128,128]{3,2,1,0:T(8,128)} %broadcast_in_dim.16), calls=%async_computation | async-start | bytes 2097152 | tf_op jit(solution)/shard_map/all_to_all | solution.py:36
  9.6 5.3 %copy-start.4 = (s32[9,2]{0,1:T(2,128)S(1)}, s32[9,2]{0,1:T(2,128)}, u32[]{:S(2)}) copy-start(s32[9,2]{0,1:T(2,128)} %param.10) | copy-start | bytes 220
  9.7 16.8 %collective-permute-start = (f32[3,128,128]{1,2,0:T(8,128)S(1)}, f32[3,128,128]{1,2,0:T(8,128)S(1)}, u32[]{:S(2)}, u32[]{:S(2)}) collective-permute-start(f32[3,128,128]{1,2,0:T(8,128)S(1)} %get-tuple-element.23), channel_id=1, source_target_pairs={{0,1},{1,2},{2,3},{3,4},{4,5},{5,6},{6,7},{7,8},{8,9},{9,10},{10,1... | collective-permute-start | bytes 589832 | tf_op jit(solution)/shard_map/ppermute | solution.py:19
  12.8 13.7 %collective-permute-start.1 = (f32[3,128,128]{1,2,0:T(8,128)S(1)}, f32[3,128,128]{1,2,0:T(8,128)S(1)}, u32[]{:S(2)}, u32[]{:S(2)}) collective-permute-start(f32[3,128,128]{1,2,0:T(8,128)S(1)} %get-tuple-element.24), channel_id=1, source_target_pairs={{1,0},{2,1},{3,2},{4,3},{5,4},{6,5},{7,6},{8,7},{9,8},{10,9},{11,1... | collective-permute-start | bytes 589832 | tf_op jit(solution)/shard_map/ppermute | solution.py:19
  23.3 1.7 %copy-start.1 = (f32[9,2,128,128]{3,2,1,0:T(8,128)S(1)}, f32[9,2,128,128]{3,2,1,0:T(8,128)}, u32[]{:S(2)}) copy-start(f32[9,2,128,128]{3,2,1,0:T(8,128)} %param.7) | copy-start | bytes 3538948
  26.3 1.0 copy-start.2
  29.2 7.0 %collective-permute-start.2 = (f32[3,128,128]{2,1,0:T(8,128)S(1)}, f32[3,128,128]{2,1,0:T(8,128)S(1)}, u32[]{:S(2)}, u32[]{:S(2)}) collective-permute-start(f32[3,128,128]{2,1,0:T(8,128)S(1)} %get-tuple-element.16), channel_id=1, source_target_pairs={{0,1},{1,2},{2,3},{3,4},{4,5},{5,6},{6,7},{7,8},{8,9},{9,10},{10,1... | collective-permute-start | bytes 589832 | tf_op jit(solution)/shard_map/ppermute | solution.py:19
  32.3 8.2 %collective-permute-start.3 = (f32[3,128,128]{2,1,0:T(8,128)S(1)}, f32[3,128,128]{2,1,0:T(8,128)S(1)}, u32[]{:S(2)}, u32[]{:S(2)}) collective-permute-start(f32[3,128,128]{2,1,0:T(8,128)S(1)} %get-tuple-element.17), channel_id=1, source_target_pairs={{1,0},{2,1},{3,2},{4,3},{5,4},{6,5},{7,6},{8,7},{9,8},{10,9},{11,1... | collective-permute-start | bytes 589832 | tf_op jit(solution)/shard_map/ppermute | solution.py:19
  42.4 21.1 %all-to-all-start.1 = ((f32[32,3,128]{2,1,0:T(4,128)}), f32[32,3,128]{2,1,0:T(4,128)}, u32[]{:S(2)}, u32[]{:S(2)}) async-start(f32[32,3,128]{2,1,0:T(4,128)} %broadcast_in_dim.17), calls=%async_computation.1 | async-start | bytes 131072 | tf_op jit(solution)/shard_map/all_to_all | solution.py:25
  55.2 9.2 %collective-permute-start.4 = (f32[3,128,128]{2,1,0:T(8,128)}, f32[3,128,128]{2,1,0:T(8,128)S(1)}, u32[]{:S(2)}, u32[]{:S(2)}) collective-permute-start(f32[3,128,128]{2,1,0:T(8,128)} %get-tuple-element.12), channel_id=1, source_target_pairs={{0,1},{1,2},{2,3},{3,4},{4,5},{5,6},{6,7},{7,8},{8,9},{9,10},{10,1... | collective-permute-start | bytes 589832 | tf_op jit(solution)/shard_map/ppermute | solution.py:19
  58.9 7.8 %collective-permute-start.5 = (f32[3,128,128]{2,1,0:T(8,128)}, f32[3,128,128]{2,1,0:T(8,128)S(1)}, u32[]{:S(2)}, u32[]{:S(2)}) collective-permute-start(f32[3,128,128]{2,1,0:T(8,128)} %get-tuple-element.13), channel_id=1, source_target_pairs={{1,0},{2,1},{3,2},{4,3},{5,4},{6,5},{7,6},{8,7},{9,8},{10,9},{11,1... | collective-permute-start | bytes 589832 | tf_op jit(solution)/shard_map/ppermute | solution.py:19
  69.6 3.5 %copy-start.5 = (s32[1,2]{1,0:T(1,128)S(1)}, s32[1,2]{1,0:T(1,128)}, u32[]{:S(2)}) copy-start(s32[1,2]{1,0:T(1,128)} %param.11) | copy-start | bytes 28
  69.7 6.5 %collective-permute-start.6 = (f32[3,128,128]{2,1,0:T(8,128)S(1)}, f32[3,128,128]{2,1,0:T(8,128)S(1)}, u32[]{:S(2)}, u32[]{:S(2)}) collective-permute-start(f32[3,128,128]{2,1,0:T(8,128)S(1)} %get-tuple-element.8), channel_id=1, source_target_pairs={{0,1},{1,2},{2,3},{3,4},{4,5},{5,6},{6,7},{7,8},{8,9},{9,10},{10,1... | collective-permute-start | bytes 589832 | tf_op jit(solution)/shard_map/ppermute | solution.py:19
  73.2 7.7 %collective-permute-start.7 = (f32[3,128,128]{2,1,0:T(8,128)S(1)}, f32[3,128,128]{2,1,0:T(8,128)S(1)}, u32[]{:S(2)}, u32[]{:S(2)}) collective-permute-start(f32[3,128,128]{2,1,0:T(8,128)S(1)} %get-tuple-element.9), channel_id=1, source_target_pairs={{1,0},{2,1},{3,2},{4,3},{5,4},{6,5},{7,6},{8,7},{9,8},{10,9},{11,1... | collective-permute-start | bytes 589832 | tf_op jit(solution)/shard_map/ppermute | solution.py:19
  82.8 19.4 %all-to-all-start.2 = ((f32[32,3,128]{2,1,0:T(4,128)}), f32[32,3,128]{2,1,0:T(4,128)S(1)}, u32[]{:S(2)}, u32[]{:S(2)}) async-start(f32[32,3,128]{2,1,0:T(4,128)} %broadcast_in_dim.18), calls=%async_computation.2 | async-start | bytes 131072 | tf_op jit(solution)/shard_map/all_to_all | solution.py:25

commit v14 on v13

--- a/solution.py
+++ b/solution.py
@@ -58,16 +58,20 @@
     return mm("wkab,wkbc->kac", ordered, terms)
 
 
-def apply_terms(vector, right, ordered, split=False):
-    if not split:
-        return combine(exchange(vector, right), ordered)
-    products, from_left, from_right = exchange(vector, right)
+def split_image(parts, ordered):
+    products, from_left, from_right = parts
     group = ordered.shape[0] // 3
     blank = jnp.zeros_like(from_left)
     inner = combine((products, blank, blank), ordered)
     lower = inner[0] + mm("wab,wbc->ac", ordered[:group, 0], from_left)
     upper = inner[1] + mm("wab,wbc->ac", ordered[2 * group :, 1], from_right)
     return jnp.stack([lower, upper], axis=0)
+
+
+def apply_terms(vector, right, ordered, split=False):
+    if not split:
+        return combine(exchange(vector, right), ordered)
+    return split_image(exchange(vector, right), ordered)
 
 
 def square_sums(normal, lifted):
@@ -108,7 +112,7 @@
             gram, peak = lax.optimization_barrier((mm("kab,kcb->kac", unit, unit), peak))
         first, second = scales(gathered_sums(square_sums(current, lifted), "sec"), cells)
         if more:
-            current = combine(parts, ordered * (first / LIFT)) * (second / LIFT)
+            current = split_image(parts, ordered * (first / LIFT)) * (second / LIFT)
         else:
             factor = (first / LIFT) * second
             current = lifted * factor

time: 104 us -> 103 us (level)
  waiting for transfers between devices: 32.8 us -> 30.7 us
    ppermute x8, waiting for transfers between devices: 12.3 us -> 10.3 us  [shifted(): return lax.ppermute(block, axis, route)]
    dot_general x22 -> x24, matrix products: 13.7 us -> 13.1 us  [mm(): return jnp.einsum(spec, a, b, precision=precision)]
  transfers between devices with their start and end apart: 11 -> 11, of which waited for: 8 -> 7; matrix products, arithmetic and copies ran while one was open for 11% -> 13% of each run, Pallas kernels for 0% -> 0%
where the time goes in v14:
time: 103 us; the launch traced here: 102 us
  starting transfers between devices  44.7 us (43%)
  waiting for transfers between devices  30.7 us (30%)
  matrix products  13.1 us (13%)
  local copies, waits for them, and re-layouts  8.11 us (8%)
  other arithmetic  3.63 us (4%)
  between operations  1.76 us (2%)
    all_to_all x2, starting transfers between devices, gathered_sums(): return jnp.sum(lax.all_to_all(spread, axis, 0, 0, tiled=True), axis=0)  20.5 us
    ppermute x8, starting transfers between devices, shifted(): return lax.ppermute(block, axis, route)  18.4 us
    dot_general x24, matrix products, mm(): return jnp.einsum(spec, a, b, precision=precision)  13.1 us
    all_to_all x2, waiting for transfers between devices, gathered_sums(): return jnp.sum(lax.all_to_all(spread, axis, 0, 0, tiled=True), axis=0)  12.2 us
    ppermute x8, waiting for transfers between devices, shifted(): return lax.ppermute(block, axis, route)  10.3 us
    all_to_all x1, waiting for transfers between devices, left_environment(): every = lax.all_to_all(spread, 'seg', 0, 0, tiled=True)  8.13 us
    all_to_all x1, starting transfers between devices, left_environment(): every = lax.all_to_all(spread, 'seg', 0, 0, tiled=True)  5.78 us
    broadcast_in_dim x1, local copies, waits for them, and re-layouts, left_environment(): spread = jnp.broadcast_to(maps[None], (segments,) + maps.shape)  2.08 us
  transfers between devices with their start and end apart: 11, of which 7 were waited for; matrix products, arithmetic and copies ran while one was open for 13% of the time, Pallas kernels for 0%

profile of v14, /device:TPU:8, one launch (start us, length us, event | category | flops | bytes accessed | tf_op | source)
XLA Modules:
  0.0 102.0 jit_solution(9892510690585741232)
XLA Ops:
  0.6 2.1 %broadcast_in_dim.16 = f32[8,2,128,128]{3,2,1,0:T(8,128)} broadcast(f32[2,128,128]{2,1,0:T(8,128)} %bitcast.263), dimensions={1,2,3} | broadcast | bytes 1179648 | tf_op jit(solution)/shard_map/broadcast_in_dim | solution.py:35
  2.7 5.8 %all-to-all-start = ((f32[8,2,128,128]{3,2,1,0:T(8,128)}), f32[8,2,128,128]{3,2,1,0:T(8,128)S(1)}, u32[]{:S(2)}, u32[]{:S(2)}) async-start(f32[8,2,128,128]{3,2,1,0:T(8,128)} %broadcast_in_dim.16), calls=%async_computation | async-start | bytes 2097152 | tf_op jit(solution)/shard_map/all_to_all | solution.py:36
  8.5 1.1 %convolution_bitcast_fusion.3 = f32[9,2,128,128]{2,3,0,1:T(8,128)S(1)} fusion(f32[1,2,128,128]{3,2,1,0:T(8,128)S(1)} %copy-done.6, f32[1,9,2,128,128]{4,3,2,1,0:T(8,128)S(1)} %copy-done), kind=kOutput, calls=%fused_computation.3 | convolution fusion | flops 226492416 | bytes 2490368 | tf_op jit(solution)/shard_map/kab,wkbc->wkac/dot_general | solution.py:29
  9.6 0.1 slice_bitcast_fusion.13
  9.7 3.1 %collective-permute-start = (f32[3,128,128]{1,2,0:T(8,128)S(1)}, f32[3,128,128]{1,2,0:T(8,128)S(1)}, u32[]{:S(2)}, u32[]{:S(2)}) collective-permute-start(f32[3,128,128]{1,2,0:T(8,128)S(1)} %get-tuple-element.23), channel_id=1, source_target_pairs={{0,1},{1,2},{2,3},{3,4},{4,5},{5,6},{6,7},{7,8},{8,9},{9,10},{10,1... | collective-permute-start | bytes 589832 | tf_op jit(solution)/shard_map/ppermute | solution.py:19
  12.8 1.3 %collective-permute-start.1 = (f32[3,128,128]{1,2,0:T(8,128)S(1)}, f32[3,128,128]{1,2,0:T(8,128)S(1)}, u32[]{:S(2)}, u32[]{:S(2)}) collective-permute-start(f32[3,128,128]{1,2,0:T(8,128)S(1)} %get-tuple-element.24), channel_id=1, source_target_pairs={{1,0},{2,1},{3,2},{4,3},{5,4},{6,5},{7,6},{8,7},{9,8},{10,9},{11,1... | collective-permute-start | bytes 589832 | tf_op jit(solution)/shard_map/ppermute | solution.py:19
  14.1 0.8 slice.154
  14.9 8.1 %all-to-all-done = f32[8,2,128,128]{3,2,1,0:T(8,128)S(1)} async-done(((f32[8,2,128,128]{3,2,1,0:T(8,128)}), f32[8,2,128,128]{3,2,1,0:T(8,128)S(1)}, u32[]{:S(2)}, u32[]{:S(2)}) %all-to-all-start) | async-done | bytes 1048608 | tf_op jit(solution)/shard_map/all_to_all | solution.py:36
  23.0 0.3 convolution_select_fusion.6
  23.3 0.3 convolution_select_fusion.5
  23.6 0.3 convolution_select_fusion.4
  23.9 0.3 convolution_select_fusion.3
  24.1 0.3 convolution_select_fusion.2
  24.4 0.3 convolution_select_fusion.1
  24.7 0.3 fusion.41
  25.0 0.7 convolution_bitcast_fusion.5
  25.7 0.6 fusion
  26.3 0.1 fusion.108
  26.5 0.9 copy-done.2
  27.3 1.1 %fusion.20 = f32[2,128,128,1]{2,1,3,0:T(8,128)S(1)} fusion(f32[3,1,128,128]{2,3,0,1:T(8,128)S(1)} %bitcast.265, f32[3,1,128,128]{2,3,0,1:T(8,128)S(1)} %get-tuple-element.25, f32[3,2,128,128]{2,3,0,1:T(8,128)S(1)} %copy-done.2, f32[3,1,128,128]{2,3,0,1:T(8,128)S(1)} %get-tuple-element.26, f32[3,1,128,128]{2,3,0,1:T(8,128)S(1)} %bitcast.264, ...), kind=kOutput, calls=%fused_computation.29 | convolution fusion | flops 228261888 | bytes 2490368 | tf_op jit(solution)/shard_map/wkab,wkbc->kac/dot_general | solution.py:29
  28.5 0.6 convolution_bitcast_fusion.2
  29.1 0.1 slice_bitcast_fusion.11
  29.2 3.1 %collective-permute-start.2 = (f32[3,128,128]{2,1,0:T(8,128)S(1)}, f32[3,128,128]{2,1,0:T(8,128)S(1)}, u32[]{:S(2)}, u32[]{:S(2)}) collective-permute-start(f32[3,128,128]{2,1,0:T(8,128)S(1)} %get-tuple-element.16), channel_id=1, source_target_pairs={{0,1},{1,2},{2,3},{3,4},{4,5},{5,6},{6,7},{7,8},{8,9},{9,10},{10,1... | collective-permute-start | bytes 589832 | tf_op jit(solution)/shard_map/ppermute | solution.py:19
  32.3 1.3 %collective-permute-start.3 = (f32[3,128,128]{2,1,0:T(8,128)S(1)}, f32[3,128,128]{2,1,0:T(8,128)S(1)}, u32[]{:S(2)}, u32[]{:S(2)}) collective-permute-start(f32[3,128,128]{2,1,0:T(8,128)S(1)} %get-tuple-element.17), channel_id=1, source_target_pairs={{1,0},{2,1},{3,2},{4,3},{5,4},{6,5},{7,6},{8,7},{9,8},{10,9},{11,1... | collective-permute-start | bytes 589832 | tf_op jit(solution)/shard_map/ppermute | solution.py:19
  33.6 1.1 %fusion.37 = f32[2,128,128]{2,1,0:T(8,128)S(1)} fusion(f32[3,1,128,128]{3,2,0,1:T(8,128)S(1)} %get-tuple-element.18, f32[3,1,128,128]{3,2,0,1:T(8,128)S(1)} %get-tuple-element.19, f32[3,2,128,128]{3,2,0,1:T(8,128)S(1)} %slice.158, f32[3,2,128,128]{2,3,0,1:T(8,128)S(1)} %get-tuple-element.21, f32[3,2,128,128]{2,3,0,1:T(8,128)S(1)} %get-tuple-element.22, ...), kind=kOutput, calls=%fused_computation.51 | convolution fusion | flops 228851712 | bytes 2097152 | tf_op jit(solution)/shard_map/wkab,wkbc->kac/dot_general | solution.py:29
  34.7 1.5 %collective-permute-done.2 = f32[3,128,128]{2,1,0:T(8,128)S(1)} collective-permute-done((f32[3,128,128]{2,1,0:T(8,128)S(1)}, f32[3,128,128]{2,1,0:T(8,128)S(1)}, u32[]{:S(2)}, u32[]{:S(2)}) %collective-permute-start.2) | collective-permute-done | bytes 196640 | tf_op jit(solution)/shard_map/ppermute | solution.py:19
  36.2 0.4 fusion.42
  36.6 4.0 %collective-permute-done.3 = f32[3,128,128]{2,1,0:T(8,128)S(1)} collective-permute-done((f32[3,128,128]{2,1,0:T(8,128)S(1)}, f32[3,128,128]{2,1,0:T(8,128)S(1)}, u32[]{:S(2)}, u32[]{:S(2)}) %collective-permute-start.3) | collective-permute-done | bytes 196640 | tf_op jit(solution)/shard_map/ppermute | solution.py:19
  40.5 0.4 fusion.43
  40.9 0.6 convolution_bitcast_fusion.1
  41.6 0.1 fusion.61
  41.7 0.7 broadcast_in_dim.17
  42.4 11.1 %all-to-all-start.1 = ((f32[32,3,128]{2,1,0:T(4,128)}), f32[32,3,128]{2,1,0:T(4,128)}, u32[]{:S(2)}, u32[]{:S(2)}) async-start(f32[32,3,128]{2,1,0:T(4,128)} %broadcast_in_dim.17), calls=%async_computation.1 | async-start | bytes 131072 | tf_op jit(solution)/shard_map/all_to_all | solution.py:25
  53.5 0.9 slice_bitcast_fusion.9
  54.4 0.8 slice.168
  55.2 3.6 %collective-permute-start.4 = (f32[3,128,128]{2,1,0:T(8,128)}, f32[3,128,128]{2,1,0:T(8,128)S(1)}, u32[]{:S(2)}, u32[]{:S(2)}) collective-permute-start(f32[3,128,128]{2,1,0:T(8,128)} %get-tuple-element.12), channel_id=1, source_target_pairs={{0,1},{1,2},{2,3},{3,4},{4,5},{5,6},{6,7},{7,8},{8,9},{9,10},{10,1... | collective-permute-start | bytes 589832 | tf_op jit(solution)/shard_map/ppermute | solution.py:19
  58.9 1.5 %collective-permute-start.5 = (f32[3,128,128]{2,1,0:T(8,128)}, f32[3,128,128]{2,1,0:T(8,128)S(1)}, u32[]{:S(2)}, u32[]{:S(2)}) collective-permute-start(f32[3,128,128]{2,1,0:T(8,128)} %get-tuple-element.13), channel_id=1, source_target_pairs={{1,0},{2,1},{3,2},{4,3},{5,4},{6,5},{7,6},{8,7},{9,8},{10,9},{11,1... | collective-permute-start | bytes 589832 | tf_op jit(solution)/shard_map/ppermute | solution.py:19
  60.3 3.2 %all-to-all-done.1 = f32[32,3,128]{2,1,0:T(4,128)} async-done(((f32[32,3,128]{2,1,0:T(4,128)}), f32[32,3,128]{2,1,0:T(4,128)}, u32[]{:S(2)}, u32[]{:S(2)}) %all-to-all-start.1) | async-done | bytes 49184 | tf_op jit(solution)/shard_map/all_to_all | solution.py:25
  63.5 0.9 reduce_sum.37
  64.4 0.2 broadcast_multiply_fusion
  64.6 0.8 copy-done.3
  65.4 0.0 copy-done.4
  65.5 0.1 copy-done.5
  65.6 1.1 %fusion.34 = f32[2,128,128]{2,1,0:T(8,128)S(1)} fusion(f32[9,2,128,128]{2,3,0,1:T(8,128)S(1)} %broadcast_multiply_fusion, f32[3,1,128,128]{3,2,0,1:T(8,128)S(1)} %copy-done.4, f32[3,1,128,128]{3,2,0,1:T(8,128)S(1)} %copy-done.5, f32[3,2,128,128]{3,2,0,1:T(8,128)S(1)} %copy-done.3), kind=kOutput, calls=%fused_computation.50 | convolution fusion | flops 228261888 | bytes 2097152 | tf_op jit(solution)/shard_map/wkab,wkbc->kac/dot_general | solution.py:29
  66.7 0.4 fusion.45
  67.1 0.4 fusion.44
  67.4 0.6 convolution_bitcast_fusion
  68.1 0.1 slice_bitcast_fusion.7
  68.2 3.3 %collective-permute-start.6 = (f32[3,128,128]{2,1,0:T(8,128)S(1)}, f32[3,128,128]{2,1,0:T(8,128)S(1)}, u32[]{:S(2)}, u32[]{:S(2)}) collective-permute-start(f32[3,128,128]{2,1,0:T(8,128)S(1)} %get-tuple-element.8), channel_id=1, source_target_pairs={{0,1},{1,2},{2,3},{3,4},{4,5},{5,6},{6,7},{7,8},{8,9},{9,10},{10,1... | collective-permute-start | bytes 589832 | tf_op jit(solution)/shard_map/ppermute | solution.py:19
  71.5 0.1 compare_convert_fusion
  71.6 1.3 %collective-permute-start.7 = (f32[3,128,128]{2,1,0:T(8,128)S(1)}, f32[3,128,128]{2,1,0:T(8,128)S(1)}, u32[]{:S(2)}, u32[]{:S(2)}) collective-permute-start(f32[3,128,128]{2,1,0:T(8,128)S(1)} %get-tuple-element.9), channel_id=1, source_target_pairs={{1,0},{2,1},{3,2},{4,3},{5,4},{6,5},{7,6},{8,7},{9,8},{10,9},{11,1... | collective-permute-start | bytes 589832 | tf_op jit(solution)/shard_map/ppermute | solution.py:19
  72.9 1.1 %fusion.40 = f32[2,128,128]{2,1,0:T(8,128)S(1)} fusion(f32[3,1,128,128]{3,2,0,1:T(8,128)S(1)} %get-tuple-element.10, f32[3,1,128,128]{3,2,0,1:T(8,128)S(1)} %get-tuple-element.11, f32[3,2,128,128]{3,2,0,1:T(8,128)S(1)} %slice.179, f32[3,2,128,128]{2,3,0,1:T(8,128)S(1)} %get-tuple-element.21, f32[3,2,128,128]{2,3,0,1:T(8,128)S(1)} %get-tuple-element.22, ...), kind=kOutput, calls=%fused_computation.52 | convolution fusion | flops 228851712 | bytes 2097152 | tf_op jit(solution)/shard_map/wkab,wkbc->kac/dot_general | solution.py:29
  74.0 0.6 collective-permute-done.6
  74.6 0.4 fusion.46
  75.0 4.3 %collective-permute-done.7 = f32[3,128,128]{2,1,0:T(8,128)S(1)} collective-permute-done((f32[3,128,128]{2,1,0:T(8,128)S(1)}, f32[3,128,128]{2,1,0:T(8,128)S(1)}, u32[]{:S(2)}, u32[]{:S(2)}) %collective-permute-start.7) | collective-permute-done | bytes 196640 | tf_op jit(solution)/shard_map/ppermute | solution.py:19
  79.2 0.4 fusion.47
  79.6 0.7 fusion.78
  80.3 0.1 fusion.62
  80.5 0.7 broadcast_in_dim.18
  81.2 9.4 %all-to-all-start.2 = ((f32[32,3,128]{2,1,0:T(4,128)}), f32[32,3,128]{2,1,0:T(4,128)S(1)}, u32[]{:S(2)}, u32[]{:S(2)}) async-start(f32[32,3,128]{2,1,0:T(4,128)} %broadcast_in_dim.18), calls=%async_computation.2 | async-start | bytes 131072 | tf_op jit(solution)/shard_map/all_to_all | solution.py:25
  91.3 0.3 fusion.71
  91.6 9.0 %all-to-all-done.2 = f32[32,3,128]{2,1,0:T(4,128)S(1)} async-done(((f32[32,3,128]{2,1,0:T(4,128)}), f32[32,3,128]{2,1,0:T(4,128)S(1)}, u32[]{:S(2)}, u32[]{:S(2)}) %all-to-all-start.2) | async-done | bytes 49184 | tf_op jit(solution)/shard_map/all_to_all | solution.py:25
  100.7 0.7 fusion.75
  101.4 0.7 multiply_bitcast_fusion
  (29 shorter events, 0.3 us)
Async XLA Ops:
  0.6 7.9 %copy-start = (f32[1,9,2,128,128]{4,3,2,1,0:T(8,128)S(1)}, f32[1,9,2,128,128]{4,3,2,1,0:T(8,128)}, u32[]{:S(2)}) copy-start(f32[1,9,2,128,128]{4,3,2,1,0:T(8,128)} %param.9) | copy-start | bytes 3538948
  2.7 5.8 %copy-start.6 = (f32[1,2,128,128]{3,2,1,0:T(8,128)S(1)}, f32[1,2,128,128]{3,2,1,0:T(8,128)}, u32[]{:S(2)}) copy-start(f32[1,2,128,128]{3,2,1,0:T(8,128)} %param.6) | copy-start | bytes 393220
  2.7 20.3 %all-to-all-start = ((f32[8,2,128,128]{3,2,1,0:T(8,128)}), f32[8,2,128,128]{3,2,1,0:T(8,128)S(1)}, u32[]{:S(2)}, u32[]{:S(2)}) async-start(f32[8,2,128,128]{3,2,1,0:T(8,128)} %broadcast_in_dim.16), calls=%async_computation | async-start | bytes 2097152 | tf_op jit(solution)/shard_map/all_to_all | solution.py:36
  9.6 5.3 %copy-start.7 = (s32[9,2]{0,1:T(2,128)S(1)}, s32[9,2]{0,1:T(2,128)}, u32[]{:S(2)}) copy-start(s32[9,2]{0,1:T(2,128)} %param.10) | copy-start | bytes 220
  9.7 16.8 %collective-permute-start = (f32[3,128,128]{1,2,0:T(8,128)S(1)}, f32[3,128,128]{1,2,0:T(8,128)S(1)}, u32[]{:S(2)}, u32[]{:S(2)}) collective-permute-start(f32[3,128,128]{1,2,0:T(8,128)S(1)} %get-tuple-element.23), channel_id=1, source_target_pairs={{0,1},{1,2},{2,3},{3,4},{4,5},{5,6},{6,7},{7,8},{8,9},{9,10},{10,1... | collective-permute-start | bytes 589832 | tf_op jit(solution)/shard_map/ppermute | solution.py:19
  12.8 13.7 %collective-permute-start.1 = (f32[3,128,128]{1,2,0:T(8,128)S(1)}, f32[3,128,128]{1,2,0:T(8,128)S(1)}, u32[]{:S(2)}, u32[]{:S(2)}) collective-permute-start(f32[3,128,128]{1,2,0:T(8,128)S(1)} %get-tuple-element.24), channel_id=1, source_target_pairs={{1,0},{2,1},{3,2},{4,3},{5,4},{6,5},{7,6},{8,7},{9,8},{10,9},{11,1... | collective-permute-start | bytes 589832 | tf_op jit(solution)/shard_map/ppermute | solution.py:19
  23.3 1.7 %copy-start.1 = (f32[9,2,128,128]{3,2,1,0:T(8,128)S(1)}, f32[9,2,128,128]{3,2,1,0:T(8,128)}, u32[]{:S(2)}) copy-start(f32[9,2,128,128]{3,2,1,0:T(8,128)} %param.7) | copy-start | bytes 3538948
  26.3 1.0 copy-start.2
  29.2 7.0 %collective-permute-start.2 = (f32[3,128,128]{2,1,0:T(8,128)S(1)}, f32[3,128,128]{2,1,0:T(8,128)S(1)}, u32[]{:S(2)}, u32[]{:S(2)}) collective-permute-start(f32[3,128,128]{2,1,0:T(8,128)S(1)} %get-tuple-element.16), channel_id=1, source_target_pairs={{0,1},{1,2},{2,3},{3,4},{4,5},{5,6},{6,7},{7,8},{8,9},{9,10},{10,1... | collective-permute-start | bytes 589832 | tf_op jit(solution)/shard_map/ppermute | solution.py:19
  32.3 8.2 %collective-permute-start.3 = (f32[3,128,128]{2,1,0:T(8,128)S(1)}, f32[3,128,128]{2,1,0:T(8,128)S(1)}, u32[]{:S(2)}, u32[]{:S(2)}) collective-permute-start(f32[3,128,128]{2,1,0:T(8,128)S(1)} %get-tuple-element.17), channel_id=1, source_target_pairs={{1,0},{2,1},{3,2},{4,3},{5,4},{6,5},{7,6},{8,7},{9,8},{10,9},{11,1... | collective-permute-start | bytes 589832 | tf_op jit(solution)/shard_map/ppermute | solution.py:19
  42.4 21.1 %all-to-all-start.1 = ((f32[32,3,128]{2,1,0:T(4,128)}), f32[32,3,128]{2,1,0:T(4,128)}, u32[]{:S(2)}, u32[]{:S(2)}) async-start(f32[32,3,128]{2,1,0:T(4,128)} %broadcast_in_dim.17), calls=%async_computation.1 | async-start | bytes 131072 | tf_op jit(solution)/shard_map/all_to_all | solution.py:25
  55.2 11.9 %collective-permute-start.4 = (f32[3,128,128]{2,1,0:T(8,128)}, f32[3,128,128]{2,1,0:T(8,128)S(1)}, u32[]{:S(2)}, u32[]{:S(2)}) collective-permute-start(f32[3,128,128]{2,1,0:T(8,128)} %get-tuple-element.12), channel_id=1, source_target_pairs={{0,1},{1,2},{2,3},{3,4},{4,5},{5,6},{6,7},{7,8},{8,9},{9,10},{10,1... | collective-permute-start | bytes 589832 | tf_op jit(solution)/shard_map/ppermute | solution.py:19
  58.9 7.9 %collective-permute-start.5 = (f32[3,128,128]{2,1,0:T(8,128)}, f32[3,128,128]{2,1,0:T(8,128)S(1)}, u32[]{:S(2)}, u32[]{:S(2)}) collective-permute-start(f32[3,128,128]{2,1,0:T(8,128)} %get-tuple-element.13), channel_id=1, source_target_pairs={{1,0},{2,1},{3,2},{4,3},{5,4},{6,5},{7,6},{8,7},{9,8},{10,9},{11,1... | collective-permute-start | bytes 589832 | tf_op jit(solution)/shard_map/ppermute | solution.py:19
  64.4 1.0 copy-start.3
  64.4 1.0 %copy-start.4 = (f32[3,1,128,128]{3,2,0,1:T(8,128)S(1)}, f32[3,1,128,128]{3,2,0,1:T(8,128)}, u32[]{:S(2)}) copy-start(f32[3,1,128,128]{3,2,0,1:T(8,128)} %get-tuple-element.14) | copy-start | bytes 589828
  64.4 1.1 %copy-start.5 = (f32[3,1,128,128]{3,2,0,1:T(8,128)S(1)}, f32[3,1,128,128]{3,2,0,1:T(8,128)}, u32[]{:S(2)}) copy-start(f32[3,1,128,128]{3,2,0,1:T(8,128)} %get-tuple-element.15) | copy-start | bytes 589828
  68.1 3.4 %copy-start.8 = (s32[1,2]{1,0:T(1,128)S(1)}, s32[1,2]{1,0:T(1,128)}, u32[]{:S(2)}) copy-start(s32[1,2]{1,0:T(1,128)} %param.11) | copy-start | bytes 28
  68.2 6.4 %collective-permute-start.6 = (f32[3,128,128]{2,1,0:T(8,128)S(1)}, f32[3,128,128]{2,1,0:T(8,128)S(1)}, u32[]{:S(2)}, u32[]{:S(2)}) collective-permute-start(f32[3,128,128]{2,1,0:T(8,128)S(1)} %get-tuple-element.8), channel_id=1, source_target_pairs={{0,1},{1,2},{2,3},{3,4},{4,5},{5,6},{6,7},{7,8},{8,9},{9,10},{10,1... | collective-permute-start | bytes 589832 | tf_op jit(solution)/shard_map/ppermute | solution.py:19
  71.6 7.7 %collective-permute-start.7 = (f32[3,128,128]{2,1,0:T(8,128)S(1)}, f32[3,128,128]{2,1,0:T(8,128)S(1)}, u32[]{:S(2)}, u32[]{:S(2)}) collective-permute-start(f32[3,128,128]{2,1,0:T(8,128)S(1)} %get-tuple-element.9), channel_id=1, source_target_pairs={{1,0},{2,1},{3,2},{4,3},{5,4},{6,5},{7,6},{8,7},{9,8},{10,9},{11,1... | collective-permute-start | bytes 589832 | tf_op jit(solution)/shard_map/ppermute | solution.py:19
  81.2 19.4 %all-to-all-start.2 = ((f32[32,3,128]{2,1,0:T(4,128)}), f32[32,3,128]{2,1,0:T(4,128)S(1)}, u32[]{:S(2)}, u32[]{:S(2)}) async-start(f32[32,3,128]{2,1,0:T(4,128)} %broadcast_in_dim.18), calls=%async_computation.2 | async-start | bytes 131072 | tf_op jit(solution)/shard_map/all_to_all | solution.py:25

commit v15 on v14

--- a/solution.py
+++ b/solution.py
@@ -21,8 +21,9 @@
 
 def gathered_sums(values, axis):
     count = lax.axis_size(axis)
-    spread = jnp.broadcast_to(values[None, :, None], (count, values.shape[0], 128))
-    return jnp.sum(lax.all_to_all(spread, axis, 0, 0, tiled=True), axis=0)
+    rows = jnp.concatenate([values, jnp.zeros((8 - values.shape[0],), values.dtype)])
+    spread = jnp.broadcast_to(rows[None, :, None], (count, 8, 128))
+    return jnp.sum(lax.all_to_all(spread, axis, 0, 0, tiled=True), axis=0)[: values.shape[0]]
 
 
 def mm(spec, a, b, precision=HIGH):

time: 103 us -> 104 us (level)
  matrix products: 13.1 us -> 16 us
  local copies, waits for them, and re-layouts: 8.11 us -> 5.47 us
  waiting for transfers between devices: 30.7 us -> 32.1 us
    dot_general x24, matrix products: 13.1 us -> 16 us  [mm(): return jnp.einsum(spec, a, b, precision=precision)]
    slice x4, local copies, waits for them, and re-layouts: 1.63 us -> 0.11 us  [combine(): terms = jnp.concatenate([lower, products[1::3], upper], axis=0)]
    ppermute x8, waiting for transfers between devices: 10.3 us -> 11.5 us  [shifted(): return lax.ppermute(block, axis, route)]
    unnamed x18 -> x12, local copies, waits for them, and re-layouts: 1.82 us -> 0.76 us
  transfers between devices with their start and end apart: 11 -> 11, of which waited for: 7 -> 8; matrix products, arithmetic and copies ran while one was open for 13% -> 12% of each run, Pallas kernels for 0% -> 0%
where the time goes in v15:
time: 104 us
  starting transfers between devices  45.4 us (44%)
  waiting for transfers between devices  32.1 us (31%)
  matrix products  16 us (15%)
  local copies, waits for them, and re-layouts  5.47 us (5%)
  other arithmetic  2.77 us (3%)
  between operations  1.77 us (2%)
    all_to_all x2, starting transfers between devices, gathered_sums(): lax.all_to_all(spread, axis, 0, 0, tiled=True)  20.4 us
    ppermute x8, starting transfers between devices, shifted(): return lax.ppermute(block, axis, route)  19.3 us
    dot_general x24, matrix products, mm(): return jnp.einsum(spec, a, b, precision=precision)  16 us
    all_to_all x2, waiting for transfers between devices, gathered_sums(): lax.all_to_all(spread, axis, 0, 0, tiled=True)  12.4 us
    ppermute x8, waiting for transfers between devices, shifted(): return lax.ppermute(block, axis, route)  11.5 us
    all_to_all x1, waiting for transfers between devices, left_environment(): every = lax.all_to_all(spread, 'seg', 0, 0, tiled=True)  8.21 us
    all_to_all x1, starting transfers between devices, left_environment(): every = lax.all_to_all(spread, 'seg', 0, 0, tiled=True)  5.78 us
  transfers between devices with their start and end apart: 11, of which 8 were waited for; matrix products, arithmetic and copies ran while one was open for 12% of the time, Pallas kernels for 0%

profile of v15, /device:TPU:8, one launch (start us, length us, event | category | flops | bytes accessed | tf_op | source)
XLA Modules:
  0.0 103.6 jit_solution(13118069986920546419)
XLA Ops:
  0.6 0.0 copy-start
  0.6 2.1 %broadcast_in_dim.16 = f32[8,2,128,128]{3,2,1,0:T(8,128)} broadcast(f32[2,128,128]{2,1,0:T(8,128)} %bitcast.260), dimensions={1,2,3} | broadcast | bytes 1179648 | tf_op jit(solution)/shard_map/broadcast_in_dim | solution.py:36
  2.7 5.8 %all-to-all-start = ((f32[8,2,128,128]{3,2,1,0:T(8,128)}), f32[8,2,128,128]{3,2,1,0:T(8,128)S(1)}, u32[]{:S(2)}, u32[]{:S(2)}) async-start(f32[8,2,128,128]{3,2,1,0:T(8,128)} %broadcast_in_dim.16), calls=%async_computation | async-start | bytes 2097152 | tf_op jit(solution)/shard_map/all_to_all | solution.py:37
  8.5 1.1 %convolution_bitcast_fusion.3 = f32[9,2,128,128]{2,3,0,1:T(8,128)S(1)} fusion(f32[1,2,128,128]{3,2,1,0:T(8,128)S(1)} %copy-done.3, f32[1,9,2,128,128]{4,3,2,1,0:T(8,128)S(1)} %copy-done), kind=kOutput, calls=%fused_computation.3 | convolution fusion | flops 226492416 | bytes 2490368 | tf_op jit(solution)/shard_map/kab,wkbc->wkac/dot_general | solution.py:30
  9.6 0.0 copy-start.4
  9.6 0.1 slice_bitcast_fusion.13
  9.7 3.8 %collective-permute-start = (f32[3,128,128]{1,2,0:T(8,128)S(1)}, f32[3,128,128]{1,2,0:T(8,128)}, u32[]{:S(2)}, u32[]{:S(2)}) collective-permute-start(f32[3,128,128]{1,2,0:T(8,128)S(1)} %get-tuple-element.23), channel_id=1, source_target_pairs={{0,1},{1,2},{2,3},{3,4},{4,5},{5,6},{6,7},{7,8},{8,9},{9,10},{10,1... | collective-permute-start | bytes 589832 | tf_op jit(solution)/shard_map/ppermute | solution.py:19
  13.4 1.3 %collective-permute-start.1 = (f32[3,128,128]{1,2,0:T(8,128)S(1)}, f32[3,128,128]{1,2,0:T(8,128)}, u32[]{:S(2)}, u32[]{:S(2)}) collective-permute-start(f32[3,128,128]{1,2,0:T(8,128)S(1)} %get-tuple-element.24), channel_id=1, source_target_pairs={{1,0},{2,1},{3,2},{4,3},{5,4},{6,5},{7,6},{8,7},{9,8},{10,9},{11,1... | collective-permute-start | bytes 589832 | tf_op jit(solution)/shard_map/ppermute | solution.py:19
  14.8 8.2 %all-to-all-done = f32[8,2,128,128]{3,2,1,0:T(8,128)S(1)} async-done(((f32[8,2,128,128]{3,2,1,0:T(8,128)}), f32[8,2,128,128]{3,2,1,0:T(8,128)S(1)}, u32[]{:S(2)}, u32[]{:S(2)}) %all-to-all-start) | async-done | bytes 1048608 | tf_op jit(solution)/shard_map/all_to_all | solution.py:37
  23.0 0.3 convolution_select_fusion.6
  23.3 0.0 copy-start.1
  23.3 0.3 convolution_select_fusion.5
  23.6 0.3 convolution_select_fusion.4
  23.9 0.3 convolution_select_fusion.3
  24.1 0.3 convolution_select_fusion.2
  24.4 0.3 convolution_select_fusion.1
  24.7 0.3 fusion.41
  25.0 0.7 convolution_bitcast_fusion.5
  25.7 0.6 fusion
  26.3 0.1 fusion.108
  26.5 0.0 collective-permute-done.1
  26.5 2.1 %fusion.20 = f32[2,128,128,1]{2,1,3,0:T(8,128)S(1)} fusion(f32[3,1,128,128]{2,3,0,1:T(8,128)} %bitcast.20, f32[3,1,128,128]{2,3,0,1:T(8,128)S(1)} %get-tuple-element.25, f32[3,2,128,128]{2,3,0,1:T(8,128)S(1)} %slice.162, f32[3,1,128,128]{2,3,0,1:T(8,128)S(1)} %get-tuple-element.26, f32[3,1,128,128]{2,3,0,1:T(8,128)} %bitcast.18, ...), kind=kOutput, calls=%fused_computation.29 | convolution fusion | flops 228261888 | bytes 2490368 | tf_op jit(solution)/shard_map/wkab,wkbc->kac/dot_general | solution.py:30
  28.6 0.6 convolution_bitcast_fusion.2
  29.2 0.1 slice_bitcast_fusion.11
  29.3 3.1 %collective-permute-start.2 = (f32[3,128,128]{2,1,0:T(8,128)S(1)}, f32[3,128,128]{2,1,0:T(8,128)S(1)}, u32[]{:S(2)}, u32[]{:S(2)}) collective-permute-start(f32[3,128,128]{2,1,0:T(8,128)S(1)} %get-tuple-element.16), channel_id=1, source_target_pairs={{0,1},{1,2},{2,3},{3,4},{4,5},{5,6},{6,7},{7,8},{8,9},{9,10},{10,1... | collective-permute-start | bytes 589832 | tf_op jit(solution)/shard_map/ppermute | solution.py:19
  32.4 1.3 %collective-permute-start.3 = (f32[3,128,128]{2,1,0:T(8,128)S(1)}, f32[3,128,128]{2,1,0:T(8,128)S(1)}, u32[]{:S(2)}, u32[]{:S(2)}) collective-permute-start(f32[3,128,128]{2,1,0:T(8,128)S(1)} %get-tuple-element.17), channel_id=1, source_target_pairs={{1,0},{2,1},{3,2},{4,3},{5,4},{6,5},{7,6},{8,7},{9,8},{10,9},{11,1... | collective-permute-start | bytes 589832 | tf_op jit(solution)/shard_map/ppermute | solution.py:19
  33.7 1.1 %fusion.37 = f32[2,128,128]{2,1,0:T(8,128)S(1)} fusion(f32[3,1,128,128]{3,2,0,1:T(8,128)S(1)} %get-tuple-element.18, f32[3,1,128,128]{3,2,0,1:T(8,128)S(1)} %get-tuple-element.19, f32[3,2,128,128]{3,2,0,1:T(8,128)S(1)} %slice.166, f32[3,2,128,128]{2,3,0,1:T(8,128)S(1)} %get-tuple-element.21, f32[3,2,128,128]{2,3,0,1:T(8,128)S(1)} %get-tuple-element.22, ...), kind=kOutput, calls=%fused_computation.51 | convolution fusion | flops 228851712 | bytes 2097152 | tf_op jit(solution)/shard_map/wkab,wkbc->kac/dot_general | solution.py:30
  34.9 1.5 %collective-permute-done.2 = f32[3,128,128]{2,1,0:T(8,128)S(1)} collective-permute-done((f32[3,128,128]{2,1,0:T(8,128)S(1)}, f32[3,128,128]{2,1,0:T(8,128)S(1)}, u32[]{:S(2)}, u32[]{:S(2)}) %collective-permute-start.2) | collective-permute-done | bytes 196640 | tf_op jit(solution)/shard_map/ppermute | solution.py:19
  36.3 0.4 fusion.42
  36.7 4.0 %collective-permute-done.3 = f32[3,128,128]{2,1,0:T(8,128)S(1)} collective-permute-done((f32[3,128,128]{2,1,0:T(8,128)S(1)}, f32[3,128,128]{2,1,0:T(8,128)S(1)}, u32[]{:S(2)}, u32[]{:S(2)}) %collective-permute-start.3) | collective-permute-done | bytes 196640 | tf_op jit(solution)/shard_map/ppermute | solution.py:19
  40.6 0.4 fusion.43
  41.0 0.1 fusion.61
  41.2 0.7 broadcast_in_dim.17
  41.9 11.0 %all-to-all-start.1 = ((f32[32,8,128]{2,1,0:T(8,128)}), f32[32,8,128]{2,1,0:T(8,128)S(1)}, u32[]{:S(2)}, u32[]{:S(2)}) async-start(f32[32,8,128]{2,1,0:T(8,128)} %broadcast_in_dim.17), calls=%async_computation.1 | async-start | bytes 262144 | tf_op jit(solution)/shard_map/all_to_all | solution.py:26
  52.9 0.6 convolution_bitcast_fusion.1
  53.6 0.8 slice_bitcast_fusion.9
  54.4 4.4 %collective-permute-start.4 = (f32[3,128,128]{2,1,0:T(8,128)S(1)}, f32[3,128,128]{2,1,0:T(8,128)}, u32[]{:S(2)}, u32[]{:S(2)}) collective-permute-start(f32[3,128,128]{2,1,0:T(8,128)S(1)} %get-tuple-element.12), channel_id=1, source_target_pairs={{0,1},{1,2},{2,3},{3,4},{4,5},{5,6},{6,7},{7,8},{8,9},{9,10},{10,1... | collective-permute-start | bytes 589832 | tf_op jit(solution)/shard_map/ppermute | solution.py:19
  58.8 1.5 %collective-permute-start.5 = (f32[3,128,128]{2,1,0:T(8,128)}, f32[3,128,128]{2,1,0:T(8,128)}, u32[]{:S(2)}, u32[]{:S(2)}) collective-permute-start(f32[3,128,128]{2,1,0:T(8,128)} %get-tuple-element.13), channel_id=1, source_target_pairs={{1,0},{2,1},{3,2},{4,3},{5,4},{6,5},{7,6},{8,7},{9,8},{10,9},{11,1... | collective-permute-start | bytes 589832 | tf_op jit(solution)/shard_map/ppermute | solution.py:19
  60.2 3.1 %all-to-all-done.1 = f32[32,8,128]{2,1,0:T(8,128)S(1)} async-done(((f32[32,8,128]{2,1,0:T(8,128)}), f32[32,8,128]{2,1,0:T(8,128)S(1)}, u32[]{:S(2)}, u32[]{:S(2)}) %all-to-all-start.1) | async-done | bytes 131104 | tf_op jit(solution)/shard_map/all_to_all | solution.py:26
  63.4 0.2 broadcast_multiply_fusion
  63.6 0.7 copy-done.2
  64.3 1.1 %fusion.34 = f32[2,128,128]{2,1,0:T(8,128)S(1)} fusion(f32[9,2,128,128]{2,3,0,1:T(8,128)S(1)} %broadcast_multiply_fusion, f32[3,1,128,128]{3,2,0,1:T(8,128)S(1)} %get-tuple-element.14, f32[3,1,128,128]{3,2,0,1:T(8,128)S(1)} %copy-done.2, f32[3,2,128,128]{3,2,0,1:T(8,128)S(1)} %slice.176), kind=kOutput, calls=%fused_computation.50 | convolution fusion | flops 228261888 | bytes 2097152 | tf_op jit(solution)/shard_map/wkab,wkbc->kac/dot_general | solution.py:30
  65.5 1.2 %collective-permute-done.5 = f32[3,128,128]{2,1,0:T(8,128)} collective-permute-done((f32[3,128,128]{2,1,0:T(8,128)}, f32[3,128,128]{2,1,0:T(8,128)}, u32[]{:S(2)}, u32[]{:S(2)}) %collective-permute-start.5) | collective-permute-done | bytes 196640 | tf_op jit(solution)/shard_map/ppermute | solution.py:19
  66.6 1.3 %fusion.45 = f32[128,128]{1,0:T(8,128)S(1)} fusion(f32[3,128,128]{2,1,0:T(8,128)} %collective-permute-done.5, f32[9,2,128,128]{2,3,0,1:T(8,128)S(1)} %broadcast_multiply_fusion, f32[2,128,128]{2,1,0:T(8,128)S(1)} %fusion.34), kind=kOutput, calls=%fused_computation.63 | convolution fusion | flops 37765120 | bytes 524288 | tf_op jit(solution)/shard_map/wab,wbc->ac/dot_general | solution.py:30
  67.9 1.3 %fusion.44 = f32[128,128]{1,0:T(8,128)S(1)} fusion(f32[3,128,128]{2,1,0:T(8,128)} %collective-permute-done.4, f32[9,2,128,128]{2,3,0,1:T(8,128)S(1)} %broadcast_multiply_fusion, f32[2,128,128]{2,1,0:T(8,128)S(1)} %fusion.34), kind=kOutput, calls=%fused_computation.62 | convolution fusion | flops 37765120 | bytes 524288 | tf_op jit(solution)/shard_map/wab,wbc->ac/dot_general | solution.py:30
  69.2 0.6 convolution_bitcast_fusion
  69.9 0.0 copy-start.5
  69.9 0.1 slice_bitcast_fusion.7
  69.9 2.7 %collective-permute-start.6 = (f32[3,128,128]{2,1,0:T(8,128)S(1)}, f32[3,128,128]{2,1,0:T(8,128)S(1)}, u32[]{:S(2)}, u32[]{:S(2)}) collective-permute-start(f32[3,128,128]{2,1,0:T(8,128)S(1)} %get-tuple-element.8), channel_id=1, source_target_pairs={{0,1},{1,2},{2,3},{3,4},{4,5},{5,6},{6,7},{7,8},{8,9},{9,10},{10,1... | collective-permute-start | bytes 589832 | tf_op jit(solution)/shard_map/ppermute | solution.py:19
  72.7 0.1 compare_convert_fusion
  72.8 1.3 %collective-permute-start.7 = (f32[3,128,128]{2,1,0:T(8,128)S(1)}, f32[3,128,128]{2,1,0:T(8,128)S(1)}, u32[]{:S(2)}, u32[]{:S(2)}) collective-permute-start(f32[3,128,128]{2,1,0:T(8,128)S(1)} %get-tuple-element.9), channel_id=1, source_target_pairs={{1,0},{2,1},{3,2},{4,3},{5,4},{6,5},{7,6},{8,7},{9,8},{10,9},{11,1... | collective-permute-start | bytes 589832 | tf_op jit(solution)/shard_map/ppermute | solution.py:19
  74.1 1.1 %fusion.40 = f32[2,128,128]{2,1,0:T(8,128)S(1)} fusion(f32[3,1,128,128]{3,2,0,1:T(8,128)S(1)} %get-tuple-element.10, f32[3,1,128,128]{3,2,0,1:T(8,128)S(1)} %get-tuple-element.11, f32[3,2,128,128]{3,2,0,1:T(8,128)S(1)} %slice.187, f32[3,2,128,128]{2,3,0,1:T(8,128)S(1)} %get-tuple-element.21, f32[3,2,128,128]{2,3,0,1:T(8,128)S(1)} %get-tuple-element.22, ...), kind=kOutput, calls=%fused_computation.52 | convolution fusion | flops 228851712 | bytes 2097152 | tf_op jit(solution)/shard_map/wkab,wkbc->kac/dot_general | solution.py:30
  75.2 0.6 collective-permute-done.6
  75.8 0.4 fusion.46
  76.2 4.3 %collective-permute-done.7 = f32[3,128,128]{2,1,0:T(8,128)S(1)} collective-permute-done((f32[3,128,128]{2,1,0:T(8,128)S(1)}, f32[3,128,128]{2,1,0:T(8,128)S(1)}, u32[]{:S(2)}, u32[]{:S(2)}) %collective-permute-start.7) | collective-permute-done | bytes 196640 | tf_op jit(solution)/shard_map/ppermute | solution.py:19
  80.5 0.4 fusion.47
  80.8 0.7 fusion.78
  81.6 0.1 fusion.62
  81.7 0.7 broadcast_in_dim.18
  82.4 9.4 %all-to-all-start.2 = ((f32[32,8,128]{2,1,0:T(8,128)}), f32[32,8,128]{2,1,0:T(8,128)S(1)}, u32[]{:S(2)}, u32[]{:S(2)}) async-start(f32[32,8,128]{2,1,0:T(8,128)} %broadcast_in_dim.18), calls=%async_computation.2 | async-start | bytes 262144 | tf_op jit(solution)/shard_map/all_to_all | solution.py:26
  92.5 0.3 fusion.71
  92.9 9.3 %all-to-all-done.2 = f32[32,8,128]{2,1,0:T(8,128)S(1)} async-done(((f32[32,8,128]{2,1,0:T(8,128)}), f32[32,8,128]{2,1,0:T(8,128)S(1)}, u32[]{:S(2)}, u32[]{:S(2)}) %all-to-all-start.2) | async-done | bytes 131104 | tf_op jit(solution)/shard_map/all_to_all | solution.py:26
  102.2 0.7 fusion.75
  102.9 0.7 multiply_bitcast_fusion
  (25 shorter events, 0.3 us)
Async XLA Ops:
  0.6 7.9 %copy-start = (f32[1,9,2,128,128]{4,3,2,1,0:T(8,128)S(1)}, f32[1,9,2,128,128]{4,3,2,1,0:T(8,128)}, u32[]{:S(2)}) copy-start(f32[1,9,2,128,128]{4,3,2,1,0:T(8,128)} %param.9) | copy-start | bytes 3538948
  2.7 5.8 %copy-start.3 = (f32[1,2,128,128]{3,2,1,0:T(8,128)S(1)}, f32[1,2,128,128]{3,2,1,0:T(8,128)}, u32[]{:S(2)}) copy-start(f32[1,2,128,128]{3,2,1,0:T(8,128)} %param.6) | copy-start | bytes 393220
  2.7 20.3 %all-to-all-start = ((f32[8,2,128,128]{3,2,1,0:T(8,128)}), f32[8,2,128,128]{3,2,1,0:T(8,128)S(1)}, u32[]{:S(2)}, u32[]{:S(2)}) async-start(f32[8,2,128,128]{3,2,1,0:T(8,128)} %broadcast_in_dim.16), calls=%async_computation | async-start | bytes 2097152 | tf_op jit(solution)/shard_map/all_to_all | solution.py:37
  9.6 5.2 %copy-start.4 = (s32[9,2]{0,1:T(2,128)S(1)}, s32[9,2]{0,1:T(2,128)}, u32[]{:S(2)}) copy-start(s32[9,2]{0,1:T(2,128)} %param.10) | copy-start | bytes 220
  9.7 16.8 %collective-permute-start = (f32[3,128,128]{1,2,0:T(8,128)S(1)}, f32[3,128,128]{1,2,0:T(8,128)}, u32[]{:S(2)}, u32[]{:S(2)}) collective-permute-start(f32[3,128,128]{1,2,0:T(8,128)S(1)} %get-tuple-element.23), channel_id=1, source_target_pairs={{0,1},{1,2},{2,3},{3,4},{4,5},{5,6},{6,7},{7,8},{8,9},{9,10},{10,1... | collective-permute-start | bytes 589832 | tf_op jit(solution)/shard_map/ppermute | solution.py:19
  13.4 13.0 %collective-permute-start.1 = (f32[3,128,128]{1,2,0:T(8,128)S(1)}, f32[3,128,128]{1,2,0:T(8,128)}, u32[]{:S(2)}, u32[]{:S(2)}) collective-permute-start(f32[3,128,128]{1,2,0:T(8,128)S(1)} %get-tuple-element.24), channel_id=1, source_target_pairs={{1,0},{2,1},{3,2},{4,3},{5,4},{6,5},{7,6},{8,7},{9,8},{10,9},{11,1... | collective-permute-start | bytes 589832 | tf_op jit(solution)/shard_map/ppermute | solution.py:19
  23.3 1.7 %copy-start.1 = (f32[9,2,128,128]{3,2,1,0:T(8,128)S(1)}, f32[9,2,128,128]{3,2,1,0:T(8,128)}, u32[]{:S(2)}) copy-start(f32[9,2,128,128]{3,2,1,0:T(8,128)} %param.7) | copy-start | bytes 3538948
  29.3 7.0 %collective-permute-start.2 = (f32[3,128,128]{2,1,0:T(8,128)S(1)}, f32[3,128,128]{2,1,0:T(8,128)S(1)}, u32[]{:S(2)}, u32[]{:S(2)}) collective-permute-start(f32[3,128,128]{2,1,0:T(8,128)S(1)} %get-tuple-element.16), channel_id=1, source_target_pairs={{0,1},{1,2},{2,3},{3,4},{4,5},{5,6},{6,7},{7,8},{8,9},{9,10},{10,1... | collective-permute-start | bytes 589832 | tf_op jit(solution)/shard_map/ppermute | solution.py:19
  32.4 8.2 %collective-permute-start.3 = (f32[3,128,128]{2,1,0:T(8,128)S(1)}, f32[3,128,128]{2,1,0:T(8,128)S(1)}, u32[]{:S(2)}, u32[]{:S(2)}) collective-permute-start(f32[3,128,128]{2,1,0:T(8,128)S(1)} %get-tuple-element.17), channel_id=1, source_target_pairs={{1,0},{2,1},{3,2},{4,3},{5,4},{6,5},{7,6},{8,7},{9,8},{10,9},{11,1... | collective-permute-start | bytes 589832 | tf_op jit(solution)/shard_map/ppermute | solution.py:19
  41.9 21.4 %all-to-all-start.1 = ((f32[32,8,128]{2,1,0:T(8,128)}), f32[32,8,128]{2,1,0:T(8,128)S(1)}, u32[]{:S(2)}, u32[]{:S(2)}) async-start(f32[32,8,128]{2,1,0:T(8,128)} %broadcast_in_dim.17), calls=%async_computation.1 | async-start | bytes 262144 | tf_op jit(solution)/shard_map/all_to_all | solution.py:26
  54.4 13.5 %collective-permute-start.4 = (f32[3,128,128]{2,1,0:T(8,128)S(1)}, f32[3,128,128]{2,1,0:T(8,128)}, u32[]{:S(2)}, u32[]{:S(2)}) collective-permute-start(f32[3,128,128]{2,1,0:T(8,128)S(1)} %get-tuple-element.12), channel_id=1, source_target_pairs={{0,1},{1,2},{2,3},{3,4},{4,5},{5,6},{6,7},{7,8},{8,9},{9,10},{10,1... | collective-permute-start | bytes 589832 | tf_op jit(solution)/shard_map/ppermute | solution.py:19
  58.8 7.9 %collective-permute-start.5 = (f32[3,128,128]{2,1,0:T(8,128)}, f32[3,128,128]{2,1,0:T(8,128)}, u32[]{:S(2)}, u32[]{:S(2)}) collective-permute-start(f32[3,128,128]{2,1,0:T(8,128)} %get-tuple-element.13), channel_id=1, source_target_pairs={{1,0},{2,1},{3,2},{4,3},{5,4},{6,5},{7,6},{8,7},{9,8},{10,9},{11,1... | collective-permute-start | bytes 589832 | tf_op jit(solution)/shard_map/ppermute | solution.py:19
  63.4 0.9 copy-start.2
  69.9 2.8 %copy-start.5 = (s32[1,2]{1,0:T(1,128)S(1)}, s32[1,2]{1,0:T(1,128)}, u32[]{:S(2)}) copy-start(s32[1,2]{1,0:T(1,128)} %param.11) | copy-start | bytes 28
  69.9 5.9 %collective-permute-start.6 = (f32[3,128,128]{2,1,0:T(8,128)S(1)}, f32[3,128,128]{2,1,0:T(8,128)S(1)}, u32[]{:S(2)}, u32[]{:S(2)}) collective-permute-start(f32[3,128,128]{2,1,0:T(8,128)S(1)} %get-tuple-element.8), channel_id=1, source_target_pairs={{0,1},{1,2},{2,3},{3,4},{4,5},{5,6},{6,7},{7,8},{8,9},{9,10},{10,1... | collective-permute-start | bytes 589832 | tf_op jit(solution)/shard_map/ppermute | solution.py:19
  72.8 7.7 %collective-permute-start.7 = (f32[3,128,128]{2,1,0:T(8,128)S(1)}, f32[3,128,128]{2,1,0:T(8,128)S(1)}, u32[]{:S(2)}, u32[]{:S(2)}) collective-permute-start(f32[3,128,128]{2,1,0:T(8,128)S(1)} %get-tuple-element.9), channel_id=1, source_target_pairs={{1,0},{2,1},{3,2},{4,3},{5,4},{6,5},{7,6},{8,7},{9,8},{10,9},{11,1... | collective-permute-start | bytes 589832 | tf_op jit(solution)/shard_map/ppermute | solution.py:19
  82.4 19.7 %all-to-all-start.2 = ((f32[32,8,128]{2,1,0:T(8,128)}), f32[32,8,128]{2,1,0:T(8,128)S(1)}, u32[]{:S(2)}, u32[]{:S(2)}) async-start(f32[32,8,128]{2,1,0:T(8,128)} %broadcast_in_dim.18), calls=%async_computation.2 | async-start | bytes 262144 | tf_op jit(solution)/shard_map/all_to_all | solution.py:26
